TPU v7x, 128 devices: a whole 4x4x4 slice. The times are simulated.
128 devices in a mesh: section: 8 (over x, core), expert: 16 (over z, y).
Axes of the slice: x: 4, y: 4, z: 4, core: 2. Of those that a mesh axis runs over, the one named last changes fastest.
Arguments:
- inputs: bfloat16 [4, 512, 4096], P(None, 'expert'), may hold values from -6 to 6
- cotangent: bfloat16 [4, 512, 4096], P(None, 'expert'), may hold values from -6 to 6
- gain: float32 [8, 4096], P('section'), may hold values from 0.25 to 1.75
- route: int32 [8, 4, 512, 2], P('section', None, 'expert'), may hold values from 0 to 15, all different within a row; in each aligned block of 32 rows (0 to 31, 32 to 63, ..., all dimensions but the last counted through in order) at most 4 rows name the same one
- gate: float32 [8, 4, 512, 2], P('section', None, 'expert'), may hold values from 0.3 to 1
- w_gate: bfloat16 [8, 16, 4096, 768], P('section', 'expert'), may hold values from -0.09375 to 0.09375
- w_up: bfloat16 [8, 16, 4096, 768], P('section', 'expert'), may hold values from -0.09375 to 0.09375
- w_down: bfloat16 [8, 16, 768, 4096], P('section', 'expert'), may hold values from -0.21875 to 0.21875
Outputs:
- hidden: bfloat16 [8, 4, 512, 4096], P('section', None, 'expert')
- grads: bfloat16 [8, 4, 512, 4096], P('section', None, 'expert')
Inputs may be any that keep to these rules, and one draw needn't show every extreme that they name: `route`: each token names 2 different experts. Among the 32 tokens that one device holds of one micro-batch in one section, no expert is named by more than 4 tokens, a bound that some block reaches.
All inputs are finite; a program needn't handle non-finite values.
Results may differ from a plain program's by a relative error of at most 0.03.
Values may be sent and summed in bfloat16 or wider, within the bound.
No kernel may reach another device: no remote copies, remote signals or barrier semaphores. Data moves between devices by JAX's collectives and lax.ppermute only.
A program may use at most 64 MiB of HBM per device.

v0:
```python
import jax
import jax.numpy as jnp
from jax import lax
from jax.sharding import PartitionSpec as P

EPS = 1e-06


def passed_along(value, axis, steps):
    count = lax.axis_size(axis)
    leading, last = (max(0, -steps), min(count, count - steps))
    return lax.ppermute(value, axis, [(source, source + steps) for source in range(leading, last)])


def slot_places(route, experts, capacity):
    flat = route.reshape(-1)
    onehot = (flat[:, None] == jnp.arange(experts, dtype=jnp.int32)[None, :]).astype(jnp.int32)
    before = jnp.cumsum(onehot, axis=0) - onehot
    slot = jnp.sum(before * onehot, axis=1)
    return (flat * capacity + slot).reshape(route.shape)


def slot_table(places, total_rows):
    grid = jnp.arange(total_rows, dtype=jnp.int32)
    return (places.T[:, :, None] == grid[None, None, :]).astype(jnp.bfloat16)


def normalize(tokens, gain):
    values = tokens.astype(jnp.float32)
    scale = lax.rsqrt(jnp.mean(values * values, axis=-1, keepdims=True) + EPS)
    return (values, scale, (values * scale * gain).astype(jnp.bfloat16))


def pre_products(rows, w_gate, w_up):
    flat = rows.reshape(-1, rows.shape[-1])
    pre_gate = jnp.dot(flat, w_gate, preferred_element_type=jnp.float32)
    pre_up = jnp.dot(flat, w_up, preferred_element_type=jnp.float32)
    inner = rows.shape[:-1] + (w_gate.shape[1],)
    return (pre_gate.reshape(inner), pre_up.reshape(inner))


def expert_forward(rows, w_gate, w_up, w_down):
    pre_gate, pre_up = pre_products(rows, w_gate, w_up)
    width = w_gate.shape[1]
    product = (pre_gate * jax.nn.sigmoid(pre_gate) * pre_up).astype(jnp.bfloat16)
    output = jnp.dot(product.reshape(-1, width), w_down, preferred_element_type=jnp.float32).astype(
        jnp.bfloat16
    )
    return (output.reshape(rows.shape), pre_gate, pre_up)


def contract_last(left, right):
    return lax.dot_general(
        left, right, (((1,), (1,)), ((), ())), preferred_element_type=jnp.float32
    )


def expert_backward(grad_rows, pre_gate, pre_up, w_gate, w_up, w_down):
    shape = grad_rows.shape
    width = w_gate.shape[1]
    flat = grad_rows.reshape(-1, shape[-1])
    gate_pre = pre_gate.reshape(-1, width)
    up_pre = pre_up.reshape(-1, width)
    d_hidden = contract_last(flat, w_down)
    sigma = jax.nn.sigmoid(gate_pre)
    d_gate = (d_hidden * up_pre * sigma * (1.0 + gate_pre * (1.0 - sigma))).astype(jnp.bfloat16)
    d_up = (d_hidden * gate_pre * sigma).astype(jnp.bfloat16)
    back = contract_last(d_gate, w_gate) + contract_last(d_up, w_up)
    return back.astype(jnp.bfloat16).reshape(shape)


def return_rows(rows):
    return lax.all_to_all(rows, "expert", split_axis=0, concat_axis=0, tiled=True)


def local(inputs, cotangent, gain, route, gate, w_gate, w_up, w_down):
    micro, tok, width = inputs.shape
    top = route.shape[-1]
    experts = lax.axis_size("expert")
    capacity = tok * top * 7 // (6 * experts)
    total_rows = experts * capacity
    sections = lax.axis_size("section")
    section = lax.axis_index("section")
    ticks = sections + micro - 1
    gain_row = gain[0]
    weight_gate = w_gate[0, 0]
    weight_up = w_up[0, 0]
    weight_down = w_down[0, 0]
    inner = weight_gate.shape[1]
    routes = route[0]
    gates = gate[0]

    def forward_work(tokens, route_now, gate_now, live):
        values, scale, normed = normalize(tokens, gain_row)
        places = slot_places(route_now, experts, capacity)
        table = slot_table(places, total_rows)
        send = jnp.einsum("ktj,td->jd", table, normed, preferred_element_type=jnp.float32).astype(
            jnp.bfloat16
        )
        send = send.reshape(experts, capacity, width)

        def forward_active(operand):
            return expert_forward(operand, weight_gate, weight_up, weight_down)

        def forward_resting(operand):
            pre_zero = jnp.zeros(operand.shape[:-1] + (inner,), jnp.float32)
            return (jnp.zeros_like(operand), pre_zero, pre_zero)

        output, pre_gate, pre_up = lax.cond(
            live,
            forward_active,
            forward_resting,
            lax.all_to_all(send, "expert", split_axis=0, concat_axis=0, tiled=True),
        )
        back = return_rows(output)
        picked = back.reshape(total_rows, width)[places]
        mixed = values + jnp.sum(gate_now[..., None] * picked.astype(jnp.float32), axis=1)
        return (mixed.astype(jnp.bfloat16), pre_gate, pre_up)

    def forward_tick(carry, tick):
        incoming, outputs, kept_x, kept_gate, kept_up = carry
        offset = tick - section
        live = (offset >= 0) & (offset < micro)
        index = jnp.clip(offset, 0, micro - 1)
        fresh = lax.dynamic_index_in_dim(inputs, index, 0, keepdims=False)
        tokens = jnp.where(section == 0, fresh, incoming)
        route_now = lax.dynamic_index_in_dim(routes, index, 0, keepdims=False)
        gate_now = lax.dynamic_index_in_dim(gates, index, 0, keepdims=False)
        mixed, pre_gate, pre_up = forward_work(tokens, route_now, gate_now, live)
        old_out = lax.dynamic_index_in_dim(outputs, index, 0, keepdims=False)
        outputs = lax.dynamic_update_index_in_dim(
            outputs, jnp.where(live, mixed, old_out), index, 0
        )
        old_x = lax.dynamic_index_in_dim(kept_x, index, 0, keepdims=False)
        kept_x = lax.dynamic_update_index_in_dim(kept_x, jnp.where(live, tokens, old_x), index, 0)
        incoming = passed_along(mixed, "section", 1)
        return ((incoming, outputs, kept_x, kept_gate, kept_up), None)

    start = (
        jnp.zeros((tok, width), jnp.bfloat16),
        jnp.zeros_like(inputs),
        jnp.zeros_like(inputs),
        jnp.zeros((micro, experts, capacity, inner), jnp.float32),
        jnp.zeros((micro, experts, capacity, inner), jnp.float32),
    )
    finished, _ = lax.scan(forward_tick, start, jnp.arange(ticks, dtype=jnp.int32))
    _, outputs, kept_x, kept_gate, kept_up = finished

    def backward_work(tokens, grad_out, route_now, gate_now, live):
        values, scale, normed = normalize(tokens, gain_row)
        places = slot_places(route_now, experts, capacity)
        table = slot_table(places, total_rows)
        scaled = (gate_now[..., None] * grad_out.astype(jnp.float32)[:, None, :]).astype(
            jnp.bfloat16
        )
        grad_send = jnp.einsum(
            "ktj,tkd->jd", table, scaled, preferred_element_type=jnp.float32
        ).astype(jnp.bfloat16)
        grad_send = grad_send.reshape(experts, capacity, width)
        send = jnp.einsum("ktj,td->jd", table, normed, preferred_element_type=jnp.float32).astype(
            jnp.bfloat16
        )
        send = send.reshape(experts, capacity, width)

        def backward_active(operands):
            rows_in, rows_grad = operands
            gate_again, up_again = pre_products(rows_in, weight_gate, weight_up)
            return expert_backward(
                rows_grad, gate_again, up_again, weight_gate, weight_up, weight_down
            )

        def backward_resting(operands):
            return jnp.zeros_like(operands[1])

        computed = lax.cond(
            live,
            backward_active,
            backward_resting,
            (
                lax.all_to_all(send, "expert", split_axis=0, concat_axis=0, tiled=True),
                lax.all_to_all(grad_send, "expert", split_axis=0, concat_axis=0, tiled=True),
            ),
        )
        back = return_rows(computed)
        d_norm = jnp.sum(back.reshape(total_rows, width)[places].astype(jnp.float32), axis=1)
        weighted = d_norm * gain_row
        result = (
            grad_out.astype(jnp.float32)
            + scale * weighted
            - values * (scale * scale * scale) * jnp.mean(values * weighted, axis=-1, keepdims=True)
        )
        return result.astype(jnp.bfloat16)

    def backward_tick(carry, tick):
        incoming, results = carry
        offset = tick - (sections - 1 - section)
        live = (offset >= 0) & (offset < micro)
        index = jnp.clip(offset, 0, micro - 1)
        fresh = lax.dynamic_index_in_dim(cotangent, index, 0, keepdims=False)
        grad_out = jnp.where(section == sections - 1, fresh, incoming)
        tokens = lax.dynamic_index_in_dim(kept_x, index, 0, keepdims=False)
        route_now = lax.dynamic_index_in_dim(routes, index, 0, keepdims=False)
        gate_now = lax.dynamic_index_in_dim(gates, index, 0, keepdims=False)
        result = backward_work(tokens, grad_out, route_now, gate_now, live)
        old_result = lax.dynamic_index_in_dim(results, index, 0, keepdims=False)
        results = lax.dynamic_update_index_in_dim(
            results, jnp.where(live, result, old_result), index, 0
        )
        incoming = passed_along(result, "section", -1)
        return ((incoming, results), None)

    done, _ = lax.scan(
        backward_tick,
        (jnp.zeros((tok, width), jnp.bfloat16), jnp.zeros_like(cotangent)),
        jnp.arange(ticks, dtype=jnp.int32),
    )
    results = done[1]
    return (outputs[None], results[None])


def solution(mesh):
    placed = (
        P(None, "expert", None),
        P(None, "expert", None),
        P("section", None),
        P("section", None, "expert", None),
        P("section", None, "expert", None),
        P("section", "expert", None, None),
        P("section", "expert", None, None),
        P("section", "expert", None, None),
    )
    return jax.shard_map(
        local,
        mesh=mesh,
        in_specs=placed,
        out_specs=(P("section", None, "expert", None), P("section", None, "expert", None)),
        check_vma=False,
    )
```

profile of v0, /device:TPU:1, one launch (start us, length us, event | category | flops | bytes accessed | tf_op | source)
XLA Modules:
  0.0 1502.3 jit_solution(15946252955881989337)
XLA Ops:
  1.9 582.0 %while.29 = (s32[]{:T(128)}, bf16[32,4096]{1,0:T(8,128)(2,1)S(1)}, bf16[4,32,4096]{2,1,0:T(8,128)(2,1)}, bf16[4,32,4096]{2,1,0:T(8,128)(2,1)S(1)}, pred[]{:T(512...) while((s32[]{:T(128)}, bf16[32,4096]{1,0:T(8,128)(2,1)S(1)}, ...), condition=%wide.region_8.9_spmd, body=%wide.region_0.8_spmd.sunk | while | flops 1227478528 | bytes 63166144 | solution.py:146
  8.7 8.6 all-to-all-start
  18.4 9.3 all-to-all-done
  51.7 9.1 collective-permute-done
  72.3 10.1 all-to-all-done
  82.4 11.2 conditional.4
  98.9 8.6 all-to-all-done.1
  128.1 10.7 all-to-all-done
  138.8 11.2 conditional.4
  155.3 9.2 all-to-all-done.1
  185.4 9.6 all-to-all-done
  195.0 11.2 conditional.4
  211.5 10.1 all-to-all-done.1
  242.3 9.3 all-to-all-done
  251.6 11.2 conditional.4
  299.3 7.9 all-to-all-done
  324.6 16.9 %collective-permute-start = (bf16[32,4096]{1,0:T(8,128)(2,1)S(1)}, bf16[32,4096]{1,0:T(8,128)(2,1)S(1)}, u32[]{:S(2)}, u32[]{:S(2)}) collective-permute-start(bf16[32,4096]{1,0:T(8,128)(2,1)S(1)} %get-tuple-element.557), channel_id=1, source_target_pairs={{0,16},{16,32},{32,48},{48,64},{64,80},{80,96},{96,112},{1,17},{17... | collective-permute-start | bytes 786440 | tf_op jit(solution)/shard_map/while/body/eval_jaxpr/ppermute | solution.py:12
  356.3 9.2 all-to-all-done
  403.1 7.9 all-to-all-done
  428.4 11.4 collective-permute-start
  454.6 7.9 all-to-all-done
  501.5 7.9 all-to-all-done
  548.5 7.9 all-to-all-done
  584.9 917.4 %while.30 = (s32[]{:T(128)}, bf16[32,4096]{1,0:T(8,128)(2,1)S(1)}, bf16[4,32,4096]{2,1,0:T(8,128)(2,1)}, pred[]{:T(512)}, s32[11]{0:T(128)S(1)}, /*index=5*/s32[...) while((s32[]{:T(128)}, bf16[32,4096]{1,0:T(8,128)(2,1)S(1)}, ...), condition=%wide.region_18.19_spmd, body=%wide.region_9.18_spmd.sunk | while | flops 2068801024 | bytes 59796220 | solution.py:212
  608.9 7.9 all-to-all-done.3
  622.5 8.0 all-to-all-done.4
  638.3 14.2 collective-permute-done.1
  665.0 8.0 all-to-all-done.2
  677.7 7.9 all-to-all-done.3
  691.2 8.0 all-to-all-done.4
  737.3 7.9 all-to-all-done.3
  750.8 8.9 all-to-all-done.4
  767.6 10.2 collective-permute-done.1
  801.5 7.9 all-to-all-done.3
  815.1 8.0 all-to-all-done.4
  830.9 7.3 collective-permute-done.1
  862.0 7.9 all-to-all-done.3
  875.6 8.0 all-to-all-done.4
  891.4 10.9 collective-permute-done.1
  926.2 7.9 all-to-all-done.3
  939.8 8.0 all-to-all-done.4
  955.6 134.3 %collective-permute-done.1 = bf16[32,4096]{1,0:T(8,128)(2,1)S(1)} collective-permute-done((bf16[32,4096]{1,0:T(8,128)(2,1)S(1)}, bf16[32,4096]{1,0:T(8,128)(2,1)S(1)}, u32[]{:S(2)}, u32[]{:S(2)}) %collective-permute-start.1) | collective-permute-done | bytes 262176 | tf_op jit(solution)/shard_map/while/body/eval_jaxpr/ppermute | solution.py:12
  1113.7 7.9 all-to-all-done.3
  1121.6 22.7 %conditional.5 = (bf16[16,4,4096]{2,1,0:T(4,128)(2,1)}) conditional(s32[]{:T(128)} %convert_element_type.200, () %tuple.78, (bf16[16,4,4096]{2,1,0:T(4,128)(2,1)S(1)}, bf16[768,4096]{1,0:T(8,128)(2,1)}, bf16[16,4,4096]{2,1,0:T(4,128)(2,1)S(1)}, bf16[4096,768]{1,0:T(8,128)(2,1)}, bf16[4096,768]{1,0:T(8,128)(2,1)}) %tuple.79), branch_computations={%region_14.14_spmd, %region_15.15_spmd} | conditional | flops 2014576640 | bytes 39976968 | solution.py:175
  1130.6 7.9 fusion.16
  1149.0 8.0 all-to-all-done.4
  1164.8 8.2 collective-permute-done.1
  1196.8 7.9 all-to-all-done.3
  1204.7 22.7 %conditional.5 = (bf16[16,4,4096]{2,1,0:T(4,128)(2,1)}) conditional(s32[]{:T(128)} %convert_element_type.200, () %tuple.78, (bf16[16,4,4096]{2,1,0:T(4,128)(2,1)S(1)}, bf16[768,4096]{1,0:T(8,128)(2,1)}, bf16[16,4,4096]{2,1,0:T(4,128)(2,1)S(1)}, bf16[4096,768]{1,0:T(8,128)(2,1)}, bf16[4096,768]{1,0:T(8,128)(2,1)}) %tuple.79), branch_computations={%region_14.14_spmd, %region_15.15_spmd} | conditional | flops 2014576640 | bytes 39976968 | solution.py:175
  1213.7 7.9 fusion.16
  1232.1 8.0 all-to-all-done.4
  1247.9 10.6 collective-permute-done.1
  1282.3 7.9 all-to-all-done.3
  1290.2 22.7 %conditional.5 = (bf16[16,4,4096]{2,1,0:T(4,128)(2,1)}) conditional(s32[]{:T(128)} %convert_element_type.200, () %tuple.78, (bf16[16,4,4096]{2,1,0:T(4,128)(2,1)S(1)}, bf16[768,4096]{1,0:T(8,128)(2,1)}, bf16[16,4,4096]{2,1,0:T(4,128)(2,1)S(1)}, bf16[4096,768]{1,0:T(8,128)(2,1)}, bf16[4096,768]{1,0:T(8,128)(2,1)}) %tuple.79), branch_computations={%region_14.14_spmd, %region_15.15_spmd} | conditional | flops 2014576640 | bytes 39976968 | solution.py:175
  1299.2 7.9 fusion.16
  1317.6 8.0 all-to-all-done.4
  1333.4 12.5 collective-permute-done.1
  1369.8 7.9 all-to-all-done.3
  1377.7 22.7 %conditional.5 = (bf16[16,4,4096]{2,1,0:T(4,128)(2,1)}) conditional(s32[]{:T(128)} %convert_element_type.200, () %tuple.78, (bf16[16,4,4096]{2,1,0:T(4,128)(2,1)S(1)}, bf16[768,4096]{1,0:T(8,128)(2,1)}, bf16[16,4,4096]{2,1,0:T(4,128)(2,1)S(1)}, bf16[4096,768]{1,0:T(8,128)(2,1)}, bf16[4096,768]{1,0:T(8,128)(2,1)}) %tuple.79), branch_computations={%region_14.14_spmd, %region_15.15_spmd} | conditional | flops 2014576640 | bytes 39976968 | solution.py:175
  1386.7 7.9 fusion.16
  1405.1 8.0 all-to-all-done.4
  1450.5 8.1 all-to-all-done.3
  1464.2 8.0 all-to-all-done.4
  1478.1 23.1 %collective-permute-start.1 = (bf16[32,4096]{1,0:T(8,128)(2,1)S(1)}, bf16[32,4096]{1,0:T(8,128)(2,1)S(1)}, u32[]{:S(2)}, u32[]{:S(2)}) collective-permute-start(bf16[32,4096]{1,0:T(8,128)(2,1)S(1)} %get-tuple-element.576), channel_id=1, source_target_pairs={{16,0},{32,16},{48,32},{64,48},{80,64},{96,80},{112,96},{17,1},{33... | collective-permute-start | bytes 786440 | tf_op jit(solution)/shard_map/while/body/eval_jaxpr/ppermute | solution.py:12
  (921 shorter events, 879.5 us)
Async XLA Ops:
  8.7 19.0 %all-to-all-start = ((bf16[16,4,4096]{2,1,0:T(4,128)(2,1)}), bf16[16,4,4096]{2,1,0:T(4,128)(2,1)S(1)}, u32[]{:S(2)}, u32[]{:S(2)}) async-start(bf16[16,4,4096]{2,1,0:T(4,128)(2,1)} %reshape.221), calls=%async_computation | async-start | bytes 1048576 | tf_op jit(solution)/shard_map/while/body/eval_jaxpr/all_to_all | solution.py:113
  28.7 12.5 all-to-all-start.1
  45.1 15.7 %collective-permute-start = (bf16[32,4096]{1,0:T(8,128)(2,1)S(1)}, bf16[32,4096]{1,0:T(8,128)(2,1)S(1)}, u32[]{:S(2)}, u32[]{:S(2)}) collective-permute-start(bf16[32,4096]{1,0:T(8,128)(2,1)S(1)} %get-tuple-element.557), channel_id=1, source_target_pairs={{0,16},{16,32},{32,48},{48,64},{64,80},{80,96},{96,112},{1,17},{17... | collective-permute-start | bytes 786440 | tf_op jit(solution)/shard_map/while/body/eval_jaxpr/ppermute | solution.py:12
  67.6 14.7 all-to-all-start
  93.6 13.9 all-to-all-start.1
  123.5 15.3 %all-to-all-start = ((bf16[16,4,4096]{2,1,0:T(4,128)(2,1)}), bf16[16,4,4096]{2,1,0:T(4,128)(2,1)S(1)}, u32[]{:S(2)}, u32[]{:S(2)}) async-start(bf16[16,4,4096]{2,1,0:T(4,128)(2,1)} %reshape.221), calls=%async_computation | async-start | bytes 1048576 | tf_op jit(solution)/shard_map/while/body/eval_jaxpr/all_to_all | solution.py:113
  150.0 14.5 all-to-all-start.1
  180.7 14.2 all-to-all-start
  206.1 15.4 %all-to-all-start.1 = ((bf16[16,4,4096]{2,1,0:T(4,128)(2,1)}), bf16[16,4,4096]{2,1,0:T(4,128)(2,1)S(1)}, u32[]{:S(2)}, u32[]{:S(2)}) async-start(bf16[16,4,4096]{2,1,0:T(4,128)(2,1)} %get-tuple-element.689), calls=%async_computation.1 | async-start | bytes 1048576 | tf_op jit(solution)/shard_map/while/body/eval_jaxpr/all_to_all | solution.py:73
  237.7 14.0 all-to-all-start
  262.8 12.5 all-to-all-start.1
  294.6 12.5 all-to-all-start
  308.2 12.5 all-to-all-start.1
  324.6 20.2 %collective-permute-start = (bf16[32,4096]{1,0:T(8,128)(2,1)S(1)}, bf16[32,4096]{1,0:T(8,128)(2,1)S(1)}, u32[]{:S(2)}, u32[]{:S(2)}) collective-permute-start(bf16[32,4096]{1,0:T(8,128)(2,1)S(1)} %get-tuple-element.557), channel_id=1, source_target_pairs={{0,16},{16,32},{32,48},{48,64},{64,80},{80,96},{96,112},{1,17},{17... | collective-permute-start | bytes 786440 | tf_op jit(solution)/shard_map/while/body/eval_jaxpr/ppermute | solution.py:12
  351.6 13.9 all-to-all-start
  366.5 12.5 all-to-all-start.1
  398.4 12.5 all-to-all-start
  411.9 12.5 all-to-all-start.1
  428.4 14.7 collective-permute-start
  449.9 12.6 all-to-all-start
  463.5 12.5 all-to-all-start.1
  496.8 12.5 all-to-all-start
  510.3 12.5 all-to-all-start.1
  543.8 12.5 all-to-all-start
  557.4 12.5 all-to-all-start.1
  591.7 12.5 all-to-all-start.2
  604.2 12.5 all-to-all-start.3
  617.8 12.7 all-to-all-start.4
  636.3 16.1 %collective-permute-start.1 = (bf16[32,4096]{1,0:T(8,128)(2,1)S(1)}, bf16[32,4096]{1,0:T(8,128)(2,1)S(1)}, u32[]{:S(2)}, u32[]{:S(2)}) collective-permute-start(bf16[32,4096]{1,0:T(8,128)(2,1)S(1)} %get-tuple-element.576), channel_id=1, source_target_pairs={{16,0},{32,16},{48,32},{64,48},{80,64},{96,80},{112,96},{17,1},{33... | collective-permute-start | bytes 786440 | tf_op jit(solution)/shard_map/while/body/eval_jaxpr/ppermute | solution.py:12
  659.1 13.9 all-to-all-start.2
  673.0 12.5 all-to-all-start.3
  686.5 12.7 all-to-all-start.4
  720.1 12.5 all-to-all-start.2
  732.6 12.5 all-to-all-start.3
  746.1 13.6 all-to-all-start.4
  784.4 12.5 all-to-all-start.2
  796.9 12.5 all-to-all-start.3
  810.4 12.7 all-to-all-start.4
  844.8 12.5 all-to-all-start.2
  857.4 12.5 all-to-all-start.3
  870.9 12.7 all-to-all-start.4
  889.5 12.9 collective-permute-start.1
  908.9 12.6 all-to-all-start.2
  921.6 12.5 all-to-all-start.3
  935.1 12.7 all-to-all-start.4
  953.7 136.2 %collective-permute-start.1 = (bf16[32,4096]{1,0:T(8,128)(2,1)S(1)}, bf16[32,4096]{1,0:T(8,128)(2,1)S(1)}, u32[]{:S(2)}, u32[]{:S(2)}) collective-permute-start(bf16[32,4096]{1,0:T(8,128)(2,1)S(1)} %get-tuple-element.576), channel_id=1, source_target_pairs={{16,0},{32,16},{48,32},{64,48},{80,64},{96,80},{112,96},{17,1},{33... | collective-permute-start | bytes 786440 | tf_op jit(solution)/shard_map/while/body/eval_jaxpr/ppermute | solution.py:12
  1096.5 12.5 all-to-all-start.2
  1109.0 12.5 all-to-all-start.3
  1144.3 12.7 all-to-all-start.4
  1179.6 12.5 all-to-all-start.2
  1192.1 12.5 all-to-all-start.3
  1227.4 12.7 all-to-all-start.4
  1246.0 12.6 collective-permute-start.1
  1265.1 12.6 all-to-all-start.2
  1277.7 12.5 all-to-all-start.3
  1312.9 12.7 all-to-all-start.4
  1331.5 14.4 collective-permute-start.1
  1352.5 12.7 all-to-all-start.2
  1365.2 12.5 all-to-all-start.3
  1400.4 12.7 all-to-all-start.4
  1433.3 12.5 all-to-all-start.2
  1445.8 12.7 all-to-all-start.3
  1459.5 12.7 all-to-all-start.4
  1478.1 24.2 %collective-permute-start.1 = (bf16[32,4096]{1,0:T(8,128)(2,1)S(1)}, bf16[32,4096]{1,0:T(8,128)(2,1)S(1)}, u32[]{:S(2)}, u32[]{:S(2)}) collective-permute-start(bf16[32,4096]{1,0:T(8,128)(2,1)S(1)} %get-tuple-element.576), channel_id=1, source_target_pairs={{16,0},{32,16},{48,32},{64,48},{80,64},{96,80},{112,96},{17,1},{33... | collective-permute-start | bytes 786440 | tf_op jit(solution)/shard_map/while/body/eval_jaxpr/ppermute | solution.py:12
  (28 other events, 322.3 us)
where the time goes:
time: 1510 us; the launch traced here: 1500 us
  waiting for transfers between devices  696 us (46%)
  starting transfers between devices  317 us (21%)
  local copies, waits for them, and re-layouts  198 us (13%)
  matrix products  153 us (10%)
  other arithmetic  118 us (8%)
  loops' own time  18.5 us (1%)
    ppermute x22, waiting for transfers between devices, passed_along(): lax.ppermute(value, axis, [(source, source + steps) for source in range(l...  264 us
    all_to_all x22, waiting for transfers between devices, return_rows(): lax.all_to_all(rows, 'expert', split_axis=0, concat_axis=0, tiled=True)  174 us
    ppermute x22, starting transfers between devices, passed_along(): lax.ppermute(value, axis, [(source, source + steps) for source in range(l...  114 us
    all_to_all x11, waiting for transfers between devices, forward_work(): lax.all_to_all(send, 'expert', split_axis=0, concat_axis=0, tiled=True)  97.5 us
    all_to_all x11, waiting for transfers between devices, backward_work(): lax.all_to_all(send, 'expert', split_axis=0, concat_axis=0, tiled=True)  86.8 us
    all_to_all x22, starting transfers between devices, return_rows(): lax.all_to_all(rows, 'expert', split_axis=0, concat_axis=0, tiled=True)  80 us
    all_to_all x11, waiting for transfers between devices, backward_work(): lax.all_to_all(grad_send, 'expert', split_axis=0, concat_axis=0, tiled=True)  74.5 us
    dot_general x12, matrix products, contract_last(): lax.dot_general(left, right, (((1,), (1,)), ((), ())), preferred_element_...  70 us
  transfers between devices with their start and end apart: 77, of which 77 were waited for; matrix products, arithmetic and copies ran while one was open for 5% of the time, Pallas kernels for 0%

commit v1 on v0

--- a/solution.py
+++ b/solution.py
@@ -90,10 +90,11 @@
     routes = route[0]
     gates = gate[0]
 
-    def forward_work(tokens, route_now, gate_now, live):
+    all_places = jax.vmap(lambda r: slot_places(r, experts, capacity))(routes)
+    all_tables = jax.vmap(lambda p: slot_table(p, total_rows))(all_places)
+
+    def forward_work(tokens, places, table, gate_now, live):
         values, scale, normed = normalize(tokens, gain_row)
-        places = slot_places(route_now, experts, capacity)
-        table = slot_table(places, total_rows)
         send = jnp.einsum("ktj,td->jd", table, normed, preferred_element_type=jnp.float32).astype(
             jnp.bfloat16
         )
@@ -124,15 +125,22 @@
         index = jnp.clip(offset, 0, micro - 1)
         fresh = lax.dynamic_index_in_dim(inputs, index, 0, keepdims=False)
         tokens = jnp.where(section == 0, fresh, incoming)
-        route_now = lax.dynamic_index_in_dim(routes, index, 0, keepdims=False)
+        places = lax.dynamic_index_in_dim(all_places, index, 0, keepdims=False)
+        table = lax.dynamic_index_in_dim(all_tables, index, 0, keepdims=False)
         gate_now = lax.dynamic_index_in_dim(gates, index, 0, keepdims=False)
-        mixed, pre_gate, pre_up = forward_work(tokens, route_now, gate_now, live)
+        mixed, pre_gate, pre_up = forward_work(tokens, places, table, gate_now, live)
         old_out = lax.dynamic_index_in_dim(outputs, index, 0, keepdims=False)
         outputs = lax.dynamic_update_index_in_dim(
             outputs, jnp.where(live, mixed, old_out), index, 0
         )
         old_x = lax.dynamic_index_in_dim(kept_x, index, 0, keepdims=False)
         kept_x = lax.dynamic_update_index_in_dim(kept_x, jnp.where(live, tokens, old_x), index, 0)
+        old_gate = lax.dynamic_index_in_dim(kept_gate, index, 0, keepdims=False)
+        kept_gate = lax.dynamic_update_index_in_dim(
+            kept_gate, jnp.where(live, pre_gate, old_gate), index, 0
+        )
+        old_up = lax.dynamic_index_in_dim(kept_up, index, 0, keepdims=False)
+        kept_up = lax.dynamic_update_index_in_dim(kept_up, jnp.where(live, pre_up, old_up), index, 0)
         incoming = passed_along(mixed, "section", 1)
         return ((incoming, outputs, kept_x, kept_gate, kept_up), None)
 
@@ -146,10 +154,8 @@
     finished, _ = lax.scan(forward_tick, start, jnp.arange(ticks, dtype=jnp.int32))
     _, outputs, kept_x, kept_gate, kept_up = finished
 
-    def backward_work(tokens, grad_out, route_now, gate_now, live):
+    def backward_work(tokens, grad_out, places, table, gate_now, gate_kept, up_kept, live):
         values, scale, normed = normalize(tokens, gain_row)
-        places = slot_places(route_now, experts, capacity)
-        table = slot_table(places, total_rows)
         scaled = (gate_now[..., None] * grad_out.astype(jnp.float32)[:, None, :]).astype(
             jnp.bfloat16
         )
@@ -157,28 +163,24 @@
             "ktj,tkd->jd", table, scaled, preferred_element_type=jnp.float32
         ).astype(jnp.bfloat16)
         grad_send = grad_send.reshape(experts, capacity, width)
-        send = jnp.einsum("ktj,td->jd", table, normed, preferred_element_type=jnp.float32).astype(
-            jnp.bfloat16
-        )
-        send = send.reshape(experts, capacity, width)
 
         def backward_active(operands):
-            rows_in, rows_grad = operands
-            gate_again, up_again = pre_products(rows_in, weight_gate, weight_up)
+            rows_grad, gate_again, up_again = operands
             return expert_backward(
                 rows_grad, gate_again, up_again, weight_gate, weight_up, weight_down
             )
 
         def backward_resting(operands):
-            return jnp.zeros_like(operands[1])
+            return jnp.zeros_like(operands[0])
 
         computed = lax.cond(
             live,
             backward_active,
             backward_resting,
             (
-                lax.all_to_all(send, "expert", split_axis=0, concat_axis=0, tiled=True),
                 lax.all_to_all(grad_send, "expert", split_axis=0, concat_axis=0, tiled=True),
+                gate_kept,
+                up_kept,
             ),
         )
         back = return_rows(computed)
@@ -199,9 +201,14 @@
         fresh = lax.dynamic_index_in_dim(cotangent, index, 0, keepdims=False)
         grad_out = jnp.where(section == sections - 1, fresh, incoming)
         tokens = lax.dynamic_index_in_dim(kept_x, index, 0, keepdims=False)
-        route_now = lax.dynamic_index_in_dim(routes, index, 0, keepdims=False)
+        places = lax.dynamic_index_in_dim(all_places, index, 0, keepdims=False)
+        table = lax.dynamic_index_in_dim(all_tables, index, 0, keepdims=False)
         gate_now = lax.dynamic_index_in_dim(gates, index, 0, keepdims=False)
-        result = backward_work(tokens, grad_out, route_now, gate_now, live)
+        gate_kept = lax.dynamic_index_in_dim(kept_gate, index, 0, keepdims=False)
+        up_kept = lax.dynamic_index_in_dim(kept_up, index, 0, keepdims=False)
+        result = backward_work(
+            tokens, grad_out, places, table, gate_now, gate_kept, up_kept, live
+        )
         old_result = lax.dynamic_index_in_dim(results, index, 0, keepdims=False)
         results = lax.dynamic_update_index_in_dim(
             results, jnp.where(live, result, old_result), index, 0

time: 1510 us -> 1290 us (0.85)
  waiting for transfers between devices: 696 us -> 569 us
  starting transfers between devices: 317 us -> 270 us
  matrix products: 153 us -> 117 us
    all_to_all x11 -> x0, waiting for transfers between devices: 86.8 us -> none  [backward_work(): lax.all_to_all(send, 'expert', split_axis=0, concat_axis=0, tiled=True)]
    ppermute x22, waiting for transfers between devices: 264 us -> 197 us  [passed_along(): lax.ppermute(value, axis, [(source, source + steps) for source in range(l...]
    all_to_all x11 -> x0, starting transfers between devices: 39.3 us -> none  [backward_work(): lax.all_to_all(send, 'expert', split_axis=0, concat_axis=0, tiled=True)]
    dot_general x12, matrix products: 70 us -> 47.6 us  [contract_last(): lax.dot_general(left, right, (((1,), (1,)), ((), ())), preferred_element_...]
    all_to_all x11, waiting for transfers between devices: 74.5 us -> 96.3 us  [backward_work(): lax.all_to_all(grad_send, 'expert', split_axis=0, concat_axis=0, tiled=True)]
    dynamic_update_slice x0 -> x22, local copies, waits for them, and re-layouts: none -> 17.8 us  [the longest x11 8.92 us: forward_tick(): lax.dynamic_update_index_in_dim(kept_up, jnp.where(live, pre_up, old_up),...]
    transpose x22 -> x0, other arithmetic: 15.3 us -> none  [slot_table(): return (places.T[:, :, None] == grid[None, None, :]).astype(jnp.bfloat16)]
    dot_general x8 -> x4, matrix products: 33.5 us -> 20.4 us  [pre_products(): pre_gate = jnp.dot(flat, w_gate, preferred_element_type=jnp.float32)]
  transfers between devices with their start and end apart: 77 -> 66, of which waited for: 77 -> 66; matrix products, arithmetic and copies ran while one was open for 5% -> 5% of each run, Pallas kernels for 0% -> 0%
where the time goes in v1:
time: 1290 us; the launch traced here: 1280 us
  waiting for transfers between devices  569 us (44%)
  starting transfers between devices  270 us (21%)
  local copies, waits for them, and re-layouts  188 us (15%)
  other arithmetic  120 us (9%)
  matrix products  117 us (9%)
  loops' own time  17.4 us (1%)
    ppermute x22, waiting for transfers between devices, passed_along(): lax.ppermute(value, axis, [(source, source + steps) for source in range(l...  197 us
    all_to_all x22, waiting for transfers between devices, return_rows(): lax.all_to_all(rows, 'expert', split_axis=0, concat_axis=0, tiled=True)  180 us
    ppermute x22, starting transfers between devices, passed_along(): lax.ppermute(value, axis, [(source, source + steps) for source in range(l...  106 us
    all_to_all x11, waiting for transfers between devices, backward_work(): lax.all_to_all(grad_send, 'expert', split_axis=0, concat_axis=0, tiled=True)  96.3 us
    all_to_all x11, waiting for transfers between devices, forward_work(): lax.all_to_all(send, 'expert', split_axis=0, concat_axis=0, tiled=True)  95.8 us
    all_to_all x22, starting transfers between devices, return_rows(): lax.all_to_all(rows, 'expert', split_axis=0, concat_axis=0, tiled=True)  80.1 us
    dot_general x12, matrix products, contract_last(): lax.dot_general(left, right, (((1,), (1,)), ((), ())), preferred_element_...  47.6 us
    all_to_all x11, starting transfers between devices, forward_work(): lax.all_to_all(send, 'expert', split_axis=0, concat_axis=0, tiled=True)  44.3 us
  transfers between devices with their start and end apart: 66, of which 66 were waited for; matrix products, arithmetic and copies ran while one was open for 5% of the time, Pallas kernels for 0%

profile of v1, /device:TPU:1, one launch (start us, length us, event | category | flops | bytes accessed | tf_op | source)
XLA Modules:
  0.0 1281.2 jit_solution(4604273201662640541)
XLA Ops:
  7.2 597.2 %while.33 = (s32[]{:T(128)}, bf16[32,4096]{1,0:T(8,128)(2,1)S(1)}, bf16[4,32,4096]{2,1,0:T(8,128)(2,1)}, bf16[4,32,4096]{2,1,0:T(8,128)(2,1)}, f32[4,16,4,768]{3...) while((s32[]{:T(128)}, bf16[32,4096]{1,0:T(8,128)(2,1)S(1)}, ...), condition=%wide.region_8.9_spmd, body=%wide.region_2.8_spmd.sunk | while | flops 1227496704 | bytes 66101992 | solution.py:154
  14.2 8.6 all-to-all-start
  24.1 9.1 all-to-all-done
  39.5 8.1 all-to-all-done.1
  59.6 8.2 collective-permute-done
  79.7 9.4 all-to-all-done
  89.2 12.6 conditional.4
  107.2 8.2 all-to-all-done.1
  136.4 9.9 all-to-all-done
  146.3 12.6 conditional.4
  164.3 8.5 all-to-all-done.1
  195.4 9.2 all-to-all-done
  204.6 12.6 conditional.4
  222.6 10.4 all-to-all-done.1
  254.0 9.7 all-to-all-done
  263.8 12.6 conditional.4
  312.6 7.7 all-to-all-done
  326.5 8.6 all-to-all-done.1
  339.1 17.0 %collective-permute-start = (bf16[32,4096]{1,0:T(8,128)(2,1)S(1)}, bf16[32,4096]{1,0:T(8,128)(2,1)S(1)}, u32[]{:S(2)}, u32[]{:S(2)}) collective-permute-start(bf16[32,4096]{1,0:T(8,128)(2,1)S(1)} %get-tuple-element.812), channel_id=1, source_target_pairs={{0,16},{16,32},{32,48},{48,64},{64,80},{80,96},{96,112},{1,17},{17... | collective-permute-start | bytes 786440 | tf_op jit(solution)/shard_map/while/body/eval_jaxpr/ppermute | solution.py:12
  371.2 10.1 all-to-all-done
  387.6 8.1 all-to-all-done.1
  419.1 7.7 all-to-all-done
  433.0 9.0 all-to-all-done.1
  445.9 10.2 collective-permute-start
  471.3 7.7 all-to-all-done
  485.2 8.1 all-to-all-done.1
  519.1 7.7 all-to-all-done
  532.9 8.1 all-to-all-done.1
  544.9 8.5 collective-permute-start
  568.6 7.7 all-to-all-done
  582.5 8.1 all-to-all-done.1
  605.5 675.7 %while.34 = (s32[]{:T(128)}, bf16[32,4096]{1,0:T(8,128)(2,1)S(1)}, bf16[4,32,4096]{2,1,0:T(8,128)(2,1)}, pred[]{:T(512)}, s32[11]{0:T(128)S(1)}, /*index=5*/s32[...) while((s32[]{:T(128)}, bf16[32,4096]{1,0:T(8,128)(2,1)S(1)}, ...), condition=%wide.region_15.16_spmd, body=%wide.region_9.15_spmd.sunk | while | flops 1245971840 | bytes 61859360 | solution.py:219
  614.5 8.7 all-to-all-done.2
  629.0 8.0 all-to-all-done.3
  644.9 13.9 %collective-permute-done.1 = bf16[32,4096]{1,0:T(8,128)(2,1)S(1)} collective-permute-done((bf16[32,4096]{1,0:T(8,128)(2,1)S(1)}, bf16[32,4096]{1,0:T(8,128)(2,1)S(1)}, u32[]{:S(2)}, u32[]{:S(2)}) %collective-permute-start.1) | collective-permute-done | bytes 262176 | tf_op jit(solution)/shard_map/while/body/eval_jaxpr/ppermute | solution.py:12
  667.6 9.0 all-to-all-done.2
  682.4 8.0 all-to-all-done.3
  713.6 8.7 all-to-all-done.2
  728.1 8.0 all-to-all-done.3
  744.0 10.9 collective-permute-done.1
  763.8 8.7 all-to-all-done.2
  778.2 8.0 all-to-all-done.3
  810.0 8.7 all-to-all-done.2
  824.5 8.0 all-to-all-done.3
  840.4 10.6 collective-permute-done.1
  859.8 8.7 all-to-all-done.2
  874.2 8.0 all-to-all-done.3
  890.1 93.1 %collective-permute-done.1 = bf16[32,4096]{1,0:T(8,128)(2,1)S(1)} collective-permute-done((bf16[32,4096]{1,0:T(8,128)(2,1)S(1)}, bf16[32,4096]{1,0:T(8,128)(2,1)S(1)}, u32[]{:S(2)}, u32[]{:S(2)}) %collective-permute-start.1) | collective-permute-done | bytes 262176 | tf_op jit(solution)/shard_map/while/body/eval_jaxpr/ppermute | solution.py:12
  992.1 8.7 all-to-all-done.2
  1000.8 15.9 %conditional.5 = (bf16[16,4,4096]{2,1,0:T(4,128)(2,1)}) conditional(s32[]{:T(128)} %convert_element_type.153, () %tuple.99, (bf16[16,4,4096]{2,1,0:T(4,128)(2,1)S(1)}, bf16[768,4096]{1,0:T(8,128)(2,1)}, f32[4,16,4,768]{3,2,1,0:T(4,128)}, s32[]{:T(128)}, f32[4,16,4,768]{3,2,1,0:T(4,128)}, /*index=5*/bf16[4096,768]{1,0:T(8,128)(2,1)}, ...), branch_computations={%region_11.11_spmd, %region_12.12_spmd} | conditional | flops 1209270272 | bytes 45744188 | solution.py:176
  1021.4 8.0 all-to-all-done.3
  1053.2 8.7 all-to-all-done.2
  1062.0 15.9 %conditional.5 = (bf16[16,4,4096]{2,1,0:T(4,128)(2,1)}) conditional(s32[]{:T(128)} %convert_element_type.153, () %tuple.99, (bf16[16,4,4096]{2,1,0:T(4,128)(2,1)S(1)}, bf16[768,4096]{1,0:T(8,128)(2,1)}, f32[4,16,4,768]{3,2,1,0:T(4,128)}, s32[]{:T(128)}, f32[4,16,4,768]{3,2,1,0:T(4,128)}, /*index=5*/bf16[4096,768]{1,0:T(8,128)(2,1)}, ...), branch_computations={%region_11.11_spmd, %region_12.12_spmd} | conditional | flops 1209270272 | bytes 45744188 | solution.py:176
  1082.5 8.0 all-to-all-done.3
  1098.5 8.6 collective-permute-done.1
  1115.8 8.7 all-to-all-done.2
  1124.6 15.9 %conditional.5 = (bf16[16,4,4096]{2,1,0:T(4,128)(2,1)}) conditional(s32[]{:T(128)} %convert_element_type.153, () %tuple.99, (bf16[16,4,4096]{2,1,0:T(4,128)(2,1)S(1)}, bf16[768,4096]{1,0:T(8,128)(2,1)}, f32[4,16,4,768]{3,2,1,0:T(4,128)}, s32[]{:T(128)}, f32[4,16,4,768]{3,2,1,0:T(4,128)}, /*index=5*/bf16[4096,768]{1,0:T(8,128)(2,1)}, ...), branch_computations={%region_11.11_spmd, %region_12.12_spmd} | conditional | flops 1209270272 | bytes 45744188 | solution.py:176
  1145.2 8.0 all-to-all-done.3
  1177.0 8.7 all-to-all-done.2
  1185.8 15.9 %conditional.5 = (bf16[16,4,4096]{2,1,0:T(4,128)(2,1)}) conditional(s32[]{:T(128)} %convert_element_type.153, () %tuple.99, (bf16[16,4,4096]{2,1,0:T(4,128)(2,1)S(1)}, bf16[768,4096]{1,0:T(8,128)(2,1)}, f32[4,16,4,768]{3,2,1,0:T(4,128)}, s32[]{:T(128)}, f32[4,16,4,768]{3,2,1,0:T(4,128)}, /*index=5*/bf16[4096,768]{1,0:T(8,128)(2,1)}, ...), branch_computations={%region_11.11_spmd, %region_12.12_spmd} | conditional | flops 1209270272 | bytes 45744188 | solution.py:176
  1206.4 8.0 all-to-all-done.3
  1236.9 8.7 all-to-all-done.2
  1251.3 8.0 all-to-all-done.3
  1265.3 14.8 %collective-permute-start.1 = (bf16[32,4096]{1,0:T(8,128)(2,1)S(1)}, bf16[32,4096]{1,0:T(8,128)(2,1)S(1)}, u32[]{:S(2)}, u32[]{:S(2)}) collective-permute-start(bf16[32,4096]{1,0:T(8,128)(2,1)S(1)} %get-tuple-element.841), channel_id=1, source_target_pairs={{16,0},{32,16},{48,32},{64,48},{80,64},{96,80},{112,96},{17,1},{33... | collective-permute-start | bytes 786440 | tf_op jit(solution)/shard_map/while/body/eval_jaxpr/ppermute | solution.py:12
  (696 shorter events, 713.0 us)
Async XLA Ops:
  14.2 19.0 %all-to-all-start = ((bf16[16,4,4096]{2,1,0:T(4,128)(2,1)}), bf16[16,4,4096]{2,1,0:T(4,128)(2,1)S(1)}, u32[]{:S(2)}, u32[]{:S(2)}) async-start(bf16[16,4,4096]{2,1,0:T(4,128)(2,1)} %reshape.203), calls=%async_computation | async-start | bytes 1048576 | tf_op jit(solution)/shard_map/while/body/eval_jaxpr/all_to_all | solution.py:114
  35.0 12.5 all-to-all-start.1
  51.5 16.4 %collective-permute-start = (bf16[32,4096]{1,0:T(8,128)(2,1)S(1)}, bf16[32,4096]{1,0:T(8,128)(2,1)S(1)}, u32[]{:S(2)}, u32[]{:S(2)}) collective-permute-start(bf16[32,4096]{1,0:T(8,128)(2,1)S(1)} %get-tuple-element.812), channel_id=1, source_target_pairs={{0,16},{16,32},{32,48},{48,64},{64,80},{80,96},{96,112},{1,17},{17... | collective-permute-start | bytes 786440 | tf_op jit(solution)/shard_map/while/body/eval_jaxpr/ppermute | solution.py:12
  74.9 14.3 %all-to-all-start = ((bf16[16,4,4096]{2,1,0:T(4,128)(2,1)}), bf16[16,4,4096]{2,1,0:T(4,128)(2,1)S(1)}, u32[]{:S(2)}, u32[]{:S(2)}) async-start(bf16[16,4,4096]{2,1,0:T(4,128)(2,1)} %reshape.203), calls=%async_computation | async-start | bytes 1048576 | tf_op jit(solution)/shard_map/while/body/eval_jaxpr/all_to_all | solution.py:114
  101.8 13.6 %all-to-all-start.1 = ((bf16[16,4,4096]{2,1,0:T(4,128)(2,1)}), bf16[16,4,4096]{2,1,0:T(4,128)(2,1)S(1)}, u32[]{:S(2)}, u32[]{:S(2)}) async-start(bf16[16,4,4096]{2,1,0:T(4,128)(2,1)} %get-tuple-element.811), calls=%async_computation.1 | async-start | bytes 1048576 | tf_op jit(solution)/shard_map/while/body/eval_jaxpr/all_to_all | solution.py:73
  131.6 14.7 %all-to-all-start = ((bf16[16,4,4096]{2,1,0:T(4,128)(2,1)}), bf16[16,4,4096]{2,1,0:T(4,128)(2,1)S(1)}, u32[]{:S(2)}, u32[]{:S(2)}) async-start(bf16[16,4,4096]{2,1,0:T(4,128)(2,1)} %reshape.203), calls=%async_computation | async-start | bytes 1048576 | tf_op jit(solution)/shard_map/while/body/eval_jaxpr/all_to_all | solution.py:114
  158.9 13.9 %all-to-all-start.1 = ((bf16[16,4,4096]{2,1,0:T(4,128)(2,1)}), bf16[16,4,4096]{2,1,0:T(4,128)(2,1)S(1)}, u32[]{:S(2)}, u32[]{:S(2)}) async-start(bf16[16,4,4096]{2,1,0:T(4,128)(2,1)} %get-tuple-element.811), calls=%async_computation.1 | async-start | bytes 1048576 | tf_op jit(solution)/shard_map/while/body/eval_jaxpr/all_to_all | solution.py:73
  176.7 6.8 collective-permute-start
  190.6 14.0 %all-to-all-start = ((bf16[16,4,4096]{2,1,0:T(4,128)(2,1)}), bf16[16,4,4096]{2,1,0:T(4,128)(2,1)S(1)}, u32[]{:S(2)}, u32[]{:S(2)}) async-start(bf16[16,4,4096]{2,1,0:T(4,128)(2,1)} %reshape.203), calls=%async_computation | async-start | bytes 1048576 | tf_op jit(solution)/shard_map/while/body/eval_jaxpr/all_to_all | solution.py:114
  217.2 15.7 %all-to-all-start.1 = ((bf16[16,4,4096]{2,1,0:T(4,128)(2,1)}), bf16[16,4,4096]{2,1,0:T(4,128)(2,1)S(1)}, u32[]{:S(2)}, u32[]{:S(2)}) async-start(bf16[16,4,4096]{2,1,0:T(4,128)(2,1)} %get-tuple-element.811), calls=%async_computation.1 | async-start | bytes 1048576 | tf_op jit(solution)/shard_map/while/body/eval_jaxpr/all_to_all | solution.py:73
  249.2 14.6 %all-to-all-start = ((bf16[16,4,4096]{2,1,0:T(4,128)(2,1)}), bf16[16,4,4096]{2,1,0:T(4,128)(2,1)S(1)}, u32[]{:S(2)}, u32[]{:S(2)}) async-start(bf16[16,4,4096]{2,1,0:T(4,128)(2,1)} %reshape.203), calls=%async_computation | async-start | bytes 1048576 | tf_op jit(solution)/shard_map/while/body/eval_jaxpr/all_to_all | solution.py:114
  276.4 12.5 all-to-all-start.1
  292.8 7.9 collective-permute-start
  307.8 12.5 all-to-all-start
  322.0 13.1 %all-to-all-start.1 = ((bf16[16,4,4096]{2,1,0:T(4,128)(2,1)}), bf16[16,4,4096]{2,1,0:T(4,128)(2,1)S(1)}, u32[]{:S(2)}, u32[]{:S(2)}) async-start(bf16[16,4,4096]{2,1,0:T(4,128)(2,1)} %get-tuple-element.811), calls=%async_computation.1 | async-start | bytes 1048576 | tf_op jit(solution)/shard_map/while/body/eval_jaxpr/all_to_all | solution.py:73
  339.1 20.3 %collective-permute-start = (bf16[32,4096]{1,0:T(8,128)(2,1)S(1)}, bf16[32,4096]{1,0:T(8,128)(2,1)S(1)}, u32[]{:S(2)}, u32[]{:S(2)}) collective-permute-start(bf16[32,4096]{1,0:T(8,128)(2,1)S(1)} %get-tuple-element.812), channel_id=1, source_target_pairs={{0,16},{16,32},{32,48},{48,64},{64,80},{80,96},{96,112},{1,17},{17... | collective-permute-start | bytes 786440 | tf_op jit(solution)/shard_map/while/body/eval_jaxpr/ppermute | solution.py:12
  366.4 15.0 %all-to-all-start = ((bf16[16,4,4096]{2,1,0:T(4,128)(2,1)}), bf16[16,4,4096]{2,1,0:T(4,128)(2,1)S(1)}, u32[]{:S(2)}, u32[]{:S(2)}) async-start(bf16[16,4,4096]{2,1,0:T(4,128)(2,1)} %reshape.203), calls=%async_computation | async-start | bytes 1048576 | tf_op jit(solution)/shard_map/while/body/eval_jaxpr/all_to_all | solution.py:114
  383.1 12.5 all-to-all-start.1
  399.5 7.7 collective-permute-start
  414.2 12.5 all-to-all-start
  428.5 13.5 %all-to-all-start.1 = ((bf16[16,4,4096]{2,1,0:T(4,128)(2,1)}), bf16[16,4,4096]{2,1,0:T(4,128)(2,1)S(1)}, u32[]{:S(2)}, u32[]{:S(2)}) async-start(bf16[16,4,4096]{2,1,0:T(4,128)(2,1)} %get-tuple-element.811), calls=%async_computation.1 | async-start | bytes 1048576 | tf_op jit(solution)/shard_map/while/body/eval_jaxpr/all_to_all | solution.py:73
  445.9 13.5 %collective-permute-start = (bf16[32,4096]{1,0:T(8,128)(2,1)S(1)}, bf16[32,4096]{1,0:T(8,128)(2,1)S(1)}, u32[]{:S(2)}, u32[]{:S(2)}) collective-permute-start(bf16[32,4096]{1,0:T(8,128)(2,1)S(1)} %get-tuple-element.812), channel_id=1, source_target_pairs={{0,16},{16,32},{32,48},{48,64},{64,80},{80,96},{96,112},{1,17},{17... | collective-permute-start | bytes 786440 | tf_op jit(solution)/shard_map/while/body/eval_jaxpr/ppermute | solution.py:12
  466.5 12.5 all-to-all-start
  480.7 12.5 all-to-all-start.1
  497.2 10.0 collective-permute-start
  514.2 12.5 all-to-all-start
  528.4 12.5 all-to-all-start.1
  544.9 11.8 collective-permute-start
  563.7 12.5 all-to-all-start
  578.0 12.5 all-to-all-start.1
  594.5 10.0 collective-permute-start
  610.7 12.5 all-to-all-start.2
  624.3 12.7 all-to-all-start.3
  643.0 15.8 %collective-permute-start.1 = (bf16[32,4096]{1,0:T(8,128)(2,1)S(1)}, bf16[32,4096]{1,0:T(8,128)(2,1)S(1)}, u32[]{:S(2)}, u32[]{:S(2)}) collective-permute-start(bf16[32,4096]{1,0:T(8,128)(2,1)S(1)} %get-tuple-element.841), channel_id=1, source_target_pairs={{16,0},{32,16},{48,32},{64,48},{80,64},{96,80},{112,96},{17,1},{33... | collective-permute-start | bytes 786440 | tf_op jit(solution)/shard_map/while/body/eval_jaxpr/ppermute | solution.py:12
  663.8 12.9 %all-to-all-start.2 = ((bf16[16,4,4096]{2,1,0:T(4,128)(2,1)}), bf16[16,4,4096]{2,1,0:T(4,128)(2,1)S(1)}, u32[]{:S(2)}, u32[]{:S(2)}) async-start(bf16[16,4,4096]{2,1,0:T(4,128)(2,1)} %reshape.209), calls=%async_computation.2 | async-start | bytes 1048576 | tf_op jit(solution)/shard_map/while/body/eval_jaxpr/all_to_all | solution.py:181
  677.7 12.7 all-to-all-start.3
  696.4 8.4 collective-permute-start.1
  709.8 12.5 all-to-all-start.2
  723.4 12.7 all-to-all-start.3
  742.1 12.9 %collective-permute-start.1 = (bf16[32,4096]{1,0:T(8,128)(2,1)S(1)}, bf16[32,4096]{1,0:T(8,128)(2,1)S(1)}, u32[]{:S(2)}, u32[]{:S(2)}) collective-permute-start(bf16[32,4096]{1,0:T(8,128)(2,1)S(1)} %get-tuple-element.841), channel_id=1, source_target_pairs={{16,0},{32,16},{48,32},{64,48},{80,64},{96,80},{112,96},{17,1},{33... | collective-permute-start | bytes 786440 | tf_op jit(solution)/shard_map/while/body/eval_jaxpr/ppermute | solution.py:12
  760.0 12.5 all-to-all-start.2
  773.5 12.7 all-to-all-start.3
  792.2 9.0 collective-permute-start.1
  806.2 12.5 all-to-all-start.2
  819.8 12.7 all-to-all-start.3
  838.5 12.5 collective-permute-start.1
  856.0 12.5 all-to-all-start.2
  869.5 12.7 all-to-all-start.3
  888.2 95.1 %collective-permute-start.1 = (bf16[32,4096]{1,0:T(8,128)(2,1)S(1)}, bf16[32,4096]{1,0:T(8,128)(2,1)S(1)}, u32[]{:S(2)}, u32[]{:S(2)}) collective-permute-start(bf16[32,4096]{1,0:T(8,128)(2,1)S(1)} %get-tuple-element.841), channel_id=1, source_target_pairs={{16,0},{32,16},{48,32},{64,48},{80,64},{96,80},{112,96},{17,1},{33... | collective-permute-start | bytes 786440 | tf_op jit(solution)/shard_map/while/body/eval_jaxpr/ppermute | solution.py:12
  988.3 12.5 all-to-all-start.2
  1016.7 12.7 all-to-all-start.3
  1035.4 9.0 collective-permute-start.1
  1049.4 12.5 all-to-all-start.2
  1077.8 12.7 all-to-all-start.3
  1096.5 10.5 collective-permute-start.1
  1112.0 12.5 all-to-all-start.2
  1140.5 12.7 all-to-all-start.3
  1159.2 9.1 collective-permute-start.1
  1173.2 12.5 all-to-all-start.2
  1201.7 12.7 all-to-all-start.3
  1220.4 7.7 collective-permute-start.1
  1233.0 12.5 all-to-all-start.2
  1246.6 12.7 all-to-all-start.3
  1265.3 16.0 %collective-permute-start.1 = (bf16[32,4096]{1,0:T(8,128)(2,1)S(1)}, bf16[32,4096]{1,0:T(8,128)(2,1)S(1)}, u32[]{:S(2)}, u32[]{:S(2)}) collective-permute-start(bf16[32,4096]{1,0:T(8,128)(2,1)S(1)} %get-tuple-element.841), channel_id=1, source_target_pairs={{16,0},{32,16},{48,32},{64,48},{80,64},{96,80},{112,96},{17,1},{33... | collective-permute-start | bytes 786440 | tf_op jit(solution)/shard_map/while/body/eval_jaxpr/ppermute | solution.py:12
  (25 other events, 266.1 us)

commit v2 on v1

--- a/solution.py
+++ b/solution.py
@@ -92,16 +92,24 @@
 
     all_places = jax.vmap(lambda r: slot_places(r, experts, capacity))(routes)
     all_tables = jax.vmap(lambda p: slot_table(p, total_rows))(all_places)
-
-    def forward_work(tokens, places, table, gate_now, live):
+    all_weights = jnp.einsum(
+        "mktj,mtk->mtj", all_tables.astype(jnp.float32), gates, precision=lax.Precision.HIGHEST
+    )
+    all_tables4 = all_tables.reshape(micro, top, tok, experts, capacity)
+
+    def forward_work(tokens, table4, weights, live):
         values, scale, normed = normalize(tokens, gain_row)
-        send = jnp.einsum("ktj,td->jd", table, normed, preferred_element_type=jnp.float32).astype(
-            jnp.bfloat16
-        )
-        send = send.reshape(experts, capacity, width)
+        send = jnp.einsum(
+            "ktec,td->ecd", table4, normed, preferred_element_type=jnp.float32
+        ).astype(jnp.bfloat16)
 
         def forward_active(operand):
-            return expert_forward(operand, weight_gate, weight_up, weight_down)
+            pre_gate, pre_up = pre_products(operand, weight_gate, weight_up)
+            product = (pre_gate * jax.nn.sigmoid(pre_gate) * pre_up).astype(jnp.bfloat16)
+            output = jnp.einsum(
+                "ech,hd->ecd", product, weight_down, preferred_element_type=jnp.float32
+            ).astype(jnp.bfloat16)
+            return (output, pre_gate, pre_up)
 
         def forward_resting(operand):
             pre_zero = jnp.zeros(operand.shape[:-1] + (inner,), jnp.float32)
@@ -113,9 +121,10 @@
             forward_resting,
             lax.all_to_all(send, "expert", split_axis=0, concat_axis=0, tiled=True),
         )
-        back = return_rows(output)
-        picked = back.reshape(total_rows, width)[places]
-        mixed = values + jnp.sum(gate_now[..., None] * picked.astype(jnp.float32), axis=1)
+        back = return_rows(output).reshape(total_rows, width)
+        mixed = values + jnp.dot(
+            weights, back.astype(jnp.float32), precision=lax.Precision.HIGHEST
+        )
         return (mixed.astype(jnp.bfloat16), pre_gate, pre_up)
 
     def forward_tick(carry, tick):
@@ -123,46 +132,38 @@
         offset = tick - section
         live = (offset >= 0) & (offset < micro)
         index = jnp.clip(offset, 0, micro - 1)
+        slot = jnp.where(live, offset, micro)
         fresh = lax.dynamic_index_in_dim(inputs, index, 0, keepdims=False)
         tokens = jnp.where(section == 0, fresh, incoming)
-        places = lax.dynamic_index_in_dim(all_places, index, 0, keepdims=False)
-        table = lax.dynamic_index_in_dim(all_tables, index, 0, keepdims=False)
-        gate_now = lax.dynamic_index_in_dim(gates, index, 0, keepdims=False)
-        mixed, pre_gate, pre_up = forward_work(tokens, places, table, gate_now, live)
-        old_out = lax.dynamic_index_in_dim(outputs, index, 0, keepdims=False)
-        outputs = lax.dynamic_update_index_in_dim(
-            outputs, jnp.where(live, mixed, old_out), index, 0
-        )
-        old_x = lax.dynamic_index_in_dim(kept_x, index, 0, keepdims=False)
-        kept_x = lax.dynamic_update_index_in_dim(kept_x, jnp.where(live, tokens, old_x), index, 0)
-        old_gate = lax.dynamic_index_in_dim(kept_gate, index, 0, keepdims=False)
-        kept_gate = lax.dynamic_update_index_in_dim(
-            kept_gate, jnp.where(live, pre_gate, old_gate), index, 0
-        )
-        old_up = lax.dynamic_index_in_dim(kept_up, index, 0, keepdims=False)
-        kept_up = lax.dynamic_update_index_in_dim(kept_up, jnp.where(live, pre_up, old_up), index, 0)
+        table4 = lax.dynamic_index_in_dim(all_tables4, index, 0, keepdims=False)
+        weights = lax.dynamic_index_in_dim(all_weights, index, 0, keepdims=False)
+        mixed, pre_gate, pre_up = forward_work(tokens, table4, weights, live)
+        outputs = lax.dynamic_update_index_in_dim(outputs, mixed, slot, 0)
+        kept_x = lax.dynamic_update_index_in_dim(kept_x, tokens, slot, 0)
+        kept_gate = lax.dynamic_update_index_in_dim(kept_gate, pre_gate, slot, 0)
+        kept_up = lax.dynamic_update_index_in_dim(kept_up, pre_up, slot, 0)
         incoming = passed_along(mixed, "section", 1)
         return ((incoming, outputs, kept_x, kept_gate, kept_up), None)
 
+    spare = (micro + 1,)
     start = (
         jnp.zeros((tok, width), jnp.bfloat16),
-        jnp.zeros_like(inputs),
-        jnp.zeros_like(inputs),
-        jnp.zeros((micro, experts, capacity, inner), jnp.float32),
-        jnp.zeros((micro, experts, capacity, inner), jnp.float32),
+        jnp.zeros(spare + inputs.shape[1:], jnp.bfloat16),
+        jnp.zeros(spare + inputs.shape[1:], jnp.bfloat16),
+        jnp.zeros(spare + (experts, capacity, inner), jnp.float32),
+        jnp.zeros(spare + (experts, capacity, inner), jnp.float32),
     )
     finished, _ = lax.scan(forward_tick, start, jnp.arange(ticks, dtype=jnp.int32))
     _, outputs, kept_x, kept_gate, kept_up = finished
 
-    def backward_work(tokens, grad_out, places, table, gate_now, gate_kept, up_kept, live):
+    def backward_work(tokens, grad_out, table, table4, gate_now, gate_kept, up_kept, live):
         values, scale, normed = normalize(tokens, gain_row)
         scaled = (gate_now[..., None] * grad_out.astype(jnp.float32)[:, None, :]).astype(
             jnp.bfloat16
         )
         grad_send = jnp.einsum(
-            "ktj,tkd->jd", table, scaled, preferred_element_type=jnp.float32
+            "ktec,tkd->ecd", table4, scaled, preferred_element_type=jnp.float32
         ).astype(jnp.bfloat16)
-        grad_send = grad_send.reshape(experts, capacity, width)
 
         def backward_active(operands):
             rows_grad, gate_again, up_again = operands
@@ -183,8 +184,8 @@
                 up_kept,
             ),
         )
-        back = return_rows(computed)
-        d_norm = jnp.sum(back.reshape(total_rows, width)[places].astype(jnp.float32), axis=1)
+        back = return_rows(computed).reshape(total_rows, width)
+        d_norm = jnp.einsum("ktj,jd->td", table, back, preferred_element_type=jnp.float32)
         weighted = d_norm * gain_row
         result = (
             grad_out.astype(jnp.float32)
@@ -198,31 +199,32 @@
         offset = tick - (sections - 1 - section)
         live = (offset >= 0) & (offset < micro)
         index = jnp.clip(offset, 0, micro - 1)
+        slot = jnp.where(live, offset, micro)
         fresh = lax.dynamic_index_in_dim(cotangent, index, 0, keepdims=False)
         grad_out = jnp.where(section == sections - 1, fresh, incoming)
         tokens = lax.dynamic_index_in_dim(kept_x, index, 0, keepdims=False)
-        places = lax.dynamic_index_in_dim(all_places, index, 0, keepdims=False)
         table = lax.dynamic_index_in_dim(all_tables, index, 0, keepdims=False)
+        table4 = lax.dynamic_index_in_dim(all_tables4, index, 0, keepdims=False)
         gate_now = lax.dynamic_index_in_dim(gates, index, 0, keepdims=False)
         gate_kept = lax.dynamic_index_in_dim(kept_gate, index, 0, keepdims=False)
         up_kept = lax.dynamic_index_in_dim(kept_up, index, 0, keepdims=False)
         result = backward_work(
-            tokens, grad_out, places, table, gate_now, gate_kept, up_kept, live
-        )
-        old_result = lax.dynamic_index_in_dim(results, index, 0, keepdims=False)
-        results = lax.dynamic_update_index_in_dim(
-            results, jnp.where(live, result, old_result), index, 0
-        )
+            tokens, grad_out, table, table4, gate_now, gate_kept, up_kept, live
+        )
+        results = lax.dynamic_update_index_in_dim(results, result, slot, 0)
         incoming = passed_along(result, "section", -1)
         return ((incoming, results), None)
 
     done, _ = lax.scan(
         backward_tick,
-        (jnp.zeros((tok, width), jnp.bfloat16), jnp.zeros_like(cotangent)),
+        (
+            jnp.zeros((tok, width), jnp.bfloat16),
+            jnp.zeros(spare + cotangent.shape[1:], jnp.bfloat16),
+        ),
         jnp.arange(ticks, dtype=jnp.int32),
     )
     results = done[1]
-    return (outputs[None], results[None])
+    return (outputs[None, :micro], results[None, :micro])
 
 
 def solution(mesh):

time: 1290 us -> 1170 us (0.907)
  blocking collectives: 0 us -> 135 us
  waiting for transfers between devices: 569 us -> 477 us
  local copies, waits for them, and re-layouts: 188 us -> 122 us
  other arithmetic: 120 us -> 62.1 us
  starting transfers between devices: 270 us -> 232 us
    all_to_all x0 -> x11, blocking collectives: none -> 135 us  [return_rows(): lax.all_to_all(rows, 'expert', split_axis=0, concat_axis=0, tiled=True)]
    all_to_all x22 -> x11, waiting for transfers between devices: 180 us -> 90.3 us  [return_rows(): lax.all_to_all(rows, 'expert', split_axis=0, concat_axis=0, tiled=True)]
    all_to_all x22 -> x11, starting transfers between devices: 80.1 us -> 39.3 us  [return_rows(): lax.all_to_all(rows, 'expert', split_axis=0, concat_axis=0, tiled=True)]
    dynamic_slice x33 -> x11, local copies, waits for them, and re-layouts: 33 us -> 0.08 us  [forward_tick(): table4 = lax.dynamic_index_in_dim(all_tables4, index, 0, keepdims=False)]
    reduce_sum x33 -> x22, other arithmetic: 37.9 us -> 8.39 us  [the longest x11 8.04 us: backward_work(): jnp.einsum('ktj,jd->td', table, back, preferred_element_type=jnp.float32)]
    reshape x52 -> x22, local copies, waits for them, and re-layouts: 28.6 us -> 2.62 us  [the longest x11 1.31 us: forward_work(): back = return_rows(output).reshape(total_rows, width)]
    gather x22 -> x0, local copies, waits for them, and re-layouts: 19.1 us -> none  [the longest x11 9.53 us: forward_work(): picked = back.reshape(total_rows, width)[places]]
    ppermute x22, waiting for transfers between devices: 197 us -> 182 us  [passed_along(): lax.ppermute(value, axis, [(source, source + steps) for source in range(l...]
  transfers between devices with their start and end apart: 66 -> 55, of which waited for: 66 -> 55; matrix products, arithmetic and copies ran while one was open for 5% -> 3% of each run, Pallas kernels for 0% -> 0%
where the time goes in v2:
time: 1170 us; the launch traced here: 1160 us
  waiting for transfers between devices  477 us (41%)
  starting transfers between devices  232 us (20%)
  blocking collectives  135 us (12%)
  local copies, waits for them, and re-layouts  122 us (10%)
  matrix products  113 us (10%)
  other arithmetic  62.1 us (5%)
  loops' own time  16.3 us (1%)
    ppermute x22, waiting for transfers between devices, passed_along(): lax.ppermute(value, axis, [(source, source + steps) for source in range(l...  182 us
    all_to_all x11, blocking collectives, return_rows(): lax.all_to_all(rows, 'expert', split_axis=0, concat_axis=0, tiled=True)  135 us
    ppermute x22, starting transfers between devices, passed_along(): lax.ppermute(value, axis, [(source, source + steps) for source in range(l...  109 us
    all_to_all x11, waiting for transfers between devices, forward_work(): lax.all_to_all(send, 'expert', split_axis=0, concat_axis=0, tiled=True)  107 us
    all_to_all x11, waiting for transfers between devices, backward_work(): lax.all_to_all(grad_send, 'expert', split_axis=0, concat_axis=0, tiled=True)  98.4 us
    all_to_all x11, waiting for transfers between devices, return_rows(): lax.all_to_all(rows, 'expert', split_axis=0, concat_axis=0, tiled=True)  90.3 us
    dot_general x12, matrix products, contract_last(): lax.dot_general(left, right, (((1,), (1,)), ((), ())), preferred_element_...  47.6 us
    all_to_all x11, starting transfers between devices, forward_work(): lax.all_to_all(send, 'expert', split_axis=0, concat_axis=0, tiled=True)  44.3 us
  transfers between devices with their start and end apart: 55, of which 55 were waited for; matrix products, arithmetic and copies ran while one was open for 3% of the time, Pallas kernels for 0%

profile of v2, /device:TPU:1, one launch (start us, length us, event | category | flops | bytes accessed | tf_op | source)
XLA Modules:
  0.0 1157.9 jit_solution(18326451697253902095)
XLA Ops:
  8.0 515.0 %while.33 = (s32[]{:T(128)}, bf16[32,4096]{1,0:T(8,128)(2,1)S(1)}, bf16[5,32,4096]{2,1,0:T(8,128)(2,1)S(1)}, bf16[5,32,4096]{2,1,0:T(8,128)(2,1)}, f32[5,16,4,76...) while((s32[]{:T(128)}, bf16[32,4096]{1,0:T(8,128)(2,1)S(1)}, ...), condition=%wide.region_7.8_spmd, body=%wide.region_2.7_spmd.sunk | while | flops 1327405056 | bytes 82642432 | solution.py:156
  12.7 8.6 all-to-all-start
  21.3 10.5 all-to-all-done
  33.7 12.3 %all_to_all.30 = bf16[16,4,4096]{2,1,0:T(4,128)(2,1)S(1)} all-to-all(bf16[16,4,4096]{2,1,0:T(4,128)(2,1)S(1)} %copy.68), channel_id=1, replica_groups=mesh['section'=8,'expert'=16] {'expert'}, dimensions={0} | all-to-all | bytes 1048576 | tf_op jit(solution)/shard_map/while/body/eval_jaxpr/all_to_all | solution.py:73
  68.7 10.5 all-to-all-done
  79.2 10.2 conditional.4
  89.8 13.0 %all_to_all.30 = bf16[16,4,4096]{2,1,0:T(4,128)(2,1)S(1)} all-to-all(bf16[16,4,4096]{2,1,0:T(4,128)(2,1)S(1)} %copy.68), channel_id=1, replica_groups=mesh['section'=8,'expert'=16] {'expert'}, dimensions={0} | all-to-all | bytes 1048576 | tf_op jit(solution)/shard_map/while/body/eval_jaxpr/all_to_all | solution.py:73
  116.9 10.7 all-to-all-done
  127.6 10.2 conditional.4
  138.2 13.4 %all_to_all.30 = bf16[16,4,4096]{2,1,0:T(4,128)(2,1)S(1)} all-to-all(bf16[16,4,4096]{2,1,0:T(4,128)(2,1)S(1)} %copy.68), channel_id=1, replica_groups=mesh['section'=8,'expert'=16] {'expert'}, dimensions={0} | all-to-all | bytes 1048576 | tf_op jit(solution)/shard_map/while/body/eval_jaxpr/all_to_all | solution.py:73
  168.7 9.6 all-to-all-done
  178.3 10.2 conditional.4
  188.9 14.1 %all_to_all.30 = bf16[16,4,4096]{2,1,0:T(4,128)(2,1)S(1)} all-to-all(bf16[16,4,4096]{2,1,0:T(4,128)(2,1)S(1)} %copy.68), channel_id=1, replica_groups=mesh['section'=8,'expert'=16] {'expert'}, dimensions={0} | all-to-all | bytes 1048576 | tf_op jit(solution)/shard_map/while/body/eval_jaxpr/all_to_all | solution.py:73
  219.0 9.6 all-to-all-done
  228.6 10.2 conditional.4
  239.2 11.6 %all_to_all.30 = bf16[16,4,4096]{2,1,0:T(4,128)(2,1)S(1)} all-to-all(bf16[16,4,4096]{2,1,0:T(4,128)(2,1)S(1)} %copy.68), channel_id=1, replica_groups=mesh['section'=8,'expert'=16] {'expert'}, dimensions={0} | all-to-all | bytes 1048576 | tf_op jit(solution)/shard_map/while/body/eval_jaxpr/all_to_all | solution.py:73
  269.4 8.9 all-to-all-done
  280.2 11.6 %all_to_all.30 = bf16[16,4,4096]{2,1,0:T(4,128)(2,1)S(1)} all-to-all(bf16[16,4,4096]{2,1,0:T(4,128)(2,1)S(1)} %copy.68), channel_id=1, replica_groups=mesh['section'=8,'expert'=16] {'expert'}, dimensions={0} | all-to-all | bytes 1048576 | tf_op jit(solution)/shard_map/while/body/eval_jaxpr/all_to_all | solution.py:73
  292.3 15.7 %collective-permute-start = (bf16[32,4096]{1,0:T(8,128)(2,1)S(1)}, bf16[32,4096]{1,0:T(8,128)(2,1)S(1)}, u32[]{:S(2)}, u32[]{:S(2)}) collective-permute-start(bf16[32,4096]{1,0:T(8,128)(2,1)S(1)} %get-tuple-element.826), channel_id=1, source_target_pairs={{0,16},{16,32},{32,48},{48,64},{64,80},{80,96},{96,112},{1,17},{17... | collective-permute-start | bytes 786440 | tf_op jit(solution)/shard_map/while/body/eval_jaxpr/ppermute | solution.py:12
  319.7 10.9 all-to-all-done
  332.4 12.0 %all_to_all.30 = bf16[16,4,4096]{2,1,0:T(4,128)(2,1)S(1)} all-to-all(bf16[16,4,4096]{2,1,0:T(4,128)(2,1)S(1)} %copy.68), channel_id=1, replica_groups=mesh['section'=8,'expert'=16] {'expert'}, dimensions={0} | all-to-all | bytes 1048576 | tf_op jit(solution)/shard_map/while/body/eval_jaxpr/all_to_all | solution.py:73
  362.4 8.9 all-to-all-done
  373.2 11.8 %all_to_all.30 = bf16[16,4,4096]{2,1,0:T(4,128)(2,1)S(1)} all-to-all(bf16[16,4,4096]{2,1,0:T(4,128)(2,1)S(1)} %copy.68), channel_id=1, replica_groups=mesh['section'=8,'expert'=16] {'expert'}, dimensions={0} | all-to-all | bytes 1048576 | tf_op jit(solution)/shard_map/while/body/eval_jaxpr/all_to_all | solution.py:73
  405.0 8.9 all-to-all-done
  415.7 11.6 %all_to_all.30 = bf16[16,4,4096]{2,1,0:T(4,128)(2,1)S(1)} all-to-all(bf16[16,4,4096]{2,1,0:T(4,128)(2,1)S(1)} %copy.68), channel_id=1, replica_groups=mesh['section'=8,'expert'=16] {'expert'}, dimensions={0} | all-to-all | bytes 1048576 | tf_op jit(solution)/shard_map/while/body/eval_jaxpr/all_to_all | solution.py:73
  446.7 8.9 all-to-all-done
  457.5 11.6 %all_to_all.30 = bf16[16,4,4096]{2,1,0:T(4,128)(2,1)S(1)} all-to-all(bf16[16,4,4096]{2,1,0:T(4,128)(2,1)S(1)} %copy.68), channel_id=1, replica_groups=mesh['section'=8,'expert'=16] {'expert'}, dimensions={0} | all-to-all | bytes 1048576 | tf_op jit(solution)/shard_map/while/body/eval_jaxpr/all_to_all | solution.py:73
  488.6 8.9 all-to-all-done
  499.4 11.6 %all_to_all.30 = bf16[16,4,4096]{2,1,0:T(4,128)(2,1)S(1)} all-to-all(bf16[16,4,4096]{2,1,0:T(4,128)(2,1)S(1)} %copy.68), channel_id=1, replica_groups=mesh['section'=8,'expert'=16] {'expert'}, dimensions={0} | all-to-all | bytes 1048576 | tf_op jit(solution)/shard_map/while/body/eval_jaxpr/all_to_all | solution.py:73
  511.5 8.1 collective-permute-start
  524.4 630.4 %while.34 = (s32[]{:T(128)}, bf16[32,4096]{1,0:T(8,128)(2,1)S(1)}, bf16[5,32,4096]{2,1,0:T(8,128)(2,1)}, pred[]{:T(512)}, s32[11]{0:T(128)S(1)}, /*index=5*/s32[...) while((s32[]{:T(128)}, bf16[32,4096]{1,0:T(8,128)(2,1)S(1)}, ...), condition=%wide.region_14.15_spmd, body=%wide.region_8.14_spmd.sunk | while | flops 1262360704 | bytes 57610496 | solution.py:218
  532.5 8.9 all-to-all-done.2
  546.8 8.2 all-to-all-done.3
  560.3 10.0 collective-permute-done.1
  578.4 8.9 all-to-all-done.2
  592.7 8.2 all-to-all-done.3
  621.6 8.9 all-to-all-done.2
  635.8 8.2 all-to-all-done.3
  649.3 9.0 collective-permute-done.1
  666.5 8.9 all-to-all-done.2
  680.7 8.2 all-to-all-done.3
  694.2 8.5 collective-permute-done.1
  710.8 8.9 all-to-all-done.2
  725.1 8.2 all-to-all-done.3
  738.5 8.8 collective-permute-done.1
  755.5 8.9 all-to-all-done.2
  769.7 8.2 all-to-all-done.3
  783.2 90.4 %collective-permute-done.1 = bf16[32,4096]{1,0:T(8,128)(2,1)S(1)} collective-permute-done((bf16[32,4096]{1,0:T(8,128)(2,1)S(1)}, bf16[32,4096]{1,0:T(8,128)(2,1)S(1)}, u32[]{:S(2)}, u32[]{:S(2)}) %collective-permute-start.1) | collective-permute-done | bytes 262176 | tf_op jit(solution)/shard_map/while/body/eval_jaxpr/ppermute | solution.py:12
  881.7 8.9 all-to-all-done.2
  890.7 15.9 %conditional.5 = (bf16[16,4,4096]{2,1,0:T(4,128)(2,1)}) conditional(s32[]{:T(128)} %convert_element_type.161, () %tuple.107, (bf16[16,4,4096]{2,1,0:T(4,128)(2,1)S(1)}, bf16[768,4096]{1,0:T(8,128)(2,1)}, f32[5,16,4,768]{3,2,1,0:T(4,128)}, s32[]{:T(128)}, f32[5,16,4,768]{3,2,1,0:T(4,128)}, /*index=5*/bf16[4096,768]{1,0:T(8,128)(2,1)}, ...), branch_computations={%region_11.11_spmd, %region_12.12_spmd} | conditional | flops 1209270272 | bytes 45744188 | solution.py:177
  910.8 8.2 all-to-all-done.3
  939.5 8.9 all-to-all-done.2
  948.5 15.9 %conditional.5 = (bf16[16,4,4096]{2,1,0:T(4,128)(2,1)}) conditional(s32[]{:T(128)} %convert_element_type.161, () %tuple.107, (bf16[16,4,4096]{2,1,0:T(4,128)(2,1)S(1)}, bf16[768,4096]{1,0:T(8,128)(2,1)}, f32[5,16,4,768]{3,2,1,0:T(4,128)}, s32[]{:T(128)}, f32[5,16,4,768]{3,2,1,0:T(4,128)}, /*index=5*/bf16[4096,768]{1,0:T(8,128)(2,1)}, ...), branch_computations={%region_11.11_spmd, %region_12.12_spmd} | conditional | flops 1209270272 | bytes 45744188 | solution.py:177
  968.7 8.2 all-to-all-done.3
  982.1 8.6 collective-permute-done.1
  998.8 8.9 all-to-all-done.2
  1007.8 15.9 %conditional.5 = (bf16[16,4,4096]{2,1,0:T(4,128)(2,1)}) conditional(s32[]{:T(128)} %convert_element_type.161, () %tuple.107, (bf16[16,4,4096]{2,1,0:T(4,128)(2,1)S(1)}, bf16[768,4096]{1,0:T(8,128)(2,1)}, f32[5,16,4,768]{3,2,1,0:T(4,128)}, s32[]{:T(128)}, f32[5,16,4,768]{3,2,1,0:T(4,128)}, /*index=5*/bf16[4096,768]{1,0:T(8,128)(2,1)}, ...), branch_computations={%region_11.11_spmd, %region_12.12_spmd} | conditional | flops 1209270272 | bytes 45744188 | solution.py:177
  1028.0 8.2 all-to-all-done.3
  1056.6 8.9 all-to-all-done.2
  1065.5 15.9 %conditional.5 = (bf16[16,4,4096]{2,1,0:T(4,128)(2,1)}) conditional(s32[]{:T(128)} %convert_element_type.161, () %tuple.107, (bf16[16,4,4096]{2,1,0:T(4,128)(2,1)S(1)}, bf16[768,4096]{1,0:T(8,128)(2,1)}, f32[5,16,4,768]{3,2,1,0:T(4,128)}, s32[]{:T(128)}, f32[5,16,4,768]{3,2,1,0:T(4,128)}, /*index=5*/bf16[4096,768]{1,0:T(8,128)(2,1)}, ...), branch_computations={%region_11.11_spmd, %region_12.12_spmd} | conditional | flops 1209270272 | bytes 45744188 | solution.py:177
  1085.7 8.2 all-to-all-done.3
  1113.1 8.9 all-to-all-done.2
  1127.3 8.2 all-to-all-done.3
  1138.9 14.8 %collective-permute-start.1 = (bf16[32,4096]{1,0:T(8,128)(2,1)S(1)}, bf16[32,4096]{1,0:T(8,128)(2,1)S(1)}, u32[]{:S(2)}, u32[]{:S(2)}) collective-permute-start(bf16[32,4096]{1,0:T(8,128)(2,1)S(1)} %get-tuple-element.856), channel_id=1, source_target_pairs={{16,0},{32,16},{48,32},{64,48},{80,64},{96,80},{112,96},{17,1},{33... | collective-permute-start | bytes 786440 | tf_op jit(solution)/shard_map/while/body/eval_jaxpr/ppermute | solution.py:12
  (546 shorter events, 545.5 us)
Async XLA Ops:
  12.7 19.1 %all-to-all-start = ((bf16[16,4,4096]{2,1,0:T(4,128)(2,1)}), bf16[16,4,4096]{2,1,0:T(4,128)(2,1)S(1)}, u32[]{:S(2)}, u32[]{:S(2)}) async-start(bf16[16,4,4096]{2,1,0:T(4,128)(2,1)} %copy.67), calls=%async_computation | async-start | bytes 1048576 | tf_op jit(solution)/shard_map/while/body/eval_jaxpr/all_to_all | solution.py:122
  46.4 13.9 %collective-permute-start = (bf16[32,4096]{1,0:T(8,128)(2,1)S(1)}, bf16[32,4096]{1,0:T(8,128)(2,1)S(1)}, u32[]{:S(2)}, u32[]{:S(2)}) collective-permute-start(bf16[32,4096]{1,0:T(8,128)(2,1)S(1)} %get-tuple-element.826), channel_id=1, source_target_pairs={{0,16},{16,32},{32,48},{48,64},{64,80},{80,96},{96,112},{1,17},{17... | collective-permute-start | bytes 786440 | tf_op jit(solution)/shard_map/while/body/eval_jaxpr/ppermute | solution.py:12
  65.1 14.1 %all-to-all-start = ((bf16[16,4,4096]{2,1,0:T(4,128)(2,1)}), bf16[16,4,4096]{2,1,0:T(4,128)(2,1)S(1)}, u32[]{:S(2)}, u32[]{:S(2)}) async-start(bf16[16,4,4096]{2,1,0:T(4,128)(2,1)} %copy.67), calls=%async_computation | async-start | bytes 1048576 | tf_op jit(solution)/shard_map/while/body/eval_jaxpr/all_to_all | solution.py:122
  103.3 5.2 collective-permute-start
  113.3 14.3 %all-to-all-start = ((bf16[16,4,4096]{2,1,0:T(4,128)(2,1)}), bf16[16,4,4096]{2,1,0:T(4,128)(2,1)S(1)}, u32[]{:S(2)}, u32[]{:S(2)}) async-start(bf16[16,4,4096]{2,1,0:T(4,128)(2,1)} %copy.67), calls=%async_computation | async-start | bytes 1048576 | tf_op jit(solution)/shard_map/while/body/eval_jaxpr/all_to_all | solution.py:122
  152.2 8.2 collective-permute-start
  165.1 13.2 %all-to-all-start = ((bf16[16,4,4096]{2,1,0:T(4,128)(2,1)}), bf16[16,4,4096]{2,1,0:T(4,128)(2,1)S(1)}, u32[]{:S(2)}, u32[]{:S(2)}) async-start(bf16[16,4,4096]{2,1,0:T(4,128)(2,1)} %copy.67), calls=%async_computation | async-start | bytes 1048576 | tf_op jit(solution)/shard_map/while/body/eval_jaxpr/all_to_all | solution.py:122
  203.5 7.2 collective-permute-start
  215.5 13.1 %all-to-all-start = ((bf16[16,4,4096]{2,1,0:T(4,128)(2,1)}), bf16[16,4,4096]{2,1,0:T(4,128)(2,1)S(1)}, u32[]{:S(2)}, u32[]{:S(2)}) async-start(bf16[16,4,4096]{2,1,0:T(4,128)(2,1)} %copy.67), calls=%async_computation | async-start | bytes 1048576 | tf_op jit(solution)/shard_map/while/body/eval_jaxpr/all_to_all | solution.py:122
  251.3 9.7 collective-permute-start
  265.8 12.5 %all-to-all-start = ((bf16[16,4,4096]{2,1,0:T(4,128)(2,1)}), bf16[16,4,4096]{2,1,0:T(4,128)(2,1)S(1)}, u32[]{:S(2)}, u32[]{:S(2)}) async-start(bf16[16,4,4096]{2,1,0:T(4,128)(2,1)} %copy.67), calls=%async_computation | async-start | bytes 1048576 | tf_op jit(solution)/shard_map/while/body/eval_jaxpr/all_to_all | solution.py:122
  292.3 19.0 %collective-permute-start = (bf16[32,4096]{1,0:T(8,128)(2,1)S(1)}, bf16[32,4096]{1,0:T(8,128)(2,1)S(1)}, u32[]{:S(2)}, u32[]{:S(2)}) collective-permute-start(bf16[32,4096]{1,0:T(8,128)(2,1)S(1)} %get-tuple-element.826), channel_id=1, source_target_pairs={{0,16},{16,32},{32,48},{48,64},{64,80},{80,96},{96,112},{1,17},{17... | collective-permute-start | bytes 786440 | tf_op jit(solution)/shard_map/while/body/eval_jaxpr/ppermute | solution.py:12
  316.1 14.5 %all-to-all-start = ((bf16[16,4,4096]{2,1,0:T(4,128)(2,1)}), bf16[16,4,4096]{2,1,0:T(4,128)(2,1)S(1)}, u32[]{:S(2)}, u32[]{:S(2)}) async-start(bf16[16,4,4096]{2,1,0:T(4,128)(2,1)} %copy.67), calls=%async_computation | async-start | bytes 1048576 | tf_op jit(solution)/shard_map/while/body/eval_jaxpr/all_to_all | solution.py:122
  345.0 9.1 collective-permute-start
  358.8 12.5 %all-to-all-start = ((bf16[16,4,4096]{2,1,0:T(4,128)(2,1)}), bf16[16,4,4096]{2,1,0:T(4,128)(2,1)S(1)}, u32[]{:S(2)}, u32[]{:S(2)}) async-start(bf16[16,4,4096]{2,1,0:T(4,128)(2,1)} %copy.67), calls=%async_computation | async-start | bytes 1048576 | tf_op jit(solution)/shard_map/while/body/eval_jaxpr/all_to_all | solution.py:122
  385.5 11.1 collective-permute-start
  401.4 12.5 %all-to-all-start = ((bf16[16,4,4096]{2,1,0:T(4,128)(2,1)}), bf16[16,4,4096]{2,1,0:T(4,128)(2,1)S(1)}, u32[]{:S(2)}, u32[]{:S(2)}) async-start(bf16[16,4,4096]{2,1,0:T(4,128)(2,1)} %copy.67), calls=%async_computation | async-start | bytes 1048576 | tf_op jit(solution)/shard_map/while/body/eval_jaxpr/all_to_all | solution.py:122
  427.9 10.5 collective-permute-start
  443.1 12.5 %all-to-all-start = ((bf16[16,4,4096]{2,1,0:T(4,128)(2,1)}), bf16[16,4,4096]{2,1,0:T(4,128)(2,1)S(1)}, u32[]{:S(2)}, u32[]{:S(2)}) async-start(bf16[16,4,4096]{2,1,0:T(4,128)(2,1)} %copy.67), calls=%async_computation | async-start | bytes 1048576 | tf_op jit(solution)/shard_map/while/body/eval_jaxpr/all_to_all | solution.py:122
  469.7 10.5 collective-permute-start
  485.0 12.5 %all-to-all-start = ((bf16[16,4,4096]{2,1,0:T(4,128)(2,1)}), bf16[16,4,4096]{2,1,0:T(4,128)(2,1)S(1)}, u32[]{:S(2)}, u32[]{:S(2)}) async-start(bf16[16,4,4096]{2,1,0:T(4,128)(2,1)} %copy.67), calls=%async_computation | async-start | bytes 1048576 | tf_op jit(solution)/shard_map/while/body/eval_jaxpr/all_to_all | solution.py:122
  511.5 11.4 collective-permute-start
  529.0 12.5 %all-to-all-start.2 = ((bf16[16,4,4096]{2,1,0:T(4,128)(2,1)}), bf16[16,4,4096]{2,1,0:T(4,128)(2,1)S(1)}, u32[]{:S(2)}, u32[]{:S(2)}) async-start(bf16[16,4,4096]{2,1,0:T(4,128)(2,1)} %copy.69), calls=%async_computation.2 | async-start | bytes 1048576 | tf_op jit(solution)/shard_map/while/body/eval_jaxpr/all_to_all | solution.py:182
  542.5 12.5 %all-to-all-start.3 = ((bf16[16,4,4096]{2,1,0:T(4,128)(2,1)}), bf16[16,4,4096]{2,1,0:T(4,128)(2,1)S(1)}, u32[]{:S(2)}, u32[]{:S(2)}) async-start(bf16[16,4,4096]{2,1,0:T(4,128)(2,1)} %get-tuple-element.993), calls=%async_computation.3 | async-start | bytes 1048576 | tf_op jit(solution)/shard_map/while/body/eval_jaxpr/all_to_all | solution.py:73
  555.2 15.1 %copy-start.5 = (bf16[4,2,32,16,4]{2,3,1,4,0:T(8,128)(2,1)S(1)}, bf16[4,2,32,16,4]{2,3,1,4,0:T(8,128)(2,1)}, u32[]{:S(2)}) copy-start(bf16[4,2,32,16,4]{2,3,1,4,0:T(8,128)(2,1)} %copy-done.4) | copy-start | bytes 98308 | tf_op jit(solution)/shard_map/while
  555.2 15.1 %copy-start.7 = (s32[11]{0:T(128)S(1)}, s32[11]{0:T(128)}, u32[]{:S(2)}) copy-start(s32[11]{0:T(128)} %copy-done.6) | copy-start | bytes 136 | tf_op jit(solution)/shard_map/while
  558.4 11.9 %collective-permute-start.1 = (bf16[32,4096]{1,0:T(8,128)(2,1)S(1)}, bf16[32,4096]{1,0:T(8,128)(2,1)S(1)}, u32[]{:S(2)}, u32[]{:S(2)}) collective-permute-start(bf16[32,4096]{1,0:T(8,128)(2,1)S(1)} %get-tuple-element.856), channel_id=1, source_target_pairs={{16,0},{32,16},{48,32},{64,48},{80,64},{96,80},{112,96},{17,1},{33... | collective-permute-start | bytes 786440 | tf_op jit(solution)/shard_map/while/body/eval_jaxpr/ppermute | solution.py:12
  574.8 12.5 %all-to-all-start.2 = ((bf16[16,4,4096]{2,1,0:T(4,128)(2,1)}), bf16[16,4,4096]{2,1,0:T(4,128)(2,1)S(1)}, u32[]{:S(2)}, u32[]{:S(2)}) async-start(bf16[16,4,4096]{2,1,0:T(4,128)(2,1)} %copy.69), calls=%async_computation.2 | async-start | bytes 1048576 | tf_op jit(solution)/shard_map/while/body/eval_jaxpr/all_to_all | solution.py:182
  588.3 12.5 %all-to-all-start.3 = ((bf16[16,4,4096]{2,1,0:T(4,128)(2,1)}), bf16[16,4,4096]{2,1,0:T(4,128)(2,1)S(1)}, u32[]{:S(2)}, u32[]{:S(2)}) async-start(bf16[16,4,4096]{2,1,0:T(4,128)(2,1)} %get-tuple-element.993), calls=%async_computation.3 | async-start | bytes 1048576 | tf_op jit(solution)/shard_map/while/body/eval_jaxpr/all_to_all | solution.py:73
  604.2 9.2 collective-permute-start.1
  618.0 12.5 %all-to-all-start.2 = ((bf16[16,4,4096]{2,1,0:T(4,128)(2,1)}), bf16[16,4,4096]{2,1,0:T(4,128)(2,1)S(1)}, u32[]{:S(2)}, u32[]{:S(2)}) async-start(bf16[16,4,4096]{2,1,0:T(4,128)(2,1)} %copy.69), calls=%async_computation.2 | async-start | bytes 1048576 | tf_op jit(solution)/shard_map/while/body/eval_jaxpr/all_to_all | solution.py:182
  631.5 12.5 %all-to-all-start.3 = ((bf16[16,4,4096]{2,1,0:T(4,128)(2,1)}), bf16[16,4,4096]{2,1,0:T(4,128)(2,1)S(1)}, u32[]{:S(2)}, u32[]{:S(2)}) async-start(bf16[16,4,4096]{2,1,0:T(4,128)(2,1)} %get-tuple-element.993), calls=%async_computation.3 | async-start | bytes 1048576 | tf_op jit(solution)/shard_map/while/body/eval_jaxpr/all_to_all | solution.py:73
  644.2 14.2 %copy-start.5 = (bf16[4,2,32,16,4]{2,3,1,4,0:T(8,128)(2,1)S(1)}, bf16[4,2,32,16,4]{2,3,1,4,0:T(8,128)(2,1)}, u32[]{:S(2)}) copy-start(bf16[4,2,32,16,4]{2,3,1,4,0:T(8,128)(2,1)} %copy-done.4) | copy-start | bytes 98308 | tf_op jit(solution)/shard_map/while
  644.2 14.2 %copy-start.7 = (s32[11]{0:T(128)S(1)}, s32[11]{0:T(128)}, u32[]{:S(2)}) copy-start(s32[11]{0:T(128)} %copy-done.6) | copy-start | bytes 136 | tf_op jit(solution)/shard_map/while
  647.4 11.0 collective-permute-start.1
  662.9 12.5 %all-to-all-start.2 = ((bf16[16,4,4096]{2,1,0:T(4,128)(2,1)}), bf16[16,4,4096]{2,1,0:T(4,128)(2,1)S(1)}, u32[]{:S(2)}, u32[]{:S(2)}) async-start(bf16[16,4,4096]{2,1,0:T(4,128)(2,1)} %copy.69), calls=%async_computation.2 | async-start | bytes 1048576 | tf_op jit(solution)/shard_map/while/body/eval_jaxpr/all_to_all | solution.py:182
  676.4 12.5 %all-to-all-start.3 = ((bf16[16,4,4096]{2,1,0:T(4,128)(2,1)}), bf16[16,4,4096]{2,1,0:T(4,128)(2,1)S(1)}, u32[]{:S(2)}, u32[]{:S(2)}) async-start(bf16[16,4,4096]{2,1,0:T(4,128)(2,1)} %get-tuple-element.993), calls=%async_computation.3 | async-start | bytes 1048576 | tf_op jit(solution)/shard_map/while/body/eval_jaxpr/all_to_all | solution.py:73
  692.3 10.4 collective-permute-start.1
  707.2 12.5 %all-to-all-start.2 = ((bf16[16,4,4096]{2,1,0:T(4,128)(2,1)}), bf16[16,4,4096]{2,1,0:T(4,128)(2,1)S(1)}, u32[]{:S(2)}, u32[]{:S(2)}) async-start(bf16[16,4,4096]{2,1,0:T(4,128)(2,1)} %copy.69), calls=%async_computation.2 | async-start | bytes 1048576 | tf_op jit(solution)/shard_map/while/body/eval_jaxpr/all_to_all | solution.py:182
  720.7 12.5 %all-to-all-start.3 = ((bf16[16,4,4096]{2,1,0:T(4,128)(2,1)}), bf16[16,4,4096]{2,1,0:T(4,128)(2,1)S(1)}, u32[]{:S(2)}, u32[]{:S(2)}) async-start(bf16[16,4,4096]{2,1,0:T(4,128)(2,1)} %get-tuple-element.993), calls=%async_computation.3 | async-start | bytes 1048576 | tf_op jit(solution)/shard_map/while/body/eval_jaxpr/all_to_all | solution.py:73
  733.4 13.9 %copy-start.5 = (bf16[4,2,32,16,4]{2,3,1,4,0:T(8,128)(2,1)S(1)}, bf16[4,2,32,16,4]{2,3,1,4,0:T(8,128)(2,1)}, u32[]{:S(2)}) copy-start(bf16[4,2,32,16,4]{2,3,1,4,0:T(8,128)(2,1)} %copy-done.4) | copy-start | bytes 98308 | tf_op jit(solution)/shard_map/while
  736.6 10.7 collective-permute-start.1
  751.9 12.5 %all-to-all-start.2 = ((bf16[16,4,4096]{2,1,0:T(4,128)(2,1)}), bf16[16,4,4096]{2,1,0:T(4,128)(2,1)S(1)}, u32[]{:S(2)}, u32[]{:S(2)}) async-start(bf16[16,4,4096]{2,1,0:T(4,128)(2,1)} %copy.69), calls=%async_computation.2 | async-start | bytes 1048576 | tf_op jit(solution)/shard_map/while/body/eval_jaxpr/all_to_all | solution.py:182
  765.4 12.5 %all-to-all-start.3 = ((bf16[16,4,4096]{2,1,0:T(4,128)(2,1)}), bf16[16,4,4096]{2,1,0:T(4,128)(2,1)S(1)}, u32[]{:S(2)}, u32[]{:S(2)}) async-start(bf16[16,4,4096]{2,1,0:T(4,128)(2,1)} %get-tuple-element.993), calls=%async_computation.3 | async-start | bytes 1048576 | tf_op jit(solution)/shard_map/while/body/eval_jaxpr/all_to_all | solution.py:73
  778.1 95.5 %copy-start.5 = (bf16[4,2,32,16,4]{2,3,1,4,0:T(8,128)(2,1)S(1)}, bf16[4,2,32,16,4]{2,3,1,4,0:T(8,128)(2,1)}, u32[]{:S(2)}) copy-start(bf16[4,2,32,16,4]{2,3,1,4,0:T(8,128)(2,1)} %copy-done.4) | copy-start | bytes 98308 | tf_op jit(solution)/shard_map/while
  778.1 95.5 %copy-start.7 = (s32[11]{0:T(128)S(1)}, s32[11]{0:T(128)}, u32[]{:S(2)}) copy-start(s32[11]{0:T(128)} %copy-done.6) | copy-start | bytes 136 | tf_op jit(solution)/shard_map/while
  781.3 92.3 %collective-permute-start.1 = (bf16[32,4096]{1,0:T(8,128)(2,1)S(1)}, bf16[32,4096]{1,0:T(8,128)(2,1)S(1)}, u32[]{:S(2)}, u32[]{:S(2)}) collective-permute-start(bf16[32,4096]{1,0:T(8,128)(2,1)S(1)} %get-tuple-element.856), channel_id=1, source_target_pairs={{16,0},{32,16},{48,32},{64,48},{80,64},{96,80},{112,96},{17,1},{33... | collective-permute-start | bytes 786440 | tf_op jit(solution)/shard_map/while/body/eval_jaxpr/ppermute | solution.py:12
  878.1 12.5 %all-to-all-start.2 = ((bf16[16,4,4096]{2,1,0:T(4,128)(2,1)}), bf16[16,4,4096]{2,1,0:T(4,128)(2,1)S(1)}, u32[]{:S(2)}, u32[]{:S(2)}) async-start(bf16[16,4,4096]{2,1,0:T(4,128)(2,1)} %copy.69), calls=%async_computation.2 | async-start | bytes 1048576 | tf_op jit(solution)/shard_map/while/body/eval_jaxpr/all_to_all | solution.py:182
  906.5 12.5 %all-to-all-start.3 = ((bf16[16,4,4096]{2,1,0:T(4,128)(2,1)}), bf16[16,4,4096]{2,1,0:T(4,128)(2,1)S(1)}, u32[]{:S(2)}, u32[]{:S(2)}) async-start(bf16[16,4,4096]{2,1,0:T(4,128)(2,1)} %get-tuple-element.993), calls=%async_computation.3 | async-start | bytes 1048576 | tf_op jit(solution)/shard_map/while/body/eval_jaxpr/all_to_all | solution.py:73
  922.4 9.0 collective-permute-start.1
  935.9 12.5 %all-to-all-start.2 = ((bf16[16,4,4096]{2,1,0:T(4,128)(2,1)}), bf16[16,4,4096]{2,1,0:T(4,128)(2,1)S(1)}, u32[]{:S(2)}, u32[]{:S(2)}) async-start(bf16[16,4,4096]{2,1,0:T(4,128)(2,1)} %copy.69), calls=%async_computation.2 | async-start | bytes 1048576 | tf_op jit(solution)/shard_map/while/body/eval_jaxpr/all_to_all | solution.py:182
  964.3 12.5 %all-to-all-start.3 = ((bf16[16,4,4096]{2,1,0:T(4,128)(2,1)}), bf16[16,4,4096]{2,1,0:T(4,128)(2,1)S(1)}, u32[]{:S(2)}, u32[]{:S(2)}) async-start(bf16[16,4,4096]{2,1,0:T(4,128)(2,1)} %get-tuple-element.993), calls=%async_computation.3 | async-start | bytes 1048576 | tf_op jit(solution)/shard_map/while/body/eval_jaxpr/all_to_all | solution.py:73
  980.2 10.5 collective-permute-start.1
  995.2 12.5 %all-to-all-start.2 = ((bf16[16,4,4096]{2,1,0:T(4,128)(2,1)}), bf16[16,4,4096]{2,1,0:T(4,128)(2,1)S(1)}, u32[]{:S(2)}, u32[]{:S(2)}) async-start(bf16[16,4,4096]{2,1,0:T(4,128)(2,1)} %copy.69), calls=%async_computation.2 | async-start | bytes 1048576 | tf_op jit(solution)/shard_map/while/body/eval_jaxpr/all_to_all | solution.py:182
  1023.6 12.5 %all-to-all-start.3 = ((bf16[16,4,4096]{2,1,0:T(4,128)(2,1)}), bf16[16,4,4096]{2,1,0:T(4,128)(2,1)S(1)}, u32[]{:S(2)}, u32[]{:S(2)}) async-start(bf16[16,4,4096]{2,1,0:T(4,128)(2,1)} %get-tuple-element.993), calls=%async_computation.3 | async-start | bytes 1048576 | tf_op jit(solution)/shard_map/while/body/eval_jaxpr/all_to_all | solution.py:73
  1039.5 9.0 collective-permute-start.1
  1053.0 12.5 %all-to-all-start.2 = ((bf16[16,4,4096]{2,1,0:T(4,128)(2,1)}), bf16[16,4,4096]{2,1,0:T(4,128)(2,1)S(1)}, u32[]{:S(2)}, u32[]{:S(2)}) async-start(bf16[16,4,4096]{2,1,0:T(4,128)(2,1)} %copy.69), calls=%async_computation.2 | async-start | bytes 1048576 | tf_op jit(solution)/shard_map/while/body/eval_jaxpr/all_to_all | solution.py:182
  1081.4 12.5 %all-to-all-start.3 = ((bf16[16,4,4096]{2,1,0:T(4,128)(2,1)}), bf16[16,4,4096]{2,1,0:T(4,128)(2,1)S(1)}, u32[]{:S(2)}, u32[]{:S(2)}) async-start(bf16[16,4,4096]{2,1,0:T(4,128)(2,1)} %get-tuple-element.993), calls=%async_computation.3 | async-start | bytes 1048576 | tf_op jit(solution)/shard_map/while/body/eval_jaxpr/all_to_all | solution.py:73
  1097.3 7.7 collective-permute-start.1
  1109.5 12.5 %all-to-all-start.2 = ((bf16[16,4,4096]{2,1,0:T(4,128)(2,1)}), bf16[16,4,4096]{2,1,0:T(4,128)(2,1)S(1)}, u32[]{:S(2)}, u32[]{:S(2)}) async-start(bf16[16,4,4096]{2,1,0:T(4,128)(2,1)} %copy.69), calls=%async_computation.2 | async-start | bytes 1048576 | tf_op jit(solution)/shard_map/while/body/eval_jaxpr/all_to_all | solution.py:182
  1123.0 12.5 %all-to-all-start.3 = ((bf16[16,4,4096]{2,1,0:T(4,128)(2,1)}), bf16[16,4,4096]{2,1,0:T(4,128)(2,1)S(1)}, u32[]{:S(2)}, u32[]{:S(2)}) async-start(bf16[16,4,4096]{2,1,0:T(4,128)(2,1)} %get-tuple-element.993), calls=%async_computation.3 | async-start | bytes 1048576 | tf_op jit(solution)/shard_map/while/body/eval_jaxpr/all_to_all | solution.py:73
  1135.7 19.2 %copy-start.5 = (bf16[4,2,32,16,4]{2,3,1,4,0:T(8,128)(2,1)S(1)}, bf16[4,2,32,16,4]{2,3,1,4,0:T(8,128)(2,1)}, u32[]{:S(2)}) copy-start(bf16[4,2,32,16,4]{2,3,1,4,0:T(8,128)(2,1)} %copy-done.4) | copy-start | bytes 98308 | tf_op jit(solution)/shard_map/while
  1135.7 19.2 %copy-start.7 = (s32[11]{0:T(128)S(1)}, s32[11]{0:T(128)}, u32[]{:S(2)}) copy-start(s32[11]{0:T(128)} %copy-done.6) | copy-start | bytes 136 | tf_op jit(solution)/shard_map/while
  1138.9 16.0 %collective-permute-start.1 = (bf16[32,4096]{1,0:T(8,128)(2,1)S(1)}, bf16[32,4096]{1,0:T(8,128)(2,1)S(1)}, u32[]{:S(2)}, u32[]{:S(2)}) collective-permute-start(bf16[32,4096]{1,0:T(8,128)(2,1)S(1)} %get-tuple-element.856), channel_id=1, source_target_pairs={{16,0},{32,16},{48,32},{64,48},{80,64},{96,80},{112,96},{17,1},{33... | collective-permute-start | bytes 786440 | tf_op jit(solution)/shard_map/while/body/eval_jaxpr/ppermute | solution.py:12
  (53 other events, 326.5 us)

commit v3 on v2

--- a/solution.py
+++ b/solution.py
@@ -1,9 +1,121 @@
 import jax
 import jax.numpy as jnp
 from jax import lax
+from jax.experimental import pallas as pl
+from jax.experimental.pallas import tpu as pltpu
 from jax.sharding import PartitionSpec as P
 
 EPS = 1e-06
+HID_BLOCK = 256
+NT = (((1,), (1,)), ((), ()))
+
+
+def _fwd_kernel(rows_ref, wg_ref, wu_ref, wd_ref, out_ref, pg_ref, pu_ref, acc_ref):
+    step = pl.program_id(0)
+
+    @pl.when(step == 0)
+    def _():
+        acc_ref[...] = jnp.zeros_like(acc_ref)
+
+    rows = rows_ref[...]
+    pre_gate = jnp.dot(rows, wg_ref[...], preferred_element_type=jnp.float32)
+    pre_up = jnp.dot(rows, wu_ref[...], preferred_element_type=jnp.float32)
+    pg_ref[...] = pre_gate
+    pu_ref[...] = pre_up
+    product = (pre_gate * jax.nn.sigmoid(pre_gate) * pre_up).astype(jnp.bfloat16)
+    acc_ref[...] += jnp.dot(product, wd_ref[...], preferred_element_type=jnp.float32)
+
+    @pl.when(step == pl.num_programs(0) - 1)
+    def _():
+        out_ref[...] = acc_ref[...].astype(out_ref.dtype)
+
+
+def expert_forward_kernel(rows, w_gate, w_up, w_down, interpret=False):
+    n, width = rows.shape
+    inner = w_gate.shape[1]
+    steps = inner // HID_BLOCK
+    cost = pl.CostEstimate(
+        flops=6 * n * width * inner,
+        transcendentals=n * inner,
+        bytes_accessed=3 * width * inner * 2 + 2 * n * width * 2 + 2 * n * inner * 4,
+    )
+    return pl.pallas_call(
+        _fwd_kernel,
+        grid=(steps,),
+        in_specs=[
+            pl.BlockSpec((n, width), lambda h: (0, 0)),
+            pl.BlockSpec((width, HID_BLOCK), lambda h: (0, h)),
+            pl.BlockSpec((width, HID_BLOCK), lambda h: (0, h)),
+            pl.BlockSpec((HID_BLOCK, width), lambda h: (h, 0)),
+        ],
+        out_specs=[
+            pl.BlockSpec((n, width), lambda h: (0, 0)),
+            pl.BlockSpec((n, HID_BLOCK), lambda h: (0, h)),
+            pl.BlockSpec((n, HID_BLOCK), lambda h: (0, h)),
+        ],
+        out_shape=[
+            jax.ShapeDtypeStruct((n, width), jnp.bfloat16),
+            jax.ShapeDtypeStruct((n, inner), jnp.float32),
+            jax.ShapeDtypeStruct((n, inner), jnp.float32),
+        ],
+        scratch_shapes=[pltpu.VMEM((n, width), jnp.float32)],
+        compiler_params=pltpu.CompilerParams(dimension_semantics=("arbitrary",)),
+        cost_estimate=cost,
+        interpret=interpret,
+    )(rows, w_gate, w_up, w_down)
+
+
+def _bwd_kernel(grad_ref, pg_ref, pu_ref, wg_ref, wu_ref, wd_ref, back_ref, acc_ref):
+    step = pl.program_id(0)
+
+    @pl.when(step == 0)
+    def _():
+        acc_ref[...] = jnp.zeros_like(acc_ref)
+
+    d_hidden = lax.dot_general(
+        grad_ref[...], wd_ref[...], NT, preferred_element_type=jnp.float32
+    )
+    pre_gate = pg_ref[...]
+    pre_up = pu_ref[...]
+    sigma = jax.nn.sigmoid(pre_gate)
+    d_gate = (d_hidden * pre_up * sigma * (1.0 + pre_gate * (1.0 - sigma))).astype(jnp.bfloat16)
+    d_up = (d_hidden * pre_gate * sigma).astype(jnp.bfloat16)
+    acc_ref[...] += lax.dot_general(
+        d_gate, wg_ref[...], NT, preferred_element_type=jnp.float32
+    ) + lax.dot_general(d_up, wu_ref[...], NT, preferred_element_type=jnp.float32)
+
+    @pl.when(step == pl.num_programs(0) - 1)
+    def _():
+        back_ref[...] = acc_ref[...].astype(back_ref.dtype)
+
+
+def expert_backward_kernel(grad_rows, pre_gate, pre_up, w_gate, w_up, w_down, interpret=False):
+    n, width = grad_rows.shape
+    inner = w_gate.shape[1]
+    steps = inner // HID_BLOCK
+    cost = pl.CostEstimate(
+        flops=6 * n * width * inner,
+        transcendentals=n * inner,
+        bytes_accessed=3 * width * inner * 2 + 2 * n * width * 2 + 2 * n * inner * 4,
+    )
+    return pl.pallas_call(
+        _bwd_kernel,
+        grid=(steps,),
+        in_specs=[
+            pl.BlockSpec((n, width), lambda h: (0, 0)),
+            pl.BlockSpec((n, HID_BLOCK), lambda h: (0, h)),
+            pl.BlockSpec((n, HID_BLOCK), lambda h: (0, h)),
+            pl.BlockSpec((width, HID_BLOCK), lambda h: (0, h)),
+            pl.BlockSpec((width, HID_BLOCK), lambda h: (0, h)),
+            pl.BlockSpec((HID_BLOCK, width), lambda h: (h, 0)),
+        ],
+        out_specs=pl.BlockSpec((n, width), lambda h: (0, 0)),
+        out_shape=jax.ShapeDtypeStruct((n, width), jnp.bfloat16),
+        scratch_shapes=[pltpu.VMEM((n, width), jnp.float32)],
+        compiler_params=pltpu.CompilerParams(dimension_semantics=("arbitrary",)),
+        cost_estimate=cost,
+        interpret=interpret,
+    )(grad_rows, pre_gate, pre_up, w_gate, w_up, w_down)
 
 
 def passed_along(value, axis, steps):
@@ -104,15 +216,13 @@
         ).astype(jnp.bfloat16)
 
         def forward_active(operand):
-            pre_gate, pre_up = pre_products(operand, weight_gate, weight_up)
-            product = (pre_gate * jax.nn.sigmoid(pre_gate) * pre_up).astype(jnp.bfloat16)
-            output = jnp.einsum(
-                "ech,hd->ecd", product, weight_down, preferred_element_type=jnp.float32
-            ).astype(jnp.bfloat16)
-            return (output, pre_gate, pre_up)
+            output, pre_gate, pre_up = expert_forward_kernel(
+                operand.reshape(total_rows, width), weight_gate, weight_up, weight_down
+            )
+            return (output.reshape(operand.shape), pre_gate, pre_up)
 
         def forward_resting(operand):
-            pre_zero = jnp.zeros(operand.shape[:-1] + (inner,), jnp.float32)
+            pre_zero = jnp.zeros((total_rows, inner), jnp.float32)
             return (jnp.zeros_like(operand), pre_zero, pre_zero)
 
         output, pre_gate, pre_up = lax.cond(
@@ -150,8 +260,8 @@
         jnp.zeros((tok, width), jnp.bfloat16),
         jnp.zeros(spare + inputs.shape[1:], jnp.bfloat16),
         jnp.zeros(spare + inputs.shape[1:], jnp.bfloat16),
-        jnp.zeros(spare + (experts, capacity, inner), jnp.float32),
-        jnp.zeros(spare + (experts, capacity, inner), jnp.float32),
+        jnp.zeros(spare + (total_rows, inner), jnp.float32),
+        jnp.zeros(spare + (total_rows, inner), jnp.float32),
     )
     finished, _ = lax.scan(forward_tick, start, jnp.arange(ticks, dtype=jnp.int32))
     _, outputs, kept_x, kept_gate, kept_up = finished
@@ -167,9 +277,15 @@
 
         def backward_active(operands):
             rows_grad, gate_again, up_again = operands
-            return expert_backward(
-                rows_grad, gate_again, up_again, weight_gate, weight_up, weight_down
+            back = expert_backward_kernel(
+                rows_grad.reshape(total_rows, width),
+                gate_again,
+                up_again,
+                weight_gate,
+                weight_up,
+                weight_down,
             )
+            return back.reshape(rows_grad.shape)
 
         def backward_resting(operands):
             return jnp.zeros_like(operands[0])

time: 1170 us -> 1250 us (1.068)
  Pallas kernels: 0 us -> 94.3 us
  matrix products: 113 us -> 42.7 us
  waiting for transfers between devices: 477 us -> 522 us
    pallas_call x0 -> x8, Pallas kernels: none -> 94.3 us  [the longest x4 54.4 us: expert_backward_kernel(): pl.pallas_call(_bwd_kernel, grid=(steps,), in_specs=[pl.BlockSpec((n, wid...]
    dot_general x24 -> x0, matrix products: 85.6 us -> none  [the longest x12 47.6 us: contract_last(): lax.dot_general(left, right, (((1,), (1,)), ((), ())), preferred_element_...]
    ppermute x22, waiting for transfers between devices: 182 us -> 225 us  [passed_along(): lax.ppermute(value, axis, [(source, source + steps) for source in range(l...]
    dynamic_update_slice x11, local copies, waits for them, and re-layouts: 22.3 us -> 7.83 us  [forward_tick(): kept_up = lax.dynamic_update_index_in_dim(kept_up, pre_up, slot, 0)]
    dynamic_slice x22, local copies, waits for them, and re-layouts: 13.2 us -> 26.3 us  [local(): lax.scan(forward_tick, start, jnp.arange(ticks, dtype=jnp.int32))]
  transfers between devices with their start and end apart: 55 -> 55, of which waited for: 55 -> 55; matrix products, arithmetic and copies ran while one was open for 3% -> 1% of each run, Pallas kernels for 0% -> 0%
where the time goes in v3:
time: 1250 us; the launch traced here: 1240 us
  waiting for transfers between devices  522 us (42%)
  starting transfers between devices  241 us (19%)
  blocking collectives  134 us (11%)
  local copies, waits for them, and re-layouts  126 us (10%)
  Pallas kernels  94.3 us (8%)
  other arithmetic  62.5 us (5%)
  matrix products  42.7 us (3%)
  loops' own time  15.9 us (1%)
    ppermute x22, waiting for transfers between devices, passed_along(): lax.ppermute(value, axis, [(source, source + steps) for source in range(l...  225 us
    all_to_all x11, blocking collectives, return_rows(): lax.all_to_all(rows, 'expert', split_axis=0, concat_axis=0, tiled=True)  134 us
    ppermute x22, starting transfers between devices, passed_along(): lax.ppermute(value, axis, [(source, source + steps) for source in range(l...  118 us
    all_to_all x11, waiting for transfers between devices, forward_work(): lax.all_to_all(send, 'expert', split_axis=0, concat_axis=0, tiled=True)  108 us
    all_to_all x11, waiting for transfers between devices, backward_work(): lax.all_to_all(grad_send, 'expert', split_axis=0, concat_axis=0, tiled=True)  98.6 us
    all_to_all x11, waiting for transfers between devices, return_rows(): lax.all_to_all(rows, 'expert', split_axis=0, concat_axis=0, tiled=True)  90.3 us
    pallas_call x4, Pallas kernels, expert_backward_kernel(): pl.pallas_call(_bwd_kernel, grid=(steps,), in_specs=[pl.BlockSpec((n, wid...  54.4 us
    all_to_all x11, starting transfers between devices, forward_work(): lax.all_to_all(send, 'expert', split_axis=0, concat_axis=0, tiled=True)  44.3 us
  transfers between devices with their start and end apart: 55, of which 55 were waited for; matrix products, arithmetic and copies ran while one was open for 1% of the time, Pallas kernels for 0%

profile of v3, /device:TPU:1, one launch (start us, length us, event | category | flops | bytes accessed | tf_op | source)
XLA Modules:
  0.0 1238.6 jit_solution(16009607020608324124)
XLA Ops:
  9.2 542.3 %while.33 = (s32[]{:T(128)}, bf16[32,4096]{1,0:T(8,128)(2,1)S(1)}, bf16[5,32,4096]{2,1,0:T(8,128)(2,1)}, bf16[5,32,4096]{2,1,0:T(8,128)(2,1)}, f32[5,64,768]{2,1...) while((s32[]{:T(128)}, bf16[32,4096]{1,0:T(8,128)(2,1)S(1)}, ...), condition=%wide.region_7.8_spmd, body=%wide.region_2.7_spmd.sunk | while | flops 1326848000 | bytes 32441804 | solution.py:266
  15.3 8.6 all-to-all-start
  23.9 10.4 all-to-all-done
  34.6 12.3 all_to_all.30
  55.3 9.8 collective-permute-done
  74.8 11.2 all-to-all-done
  86.0 12.1 conditional.4
  86.9 10.0 branch_1_fun.4
  98.1 13.6 %all_to_all.30 = bf16[16,4,4096]{2,1,0:T(4,128)(2,1)S(1)} all-to-all(bf16[16,4,4096]{2,1,0:T(4,128)(2,1)S(1)} %get-tuple-element.775), channel_id=1, replica_groups=mesh['section'=8,'expert'=16] {'expert'}, dimensions={0} | all-to-all | bytes 1048576 | tf_op jit(solution)/shard_map/while/body/eval_jaxpr/all_to_all | solution.py:185
  127.8 11.4 all-to-all-done
  139.3 12.1 conditional.4
  140.2 10.0 branch_1_fun.4
  151.4 13.3 %all_to_all.30 = bf16[16,4,4096]{2,1,0:T(4,128)(2,1)S(1)} all-to-all(bf16[16,4,4096]{2,1,0:T(4,128)(2,1)S(1)} %get-tuple-element.775), channel_id=1, replica_groups=mesh['section'=8,'expert'=16] {'expert'}, dimensions={0} | all-to-all | bytes 1048576 | tf_op jit(solution)/shard_map/while/body/eval_jaxpr/all_to_all | solution.py:185
  181.8 10.5 all-to-all-done
  192.2 12.1 conditional.4
  193.1 10.0 branch_1_fun.4
  204.4 13.8 %all_to_all.30 = bf16[16,4,4096]{2,1,0:T(4,128)(2,1)S(1)} all-to-all(bf16[16,4,4096]{2,1,0:T(4,128)(2,1)S(1)} %get-tuple-element.775), channel_id=1, replica_groups=mesh['section'=8,'expert'=16] {'expert'}, dimensions={0} | all-to-all | bytes 1048576 | tf_op jit(solution)/shard_map/while/body/eval_jaxpr/all_to_all | solution.py:185
  235.6 9.5 all-to-all-done
  245.1 12.1 conditional.4
  246.0 10.0 branch_1_fun.4
  257.2 11.6 all_to_all.30
  289.5 8.9 all-to-all-done
  298.8 11.6 all_to_all.30
  311.6 18.8 %collective-permute-start = (bf16[32,4096]{1,0:T(8,128)(2,1)S(1)}, bf16[32,4096]{1,0:T(8,128)(2,1)S(1)}, u32[]{:S(2)}, u32[]{:S(2)}) collective-permute-start(bf16[32,4096]{1,0:T(8,128)(2,1)S(1)} %get-tuple-element.776), channel_id=1, source_target_pairs={{0,16},{16,32},{32,48},{48,64},{64,80},{80,96},{96,112},{1,17},{17... | collective-permute-start | bytes 786440 | tf_op jit(solution)/shard_map/while/body/eval_jaxpr/ppermute | solution.py:124
  343.5 8.9 all-to-all-done
  352.7 11.6 all_to_all.30
  385.5 8.9 all-to-all-done
  394.7 11.6 all_to_all.30
  407.6 11.5 collective-permute-start
  432.1 9.6 all-to-all-done
  441.9 11.6 all_to_all.30
  474.1 8.9 all-to-all-done
  483.3 11.6 all_to_all.30
  496.2 9.8 collective-permute-start
  519.0 9.3 all-to-all-done
  528.5 11.6 all_to_all.30
  553.3 682.6 %while.34 = (s32[]{:T(128)}, bf16[32,4096]{1,0:T(8,128)(2,1)S(1)}, bf16[5,32,4096]{2,1,0:T(8,128)(2,1)}, pred[]{:T(512)}, s32[11]{0:T(128)}, /*index=5*/s32[]{:T...) while((s32[]{:T(128)}, bf16[32,4096]{1,0:T(8,128)(2,1)S(1)}, ...), condition=%wide.region_14.15_spmd, body=%wide.region_8.14_spmd.sunk | while | flops 1261049984 | bytes 34803200 | solution.py:334
  562.8 8.9 all-to-all-done.2
  577.1 8.2 all-to-all-done.3
  590.5 13.5 %collective-permute-done.1 = bf16[32,4096]{1,0:T(8,128)(2,1)S(1)} collective-permute-done((bf16[32,4096]{1,0:T(8,128)(2,1)S(1)}, bf16[32,4096]{1,0:T(8,128)(2,1)S(1)}, u32[]{:S(2)}, u32[]{:S(2)}) %collective-permute-start.1) | collective-permute-done | bytes 262176 | tf_op jit(solution)/shard_map/while/body/eval_jaxpr/ppermute | solution.py:124
  613.4 9.1 all-to-all-done.2
  627.9 8.2 all-to-all-done.3
  658.2 8.9 all-to-all-done.2
  672.5 8.2 all-to-all-done.3
  685.9 11.7 collective-permute-done.1
  707.0 9.0 all-to-all-done.2
  752.1 8.9 all-to-all-done.2
  779.8 11.4 collective-permute-done.1
  800.6 8.9 all-to-all-done.2
  828.3 108.4 %collective-permute-done.1 = bf16[32,4096]{1,0:T(8,128)(2,1)S(1)} collective-permute-done((bf16[32,4096]{1,0:T(8,128)(2,1)S(1)}, bf16[32,4096]{1,0:T(8,128)(2,1)S(1)}, u32[]{:S(2)}, u32[]{:S(2)}) %collective-permute-start.1) | collective-permute-done | bytes 262176 | tf_op jit(solution)/shard_map/while/body/eval_jaxpr/ppermute | solution.py:124
  946.1 8.9 all-to-all-done.2
  955.0 18.4 %conditional.5 = (bf16[16,4,4096]{2,1,0:T(4,128)(2,1)}) conditional(s32[]{:T(128)} %convert_element_type.132, () %tuple.105, (bf16[16,4,4096]{2,1,0:T(4,128)(2,1)S(1)}, f32[5,64,768]{2,1,0:T(8,128)}, s32[]{:T(128)}, f32[5,64,768]{2,1,0:T(8,128)}, bf16[4096,768]{1,0:T(8,128)(2,1)}, /*index=5*/bf16[4096,768]{1,0:T(8,128)(2,1)}, ...), branch_computations={%region_11.11_spmd, %region_12.12_spmd} | conditional | flops 1207959552 | bytes 23199756 | solution.py:293
  957.8 13.6 %branch_1_fun.5 = bf16[64,4096]{1,0:T(8,128)(2,1)} custom-call(bf16[64,4096]{1,0:T(8,128)(2,1)} %reshape.70.grad_ref, f32[64,768]{1,0:T(8,128)} %get-tuple-element.561.pg_ref, f32[64,768]{1,0:T(8,128)} %get-tuple-element.560.pu_ref, bf16[4096,768]{1,0:T(8,128)(2,1)} %get-tuple-element.385.wg_ref, bf16[4096,768]{1,0:T(8,128)(2,1)} %get-tuple-element.386.wu_ref, ...), custom_call_target="tpu_custom_call" | custom-call | flops 1207959552 | bytes 20316160 | tf_op jit(solution)/shard_map/while/body/eval_jaxpr/cond/branch_1_fun/pallas_call | solution.py:101
  1007.5 8.9 all-to-all-done.2
  1016.4 18.4 %conditional.5 = (bf16[16,4,4096]{2,1,0:T(4,128)(2,1)}) conditional(s32[]{:T(128)} %convert_element_type.132, () %tuple.105, (bf16[16,4,4096]{2,1,0:T(4,128)(2,1)S(1)}, f32[5,64,768]{2,1,0:T(8,128)}, s32[]{:T(128)}, f32[5,64,768]{2,1,0:T(8,128)}, bf16[4096,768]{1,0:T(8,128)(2,1)}, /*index=5*/bf16[4096,768]{1,0:T(8,128)(2,1)}, ...), branch_computations={%region_11.11_spmd, %region_12.12_spmd} | conditional | flops 1207959552 | bytes 23199756 | solution.py:293
  1019.1 13.6 %branch_1_fun.5 = bf16[64,4096]{1,0:T(8,128)(2,1)} custom-call(bf16[64,4096]{1,0:T(8,128)(2,1)} %reshape.70.grad_ref, f32[64,768]{1,0:T(8,128)} %get-tuple-element.561.pg_ref, f32[64,768]{1,0:T(8,128)} %get-tuple-element.560.pu_ref, bf16[4096,768]{1,0:T(8,128)(2,1)} %get-tuple-element.385.wg_ref, bf16[4096,768]{1,0:T(8,128)(2,1)} %get-tuple-element.386.wu_ref, ...), custom_call_target="tpu_custom_call" | custom-call | flops 1207959552 | bytes 20316160 | tf_op jit(solution)/shard_map/while/body/eval_jaxpr/cond/branch_1_fun/pallas_call | solution.py:101
  1070.0 8.9 all-to-all-done.2
  1078.9 18.4 %conditional.5 = (bf16[16,4,4096]{2,1,0:T(4,128)(2,1)}) conditional(s32[]{:T(128)} %convert_element_type.132, () %tuple.105, (bf16[16,4,4096]{2,1,0:T(4,128)(2,1)S(1)}, f32[5,64,768]{2,1,0:T(8,128)}, s32[]{:T(128)}, f32[5,64,768]{2,1,0:T(8,128)}, bf16[4096,768]{1,0:T(8,128)(2,1)}, /*index=5*/bf16[4096,768]{1,0:T(8,128)(2,1)}, ...), branch_computations={%region_11.11_spmd, %region_12.12_spmd} | conditional | flops 1207959552 | bytes 23199756 | solution.py:293
  1081.6 13.6 %branch_1_fun.5 = bf16[64,4096]{1,0:T(8,128)(2,1)} custom-call(bf16[64,4096]{1,0:T(8,128)(2,1)} %reshape.70.grad_ref, f32[64,768]{1,0:T(8,128)} %get-tuple-element.561.pg_ref, f32[64,768]{1,0:T(8,128)} %get-tuple-element.560.pu_ref, bf16[4096,768]{1,0:T(8,128)(2,1)} %get-tuple-element.385.wg_ref, bf16[4096,768]{1,0:T(8,128)(2,1)} %get-tuple-element.386.wu_ref, ...), custom_call_target="tpu_custom_call" | custom-call | flops 1207959552 | bytes 20316160 | tf_op jit(solution)/shard_map/while/body/eval_jaxpr/cond/branch_1_fun/pallas_call | solution.py:101
  1131.5 8.9 all-to-all-done.2
  1140.4 18.4 %conditional.5 = (bf16[16,4,4096]{2,1,0:T(4,128)(2,1)}) conditional(s32[]{:T(128)} %convert_element_type.132, () %tuple.105, (bf16[16,4,4096]{2,1,0:T(4,128)(2,1)S(1)}, f32[5,64,768]{2,1,0:T(8,128)}, s32[]{:T(128)}, f32[5,64,768]{2,1,0:T(8,128)}, bf16[4096,768]{1,0:T(8,128)(2,1)}, /*index=5*/bf16[4096,768]{1,0:T(8,128)(2,1)}, ...), branch_computations={%region_11.11_spmd, %region_12.12_spmd} | conditional | flops 1207959552 | bytes 23199756 | solution.py:293
  1143.1 13.6 %branch_1_fun.5 = bf16[64,4096]{1,0:T(8,128)(2,1)} custom-call(bf16[64,4096]{1,0:T(8,128)(2,1)} %reshape.70.grad_ref, f32[64,768]{1,0:T(8,128)} %get-tuple-element.561.pg_ref, f32[64,768]{1,0:T(8,128)} %get-tuple-element.560.pu_ref, bf16[4096,768]{1,0:T(8,128)(2,1)} %get-tuple-element.385.wg_ref, bf16[4096,768]{1,0:T(8,128)(2,1)} %get-tuple-element.386.wu_ref, ...), custom_call_target="tpu_custom_call" | custom-call | flops 1207959552 | bytes 20316160 | tf_op jit(solution)/shard_map/while/body/eval_jaxpr/cond/branch_1_fun/pallas_call | solution.py:101
  1191.7 8.9 all-to-all-done.2
  1217.4 17.3 %collective-permute-start.1 = (bf16[32,4096]{1,0:T(8,128)(2,1)S(1)}, bf16[32,4096]{1,0:T(8,128)(2,1)S(1)}, u32[]{:S(2)}, u32[]{:S(2)}) collective-permute-start(bf16[32,4096]{1,0:T(8,128)(2,1)S(1)} %get-tuple-element.806), channel_id=1, source_target_pairs={{16,0},{32,16},{48,32},{64,48},{80,64},{96,80},{112,96},{17,1},{33... | collective-permute-start | bytes 786440 | tf_op jit(solution)/shard_map/while/body/eval_jaxpr/ppermute | solution.py:124
  (397 shorter events, 550.4 us)
Async XLA Ops:
  8.1 1.1 copy-start.2
  15.3 19.0 %all-to-all-start = ((bf16[16,4,4096]{2,1,0:T(4,128)(2,1)}), bf16[16,4,4096]{2,1,0:T(4,128)(2,1)S(1)}, u32[]{:S(2)}, u32[]{:S(2)}) async-start(bf16[16,4,4096]{2,1,0:T(4,128)(2,1)} %copy.47), calls=%async_computation | async-start | bytes 1048576 | tf_op jit(solution)/shard_map/while/body/eval_jaxpr/all_to_all | solution.py:232
  48.1 17.1 %collective-permute-start = (bf16[32,4096]{1,0:T(8,128)(2,1)S(1)}, bf16[32,4096]{1,0:T(8,128)(2,1)S(1)}, u32[]{:S(2)}, u32[]{:S(2)}) collective-permute-start(bf16[32,4096]{1,0:T(8,128)(2,1)S(1)} %get-tuple-element.776), channel_id=1, source_target_pairs={{0,16},{16,32},{32,48},{48,64},{64,80},{80,96},{96,112},{1,17},{17... | collective-permute-start | bytes 786440 | tf_op jit(solution)/shard_map/while/body/eval_jaxpr/ppermute | solution.py:124
  71.2 14.8 %all-to-all-start = ((bf16[16,4,4096]{2,1,0:T(4,128)(2,1)}), bf16[16,4,4096]{2,1,0:T(4,128)(2,1)S(1)}, u32[]{:S(2)}, u32[]{:S(2)}) async-start(bf16[16,4,4096]{2,1,0:T(4,128)(2,1)} %copy.47), calls=%async_computation | async-start | bytes 1048576 | tf_op jit(solution)/shard_map/while/body/eval_jaxpr/all_to_all | solution.py:232
  112.9 5.2 collective-permute-start
  124.3 15.0 %all-to-all-start = ((bf16[16,4,4096]{2,1,0:T(4,128)(2,1)}), bf16[16,4,4096]{2,1,0:T(4,128)(2,1)S(1)}, u32[]{:S(2)}, u32[]{:S(2)}) async-start(bf16[16,4,4096]{2,1,0:T(4,128)(2,1)} %copy.47), calls=%async_computation | async-start | bytes 1048576 | tf_op jit(solution)/shard_map/while/body/eval_jaxpr/all_to_all | solution.py:232
  165.9 6.2 collective-permute-start
  178.2 14.1 %all-to-all-start = ((bf16[16,4,4096]{2,1,0:T(4,128)(2,1)}), bf16[16,4,4096]{2,1,0:T(4,128)(2,1)S(1)}, u32[]{:S(2)}, u32[]{:S(2)}) async-start(bf16[16,4,4096]{2,1,0:T(4,128)(2,1)} %copy.47), calls=%async_computation | async-start | bytes 1048576 | tf_op jit(solution)/shard_map/while/body/eval_jaxpr/all_to_all | solution.py:232
  219.4 6.6 collective-permute-start
  232.0 13.1 %all-to-all-start = ((bf16[16,4,4096]{2,1,0:T(4,128)(2,1)}), bf16[16,4,4096]{2,1,0:T(4,128)(2,1)S(1)}, u32[]{:S(2)}, u32[]{:S(2)}) async-start(bf16[16,4,4096]{2,1,0:T(4,128)(2,1)} %copy.47), calls=%async_computation | async-start | bytes 1048576 | tf_op jit(solution)/shard_map/while/body/eval_jaxpr/all_to_all | solution.py:232
  270.1 9.8 collective-permute-start
  286.0 12.5 %all-to-all-start = ((bf16[16,4,4096]{2,1,0:T(4,128)(2,1)}), bf16[16,4,4096]{2,1,0:T(4,128)(2,1)S(1)}, u32[]{:S(2)}, u32[]{:S(2)}) async-start(bf16[16,4,4096]{2,1,0:T(4,128)(2,1)} %copy.47), calls=%async_computation | async-start | bytes 1048576 | tf_op jit(solution)/shard_map/while/body/eval_jaxpr/all_to_all | solution.py:232
  311.6 22.1 %collective-permute-start = (bf16[32,4096]{1,0:T(8,128)(2,1)S(1)}, bf16[32,4096]{1,0:T(8,128)(2,1)S(1)}, u32[]{:S(2)}, u32[]{:S(2)}) collective-permute-start(bf16[32,4096]{1,0:T(8,128)(2,1)S(1)} %get-tuple-element.776), channel_id=1, source_target_pairs={{0,16},{16,32},{32,48},{48,64},{64,80},{80,96},{96,112},{1,17},{17... | collective-permute-start | bytes 786440 | tf_op jit(solution)/shard_map/while/body/eval_jaxpr/ppermute | solution.py:124
  339.9 12.5 %all-to-all-start = ((bf16[16,4,4096]{2,1,0:T(4,128)(2,1)}), bf16[16,4,4096]{2,1,0:T(4,128)(2,1)S(1)}, u32[]{:S(2)}, u32[]{:S(2)}) async-start(bf16[16,4,4096]{2,1,0:T(4,128)(2,1)} %copy.47), calls=%async_computation | async-start | bytes 1048576 | tf_op jit(solution)/shard_map/while/body/eval_jaxpr/all_to_all | solution.py:232
  365.5 10.2 collective-permute-start
  381.9 12.5 %all-to-all-start = ((bf16[16,4,4096]{2,1,0:T(4,128)(2,1)}), bf16[16,4,4096]{2,1,0:T(4,128)(2,1)S(1)}, u32[]{:S(2)}, u32[]{:S(2)}) async-start(bf16[16,4,4096]{2,1,0:T(4,128)(2,1)} %copy.47), calls=%async_computation | async-start | bytes 1048576 | tf_op jit(solution)/shard_map/while/body/eval_jaxpr/all_to_all | solution.py:232
  407.6 14.8 %collective-permute-start = (bf16[32,4096]{1,0:T(8,128)(2,1)S(1)}, bf16[32,4096]{1,0:T(8,128)(2,1)S(1)}, u32[]{:S(2)}, u32[]{:S(2)}) collective-permute-start(bf16[32,4096]{1,0:T(8,128)(2,1)S(1)} %get-tuple-element.776), channel_id=1, source_target_pairs={{0,16},{16,32},{32,48},{48,64},{64,80},{80,96},{96,112},{1,17},{17... | collective-permute-start | bytes 786440 | tf_op jit(solution)/shard_map/while/body/eval_jaxpr/ppermute | solution.py:124
  428.5 13.2 %all-to-all-start = ((bf16[16,4,4096]{2,1,0:T(4,128)(2,1)}), bf16[16,4,4096]{2,1,0:T(4,128)(2,1)S(1)}, u32[]{:S(2)}, u32[]{:S(2)}) async-start(bf16[16,4,4096]{2,1,0:T(4,128)(2,1)} %copy.47), calls=%async_computation | async-start | bytes 1048576 | tf_op jit(solution)/shard_map/while/body/eval_jaxpr/all_to_all | solution.py:232
  454.8 9.7 collective-permute-start
  470.5 12.5 %all-to-all-start = ((bf16[16,4,4096]{2,1,0:T(4,128)(2,1)}), bf16[16,4,4096]{2,1,0:T(4,128)(2,1)S(1)}, u32[]{:S(2)}, u32[]{:S(2)}) async-start(bf16[16,4,4096]{2,1,0:T(4,128)(2,1)} %copy.47), calls=%async_computation | async-start | bytes 1048576 | tf_op jit(solution)/shard_map/while/body/eval_jaxpr/all_to_all | solution.py:232
  496.2 13.1 %collective-permute-start = (bf16[32,4096]{1,0:T(8,128)(2,1)S(1)}, bf16[32,4096]{1,0:T(8,128)(2,1)S(1)}, u32[]{:S(2)}, u32[]{:S(2)}) collective-permute-start(bf16[32,4096]{1,0:T(8,128)(2,1)S(1)} %get-tuple-element.776), channel_id=1, source_target_pairs={{0,16},{16,32},{32,48},{48,64},{64,80},{80,96},{96,112},{1,17},{17... | collective-permute-start | bytes 786440 | tf_op jit(solution)/shard_map/while/body/eval_jaxpr/ppermute | solution.py:124
  515.4 12.9 %all-to-all-start = ((bf16[16,4,4096]{2,1,0:T(4,128)(2,1)}), bf16[16,4,4096]{2,1,0:T(4,128)(2,1)S(1)}, u32[]{:S(2)}, u32[]{:S(2)}) async-start(bf16[16,4,4096]{2,1,0:T(4,128)(2,1)} %copy.47), calls=%async_computation | async-start | bytes 1048576 | tf_op jit(solution)/shard_map/while/body/eval_jaxpr/all_to_all | solution.py:232
  541.4 10.1 collective-permute-start
  551.5 1.8 copy-start.1
  553.3 682.6 %copy-start = (bf16[5,32,4096]{2,1,0:T(8,128)(2,1)S(1)}, bf16[5,32,4096]{2,1,0:T(8,128)(2,1)}, u32[]{:S(2)}) copy-start(bf16[5,32,4096]{2,1,0:T(8,128)(2,1)} %get-tuple-element.413) | copy-start | bytes 3932164
  559.2 12.5 %all-to-all-start.2 = ((bf16[16,4,4096]{2,1,0:T(4,128)(2,1)}), bf16[16,4,4096]{2,1,0:T(4,128)(2,1)S(1)}, u32[]{:S(2)}, u32[]{:S(2)}) async-start(bf16[16,4,4096]{2,1,0:T(4,128)(2,1)} %copy.48), calls=%async_computation.2 | async-start | bytes 1048576 | tf_op jit(solution)/shard_map/while/body/eval_jaxpr/all_to_all | solution.py:298
  572.7 12.5 %all-to-all-start.3 = ((bf16[16,4,4096]{2,1,0:T(4,128)(2,1)}), bf16[16,4,4096]{2,1,0:T(4,128)(2,1)S(1)}, u32[]{:S(2)}, u32[]{:S(2)}) async-start(bf16[16,4,4096]{2,1,0:T(4,128)(2,1)} %get-tuple-element.943), calls=%async_computation.3 | async-start | bytes 1048576 | tf_op jit(solution)/shard_map/while/body/eval_jaxpr/all_to_all | solution.py:185
  588.6 15.5 %collective-permute-start.1 = (bf16[32,4096]{1,0:T(8,128)(2,1)S(1)}, bf16[32,4096]{1,0:T(8,128)(2,1)S(1)}, u32[]{:S(2)}, u32[]{:S(2)}) collective-permute-start(bf16[32,4096]{1,0:T(8,128)(2,1)S(1)} %get-tuple-element.806), channel_id=1, source_target_pairs={{16,0},{32,16},{48,32},{64,48},{80,64},{96,80},{112,96},{17,1},{33... | collective-permute-start | bytes 786440 | tf_op jit(solution)/shard_map/while/body/eval_jaxpr/ppermute | solution.py:124
  609.8 12.7 %all-to-all-start.2 = ((bf16[16,4,4096]{2,1,0:T(4,128)(2,1)}), bf16[16,4,4096]{2,1,0:T(4,128)(2,1)S(1)}, u32[]{:S(2)}, u32[]{:S(2)}) async-start(bf16[16,4,4096]{2,1,0:T(4,128)(2,1)} %copy.48), calls=%async_computation.2 | async-start | bytes 1048576 | tf_op jit(solution)/shard_map/while/body/eval_jaxpr/all_to_all | solution.py:298
  623.6 12.5 %all-to-all-start.3 = ((bf16[16,4,4096]{2,1,0:T(4,128)(2,1)}), bf16[16,4,4096]{2,1,0:T(4,128)(2,1)S(1)}, u32[]{:S(2)}, u32[]{:S(2)}) async-start(bf16[16,4,4096]{2,1,0:T(4,128)(2,1)} %get-tuple-element.943), calls=%async_computation.3 | async-start | bytes 1048576 | tf_op jit(solution)/shard_map/while/body/eval_jaxpr/all_to_all | solution.py:185
  639.4 9.4 collective-permute-start.1
  654.6 12.5 %all-to-all-start.2 = ((bf16[16,4,4096]{2,1,0:T(4,128)(2,1)}), bf16[16,4,4096]{2,1,0:T(4,128)(2,1)S(1)}, u32[]{:S(2)}, u32[]{:S(2)}) async-start(bf16[16,4,4096]{2,1,0:T(4,128)(2,1)} %copy.48), calls=%async_computation.2 | async-start | bytes 1048576 | tf_op jit(solution)/shard_map/while/body/eval_jaxpr/all_to_all | solution.py:298
  668.2 12.5 %all-to-all-start.3 = ((bf16[16,4,4096]{2,1,0:T(4,128)(2,1)}), bf16[16,4,4096]{2,1,0:T(4,128)(2,1)S(1)}, u32[]{:S(2)}, u32[]{:S(2)}) async-start(bf16[16,4,4096]{2,1,0:T(4,128)(2,1)} %get-tuple-element.943), calls=%async_computation.3 | async-start | bytes 1048576 | tf_op jit(solution)/shard_map/while/body/eval_jaxpr/all_to_all | solution.py:185
  684.0 13.6 %collective-permute-start.1 = (bf16[32,4096]{1,0:T(8,128)(2,1)S(1)}, bf16[32,4096]{1,0:T(8,128)(2,1)S(1)}, u32[]{:S(2)}, u32[]{:S(2)}) collective-permute-start(bf16[32,4096]{1,0:T(8,128)(2,1)S(1)} %get-tuple-element.806), channel_id=1, source_target_pairs={{16,0},{32,16},{48,32},{64,48},{80,64},{96,80},{112,96},{17,1},{33... | collective-permute-start | bytes 786440 | tf_op jit(solution)/shard_map/while/body/eval_jaxpr/ppermute | solution.py:124
  703.4 12.6 %all-to-all-start.2 = ((bf16[16,4,4096]{2,1,0:T(4,128)(2,1)}), bf16[16,4,4096]{2,1,0:T(4,128)(2,1)S(1)}, u32[]{:S(2)}, u32[]{:S(2)}) async-start(bf16[16,4,4096]{2,1,0:T(4,128)(2,1)} %copy.48), calls=%async_computation.2 | async-start | bytes 1048576 | tf_op jit(solution)/shard_map/while/body/eval_jaxpr/all_to_all | solution.py:298
  717.0 12.5 %all-to-all-start.3 = ((bf16[16,4,4096]{2,1,0:T(4,128)(2,1)}), bf16[16,4,4096]{2,1,0:T(4,128)(2,1)S(1)}, u32[]{:S(2)}, u32[]{:S(2)}) async-start(bf16[16,4,4096]{2,1,0:T(4,128)(2,1)} %get-tuple-element.943), calls=%async_computation.3 | async-start | bytes 1048576 | tf_op jit(solution)/shard_map/while/body/eval_jaxpr/all_to_all | solution.py:185
  732.8 9.9 collective-permute-start.1
  748.5 12.5 %all-to-all-start.2 = ((bf16[16,4,4096]{2,1,0:T(4,128)(2,1)}), bf16[16,4,4096]{2,1,0:T(4,128)(2,1)S(1)}, u32[]{:S(2)}, u32[]{:S(2)}) async-start(bf16[16,4,4096]{2,1,0:T(4,128)(2,1)} %copy.48), calls=%async_computation.2 | async-start | bytes 1048576 | tf_op jit(solution)/shard_map/while/body/eval_jaxpr/all_to_all | solution.py:298
  762.0 12.5 %all-to-all-start.3 = ((bf16[16,4,4096]{2,1,0:T(4,128)(2,1)}), bf16[16,4,4096]{2,1,0:T(4,128)(2,1)S(1)}, u32[]{:S(2)}, u32[]{:S(2)}) async-start(bf16[16,4,4096]{2,1,0:T(4,128)(2,1)} %get-tuple-element.943), calls=%async_computation.3 | async-start | bytes 1048576 | tf_op jit(solution)/shard_map/while/body/eval_jaxpr/all_to_all | solution.py:185
  777.8 13.3 %collective-permute-start.1 = (bf16[32,4096]{1,0:T(8,128)(2,1)S(1)}, bf16[32,4096]{1,0:T(8,128)(2,1)S(1)}, u32[]{:S(2)}, u32[]{:S(2)}) collective-permute-start(bf16[32,4096]{1,0:T(8,128)(2,1)S(1)} %get-tuple-element.806), channel_id=1, source_target_pairs={{16,0},{32,16},{48,32},{64,48},{80,64},{96,80},{112,96},{17,1},{33... | collective-permute-start | bytes 786440 | tf_op jit(solution)/shard_map/while/body/eval_jaxpr/ppermute | solution.py:124
  797.0 12.5 %all-to-all-start.2 = ((bf16[16,4,4096]{2,1,0:T(4,128)(2,1)}), bf16[16,4,4096]{2,1,0:T(4,128)(2,1)S(1)}, u32[]{:S(2)}, u32[]{:S(2)}) async-start(bf16[16,4,4096]{2,1,0:T(4,128)(2,1)} %copy.48), calls=%async_computation.2 | async-start | bytes 1048576 | tf_op jit(solution)/shard_map/while/body/eval_jaxpr/all_to_all | solution.py:298
  810.5 12.5 %all-to-all-start.3 = ((bf16[16,4,4096]{2,1,0:T(4,128)(2,1)}), bf16[16,4,4096]{2,1,0:T(4,128)(2,1)S(1)}, u32[]{:S(2)}, u32[]{:S(2)}) async-start(bf16[16,4,4096]{2,1,0:T(4,128)(2,1)} %get-tuple-element.943), calls=%async_computation.3 | async-start | bytes 1048576 | tf_op jit(solution)/shard_map/while/body/eval_jaxpr/all_to_all | solution.py:185
  826.3 110.3 %collective-permute-start.1 = (bf16[32,4096]{1,0:T(8,128)(2,1)S(1)}, bf16[32,4096]{1,0:T(8,128)(2,1)S(1)}, u32[]{:S(2)}, u32[]{:S(2)}) collective-permute-start(bf16[32,4096]{1,0:T(8,128)(2,1)S(1)} %get-tuple-element.806), channel_id=1, source_target_pairs={{16,0},{32,16},{48,32},{64,48},{80,64},{96,80},{112,96},{17,1},{33... | collective-permute-start | bytes 786440 | tf_op jit(solution)/shard_map/while/body/eval_jaxpr/ppermute | solution.py:124
  942.5 12.5 %all-to-all-start.2 = ((bf16[16,4,4096]{2,1,0:T(4,128)(2,1)}), bf16[16,4,4096]{2,1,0:T(4,128)(2,1)S(1)}, u32[]{:S(2)}, u32[]{:S(2)}) async-start(bf16[16,4,4096]{2,1,0:T(4,128)(2,1)} %copy.48), calls=%async_computation.2 | async-start | bytes 1048576 | tf_op jit(solution)/shard_map/while/body/eval_jaxpr/all_to_all | solution.py:298
  973.4 12.5 %all-to-all-start.3 = ((bf16[16,4,4096]{2,1,0:T(4,128)(2,1)}), bf16[16,4,4096]{2,1,0:T(4,128)(2,1)S(1)}, u32[]{:S(2)}, u32[]{:S(2)}) async-start(bf16[16,4,4096]{2,1,0:T(4,128)(2,1)} %get-tuple-element.943), calls=%async_computation.3 | async-start | bytes 1048576 | tf_op jit(solution)/shard_map/while/body/eval_jaxpr/all_to_all | solution.py:185
  989.2 8.8 collective-permute-start.1
  1003.9 12.5 %all-to-all-start.2 = ((bf16[16,4,4096]{2,1,0:T(4,128)(2,1)}), bf16[16,4,4096]{2,1,0:T(4,128)(2,1)S(1)}, u32[]{:S(2)}, u32[]{:S(2)}) async-start(bf16[16,4,4096]{2,1,0:T(4,128)(2,1)} %copy.48), calls=%async_computation.2 | async-start | bytes 1048576 | tf_op jit(solution)/shard_map/while/body/eval_jaxpr/all_to_all | solution.py:298
  1034.8 12.5 %all-to-all-start.3 = ((bf16[16,4,4096]{2,1,0:T(4,128)(2,1)}), bf16[16,4,4096]{2,1,0:T(4,128)(2,1)S(1)}, u32[]{:S(2)}, u32[]{:S(2)}) async-start(bf16[16,4,4096]{2,1,0:T(4,128)(2,1)} %get-tuple-element.943), calls=%async_computation.3 | async-start | bytes 1048576 | tf_op jit(solution)/shard_map/while/body/eval_jaxpr/all_to_all | solution.py:185
  1050.6 9.9 collective-permute-start.1
  1066.4 12.5 %all-to-all-start.2 = ((bf16[16,4,4096]{2,1,0:T(4,128)(2,1)}), bf16[16,4,4096]{2,1,0:T(4,128)(2,1)S(1)}, u32[]{:S(2)}, u32[]{:S(2)}) async-start(bf16[16,4,4096]{2,1,0:T(4,128)(2,1)} %copy.48), calls=%async_computation.2 | async-start | bytes 1048576 | tf_op jit(solution)/shard_map/while/body/eval_jaxpr/all_to_all | solution.py:298
  1097.3 12.5 %all-to-all-start.3 = ((bf16[16,4,4096]{2,1,0:T(4,128)(2,1)}), bf16[16,4,4096]{2,1,0:T(4,128)(2,1)S(1)}, u32[]{:S(2)}, u32[]{:S(2)}) async-start(bf16[16,4,4096]{2,1,0:T(4,128)(2,1)} %get-tuple-element.943), calls=%async_computation.3 | async-start | bytes 1048576 | tf_op jit(solution)/shard_map/while/body/eval_jaxpr/all_to_all | solution.py:185
  1113.1 9.0 collective-permute-start.1
  1127.9 12.5 %all-to-all-start.2 = ((bf16[16,4,4096]{2,1,0:T(4,128)(2,1)}), bf16[16,4,4096]{2,1,0:T(4,128)(2,1)S(1)}, u32[]{:S(2)}, u32[]{:S(2)}) async-start(bf16[16,4,4096]{2,1,0:T(4,128)(2,1)} %copy.48), calls=%async_computation.2 | async-start | bytes 1048576 | tf_op jit(solution)/shard_map/while/body/eval_jaxpr/all_to_all | solution.py:298
  1158.8 12.5 %all-to-all-start.3 = ((bf16[16,4,4096]{2,1,0:T(4,128)(2,1)}), bf16[16,4,4096]{2,1,0:T(4,128)(2,1)S(1)}, u32[]{:S(2)}, u32[]{:S(2)}) async-start(bf16[16,4,4096]{2,1,0:T(4,128)(2,1)} %get-tuple-element.943), calls=%async_computation.3 | async-start | bytes 1048576 | tf_op jit(solution)/shard_map/while/body/eval_jaxpr/all_to_all | solution.py:185
  1174.6 7.7 collective-permute-start.1
  1188.1 12.5 %all-to-all-start.2 = ((bf16[16,4,4096]{2,1,0:T(4,128)(2,1)}), bf16[16,4,4096]{2,1,0:T(4,128)(2,1)S(1)}, u32[]{:S(2)}, u32[]{:S(2)}) async-start(bf16[16,4,4096]{2,1,0:T(4,128)(2,1)} %copy.48), calls=%async_computation.2 | async-start | bytes 1048576 | tf_op jit(solution)/shard_map/while/body/eval_jaxpr/all_to_all | solution.py:298
  1201.6 12.5 %all-to-all-start.3 = ((bf16[16,4,4096]{2,1,0:T(4,128)(2,1)}), bf16[16,4,4096]{2,1,0:T(4,128)(2,1)S(1)}, u32[]{:S(2)}, u32[]{:S(2)}) async-start(bf16[16,4,4096]{2,1,0:T(4,128)(2,1)} %get-tuple-element.943), calls=%async_computation.3 | async-start | bytes 1048576 | tf_op jit(solution)/shard_map/while/body/eval_jaxpr/all_to_all | solution.py:185
  1217.4 18.5 %collective-permute-start.1 = (bf16[32,4096]{1,0:T(8,128)(2,1)S(1)}, bf16[32,4096]{1,0:T(8,128)(2,1)S(1)}, u32[]{:S(2)}, u32[]{:S(2)}) collective-permute-start(bf16[32,4096]{1,0:T(8,128)(2,1)S(1)} %get-tuple-element.806), channel_id=1, source_target_pairs={{16,0},{32,16},{48,32},{64,48},{80,64},{96,80},{112,96},{17,1},{33... | collective-permute-start | bytes 786440 | tf_op jit(solution)/shard_map/while/body/eval_jaxpr/ppermute | solution.py:124

commit v4 on v2

--- a/solution.py
+++ b/solution.py
@@ -104,15 +104,20 @@
         ).astype(jnp.bfloat16)
 
         def forward_active(operand):
-            pre_gate, pre_up = pre_products(operand, weight_gate, weight_up)
+            pre_gate, pre_up = pre_products(
+                operand.reshape(total_rows, width), weight_gate, weight_up
+            )
             product = (pre_gate * jax.nn.sigmoid(pre_gate) * pre_up).astype(jnp.bfloat16)
             output = jnp.einsum(
-                "ech,hd->ecd", product, weight_down, preferred_element_type=jnp.float32
+                "ech,hd->ecd",
+                product.reshape(experts, capacity, inner),
+                weight_down,
+                preferred_element_type=jnp.float32,
             ).astype(jnp.bfloat16)
             return (output, pre_gate, pre_up)
 
         def forward_resting(operand):
-            pre_zero = jnp.zeros(operand.shape[:-1] + (inner,), jnp.float32)
+            pre_zero = jnp.zeros((total_rows, inner), jnp.float32)
             return (jnp.zeros_like(operand), pre_zero, pre_zero)
 
         output, pre_gate, pre_up = lax.cond(
@@ -150,11 +155,12 @@
         jnp.zeros((tok, width), jnp.bfloat16),
         jnp.zeros(spare + inputs.shape[1:], jnp.bfloat16),
         jnp.zeros(spare + inputs.shape[1:], jnp.bfloat16),
-        jnp.zeros(spare + (experts, capacity, inner), jnp.float32),
-        jnp.zeros(spare + (experts, capacity, inner), jnp.float32),
+        jnp.zeros(spare + (total_rows, inner), jnp.float32),
+        jnp.zeros(spare + (total_rows, inner), jnp.float32),
     )
     finished, _ = lax.scan(forward_tick, start, jnp.arange(ticks, dtype=jnp.int32))
     _, outputs, kept_x, kept_gate, kept_up = finished
+    down_across = lax.optimization_barrier(jnp.transpose(weight_down))
 
     def backward_work(tokens, grad_out, table, table4, gate_now, gate_kept, up_kept, live):
         values, scale, normed = normalize(tokens, gain_row)
@@ -166,10 +172,27 @@
         ).astype(jnp.bfloat16)
 
         def backward_active(operands):
-            rows_grad, gate_again, up_again = operands
-            return expert_backward(
-                rows_grad, gate_again, up_again, weight_gate, weight_up, weight_down
-            )
+            rows_grad, gate_pre, up_pre = operands
+            d_hidden = jnp.dot(
+                rows_grad.reshape(total_rows, width),
+                down_across,
+                preferred_element_type=jnp.float32,
+            )
+            sigma = jax.nn.sigmoid(gate_pre)
+            d_gate = (d_hidden * up_pre * sigma * (1.0 + gate_pre * (1.0 - sigma))).astype(
+                jnp.bfloat16
+            )
+            d_up = (d_hidden * gate_pre * sigma).astype(jnp.bfloat16)
+            shape3 = (experts, capacity, inner)
+            back = jnp.einsum(
+                "ech,dh->ecd",
+                d_gate.reshape(shape3),
+                weight_gate,
+                preferred_element_type=jnp.float32,
+            ) + jnp.einsum(
+                "ech,dh->ecd", d_up.reshape(shape3), weight_up, preferred_element_type=jnp.float32
+            )
+            return back.astype(jnp.bfloat16)
 
         def backward_resting(operands):
             return jnp.zeros_like(operands[0])

time: 1170 us -> 1190 us (1.017)
  matrix products: 113 us -> 133 us
  other arithmetic: 62.1 us -> 44.5 us
  waiting for transfers between devices: 477 us -> 490 us
    dot_general x11, matrix products: 4.18 us -> 19.8 us  [forward_work(): jnp.dot(weights, back.astype(jnp.float32), precision=lax.Precision.HIGHEST)]
    dot_general x4, matrix products: 20.3 us -> 4.84 us  [pre_products(): pre_up = jnp.dot(flat, w_up, preferred_element_type=jnp.float32)]
    dynamic_slice x22, local copies, waits for them, and re-layouts: 13.2 us -> 28.4 us  [local(): lax.scan(forward_tick, start, jnp.arange(ticks, dtype=jnp.int32))]
    dot_general x16, matrix products: 56.5 us -> 70.9 us  [the longest x4 19.1 us: backward_active(): jnp.einsum('ech,dh->ecd', d_gate.reshape(shape3), weight_gate, preferred_...]
    dynamic_update_slice x11, local copies, waits for them, and re-layouts: 22.3 us -> 8.52 us  [forward_tick(): kept_up = lax.dynamic_update_index_in_dim(kept_up, pre_up, slot, 0)]
    ppermute x22, waiting for transfers between devices: 182 us -> 195 us  [passed_along(): lax.ppermute(value, axis, [(source, source + steps) for source in range(l...]
    cond x32 -> x35, local copies, waits for them, and re-layouts: 2.74 us -> 15.4 us  [the longest x11 13.5 us: backward_work(): lax.cond(live, backward_active, backward_resting, (lax.all_to_all(grad_se...]
  transfers between devices with their start and end apart: 55 -> 55, of which waited for: 55 -> 55; matrix products, arithmetic and copies ran while one was open for 3% -> 1% of each run, Pallas kernels for 0% -> 0%
where the time goes in v4:
time: 1190 us; the launch traced here: 1180 us
  waiting for transfers between devices  490 us (41%)
  starting transfers between devices  234 us (20%)
  blocking collectives  135 us (11%)
  matrix products  133 us (11%)
  local copies, waits for them, and re-layouts  124 us (10%)
  other arithmetic  44.5 us (4%)
  loops' own time  17.4 us (1%)
    ppermute x22, waiting for transfers between devices, passed_along(): lax.ppermute(value, axis, [(source, source + steps) for source in range(l...  195 us
    all_to_all x11, blocking collectives, return_rows(): lax.all_to_all(rows, 'expert', split_axis=0, concat_axis=0, tiled=True)  135 us
    ppermute x22, starting transfers between devices, passed_along(): lax.ppermute(value, axis, [(source, source + steps) for source in range(l...  110 us
    all_to_all x11, waiting for transfers between devices, forward_work(): lax.all_to_all(send, 'expert', split_axis=0, concat_axis=0, tiled=True)  107 us
    all_to_all x11, waiting for transfers between devices, backward_work(): lax.all_to_all(grad_send, 'expert', split_axis=0, concat_axis=0, tiled=True)  98.5 us
    all_to_all x11, waiting for transfers between devices, return_rows(): lax.all_to_all(rows, 'expert', split_axis=0, concat_axis=0, tiled=True)  90.3 us
    all_to_all x11, starting transfers between devices, forward_work(): lax.all_to_all(send, 'expert', split_axis=0, concat_axis=0, tiled=True)  44.3 us
    all_to_all x11, starting transfers between devices, return_rows(): lax.all_to_all(rows, 'expert', split_axis=0, concat_axis=0, tiled=True)  40.7 us
  transfers between devices with their start and end apart: 55, of which 55 were waited for; matrix products, arithmetic and copies ran while one was open for 1% of the time, Pallas kernels for 0%

profile of v4, /device:TPU:1, one launch (start us, length us, event | category | flops | bytes accessed | tf_op | source)
XLA Modules:
  0.0 1177.8 jit_solution(13958329839326871061)
XLA Ops:
  9.7 532.2 %while.33 = (s32[]{:T(128)}, bf16[32,4096]{1,0:T(8,128)(2,1)S(1)}, bf16[5,32,4096]{2,1,0:T(8,128)(2,1)}, bf16[5,32,4096]{2,1,0:T(8,128)(2,1)S(1)}, f32[5,64,768]...) while((s32[]{:T(128)}, bf16[32,4096]{1,0:T(8,128)(2,1)S(1)}, ...), condition=%wide.region_7.8_spmd, body=%wide.region_2.7_spmd.sunk | while | flops 1327405056 | bytes 60294180 | solution.py:161
  15.3 8.6 all-to-all-start
  23.9 10.4 all-to-all-done
  34.8 12.3 %all_to_all.30 = bf16[16,4,4096]{2,1,0:T(4,128)(2,1)S(1)} all-to-all(bf16[16,4,4096]{2,1,0:T(4,128)(2,1)S(1)} %copy.76), channel_id=1, replica_groups=mesh['section'=8,'expert'=16] {'expert'}, dimensions={0} | all-to-all | bytes 1048576 | tf_op jit(solution)/shard_map/while/body/eval_jaxpr/all_to_all | solution.py:73
  73.3 11.2 all-to-all-done
  84.5 10.0 conditional.4
  94.9 13.6 %all_to_all.30 = bf16[16,4,4096]{2,1,0:T(4,128)(2,1)S(1)} all-to-all(bf16[16,4,4096]{2,1,0:T(4,128)(2,1)S(1)} %copy.76), channel_id=1, replica_groups=mesh['section'=8,'expert'=16] {'expert'}, dimensions={0} | all-to-all | bytes 1048576 | tf_op jit(solution)/shard_map/while/body/eval_jaxpr/all_to_all | solution.py:73
  124.8 11.4 all-to-all-done
  136.2 10.0 conditional.4
  146.7 13.3 %all_to_all.30 = bf16[16,4,4096]{2,1,0:T(4,128)(2,1)S(1)} all-to-all(bf16[16,4,4096]{2,1,0:T(4,128)(2,1)S(1)} %copy.76), channel_id=1, replica_groups=mesh['section'=8,'expert'=16] {'expert'}, dimensions={0} | all-to-all | bytes 1048576 | tf_op jit(solution)/shard_map/while/body/eval_jaxpr/all_to_all | solution.py:73
  177.3 10.4 all-to-all-done
  187.6 10.0 conditional.4
  198.1 14.0 %all_to_all.30 = bf16[16,4,4096]{2,1,0:T(4,128)(2,1)S(1)} all-to-all(bf16[16,4,4096]{2,1,0:T(4,128)(2,1)S(1)} %copy.76), channel_id=1, replica_groups=mesh['section'=8,'expert'=16] {'expert'}, dimensions={0} | all-to-all | bytes 1048576 | tf_op jit(solution)/shard_map/while/body/eval_jaxpr/all_to_all | solution.py:73
  229.7 9.4 all-to-all-done
  239.1 10.0 conditional.4
  249.6 11.6 all_to_all.30
  282.0 8.9 all-to-all-done
  291.5 11.6 all_to_all.30
  305.1 16.9 %collective-permute-start = (bf16[32,4096]{1,0:T(8,128)(2,1)S(1)}, bf16[32,4096]{1,0:T(8,128)(2,1)S(1)}, u32[]{:S(2)}, u32[]{:S(2)}) collective-permute-start(bf16[32,4096]{1,0:T(8,128)(2,1)S(1)} %get-tuple-element.781), channel_id=1, source_target_pairs={{0,16},{16,32},{32,48},{48,64},{64,80},{80,96},{96,112},{1,17},{17... | collective-permute-start | bytes 786440 | tf_op jit(solution)/shard_map/while/body/eval_jaxpr/ppermute | solution.py:12
  334.4 9.2 all-to-all-done
  344.1 11.6 all_to_all.30
  376.9 8.9 all-to-all-done
  386.3 11.6 all_to_all.30
  399.9 11.0 collective-permute-start
  423.4 9.0 all-to-all-done
  432.8 11.6 all_to_all.30
  466.1 8.9 all-to-all-done
  475.6 11.6 all_to_all.30
  508.6 8.9 all-to-all-done
  518.0 11.6 all_to_all.30
  541.9 8.6 copy.47
  552.4 622.4 %while.34 = (s32[]{:T(128)}, bf16[32,4096]{1,0:T(8,128)(2,1)S(1)}, bf16[5,32,4096]{2,1,0:T(8,128)(2,1)}, pred[]{:T(512)}, s32[11]{0:T(128)}, /*index=5*/s32[]{:T...) while((s32[]{:T(128)}, bf16[32,4096]{1,0:T(8,128)(2,1)S(1)}, ...), condition=%wide.region_14.15_spmd, body=%wide.region_8.14_spmd.sunk | while | flops 1262213248 | bytes 47386168 | solution.py:241
  561.9 8.9 all-to-all-done.2
  576.6 8.2 all-to-all-done.3
  588.1 12.2 %collective-permute-done.1 = bf16[32,4096]{1,0:T(8,128)(2,1)S(1)} collective-permute-done((bf16[32,4096]{1,0:T(8,128)(2,1)S(1)}, bf16[32,4096]{1,0:T(8,128)(2,1)S(1)}, u32[]{:S(2)}, u32[]{:S(2)}) %collective-permute-start.1) | collective-permute-done | bytes 262176 | tf_op jit(solution)/shard_map/while/body/eval_jaxpr/ppermute | solution.py:12
  609.9 9.0 all-to-all-done.2
  624.7 8.2 all-to-all-done.3
  653.9 8.9 all-to-all-done.2
  668.6 8.2 all-to-all-done.3
  680.1 9.1 collective-permute-done.1
  698.7 8.9 all-to-all-done.2
  713.4 8.2 all-to-all-done.3
  741.5 8.9 all-to-all-done.2
  756.2 8.2 all-to-all-done.3
  767.7 9.5 collective-permute-done.1
  786.8 8.9 all-to-all-done.2
  801.4 8.2 all-to-all-done.3
  812.9 86.2 %collective-permute-done.1 = bf16[32,4096]{1,0:T(8,128)(2,1)S(1)} collective-permute-done((bf16[32,4096]{1,0:T(8,128)(2,1)S(1)}, bf16[32,4096]{1,0:T(8,128)(2,1)S(1)}, u32[]{:S(2)}, u32[]{:S(2)}) %collective-permute-start.1) | collective-permute-done | bytes 262176 | tf_op jit(solution)/shard_map/while/body/eval_jaxpr/ppermute | solution.py:12
  908.7 8.9 all-to-all-done.2
  917.6 13.9 %conditional.5 = (bf16[16,4,4096]{2,0,1:T(8,128)(2,1)S(1)}) conditional(s32[]{:T(128)} %convert_element_type.158, () %tuple.106, (bf16[16,4,4096]{2,1,0:T(4,128)(2,1)S(1)}, bf16[4096,768]{1,0:T(8,128)(2,1)}, f32[5,64,768]{2,1,0:T(8,128)}, s32[]{:T(128)}, f32[5,64,768]{2,1,0:T(8,128)}, /*index=5*/bf16[4096,768]{1,0:T(8,128)(2,1)}, ...), branch_computations={%region_11.11_spmd, %region_12.12_spmd} | conditional | flops 1209122816 | bytes 24248332 | solution.py:200
  937.2 8.2 all-to-all-done.3
  965.3 8.9 all-to-all-done.2
  974.3 13.9 %conditional.5 = (bf16[16,4,4096]{2,0,1:T(8,128)(2,1)S(1)}) conditional(s32[]{:T(128)} %convert_element_type.158, () %tuple.106, (bf16[16,4,4096]{2,1,0:T(4,128)(2,1)S(1)}, bf16[4096,768]{1,0:T(8,128)(2,1)}, f32[5,64,768]{2,1,0:T(8,128)}, s32[]{:T(128)}, f32[5,64,768]{2,1,0:T(8,128)}, /*index=5*/bf16[4096,768]{1,0:T(8,128)(2,1)}, ...), branch_computations={%region_11.11_spmd, %region_12.12_spmd} | conditional | flops 1209122816 | bytes 24248332 | solution.py:200
  993.8 8.2 all-to-all-done.3
  1005.3 8.5 collective-permute-done.1
  1023.4 8.9 all-to-all-done.2
  1032.4 13.9 %conditional.5 = (bf16[16,4,4096]{2,0,1:T(8,128)(2,1)S(1)}) conditional(s32[]{:T(128)} %convert_element_type.158, () %tuple.106, (bf16[16,4,4096]{2,1,0:T(4,128)(2,1)S(1)}, bf16[4096,768]{1,0:T(8,128)(2,1)}, f32[5,64,768]{2,1,0:T(8,128)}, s32[]{:T(128)}, f32[5,64,768]{2,1,0:T(8,128)}, /*index=5*/bf16[4096,768]{1,0:T(8,128)(2,1)}, ...), branch_computations={%region_11.11_spmd, %region_12.12_spmd} | conditional | flops 1209122816 | bytes 24248332 | solution.py:200
  1052.0 8.2 all-to-all-done.3
  1080.1 8.9 all-to-all-done.2
  1089.1 13.9 %conditional.5 = (bf16[16,4,4096]{2,0,1:T(8,128)(2,1)S(1)}) conditional(s32[]{:T(128)} %convert_element_type.158, () %tuple.106, (bf16[16,4,4096]{2,1,0:T(4,128)(2,1)S(1)}, bf16[4096,768]{1,0:T(8,128)(2,1)}, f32[5,64,768]{2,1,0:T(8,128)}, s32[]{:T(128)}, f32[5,64,768]{2,1,0:T(8,128)}, /*index=5*/bf16[4096,768]{1,0:T(8,128)(2,1)}, ...), branch_computations={%region_11.11_spmd, %region_12.12_spmd} | conditional | flops 1209122816 | bytes 24248332 | solution.py:200
  1108.7 8.2 all-to-all-done.3
  1135.5 8.9 all-to-all-done.2
  1150.2 8.2 all-to-all-done.3
  1159.8 13.8 %collective-permute-start.1 = (bf16[32,4096]{1,0:T(8,128)(2,1)S(1)}, bf16[32,4096]{1,0:T(8,128)(2,1)S(1)}, u32[]{:S(2)}, u32[]{:S(2)}) collective-permute-start(bf16[32,4096]{1,0:T(8,128)(2,1)S(1)} %get-tuple-element.811), channel_id=1, source_target_pairs={{16,0},{32,16},{48,32},{64,48},{80,64},{96,80},{112,96},{17,1},{33... | collective-permute-start | bytes 786440 | tf_op jit(solution)/shard_map/while/body/eval_jaxpr/ppermute | solution.py:12
  (500 shorter events, 546.1 us)
Async XLA Ops:
  15.3 19.0 %all-to-all-start = ((bf16[16,4,4096]{2,1,0:T(4,128)(2,1)}), bf16[16,4,4096]{2,1,0:T(4,128)(2,1)S(1)}, u32[]{:S(2)}, u32[]{:S(2)}) async-start(bf16[16,4,4096]{2,1,0:T(4,128)(2,1)} %copy.75), calls=%async_computation | async-start | bytes 1048576 | tf_op jit(solution)/shard_map/while/body/eval_jaxpr/all_to_all | solution.py:127
  49.0 15.2 %collective-permute-start = (bf16[32,4096]{1,0:T(8,128)(2,1)S(1)}, bf16[32,4096]{1,0:T(8,128)(2,1)S(1)}, u32[]{:S(2)}, u32[]{:S(2)}) collective-permute-start(bf16[32,4096]{1,0:T(8,128)(2,1)S(1)} %get-tuple-element.781), channel_id=1, source_target_pairs={{0,16},{16,32},{32,48},{48,64},{64,80},{80,96},{96,112},{1,17},{17... | collective-permute-start | bytes 786440 | tf_op jit(solution)/shard_map/while/body/eval_jaxpr/ppermute | solution.py:12
  69.7 14.7 %all-to-all-start = ((bf16[16,4,4096]{2,1,0:T(4,128)(2,1)}), bf16[16,4,4096]{2,1,0:T(4,128)(2,1)S(1)}, u32[]{:S(2)}, u32[]{:S(2)}) async-start(bf16[16,4,4096]{2,1,0:T(4,128)(2,1)} %copy.75), calls=%async_computation | async-start | bytes 1048576 | tf_op jit(solution)/shard_map/while/body/eval_jaxpr/all_to_all | solution.py:127
  110.5 5.2 collective-permute-start
  121.2 15.0 %all-to-all-start = ((bf16[16,4,4096]{2,1,0:T(4,128)(2,1)}), bf16[16,4,4096]{2,1,0:T(4,128)(2,1)S(1)}, u32[]{:S(2)}, u32[]{:S(2)}) async-start(bf16[16,4,4096]{2,1,0:T(4,128)(2,1)} %copy.75), calls=%async_computation | async-start | bytes 1048576 | tf_op jit(solution)/shard_map/while/body/eval_jaxpr/all_to_all | solution.py:127
  161.8 6.3 collective-permute-start
  173.7 13.9 %all-to-all-start = ((bf16[16,4,4096]{2,1,0:T(4,128)(2,1)}), bf16[16,4,4096]{2,1,0:T(4,128)(2,1)S(1)}, u32[]{:S(2)}, u32[]{:S(2)}) async-start(bf16[16,4,4096]{2,1,0:T(4,128)(2,1)} %copy.75), calls=%async_computation | async-start | bytes 1048576 | tf_op jit(solution)/shard_map/while/body/eval_jaxpr/all_to_all | solution.py:127
  214.1 6.4 collective-permute-start
  226.1 13.0 %all-to-all-start = ((bf16[16,4,4096]{2,1,0:T(4,128)(2,1)}), bf16[16,4,4096]{2,1,0:T(4,128)(2,1)S(1)}, u32[]{:S(2)}, u32[]{:S(2)}) async-start(bf16[16,4,4096]{2,1,0:T(4,128)(2,1)} %copy.75), calls=%async_computation | async-start | bytes 1048576 | tf_op jit(solution)/shard_map/while/body/eval_jaxpr/all_to_all | solution.py:127
  263.1 9.8 collective-permute-start
  278.5 12.5 %all-to-all-start = ((bf16[16,4,4096]{2,1,0:T(4,128)(2,1)}), bf16[16,4,4096]{2,1,0:T(4,128)(2,1)S(1)}, u32[]{:S(2)}, u32[]{:S(2)}) async-start(bf16[16,4,4096]{2,1,0:T(4,128)(2,1)} %copy.75), calls=%async_computation | async-start | bytes 1048576 | tf_op jit(solution)/shard_map/while/body/eval_jaxpr/all_to_all | solution.py:127
  305.1 20.2 %collective-permute-start = (bf16[32,4096]{1,0:T(8,128)(2,1)S(1)}, bf16[32,4096]{1,0:T(8,128)(2,1)S(1)}, u32[]{:S(2)}, u32[]{:S(2)}) collective-permute-start(bf16[32,4096]{1,0:T(8,128)(2,1)S(1)} %get-tuple-element.781), channel_id=1, source_target_pairs={{0,16},{16,32},{32,48},{48,64},{64,80},{80,96},{96,112},{1,17},{17... | collective-permute-start | bytes 786440 | tf_op jit(solution)/shard_map/while/body/eval_jaxpr/ppermute | solution.py:12
  330.9 12.8 %all-to-all-start = ((bf16[16,4,4096]{2,1,0:T(4,128)(2,1)}), bf16[16,4,4096]{2,1,0:T(4,128)(2,1)S(1)}, u32[]{:S(2)}, u32[]{:S(2)}) async-start(bf16[16,4,4096]{2,1,0:T(4,128)(2,1)} %copy.75), calls=%async_computation | async-start | bytes 1048576 | tf_op jit(solution)/shard_map/while/body/eval_jaxpr/all_to_all | solution.py:127
  357.7 10.0 collective-permute-start
  373.3 12.5 %all-to-all-start = ((bf16[16,4,4096]{2,1,0:T(4,128)(2,1)}), bf16[16,4,4096]{2,1,0:T(4,128)(2,1)S(1)}, u32[]{:S(2)}, u32[]{:S(2)}) async-start(bf16[16,4,4096]{2,1,0:T(4,128)(2,1)} %copy.75), calls=%async_computation | async-start | bytes 1048576 | tf_op jit(solution)/shard_map/while/body/eval_jaxpr/all_to_all | solution.py:127
  399.9 14.3 %collective-permute-start = (bf16[32,4096]{1,0:T(8,128)(2,1)S(1)}, bf16[32,4096]{1,0:T(8,128)(2,1)S(1)}, u32[]{:S(2)}, u32[]{:S(2)}) collective-permute-start(bf16[32,4096]{1,0:T(8,128)(2,1)S(1)} %get-tuple-element.781), channel_id=1, source_target_pairs={{0,16},{16,32},{32,48},{48,64},{64,80},{80,96},{96,112},{1,17},{17... | collective-permute-start | bytes 786440 | tf_op jit(solution)/shard_map/while/body/eval_jaxpr/ppermute | solution.py:12
  419.8 12.5 %all-to-all-start = ((bf16[16,4,4096]{2,1,0:T(4,128)(2,1)}), bf16[16,4,4096]{2,1,0:T(4,128)(2,1)S(1)}, u32[]{:S(2)}, u32[]{:S(2)}) async-start(bf16[16,4,4096]{2,1,0:T(4,128)(2,1)} %copy.75), calls=%async_computation | async-start | bytes 1048576 | tf_op jit(solution)/shard_map/while/body/eval_jaxpr/all_to_all | solution.py:127
  446.4 10.5 collective-permute-start
  462.5 12.5 %all-to-all-start = ((bf16[16,4,4096]{2,1,0:T(4,128)(2,1)}), bf16[16,4,4096]{2,1,0:T(4,128)(2,1)S(1)}, u32[]{:S(2)}, u32[]{:S(2)}) async-start(bf16[16,4,4096]{2,1,0:T(4,128)(2,1)} %copy.75), calls=%async_computation | async-start | bytes 1048576 | tf_op jit(solution)/shard_map/while/body/eval_jaxpr/all_to_all | solution.py:127
  489.1 10.3 collective-permute-start
  505.0 12.5 %all-to-all-start = ((bf16[16,4,4096]{2,1,0:T(4,128)(2,1)}), bf16[16,4,4096]{2,1,0:T(4,128)(2,1)S(1)}, u32[]{:S(2)}, u32[]{:S(2)}) async-start(bf16[16,4,4096]{2,1,0:T(4,128)(2,1)} %copy.75), calls=%async_computation | async-start | bytes 1048576 | tf_op jit(solution)/shard_map/while/body/eval_jaxpr/all_to_all | solution.py:127
  531.6 10.3 collective-permute-start
  558.4 12.5 %all-to-all-start.2 = ((bf16[16,4,4096]{2,1,0:T(4,128)(2,1)}), bf16[16,4,4096]{2,1,0:T(4,128)(2,1)S(1)}, u32[]{:S(2)}, u32[]{:S(2)}) async-start(bf16[16,4,4096]{2,1,0:T(4,128)(2,1)} %copy.77), calls=%async_computation.2 | async-start | bytes 1048576 | tf_op jit(solution)/shard_map/while/body/eval_jaxpr/all_to_all | solution.py:205
  572.2 12.8 %copy-start.4 = (bf16[5,32,4096]{2,1,0:T(8,128)(2,1)S(1)}, bf16[5,32,4096]{2,1,0:T(8,128)(2,1)}, u32[]{:S(2)}) copy-start(bf16[5,32,4096]{2,1,0:T(8,128)(2,1)} %copy-done.3) | copy-start | bytes 3932164 | tf_op jit(solution)/shard_map/while
  572.2 12.7 %all-to-all-start.3 = ((bf16[16,4,4096]{2,1,0:T(4,128)(2,1)}), bf16[16,4,4096]{2,1,0:T(4,128)(2,1)S(1)}, u32[]{:S(2)}, u32[]{:S(2)}) async-start(bf16[16,4,4096]{2,1,0:T(4,128)(2,1)} %copy.78), calls=%async_computation.3 | async-start | bytes 1048576 | tf_op jit(solution)/shard_map/while/body/eval_jaxpr/all_to_all | solution.py:73
  586.2 14.1 %collective-permute-start.1 = (bf16[32,4096]{1,0:T(8,128)(2,1)S(1)}, bf16[32,4096]{1,0:T(8,128)(2,1)S(1)}, u32[]{:S(2)}, u32[]{:S(2)}) collective-permute-start(bf16[32,4096]{1,0:T(8,128)(2,1)S(1)} %get-tuple-element.811), channel_id=1, source_target_pairs={{16,0},{32,16},{48,32},{64,48},{80,64},{96,80},{112,96},{17,1},{33... | collective-permute-start | bytes 786440 | tf_op jit(solution)/shard_map/while/body/eval_jaxpr/ppermute | solution.py:12
  606.3 12.6 %all-to-all-start.2 = ((bf16[16,4,4096]{2,1,0:T(4,128)(2,1)}), bf16[16,4,4096]{2,1,0:T(4,128)(2,1)S(1)}, u32[]{:S(2)}, u32[]{:S(2)}) async-start(bf16[16,4,4096]{2,1,0:T(4,128)(2,1)} %copy.77), calls=%async_computation.2 | async-start | bytes 1048576 | tf_op jit(solution)/shard_map/while/body/eval_jaxpr/all_to_all | solution.py:205
  620.2 12.8 %copy-start.4 = (bf16[5,32,4096]{2,1,0:T(8,128)(2,1)S(1)}, bf16[5,32,4096]{2,1,0:T(8,128)(2,1)}, u32[]{:S(2)}) copy-start(bf16[5,32,4096]{2,1,0:T(8,128)(2,1)} %copy-done.3) | copy-start | bytes 3932164 | tf_op jit(solution)/shard_map/while
  620.2 12.7 %all-to-all-start.3 = ((bf16[16,4,4096]{2,1,0:T(4,128)(2,1)}), bf16[16,4,4096]{2,1,0:T(4,128)(2,1)S(1)}, u32[]{:S(2)}, u32[]{:S(2)}) async-start(bf16[16,4,4096]{2,1,0:T(4,128)(2,1)} %copy.78), calls=%async_computation.3 | async-start | bytes 1048576 | tf_op jit(solution)/shard_map/while/body/eval_jaxpr/all_to_all | solution.py:73
  634.3 10.0 collective-permute-start.1
  650.3 12.5 %all-to-all-start.2 = ((bf16[16,4,4096]{2,1,0:T(4,128)(2,1)}), bf16[16,4,4096]{2,1,0:T(4,128)(2,1)S(1)}, u32[]{:S(2)}, u32[]{:S(2)}) async-start(bf16[16,4,4096]{2,1,0:T(4,128)(2,1)} %copy.77), calls=%async_computation.2 | async-start | bytes 1048576 | tf_op jit(solution)/shard_map/while/body/eval_jaxpr/all_to_all | solution.py:205
  664.1 12.8 %copy-start.4 = (bf16[5,32,4096]{2,1,0:T(8,128)(2,1)S(1)}, bf16[5,32,4096]{2,1,0:T(8,128)(2,1)}, u32[]{:S(2)}) copy-start(bf16[5,32,4096]{2,1,0:T(8,128)(2,1)} %copy-done.3) | copy-start | bytes 3932164 | tf_op jit(solution)/shard_map/while
  664.1 12.7 %all-to-all-start.3 = ((bf16[16,4,4096]{2,1,0:T(4,128)(2,1)}), bf16[16,4,4096]{2,1,0:T(4,128)(2,1)S(1)}, u32[]{:S(2)}, u32[]{:S(2)}) async-start(bf16[16,4,4096]{2,1,0:T(4,128)(2,1)} %copy.78), calls=%async_computation.3 | async-start | bytes 1048576 | tf_op jit(solution)/shard_map/while/body/eval_jaxpr/all_to_all | solution.py:73
  678.1 11.0 collective-permute-start.1
  695.1 12.5 %all-to-all-start.2 = ((bf16[16,4,4096]{2,1,0:T(4,128)(2,1)}), bf16[16,4,4096]{2,1,0:T(4,128)(2,1)S(1)}, u32[]{:S(2)}, u32[]{:S(2)}) async-start(bf16[16,4,4096]{2,1,0:T(4,128)(2,1)} %copy.77), calls=%async_computation.2 | async-start | bytes 1048576 | tf_op jit(solution)/shard_map/while/body/eval_jaxpr/all_to_all | solution.py:205
  708.9 12.8 %copy-start.4 = (bf16[5,32,4096]{2,1,0:T(8,128)(2,1)S(1)}, bf16[5,32,4096]{2,1,0:T(8,128)(2,1)}, u32[]{:S(2)}) copy-start(bf16[5,32,4096]{2,1,0:T(8,128)(2,1)} %copy-done.3) | copy-start | bytes 3932164 | tf_op jit(solution)/shard_map/while
  708.9 12.7 %all-to-all-start.3 = ((bf16[16,4,4096]{2,1,0:T(4,128)(2,1)}), bf16[16,4,4096]{2,1,0:T(4,128)(2,1)S(1)}, u32[]{:S(2)}, u32[]{:S(2)}) async-start(bf16[16,4,4096]{2,1,0:T(4,128)(2,1)} %copy.78), calls=%async_computation.3 | async-start | bytes 1048576 | tf_op jit(solution)/shard_map/while/body/eval_jaxpr/all_to_all | solution.py:73
  723.0 9.0 collective-permute-start.1
  737.9 12.5 %all-to-all-start.2 = ((bf16[16,4,4096]{2,1,0:T(4,128)(2,1)}), bf16[16,4,4096]{2,1,0:T(4,128)(2,1)S(1)}, u32[]{:S(2)}, u32[]{:S(2)}) async-start(bf16[16,4,4096]{2,1,0:T(4,128)(2,1)} %copy.77), calls=%async_computation.2 | async-start | bytes 1048576 | tf_op jit(solution)/shard_map/while/body/eval_jaxpr/all_to_all | solution.py:205
  751.7 12.8 %copy-start.4 = (bf16[5,32,4096]{2,1,0:T(8,128)(2,1)S(1)}, bf16[5,32,4096]{2,1,0:T(8,128)(2,1)}, u32[]{:S(2)}) copy-start(bf16[5,32,4096]{2,1,0:T(8,128)(2,1)} %copy-done.3) | copy-start | bytes 3932164 | tf_op jit(solution)/shard_map/while
  751.7 12.7 %all-to-all-start.3 = ((bf16[16,4,4096]{2,1,0:T(4,128)(2,1)}), bf16[16,4,4096]{2,1,0:T(4,128)(2,1)S(1)}, u32[]{:S(2)}, u32[]{:S(2)}) async-start(bf16[16,4,4096]{2,1,0:T(4,128)(2,1)} %copy.78), calls=%async_computation.3 | async-start | bytes 1048576 | tf_op jit(solution)/shard_map/while/body/eval_jaxpr/all_to_all | solution.py:73
  765.8 11.4 collective-permute-start.1
  783.2 12.5 %all-to-all-start.2 = ((bf16[16,4,4096]{2,1,0:T(4,128)(2,1)}), bf16[16,4,4096]{2,1,0:T(4,128)(2,1)S(1)}, u32[]{:S(2)}, u32[]{:S(2)}) async-start(bf16[16,4,4096]{2,1,0:T(4,128)(2,1)} %copy.77), calls=%async_computation.2 | async-start | bytes 1048576 | tf_op jit(solution)/shard_map/while/body/eval_jaxpr/all_to_all | solution.py:205
  797.0 12.8 %copy-start.4 = (bf16[5,32,4096]{2,1,0:T(8,128)(2,1)S(1)}, bf16[5,32,4096]{2,1,0:T(8,128)(2,1)}, u32[]{:S(2)}) copy-start(bf16[5,32,4096]{2,1,0:T(8,128)(2,1)} %copy-done.3) | copy-start | bytes 3932164 | tf_op jit(solution)/shard_map/while
  797.0 12.7 %all-to-all-start.3 = ((bf16[16,4,4096]{2,1,0:T(4,128)(2,1)}), bf16[16,4,4096]{2,1,0:T(4,128)(2,1)S(1)}, u32[]{:S(2)}, u32[]{:S(2)}) async-start(bf16[16,4,4096]{2,1,0:T(4,128)(2,1)} %copy.78), calls=%async_computation.3 | async-start | bytes 1048576 | tf_op jit(solution)/shard_map/while/body/eval_jaxpr/all_to_all | solution.py:73
  811.0 88.1 %collective-permute-start.1 = (bf16[32,4096]{1,0:T(8,128)(2,1)S(1)}, bf16[32,4096]{1,0:T(8,128)(2,1)S(1)}, u32[]{:S(2)}, u32[]{:S(2)}) collective-permute-start(bf16[32,4096]{1,0:T(8,128)(2,1)S(1)} %get-tuple-element.811), channel_id=1, source_target_pairs={{16,0},{32,16},{48,32},{64,48},{80,64},{96,80},{112,96},{17,1},{33... | collective-permute-start | bytes 786440 | tf_op jit(solution)/shard_map/while/body/eval_jaxpr/ppermute | solution.py:12
  905.1 12.5 %all-to-all-start.2 = ((bf16[16,4,4096]{2,1,0:T(4,128)(2,1)}), bf16[16,4,4096]{2,1,0:T(4,128)(2,1)S(1)}, u32[]{:S(2)}, u32[]{:S(2)}) async-start(bf16[16,4,4096]{2,1,0:T(4,128)(2,1)} %copy.77), calls=%async_computation.2 | async-start | bytes 1048576 | tf_op jit(solution)/shard_map/while/body/eval_jaxpr/all_to_all | solution.py:205
  932.8 12.8 %copy-start.4 = (bf16[5,32,4096]{2,1,0:T(8,128)(2,1)S(1)}, bf16[5,32,4096]{2,1,0:T(8,128)(2,1)}, u32[]{:S(2)}) copy-start(bf16[5,32,4096]{2,1,0:T(8,128)(2,1)} %copy-done.3) | copy-start | bytes 3932164 | tf_op jit(solution)/shard_map/while
  932.8 12.7 %all-to-all-start.3 = ((bf16[16,4,4096]{2,1,0:T(4,128)(2,1)}), bf16[16,4,4096]{2,1,0:T(4,128)(2,1)S(1)}, u32[]{:S(2)}, u32[]{:S(2)}) async-start(bf16[16,4,4096]{2,1,0:T(4,128)(2,1)} %copy.78), calls=%async_computation.3 | async-start | bytes 1048576 | tf_op jit(solution)/shard_map/while/body/eval_jaxpr/all_to_all | solution.py:73
  946.8 9.0 collective-permute-start.1
  961.7 12.5 %all-to-all-start.2 = ((bf16[16,4,4096]{2,1,0:T(4,128)(2,1)}), bf16[16,4,4096]{2,1,0:T(4,128)(2,1)S(1)}, u32[]{:S(2)}, u32[]{:S(2)}) async-start(bf16[16,4,4096]{2,1,0:T(4,128)(2,1)} %copy.77), calls=%async_computation.2 | async-start | bytes 1048576 | tf_op jit(solution)/shard_map/while/body/eval_jaxpr/all_to_all | solution.py:205
  989.4 12.8 %copy-start.4 = (bf16[5,32,4096]{2,1,0:T(8,128)(2,1)S(1)}, bf16[5,32,4096]{2,1,0:T(8,128)(2,1)}, u32[]{:S(2)}) copy-start(bf16[5,32,4096]{2,1,0:T(8,128)(2,1)} %copy-done.3) | copy-start | bytes 3932164 | tf_op jit(solution)/shard_map/while
  989.4 12.7 %all-to-all-start.3 = ((bf16[16,4,4096]{2,1,0:T(4,128)(2,1)}), bf16[16,4,4096]{2,1,0:T(4,128)(2,1)S(1)}, u32[]{:S(2)}, u32[]{:S(2)}) async-start(bf16[16,4,4096]{2,1,0:T(4,128)(2,1)} %copy.78), calls=%async_computation.3 | async-start | bytes 1048576 | tf_op jit(solution)/shard_map/while/body/eval_jaxpr/all_to_all | solution.py:73
  1003.4 10.5 collective-permute-start.1
  1019.9 12.5 %all-to-all-start.2 = ((bf16[16,4,4096]{2,1,0:T(4,128)(2,1)}), bf16[16,4,4096]{2,1,0:T(4,128)(2,1)S(1)}, u32[]{:S(2)}, u32[]{:S(2)}) async-start(bf16[16,4,4096]{2,1,0:T(4,128)(2,1)} %copy.77), calls=%async_computation.2 | async-start | bytes 1048576 | tf_op jit(solution)/shard_map/while/body/eval_jaxpr/all_to_all | solution.py:205
  1047.5 12.8 %copy-start.4 = (bf16[5,32,4096]{2,1,0:T(8,128)(2,1)S(1)}, bf16[5,32,4096]{2,1,0:T(8,128)(2,1)}, u32[]{:S(2)}) copy-start(bf16[5,32,4096]{2,1,0:T(8,128)(2,1)} %copy-done.3) | copy-start | bytes 3932164 | tf_op jit(solution)/shard_map/while
  1047.5 12.7 %all-to-all-start.3 = ((bf16[16,4,4096]{2,1,0:T(4,128)(2,1)}), bf16[16,4,4096]{2,1,0:T(4,128)(2,1)S(1)}, u32[]{:S(2)}, u32[]{:S(2)}) async-start(bf16[16,4,4096]{2,1,0:T(4,128)(2,1)} %copy.78), calls=%async_computation.3 | async-start | bytes 1048576 | tf_op jit(solution)/shard_map/while/body/eval_jaxpr/all_to_all | solution.py:73
  1061.6 9.0 collective-permute-start.1
  1076.6 12.5 %all-to-all-start.2 = ((bf16[16,4,4096]{2,1,0:T(4,128)(2,1)}), bf16[16,4,4096]{2,1,0:T(4,128)(2,1)S(1)}, u32[]{:S(2)}, u32[]{:S(2)}) async-start(bf16[16,4,4096]{2,1,0:T(4,128)(2,1)} %copy.77), calls=%async_computation.2 | async-start | bytes 1048576 | tf_op jit(solution)/shard_map/while/body/eval_jaxpr/all_to_all | solution.py:205
  1104.2 12.7 %all-to-all-start.3 = ((bf16[16,4,4096]{2,1,0:T(4,128)(2,1)}), bf16[16,4,4096]{2,1,0:T(4,128)(2,1)S(1)}, u32[]{:S(2)}, u32[]{:S(2)}) async-start(bf16[16,4,4096]{2,1,0:T(4,128)(2,1)} %copy.78), calls=%async_computation.3 | async-start | bytes 1048576 | tf_op jit(solution)/shard_map/while/body/eval_jaxpr/all_to_all | solution.py:73
  1118.3 7.7 collective-permute-start.1
  1131.9 12.5 %all-to-all-start.2 = ((bf16[16,4,4096]{2,1,0:T(4,128)(2,1)}), bf16[16,4,4096]{2,1,0:T(4,128)(2,1)S(1)}, u32[]{:S(2)}, u32[]{:S(2)}) async-start(bf16[16,4,4096]{2,1,0:T(4,128)(2,1)} %copy.77), calls=%async_computation.2 | async-start | bytes 1048576 | tf_op jit(solution)/shard_map/while/body/eval_jaxpr/all_to_all | solution.py:205
  1145.7 12.7 %all-to-all-start.3 = ((bf16[16,4,4096]{2,1,0:T(4,128)(2,1)}), bf16[16,4,4096]{2,1,0:T(4,128)(2,1)S(1)}, u32[]{:S(2)}, u32[]{:S(2)}) async-start(bf16[16,4,4096]{2,1,0:T(4,128)(2,1)} %copy.78), calls=%async_computation.3 | async-start | bytes 1048576 | tf_op jit(solution)/shard_map/while/body/eval_jaxpr/all_to_all | solution.py:73
  1159.8 15.0 %collective-permute-start.1 = (bf16[32,4096]{1,0:T(8,128)(2,1)S(1)}, bf16[32,4096]{1,0:T(8,128)(2,1)S(1)}, u32[]{:S(2)}, u32[]{:S(2)}) collective-permute-start(bf16[32,4096]{1,0:T(8,128)(2,1)S(1)} %get-tuple-element.811), channel_id=1, source_target_pairs={{16,0},{32,16},{48,32},{64,48},{80,64},{96,80},{112,96},{17,1},{33... | collective-permute-start | bytes 786440 | tf_op jit(solution)/shard_map/while/body/eval_jaxpr/ppermute | solution.py:12
  (26 other events, 134.8 us)

commit v5 on v2

--- a/solution.py
+++ b/solution.py
@@ -140,8 +140,12 @@
         mixed, pre_gate, pre_up = forward_work(tokens, table4, weights, live)
         outputs = lax.dynamic_update_index_in_dim(outputs, mixed, slot, 0)
         kept_x = lax.dynamic_update_index_in_dim(kept_x, tokens, slot, 0)
-        kept_gate = lax.dynamic_update_index_in_dim(kept_gate, pre_gate, slot, 0)
-        kept_up = lax.dynamic_update_index_in_dim(kept_up, pre_up, slot, 0)
+        kept_gate = lax.dynamic_update_index_in_dim(
+            kept_gate, pre_gate.reshape(total_rows, inner), slot, 0
+        )
+        kept_up = lax.dynamic_update_index_in_dim(
+            kept_up, pre_up.reshape(total_rows, inner), slot, 0
+        )
         incoming = passed_along(mixed, "section", 1)
         return ((incoming, outputs, kept_x, kept_gate, kept_up), None)
 
@@ -150,11 +154,12 @@
         jnp.zeros((tok, width), jnp.bfloat16),
         jnp.zeros(spare + inputs.shape[1:], jnp.bfloat16),
         jnp.zeros(spare + inputs.shape[1:], jnp.bfloat16),
-        jnp.zeros(spare + (experts, capacity, inner), jnp.float32),
-        jnp.zeros(spare + (experts, capacity, inner), jnp.float32),
+        jnp.zeros(spare + (total_rows, inner), jnp.float32),
+        jnp.zeros(spare + (total_rows, inner), jnp.float32),
     )
     finished, _ = lax.scan(forward_tick, start, jnp.arange(ticks, dtype=jnp.int32))
     _, outputs, kept_x, kept_gate, kept_up = finished
+    down_across = lax.optimization_barrier(jnp.transpose(weight_down))
 
     def backward_work(tokens, grad_out, table, table4, gate_now, gate_kept, up_kept, live):
         values, scale, normed = normalize(tokens, gain_row)
@@ -166,10 +171,19 @@
         ).astype(jnp.bfloat16)
 
         def backward_active(operands):
-            rows_grad, gate_again, up_again = operands
-            return expert_backward(
-                rows_grad, gate_again, up_again, weight_gate, weight_up, weight_down
+            rows_grad, gate_pre, up_pre = operands
+            d_hidden = jnp.dot(
+                rows_grad.reshape(total_rows, width),
+                down_across,
+                preferred_element_type=jnp.float32,
             )
+            sigma = jax.nn.sigmoid(gate_pre)
+            d_gate = (d_hidden * up_pre * sigma * (1.0 + gate_pre * (1.0 - sigma))).astype(
+                jnp.bfloat16
+            )
+            d_up = (d_hidden * gate_pre * sigma).astype(jnp.bfloat16)
+            back = contract_last(d_gate, weight_gate) + contract_last(d_up, weight_up)
+            return back.astype(jnp.bfloat16).reshape(rows_grad.shape)
 
         def backward_resting(operands):
             return jnp.zeros_like(operands[0])

time: 1170 us -> 1130 us (0.966)
  other arithmetic: 62.1 us -> 35.9 us
    dot_general x12 -> x8, matrix products: 47.6 us -> 24.4 us  [contract_last(): lax.dot_general(left, right, (((1,), (1,)), ((), ())), preferred_element_...]
    dot_general x0 -> x4, matrix products: none -> 16.5 us  [backward_active(): jnp.dot(rows_grad.reshape(total_rows, width), down_across, preferred_elem...]
    dot_general x11, matrix products: 4.18 us -> 20 us  [forward_work(): jnp.dot(weights, back.astype(jnp.float32), precision=lax.Precision.HIGHEST)]
    dynamic_update_slice x11, local copies, waits for them, and re-layouts: 22.3 us -> 8.52 us  [forward_tick(): lax.dynamic_update_index_in_dim(kept_up, pre_up.reshape(total_rows, inner...]
  transfers between devices with their start and end apart: 55 -> 55, of which waited for: 55 -> 55; matrix products, arithmetic and copies ran while one was open for 3% -> 1% of each run, Pallas kernels for 0% -> 0%
where the time goes in v5:
time: 1130 us; the launch traced here: 1120 us
  waiting for transfers between devices  475 us (42%)
  starting transfers between devices  230 us (20%)
  blocking collectives  134 us (12%)
  local copies, waits for them, and re-layouts  121 us (11%)
  matrix products  110 us (10%)
  other arithmetic  35.9 us (3%)
  loops' own time  16.5 us (1%)
    ppermute x22, waiting for transfers between devices, passed_along(): lax.ppermute(value, axis, [(source, source + steps) for source in range(l...  172 us
    all_to_all x11, blocking collectives, return_rows(): lax.all_to_all(rows, 'expert', split_axis=0, concat_axis=0, tiled=True)  134 us
    ppermute x22, starting transfers between devices, passed_along(): lax.ppermute(value, axis, [(source, source + steps) for source in range(l...  107 us
    all_to_all x11, waiting for transfers between devices, forward_work(): lax.all_to_all(send, 'expert', split_axis=0, concat_axis=0, tiled=True)  106 us
    all_to_all x11, waiting for transfers between devices, backward_work(): lax.all_to_all(grad_send, 'expert', split_axis=0, concat_axis=0, tiled=True)  98.4 us
    all_to_all x11, waiting for transfers between devices, return_rows(): lax.all_to_all(rows, 'expert', split_axis=0, concat_axis=0, tiled=True)  98.1 us
    all_to_all x11, starting transfers between devices, forward_work(): lax.all_to_all(send, 'expert', split_axis=0, concat_axis=0, tiled=True)  44.3 us
    all_to_all x11, starting transfers between devices, return_rows(): lax.all_to_all(rows, 'expert', split_axis=0, concat_axis=0, tiled=True)  39.3 us
  transfers between devices with their start and end apart: 55, of which 55 were waited for; matrix products, arithmetic and copies ran while one was open for 1% of the time, Pallas kernels for 0%

profile of v5, /device:TPU:1, one launch (start us, length us, event | category | flops | bytes accessed | tf_op | source)
XLA Modules:
  0.0 1122.5 jit_solution(2976947475419174324)
XLA Ops:
  9.2 526.3 %while.33 = (s32[]{:T(128)}, bf16[32,4096]{1,0:T(8,128)(2,1)S(1)}, bf16[5,32,4096]{2,1,0:T(8,128)(2,1)}, bf16[5,32,4096]{2,1,0:T(8,128)(2,1)S(1)}, f32[5,64,768]...) while((s32[]{:T(128)}, bf16[32,4096]{1,0:T(8,128)(2,1)S(1)}, ...), condition=%wide.region_7.8_spmd, body=%wide.region_2.7_spmd.sunk | while | flops 1327405056 | bytes 84214784 | solution.py:160
  14.8 8.6 all-to-all-start
  23.4 10.4 all-to-all-done
  34.3 12.3 %all_to_all.30 = bf16[16,4,4096]{2,1,0:T(4,128)(2,1)S(1)} all-to-all(bf16[16,4,4096]{2,1,0:T(4,128)(2,1)S(1)} %copy.65), channel_id=1, replica_groups=mesh['section'=8,'expert'=16] {'expert'}, dimensions={0} | all-to-all | bytes 1048576 | tf_op jit(solution)/shard_map/while/body/eval_jaxpr/all_to_all | solution.py:73
  71.8 11.2 all-to-all-done
  82.9 9.0 conditional.4
  92.4 13.6 %all_to_all.30 = bf16[16,4,4096]{2,1,0:T(4,128)(2,1)S(1)} all-to-all(bf16[16,4,4096]{2,1,0:T(4,128)(2,1)S(1)} %copy.65), channel_id=1, replica_groups=mesh['section'=8,'expert'=16] {'expert'}, dimensions={0} | all-to-all | bytes 1048576 | tf_op jit(solution)/shard_map/while/body/eval_jaxpr/all_to_all | solution.py:73
  122.3 11.4 %all-to-all-done = bf16[16,4,4096]{2,1,0:T(4,128)(2,1)S(1)} async-done(((bf16[16,4,4096]{2,1,0:T(4,128)(2,1)}), bf16[16,4,4096]{2,1,0:T(4,128)(2,1)S(1)}, u32[]{:S(2)}, u32[]{:S(2)}) %all-to-all-start) | async-done | bytes 524320 | tf_op jit(solution)/shard_map/while/body/eval_jaxpr/all_to_all | solution.py:122
  133.7 9.0 conditional.4
  143.1 13.3 %all_to_all.30 = bf16[16,4,4096]{2,1,0:T(4,128)(2,1)S(1)} all-to-all(bf16[16,4,4096]{2,1,0:T(4,128)(2,1)S(1)} %copy.65), channel_id=1, replica_groups=mesh['section'=8,'expert'=16] {'expert'}, dimensions={0} | all-to-all | bytes 1048576 | tf_op jit(solution)/shard_map/while/body/eval_jaxpr/all_to_all | solution.py:73
  175.2 9.1 all-to-all-done
  184.2 9.0 conditional.4
  193.7 13.2 %all_to_all.30 = bf16[16,4,4096]{2,1,0:T(4,128)(2,1)S(1)} all-to-all(bf16[16,4,4096]{2,1,0:T(4,128)(2,1)S(1)} %copy.65), channel_id=1, replica_groups=mesh['section'=8,'expert'=16] {'expert'}, dimensions={0} | all-to-all | bytes 1048576 | tf_op jit(solution)/shard_map/while/body/eval_jaxpr/all_to_all | solution.py:73
  226.6 8.9 all-to-all-done
  235.5 9.0 conditional.4
  245.0 11.6 %all_to_all.30 = bf16[16,4,4096]{2,1,0:T(4,128)(2,1)S(1)} all-to-all(bf16[16,4,4096]{2,1,0:T(4,128)(2,1)S(1)} %copy.65), channel_id=1, replica_groups=mesh['section'=8,'expert'=16] {'expert'}, dimensions={0} | all-to-all | bytes 1048576 | tf_op jit(solution)/shard_map/while/body/eval_jaxpr/all_to_all | solution.py:73
  278.0 8.9 all-to-all-done
  287.5 11.6 %all_to_all.30 = bf16[16,4,4096]{2,1,0:T(4,128)(2,1)S(1)} all-to-all(bf16[16,4,4096]{2,1,0:T(4,128)(2,1)S(1)} %copy.65), channel_id=1, replica_groups=mesh['section'=8,'expert'=16] {'expert'}, dimensions={0} | all-to-all | bytes 1048576 | tf_op jit(solution)/shard_map/while/body/eval_jaxpr/all_to_all | solution.py:73
  301.1 15.9 %collective-permute-start = (bf16[32,4096]{1,0:T(8,128)(2,1)S(1)}, bf16[32,4096]{1,0:T(8,128)(2,1)S(1)}, u32[]{:S(2)}, u32[]{:S(2)}) collective-permute-start(bf16[32,4096]{1,0:T(8,128)(2,1)S(1)} %get-tuple-element.773), channel_id=1, source_target_pairs={{0,16},{16,32},{32,48},{48,64},{64,80},{80,96},{96,112},{1,17},{17... | collective-permute-start | bytes 786440 | tf_op jit(solution)/shard_map/while/body/eval_jaxpr/ppermute | solution.py:12
  329.4 10.1 all-to-all-done
  340.1 11.7 %all_to_all.30 = bf16[16,4,4096]{2,1,0:T(4,128)(2,1)S(1)} all-to-all(bf16[16,4,4096]{2,1,0:T(4,128)(2,1)S(1)} %copy.65), channel_id=1, replica_groups=mesh['section'=8,'expert'=16] {'expert'}, dimensions={0} | all-to-all | bytes 1048576 | tf_op jit(solution)/shard_map/while/body/eval_jaxpr/all_to_all | solution.py:73
  372.9 8.9 all-to-all-done
  382.4 11.6 %all_to_all.30 = bf16[16,4,4096]{2,1,0:T(4,128)(2,1)S(1)} all-to-all(bf16[16,4,4096]{2,1,0:T(4,128)(2,1)S(1)} %copy.65), channel_id=1, replica_groups=mesh['section'=8,'expert'=16] {'expert'}, dimensions={0} | all-to-all | bytes 1048576 | tf_op jit(solution)/shard_map/while/body/eval_jaxpr/all_to_all | solution.py:73
  416.7 8.9 all-to-all-done
  426.1 11.6 %all_to_all.30 = bf16[16,4,4096]{2,1,0:T(4,128)(2,1)S(1)} all-to-all(bf16[16,4,4096]{2,1,0:T(4,128)(2,1)S(1)} %copy.65), channel_id=1, replica_groups=mesh['section'=8,'expert'=16] {'expert'}, dimensions={0} | all-to-all | bytes 1048576 | tf_op jit(solution)/shard_map/while/body/eval_jaxpr/all_to_all | solution.py:73
  459.3 8.9 all-to-all-done
  468.8 11.6 %all_to_all.30 = bf16[16,4,4096]{2,1,0:T(4,128)(2,1)S(1)} all-to-all(bf16[16,4,4096]{2,1,0:T(4,128)(2,1)S(1)} %copy.65), channel_id=1, replica_groups=mesh['section'=8,'expert'=16] {'expert'}, dimensions={0} | all-to-all | bytes 1048576 | tf_op jit(solution)/shard_map/while/body/eval_jaxpr/all_to_all | solution.py:73
  501.8 8.9 all-to-all-done
  511.2 11.6 %all_to_all.30 = bf16[16,4,4096]{2,1,0:T(4,128)(2,1)S(1)} all-to-all(bf16[16,4,4096]{2,1,0:T(4,128)(2,1)S(1)} %copy.65), channel_id=1, replica_groups=mesh['section'=8,'expert'=16] {'expert'}, dimensions={0} | all-to-all | bytes 1048576 | tf_op jit(solution)/shard_map/while/body/eval_jaxpr/all_to_all | solution.py:73
  535.5 8.6 copy.39
  545.4 574.0 %while.34 = (s32[]{:T(128)}, bf16[32,4096]{1,0:T(8,128)(2,1)S(1)}, bf16[5,32,4096]{2,1,0:T(8,128)(2,1)}, pred[]{:T(512)}, s32[11]{0:T(128)S(1)}, /*index=5*/s32[...) while((s32[]{:T(128)}, bf16[32,4096]{1,0:T(8,128)(2,1)S(1)}, ...), condition=%wide.region_14.15_spmd, body=%wide.region_8.14_spmd.sunk | while | flops 1262360704 | bytes 87233072 | solution.py:232
  554.3 8.9 all-to-all-done.2
  567.9 8.9 all-to-all-done.3
  580.1 10.1 collective-permute-done.1
  599.1 8.9 all-to-all-done.2
  612.7 8.9 all-to-all-done.3
  624.9 8.4 collective-permute-done.1
  642.2 8.9 all-to-all-done.2
  655.8 8.9 all-to-all-done.3
  668.0 8.8 collective-permute-done.1
  685.7 8.9 all-to-all-done.2
  699.3 8.9 all-to-all-done.3
  711.5 8.7 collective-permute-done.1
  729.1 8.9 all-to-all-done.2
  742.7 8.9 all-to-all-done.3
  754.9 8.8 collective-permute-done.1
  772.6 8.9 all-to-all-done.2
  786.2 8.9 all-to-all-done.3
  798.4 66.3 %collective-permute-done.1 = bf16[32,4096]{1,0:T(8,128)(2,1)S(1)} collective-permute-done((bf16[32,4096]{1,0:T(8,128)(2,1)S(1)}, bf16[32,4096]{1,0:T(8,128)(2,1)S(1)}, u32[]{:S(2)}, u32[]{:S(2)}) %collective-permute-start.1) | collective-permute-done | bytes 262176 | tf_op jit(solution)/shard_map/while/body/eval_jaxpr/ppermute | solution.py:12
  873.5 8.9 all-to-all-done.2
  882.5 11.9 %conditional.5 = (bf16[16,4,4096]{2,1,0:T(4,128)(2,1)}) conditional(s32[]{:T(128)} %convert_element_type.161, () %tuple.103, (bf16[16,4,4096]{2,1,0:T(4,128)(2,1)S(1)}, bf16[4096,768]{1,0:T(8,128)(2,1)}, f32[5,64,768]{2,1,0:T(8,128)}, s32[]{:T(128)}, f32[5,64,768]{2,1,0:T(8,128)}, /*index=5*/bf16[4096,768]{1,0:T(8,128)(2,1)}, ...), branch_computations={%region_11.11_spmd, %region_12.12_spmd} | conditional | flops 1209270272 | bytes 75629632 | solution.py:191
  898.0 8.9 all-to-all-done.3
  926.1 8.9 all-to-all-done.2
  935.0 11.9 %conditional.5 = (bf16[16,4,4096]{2,1,0:T(4,128)(2,1)}) conditional(s32[]{:T(128)} %convert_element_type.161, () %tuple.103, (bf16[16,4,4096]{2,1,0:T(4,128)(2,1)S(1)}, bf16[4096,768]{1,0:T(8,128)(2,1)}, f32[5,64,768]{2,1,0:T(8,128)}, s32[]{:T(128)}, f32[5,64,768]{2,1,0:T(8,128)}, /*index=5*/bf16[4096,768]{1,0:T(8,128)(2,1)}, ...), branch_computations={%region_11.11_spmd, %region_12.12_spmd} | conditional | flops 1209270272 | bytes 75629632 | solution.py:191
  950.5 8.9 all-to-all-done.3
  979.7 8.9 all-to-all-done.2
  988.6 11.9 %conditional.5 = (bf16[16,4,4096]{2,1,0:T(4,128)(2,1)}) conditional(s32[]{:T(128)} %convert_element_type.161, () %tuple.103, (bf16[16,4,4096]{2,1,0:T(4,128)(2,1)S(1)}, bf16[4096,768]{1,0:T(8,128)(2,1)}, f32[5,64,768]{2,1,0:T(8,128)}, s32[]{:T(128)}, f32[5,64,768]{2,1,0:T(8,128)}, /*index=5*/bf16[4096,768]{1,0:T(8,128)(2,1)}, ...), branch_computations={%region_11.11_spmd, %region_12.12_spmd} | conditional | flops 1209270272 | bytes 75629632 | solution.py:191
  1004.1 8.9 all-to-all-done.3
  1032.3 8.9 all-to-all-done.2
  1041.2 11.9 %conditional.5 = (bf16[16,4,4096]{2,1,0:T(4,128)(2,1)}) conditional(s32[]{:T(128)} %convert_element_type.161, () %tuple.103, (bf16[16,4,4096]{2,1,0:T(4,128)(2,1)S(1)}, bf16[4096,768]{1,0:T(8,128)(2,1)}, f32[5,64,768]{2,1,0:T(8,128)}, s32[]{:T(128)}, f32[5,64,768]{2,1,0:T(8,128)}, /*index=5*/bf16[4096,768]{1,0:T(8,128)(2,1)}, ...), branch_computations={%region_11.11_spmd, %region_12.12_spmd} | conditional | flops 1209270272 | bytes 75629632 | solution.py:191
  1056.7 8.9 all-to-all-done.3
  1083.6 8.9 all-to-all-done.2
  1097.2 8.9 all-to-all-done.3
  1107.5 10.8 collective-permute-start.1
  (457 shorter events, 521.9 us)
Async XLA Ops:
  14.8 19.0 %all-to-all-start = ((bf16[16,4,4096]{2,1,0:T(4,128)(2,1)}), bf16[16,4,4096]{2,1,0:T(4,128)(2,1)S(1)}, u32[]{:S(2)}, u32[]{:S(2)}) async-start(bf16[16,4,4096]{2,1,0:T(4,128)(2,1)} %copy.64), calls=%async_computation | async-start | bytes 1048576 | tf_op jit(solution)/shard_map/while/body/eval_jaxpr/all_to_all | solution.py:122
  48.5 14.1 %collective-permute-start = (bf16[32,4096]{1,0:T(8,128)(2,1)S(1)}, bf16[32,4096]{1,0:T(8,128)(2,1)S(1)}, u32[]{:S(2)}, u32[]{:S(2)}) collective-permute-start(bf16[32,4096]{1,0:T(8,128)(2,1)S(1)} %get-tuple-element.773), channel_id=1, source_target_pairs={{0,16},{16,32},{32,48},{48,64},{64,80},{80,96},{96,112},{1,17},{17... | collective-permute-start | bytes 786440 | tf_op jit(solution)/shard_map/while/body/eval_jaxpr/ppermute | solution.py:12
  68.2 14.7 %all-to-all-start = ((bf16[16,4,4096]{2,1,0:T(4,128)(2,1)}), bf16[16,4,4096]{2,1,0:T(4,128)(2,1)S(1)}, u32[]{:S(2)}, u32[]{:S(2)}) async-start(bf16[16,4,4096]{2,1,0:T(4,128)(2,1)} %copy.64), calls=%async_computation | async-start | bytes 1048576 | tf_op jit(solution)/shard_map/while/body/eval_jaxpr/all_to_all | solution.py:122
  82.9 4.6 copy-start
  107.9 5.2 collective-permute-start
  118.7 15.0 %all-to-all-start = ((bf16[16,4,4096]{2,1,0:T(4,128)(2,1)}), bf16[16,4,4096]{2,1,0:T(4,128)(2,1)S(1)}, u32[]{:S(2)}, u32[]{:S(2)}) async-start(bf16[16,4,4096]{2,1,0:T(4,128)(2,1)} %copy.64), calls=%async_computation | async-start | bytes 1048576 | tf_op jit(solution)/shard_map/while/body/eval_jaxpr/all_to_all | solution.py:122
  133.7 4.6 copy-start
  158.3 7.7 collective-permute-start
  171.6 12.6 %all-to-all-start = ((bf16[16,4,4096]{2,1,0:T(4,128)(2,1)}), bf16[16,4,4096]{2,1,0:T(4,128)(2,1)S(1)}, u32[]{:S(2)}, u32[]{:S(2)}) async-start(bf16[16,4,4096]{2,1,0:T(4,128)(2,1)} %copy.64), calls=%async_computation | async-start | bytes 1048576 | tf_op jit(solution)/shard_map/while/body/eval_jaxpr/all_to_all | solution.py:122
  184.3 4.6 copy-start
  208.8 8.6 collective-permute-start
  223.0 12.5 %all-to-all-start = ((bf16[16,4,4096]{2,1,0:T(4,128)(2,1)}), bf16[16,4,4096]{2,1,0:T(4,128)(2,1)S(1)}, u32[]{:S(2)}, u32[]{:S(2)}) async-start(bf16[16,4,4096]{2,1,0:T(4,128)(2,1)} %copy.64), calls=%async_computation | async-start | bytes 1048576 | tf_op jit(solution)/shard_map/while/body/eval_jaxpr/all_to_all | solution.py:122
  235.5 4.6 copy-start
  258.6 10.3 collective-permute-start
  274.4 12.5 %all-to-all-start = ((bf16[16,4,4096]{2,1,0:T(4,128)(2,1)}), bf16[16,4,4096]{2,1,0:T(4,128)(2,1)S(1)}, u32[]{:S(2)}, u32[]{:S(2)}) async-start(bf16[16,4,4096]{2,1,0:T(4,128)(2,1)} %copy.64), calls=%async_computation | async-start | bytes 1048576 | tf_op jit(solution)/shard_map/while/body/eval_jaxpr/all_to_all | solution.py:122
  301.1 19.2 %collective-permute-start = (bf16[32,4096]{1,0:T(8,128)(2,1)S(1)}, bf16[32,4096]{1,0:T(8,128)(2,1)S(1)}, u32[]{:S(2)}, u32[]{:S(2)}) collective-permute-start(bf16[32,4096]{1,0:T(8,128)(2,1)S(1)} %get-tuple-element.773), channel_id=1, source_target_pairs={{0,16},{16,32},{32,48},{48,64},{64,80},{80,96},{96,112},{1,17},{17... | collective-permute-start | bytes 786440 | tf_op jit(solution)/shard_map/while/body/eval_jaxpr/ppermute | solution.py:12
  325.9 13.7 %all-to-all-start = ((bf16[16,4,4096]{2,1,0:T(4,128)(2,1)}), bf16[16,4,4096]{2,1,0:T(4,128)(2,1)S(1)}, u32[]{:S(2)}, u32[]{:S(2)}) async-start(bf16[16,4,4096]{2,1,0:T(4,128)(2,1)} %copy.64), calls=%async_computation | async-start | bytes 1048576 | tf_op jit(solution)/shard_map/while/body/eval_jaxpr/all_to_all | solution.py:122
  353.7 10.1 collective-permute-start
  369.3 12.5 %all-to-all-start = ((bf16[16,4,4096]{2,1,0:T(4,128)(2,1)}), bf16[16,4,4096]{2,1,0:T(4,128)(2,1)S(1)}, u32[]{:S(2)}, u32[]{:S(2)}) async-start(bf16[16,4,4096]{2,1,0:T(4,128)(2,1)} %copy.64), calls=%async_computation | async-start | bytes 1048576 | tf_op jit(solution)/shard_map/while/body/eval_jaxpr/all_to_all | solution.py:122
  396.0 11.6 %collective-permute-start = (bf16[32,4096]{1,0:T(8,128)(2,1)S(1)}, bf16[32,4096]{1,0:T(8,128)(2,1)S(1)}, u32[]{:S(2)}, u32[]{:S(2)}) collective-permute-start(bf16[32,4096]{1,0:T(8,128)(2,1)S(1)} %get-tuple-element.773), channel_id=1, source_target_pairs={{0,16},{16,32},{32,48},{48,64},{64,80},{80,96},{96,112},{1,17},{17... | collective-permute-start | bytes 786440 | tf_op jit(solution)/shard_map/while/body/eval_jaxpr/ppermute | solution.py:12
  413.1 12.5 %all-to-all-start = ((bf16[16,4,4096]{2,1,0:T(4,128)(2,1)}), bf16[16,4,4096]{2,1,0:T(4,128)(2,1)S(1)}, u32[]{:S(2)}, u32[]{:S(2)}) async-start(bf16[16,4,4096]{2,1,0:T(4,128)(2,1)} %copy.64), calls=%async_computation | async-start | bytes 1048576 | tf_op jit(solution)/shard_map/while/body/eval_jaxpr/all_to_all | solution.py:122
  439.7 10.4 collective-permute-start
  455.7 12.5 %all-to-all-start = ((bf16[16,4,4096]{2,1,0:T(4,128)(2,1)}), bf16[16,4,4096]{2,1,0:T(4,128)(2,1)S(1)}, u32[]{:S(2)}, u32[]{:S(2)}) async-start(bf16[16,4,4096]{2,1,0:T(4,128)(2,1)} %copy.64), calls=%async_computation | async-start | bytes 1048576 | tf_op jit(solution)/shard_map/while/body/eval_jaxpr/all_to_all | solution.py:122
  482.3 10.3 collective-permute-start
  498.2 12.5 %all-to-all-start = ((bf16[16,4,4096]{2,1,0:T(4,128)(2,1)}), bf16[16,4,4096]{2,1,0:T(4,128)(2,1)S(1)}, u32[]{:S(2)}, u32[]{:S(2)}) async-start(bf16[16,4,4096]{2,1,0:T(4,128)(2,1)} %copy.64), calls=%async_computation | async-start | bytes 1048576 | tf_op jit(solution)/shard_map/while/body/eval_jaxpr/all_to_all | solution.py:122
  524.8 10.7 collective-permute-start
  550.7 12.5 %all-to-all-start.2 = ((bf16[16,4,4096]{2,1,0:T(4,128)(2,1)}), bf16[16,4,4096]{2,1,0:T(4,128)(2,1)S(1)}, u32[]{:S(2)}, u32[]{:S(2)}) async-start(bf16[16,4,4096]{2,1,0:T(4,128)(2,1)} %copy.66), calls=%async_computation.2 | async-start | bytes 1048576 | tf_op jit(solution)/shard_map/while/body/eval_jaxpr/all_to_all | solution.py:196
  564.3 12.5 %all-to-all-start.3 = ((bf16[16,4,4096]{2,1,0:T(4,128)(2,1)}), bf16[16,4,4096]{2,1,0:T(4,128)(2,1)S(1)}, u32[]{:S(2)}, u32[]{:S(2)}) async-start(bf16[16,4,4096]{2,1,0:T(4,128)(2,1)} %get-tuple-element.940), calls=%async_computation.3 | async-start | bytes 1048576 | tf_op jit(solution)/shard_map/while/body/eval_jaxpr/all_to_all | solution.py:73
  578.2 12.1 %collective-permute-start.1 = (bf16[32,4096]{1,0:T(8,128)(2,1)S(1)}, bf16[32,4096]{1,0:T(8,128)(2,1)S(1)}, u32[]{:S(2)}, u32[]{:S(2)}) collective-permute-start(bf16[32,4096]{1,0:T(8,128)(2,1)S(1)} %get-tuple-element.803), channel_id=1, source_target_pairs={{16,0},{32,16},{48,32},{64,48},{80,64},{96,80},{112,96},{17,1},{33... | collective-permute-start | bytes 786440 | tf_op jit(solution)/shard_map/while/body/eval_jaxpr/ppermute | solution.py:12
  595.6 12.5 %all-to-all-start.2 = ((bf16[16,4,4096]{2,1,0:T(4,128)(2,1)}), bf16[16,4,4096]{2,1,0:T(4,128)(2,1)S(1)}, u32[]{:S(2)}, u32[]{:S(2)}) async-start(bf16[16,4,4096]{2,1,0:T(4,128)(2,1)} %copy.66), calls=%async_computation.2 | async-start | bytes 1048576 | tf_op jit(solution)/shard_map/while/body/eval_jaxpr/all_to_all | solution.py:196
  609.1 12.5 %all-to-all-start.3 = ((bf16[16,4,4096]{2,1,0:T(4,128)(2,1)}), bf16[16,4,4096]{2,1,0:T(4,128)(2,1)S(1)}, u32[]{:S(2)}, u32[]{:S(2)}) async-start(bf16[16,4,4096]{2,1,0:T(4,128)(2,1)} %get-tuple-element.940), calls=%async_computation.3 | async-start | bytes 1048576 | tf_op jit(solution)/shard_map/while/body/eval_jaxpr/all_to_all | solution.py:73
  623.0 10.3 collective-permute-start.1
  638.6 12.5 %all-to-all-start.2 = ((bf16[16,4,4096]{2,1,0:T(4,128)(2,1)}), bf16[16,4,4096]{2,1,0:T(4,128)(2,1)S(1)}, u32[]{:S(2)}, u32[]{:S(2)}) async-start(bf16[16,4,4096]{2,1,0:T(4,128)(2,1)} %copy.66), calls=%async_computation.2 | async-start | bytes 1048576 | tf_op jit(solution)/shard_map/while/body/eval_jaxpr/all_to_all | solution.py:196
  652.2 12.5 %all-to-all-start.3 = ((bf16[16,4,4096]{2,1,0:T(4,128)(2,1)}), bf16[16,4,4096]{2,1,0:T(4,128)(2,1)S(1)}, u32[]{:S(2)}, u32[]{:S(2)}) async-start(bf16[16,4,4096]{2,1,0:T(4,128)(2,1)} %get-tuple-element.940), calls=%async_computation.3 | async-start | bytes 1048576 | tf_op jit(solution)/shard_map/while/body/eval_jaxpr/all_to_all | solution.py:73
  666.1 10.7 collective-permute-start.1
  682.1 12.5 %all-to-all-start.2 = ((bf16[16,4,4096]{2,1,0:T(4,128)(2,1)}), bf16[16,4,4096]{2,1,0:T(4,128)(2,1)S(1)}, u32[]{:S(2)}, u32[]{:S(2)}) async-start(bf16[16,4,4096]{2,1,0:T(4,128)(2,1)} %copy.66), calls=%async_computation.2 | async-start | bytes 1048576 | tf_op jit(solution)/shard_map/while/body/eval_jaxpr/all_to_all | solution.py:196
  695.7 12.5 %all-to-all-start.3 = ((bf16[16,4,4096]{2,1,0:T(4,128)(2,1)}), bf16[16,4,4096]{2,1,0:T(4,128)(2,1)S(1)}, u32[]{:S(2)}, u32[]{:S(2)}) async-start(bf16[16,4,4096]{2,1,0:T(4,128)(2,1)} %get-tuple-element.940), calls=%async_computation.3 | async-start | bytes 1048576 | tf_op jit(solution)/shard_map/while/body/eval_jaxpr/all_to_all | solution.py:73
  709.6 10.6 collective-permute-start.1
  725.5 12.5 %all-to-all-start.2 = ((bf16[16,4,4096]{2,1,0:T(4,128)(2,1)}), bf16[16,4,4096]{2,1,0:T(4,128)(2,1)S(1)}, u32[]{:S(2)}, u32[]{:S(2)}) async-start(bf16[16,4,4096]{2,1,0:T(4,128)(2,1)} %copy.66), calls=%async_computation.2 | async-start | bytes 1048576 | tf_op jit(solution)/shard_map/while/body/eval_jaxpr/all_to_all | solution.py:196
  739.1 12.5 %all-to-all-start.3 = ((bf16[16,4,4096]{2,1,0:T(4,128)(2,1)}), bf16[16,4,4096]{2,1,0:T(4,128)(2,1)S(1)}, u32[]{:S(2)}, u32[]{:S(2)}) async-start(bf16[16,4,4096]{2,1,0:T(4,128)(2,1)} %get-tuple-element.940), calls=%async_computation.3 | async-start | bytes 1048576 | tf_op jit(solution)/shard_map/while/body/eval_jaxpr/all_to_all | solution.py:73
  752.9 10.7 collective-permute-start.1
  769.0 12.5 %all-to-all-start.2 = ((bf16[16,4,4096]{2,1,0:T(4,128)(2,1)}), bf16[16,4,4096]{2,1,0:T(4,128)(2,1)S(1)}, u32[]{:S(2)}, u32[]{:S(2)}) async-start(bf16[16,4,4096]{2,1,0:T(4,128)(2,1)} %copy.66), calls=%async_computation.2 | async-start | bytes 1048576 | tf_op jit(solution)/shard_map/while/body/eval_jaxpr/all_to_all | solution.py:196
  782.6 12.5 %all-to-all-start.3 = ((bf16[16,4,4096]{2,1,0:T(4,128)(2,1)}), bf16[16,4,4096]{2,1,0:T(4,128)(2,1)S(1)}, u32[]{:S(2)}, u32[]{:S(2)}) async-start(bf16[16,4,4096]{2,1,0:T(4,128)(2,1)} %get-tuple-element.940), calls=%async_computation.3 | async-start | bytes 1048576 | tf_op jit(solution)/shard_map/while/body/eval_jaxpr/all_to_all | solution.py:73
  796.4 68.2 %collective-permute-start.1 = (bf16[32,4096]{1,0:T(8,128)(2,1)S(1)}, bf16[32,4096]{1,0:T(8,128)(2,1)S(1)}, u32[]{:S(2)}, u32[]{:S(2)}) collective-permute-start(bf16[32,4096]{1,0:T(8,128)(2,1)S(1)} %get-tuple-element.803), channel_id=1, source_target_pairs={{16,0},{32,16},{48,32},{64,48},{80,64},{96,80},{112,96},{17,1},{33... | collective-permute-start | bytes 786440 | tf_op jit(solution)/shard_map/while/body/eval_jaxpr/ppermute | solution.py:12
  869.9 12.5 %all-to-all-start.2 = ((bf16[16,4,4096]{2,1,0:T(4,128)(2,1)}), bf16[16,4,4096]{2,1,0:T(4,128)(2,1)S(1)}, u32[]{:S(2)}, u32[]{:S(2)}) async-start(bf16[16,4,4096]{2,1,0:T(4,128)(2,1)} %copy.66), calls=%async_computation.2 | async-start | bytes 1048576 | tf_op jit(solution)/shard_map/while/body/eval_jaxpr/all_to_all | solution.py:196
  882.6 4.6 copy-start.1
  887.2 3.2 copy-start.2
  894.3 12.5 %all-to-all-start.3 = ((bf16[16,4,4096]{2,1,0:T(4,128)(2,1)}), bf16[16,4,4096]{2,1,0:T(4,128)(2,1)S(1)}, u32[]{:S(2)}, u32[]{:S(2)}) async-start(bf16[16,4,4096]{2,1,0:T(4,128)(2,1)} %get-tuple-element.940), calls=%async_computation.3 | async-start | bytes 1048576 | tf_op jit(solution)/shard_map/while/body/eval_jaxpr/all_to_all | solution.py:73
  908.2 9.0 collective-permute-start.1
  922.5 12.5 %all-to-all-start.2 = ((bf16[16,4,4096]{2,1,0:T(4,128)(2,1)}), bf16[16,4,4096]{2,1,0:T(4,128)(2,1)S(1)}, u32[]{:S(2)}, u32[]{:S(2)}) async-start(bf16[16,4,4096]{2,1,0:T(4,128)(2,1)} %copy.66), calls=%async_computation.2 | async-start | bytes 1048576 | tf_op jit(solution)/shard_map/while/body/eval_jaxpr/all_to_all | solution.py:196
  935.2 4.6 copy-start.1
  946.9 12.5 %all-to-all-start.3 = ((bf16[16,4,4096]{2,1,0:T(4,128)(2,1)}), bf16[16,4,4096]{2,1,0:T(4,128)(2,1)S(1)}, u32[]{:S(2)}, u32[]{:S(2)}) async-start(bf16[16,4,4096]{2,1,0:T(4,128)(2,1)} %get-tuple-element.940), calls=%async_computation.3 | async-start | bytes 1048576 | tf_op jit(solution)/shard_map/while/body/eval_jaxpr/all_to_all | solution.py:73
  960.8 10.0 collective-permute-start.1
  976.1 12.5 %all-to-all-start.2 = ((bf16[16,4,4096]{2,1,0:T(4,128)(2,1)}), bf16[16,4,4096]{2,1,0:T(4,128)(2,1)S(1)}, u32[]{:S(2)}, u32[]{:S(2)}) async-start(bf16[16,4,4096]{2,1,0:T(4,128)(2,1)} %copy.66), calls=%async_computation.2 | async-start | bytes 1048576 | tf_op jit(solution)/shard_map/while/body/eval_jaxpr/all_to_all | solution.py:196
  988.8 4.6 copy-start.1
  1000.5 12.5 %all-to-all-start.3 = ((bf16[16,4,4096]{2,1,0:T(4,128)(2,1)}), bf16[16,4,4096]{2,1,0:T(4,128)(2,1)S(1)}, u32[]{:S(2)}, u32[]{:S(2)}) async-start(bf16[16,4,4096]{2,1,0:T(4,128)(2,1)} %get-tuple-element.940), calls=%async_computation.3 | async-start | bytes 1048576 | tf_op jit(solution)/shard_map/while/body/eval_jaxpr/all_to_all | solution.py:73
  1014.4 9.0 collective-permute-start.1
  1028.7 12.5 %all-to-all-start.2 = ((bf16[16,4,4096]{2,1,0:T(4,128)(2,1)}), bf16[16,4,4096]{2,1,0:T(4,128)(2,1)S(1)}, u32[]{:S(2)}, u32[]{:S(2)}) async-start(bf16[16,4,4096]{2,1,0:T(4,128)(2,1)} %copy.66), calls=%async_computation.2 | async-start | bytes 1048576 | tf_op jit(solution)/shard_map/while/body/eval_jaxpr/all_to_all | solution.py:196
  1041.4 4.6 copy-start.1
  1053.1 12.5 %all-to-all-start.3 = ((bf16[16,4,4096]{2,1,0:T(4,128)(2,1)}), bf16[16,4,4096]{2,1,0:T(4,128)(2,1)S(1)}, u32[]{:S(2)}, u32[]{:S(2)}) async-start(bf16[16,4,4096]{2,1,0:T(4,128)(2,1)} %get-tuple-element.940), calls=%async_computation.3 | async-start | bytes 1048576 | tf_op jit(solution)/shard_map/while/body/eval_jaxpr/all_to_all | solution.py:73
  1067.0 7.7 collective-permute-start.1
  1080.0 12.5 %all-to-all-start.2 = ((bf16[16,4,4096]{2,1,0:T(4,128)(2,1)}), bf16[16,4,4096]{2,1,0:T(4,128)(2,1)S(1)}, u32[]{:S(2)}, u32[]{:S(2)}) async-start(bf16[16,4,4096]{2,1,0:T(4,128)(2,1)} %copy.66), calls=%async_computation.2 | async-start | bytes 1048576 | tf_op jit(solution)/shard_map/while/body/eval_jaxpr/all_to_all | solution.py:196
  1093.6 12.5 %all-to-all-start.3 = ((bf16[16,4,4096]{2,1,0:T(4,128)(2,1)}), bf16[16,4,4096]{2,1,0:T(4,128)(2,1)S(1)}, u32[]{:S(2)}, u32[]{:S(2)}) async-start(bf16[16,4,4096]{2,1,0:T(4,128)(2,1)} %get-tuple-element.940), calls=%async_computation.3 | async-start | bytes 1048576 | tf_op jit(solution)/shard_map/while/body/eval_jaxpr/all_to_all | solution.py:73
  1107.5 11.9 %collective-permute-start.1 = (bf16[32,4096]{1,0:T(8,128)(2,1)S(1)}, bf16[32,4096]{1,0:T(8,128)(2,1)S(1)}, u32[]{:S(2)}, u32[]{:S(2)}) collective-permute-start(bf16[32,4096]{1,0:T(8,128)(2,1)S(1)} %get-tuple-element.803), channel_id=1, source_target_pairs={{16,0},{32,16},{48,32},{64,48},{80,64},{96,80},{112,96},{17,1},{33... | collective-permute-start | bytes 786440 | tf_op jit(solution)/shard_map/while/body/eval_jaxpr/ppermute | solution.py:12
  (8 other events, 22.7 us)

commit v6 on v5

--- a/solution.py
+++ b/solution.py
@@ -96,6 +96,9 @@
         "mktj,mtk->mtj", all_tables.astype(jnp.float32), gates, precision=lax.Precision.HIGHEST
     )
     all_tables4 = all_tables.reshape(micro, top, tok, experts, capacity)
+    all_scales4 = all_tables4.astype(jnp.float32) * jnp.swapaxes(gates, 1, 2)[
+        :, :, :, None, None
+    ]
 
     def forward_work(tokens, table4, weights, live):
         values, scale, normed = normalize(tokens, gain_row)
@@ -161,13 +164,13 @@
     _, outputs, kept_x, kept_gate, kept_up = finished
     down_across = lax.optimization_barrier(jnp.transpose(weight_down))
 
-    def backward_work(tokens, grad_out, table, table4, gate_now, gate_kept, up_kept, live):
+    def backward_work(tokens, grad_out, table, scales4, gate_kept, up_kept, live):
         values, scale, normed = normalize(tokens, gain_row)
-        scaled = (gate_now[..., None] * grad_out.astype(jnp.float32)[:, None, :]).astype(
-            jnp.bfloat16
-        )
         grad_send = jnp.einsum(
-            "ktec,tkd->ecd", table4, scaled, preferred_element_type=jnp.float32
+            "ktec,td->ecd",
+            scales4,
+            grad_out.astype(jnp.float32),
+            precision=lax.Precision.HIGHEST,
         ).astype(jnp.bfloat16)
 
         def backward_active(operands):
@@ -218,12 +221,11 @@
         grad_out = jnp.where(section == sections - 1, fresh, incoming)
         tokens = lax.dynamic_index_in_dim(kept_x, index, 0, keepdims=False)
         table = lax.dynamic_index_in_dim(all_tables, index, 0, keepdims=False)
-        table4 = lax.dynamic_index_in_dim(all_tables4, index, 0, keepdims=False)
-        gate_now = lax.dynamic_index_in_dim(gates, index, 0, keepdims=False)
+        scales4 = lax.dynamic_index_in_dim(all_scales4, index, 0, keepdims=False)
         gate_kept = lax.dynamic_index_in_dim(kept_gate, index, 0, keepdims=False)
         up_kept = lax.dynamic_index_in_dim(kept_up, index, 0, keepdims=False)
         result = backward_work(
-            tokens, grad_out, table, table4, gate_now, gate_kept, up_kept, live
+            tokens, grad_out, table, scales4, gate_kept, up_kept, live
         )
         results = lax.dynamic_update_index_in_dim(results, result, slot, 0)
         incoming = passed_along(result, "section", -1)

time: 1130 us -> 1130 us (level)
  local copies, waits for them, and re-layouts: 121 us -> 105 us
where the time goes in v6:
time: 1130 us; the launch traced here: 1120 us
  waiting for transfers between devices  475 us (42%)
  starting transfers between devices  230 us (20%)
  blocking collectives  134 us (12%)
  matrix products  114 us (10%)
  local copies, waits for them, and re-layouts  105 us (9%)
  other arithmetic  45.1 us (4%)
  loops' own time  17.4 us (2%)
    ppermute x22, waiting for transfers between devices, passed_along(): lax.ppermute(value, axis, [(source, source + steps) for source in range(l...  172 us
    all_to_all x11, blocking collectives, return_rows(): lax.all_to_all(rows, 'expert', split_axis=0, concat_axis=0, tiled=True)  134 us
    ppermute x22, starting transfers between devices, passed_along(): lax.ppermute(value, axis, [(source, source + steps) for source in range(l...  107 us
    all_to_all x11, waiting for transfers between devices, forward_work(): lax.all_to_all(send, 'expert', split_axis=0, concat_axis=0, tiled=True)  106 us
    all_to_all x11, waiting for transfers between devices, backward_work(): lax.all_to_all(grad_send, 'expert', split_axis=0, concat_axis=0, tiled=True)  98.4 us
    all_to_all x11, waiting for transfers between devices, return_rows(): lax.all_to_all(rows, 'expert', split_axis=0, concat_axis=0, tiled=True)  98.1 us
    all_to_all x11, starting transfers between devices, forward_work(): lax.all_to_all(send, 'expert', split_axis=0, concat_axis=0, tiled=True)  44.3 us
    all_to_all x11, starting transfers between devices, return_rows(): lax.all_to_all(rows, 'expert', split_axis=0, concat_axis=0, tiled=True)  39.3 us
  transfers between devices with their start and end apart: 55, of which 55 were waited for; matrix products, arithmetic and copies ran while one was open for 1% of the time, Pallas kernels for 0%

profile of v6, /device:TPU:1, one launch (start us, length us, event | category | flops | bytes accessed | tf_op | source)
XLA Modules:
  0.0 1121.2 jit_solution(9866555615600722941)
XLA Ops:
  9.8 525.9 %while.33 = (s32[]{:T(128)}, bf16[32,4096]{1,0:T(8,128)(2,1)S(1)}, bf16[5,32,4096]{2,1,0:T(8,128)(2,1)}, bf16[5,32,4096]{2,1,0:T(8,128)(2,1)S(1)}, f32[5,64,768]...) while((s32[]{:T(128)}, bf16[32,4096]{1,0:T(8,128)(2,1)S(1)}, ...), condition=%wide.region_7.8_spmd, body=%wide.region_2.7_spmd.sunk | while | flops 1327405056 | bytes 84198400 | solution.py:163
  15.3 8.6 all-to-all-start
  23.9 10.4 all-to-all-done
  34.8 12.3 %all_to_all.30 = bf16[16,4,4096]{2,1,0:T(4,128)(2,1)S(1)} all-to-all(bf16[16,4,4096]{2,1,0:T(4,128)(2,1)S(1)} %copy.61), channel_id=1, replica_groups=mesh['section'=8,'expert'=16] {'expert'}, dimensions={0} | all-to-all | bytes 1048576 | tf_op jit(solution)/shard_map/while/body/eval_jaxpr/all_to_all | solution.py:73
  72.3 11.2 all-to-all-done
  83.4 9.0 conditional.4
  92.9 13.6 %all_to_all.30 = bf16[16,4,4096]{2,1,0:T(4,128)(2,1)S(1)} all-to-all(bf16[16,4,4096]{2,1,0:T(4,128)(2,1)S(1)} %copy.61), channel_id=1, replica_groups=mesh['section'=8,'expert'=16] {'expert'}, dimensions={0} | all-to-all | bytes 1048576 | tf_op jit(solution)/shard_map/while/body/eval_jaxpr/all_to_all | solution.py:73
  122.7 11.4 %all-to-all-done = bf16[16,4,4096]{2,1,0:T(4,128)(2,1)S(1)} async-done(((bf16[16,4,4096]{2,1,0:T(4,128)(2,1)}), bf16[16,4,4096]{2,1,0:T(4,128)(2,1)S(1)}, u32[]{:S(2)}, u32[]{:S(2)}) %all-to-all-start) | async-done | bytes 524320 | tf_op jit(solution)/shard_map/while/body/eval_jaxpr/all_to_all | solution.py:125
  134.1 9.0 conditional.4
  143.6 13.3 %all_to_all.30 = bf16[16,4,4096]{2,1,0:T(4,128)(2,1)S(1)} all-to-all(bf16[16,4,4096]{2,1,0:T(4,128)(2,1)S(1)} %copy.61), channel_id=1, replica_groups=mesh['section'=8,'expert'=16] {'expert'}, dimensions={0} | all-to-all | bytes 1048576 | tf_op jit(solution)/shard_map/while/body/eval_jaxpr/all_to_all | solution.py:73
  175.6 9.1 all-to-all-done
  184.7 9.0 conditional.4
  194.1 13.2 %all_to_all.30 = bf16[16,4,4096]{2,1,0:T(4,128)(2,1)S(1)} all-to-all(bf16[16,4,4096]{2,1,0:T(4,128)(2,1)S(1)} %copy.61), channel_id=1, replica_groups=mesh['section'=8,'expert'=16] {'expert'}, dimensions={0} | all-to-all | bytes 1048576 | tf_op jit(solution)/shard_map/while/body/eval_jaxpr/all_to_all | solution.py:73
  226.9 8.9 all-to-all-done
  235.9 9.0 conditional.4
  245.3 11.6 %all_to_all.30 = bf16[16,4,4096]{2,1,0:T(4,128)(2,1)S(1)} all-to-all(bf16[16,4,4096]{2,1,0:T(4,128)(2,1)S(1)} %copy.61), channel_id=1, replica_groups=mesh['section'=8,'expert'=16] {'expert'}, dimensions={0} | all-to-all | bytes 1048576 | tf_op jit(solution)/shard_map/while/body/eval_jaxpr/all_to_all | solution.py:73
  278.3 8.9 all-to-all-done
  287.8 11.6 %all_to_all.30 = bf16[16,4,4096]{2,1,0:T(4,128)(2,1)S(1)} all-to-all(bf16[16,4,4096]{2,1,0:T(4,128)(2,1)S(1)} %copy.61), channel_id=1, replica_groups=mesh['section'=8,'expert'=16] {'expert'}, dimensions={0} | all-to-all | bytes 1048576 | tf_op jit(solution)/shard_map/while/body/eval_jaxpr/all_to_all | solution.py:73
  301.4 15.9 %collective-permute-start = (bf16[32,4096]{1,0:T(8,128)(2,1)S(1)}, bf16[32,4096]{1,0:T(8,128)(2,1)S(1)}, u32[]{:S(2)}, u32[]{:S(2)}) collective-permute-start(bf16[32,4096]{1,0:T(8,128)(2,1)S(1)} %get-tuple-element.755), channel_id=1, source_target_pairs={{0,16},{16,32},{32,48},{48,64},{64,80},{80,96},{96,112},{1,17},{17... | collective-permute-start | bytes 786440 | tf_op jit(solution)/shard_map/while/body/eval_jaxpr/ppermute | solution.py:12
  329.7 10.1 all-to-all-done
  340.4 11.7 %all_to_all.30 = bf16[16,4,4096]{2,1,0:T(4,128)(2,1)S(1)} all-to-all(bf16[16,4,4096]{2,1,0:T(4,128)(2,1)S(1)} %copy.61), channel_id=1, replica_groups=mesh['section'=8,'expert'=16] {'expert'}, dimensions={0} | all-to-all | bytes 1048576 | tf_op jit(solution)/shard_map/while/body/eval_jaxpr/all_to_all | solution.py:73
  373.1 8.9 all-to-all-done
  382.6 11.6 %all_to_all.30 = bf16[16,4,4096]{2,1,0:T(4,128)(2,1)S(1)} all-to-all(bf16[16,4,4096]{2,1,0:T(4,128)(2,1)S(1)} %copy.61), channel_id=1, replica_groups=mesh['section'=8,'expert'=16] {'expert'}, dimensions={0} | all-to-all | bytes 1048576 | tf_op jit(solution)/shard_map/while/body/eval_jaxpr/all_to_all | solution.py:73
  416.9 8.9 all-to-all-done
  426.4 11.6 %all_to_all.30 = bf16[16,4,4096]{2,1,0:T(4,128)(2,1)S(1)} all-to-all(bf16[16,4,4096]{2,1,0:T(4,128)(2,1)S(1)} %copy.61), channel_id=1, replica_groups=mesh['section'=8,'expert'=16] {'expert'}, dimensions={0} | all-to-all | bytes 1048576 | tf_op jit(solution)/shard_map/while/body/eval_jaxpr/all_to_all | solution.py:73
  459.5 8.9 all-to-all-done
  468.9 11.6 %all_to_all.30 = bf16[16,4,4096]{2,1,0:T(4,128)(2,1)S(1)} all-to-all(bf16[16,4,4096]{2,1,0:T(4,128)(2,1)S(1)} %copy.61), channel_id=1, replica_groups=mesh['section'=8,'expert'=16] {'expert'}, dimensions={0} | all-to-all | bytes 1048576 | tf_op jit(solution)/shard_map/while/body/eval_jaxpr/all_to_all | solution.py:73
  501.9 8.9 all-to-all-done
  511.4 11.6 %all_to_all.30 = bf16[16,4,4096]{2,1,0:T(4,128)(2,1)S(1)} all-to-all(bf16[16,4,4096]{2,1,0:T(4,128)(2,1)S(1)} %copy.61), channel_id=1, replica_groups=mesh['section'=8,'expert'=16] {'expert'}, dimensions={0} | all-to-all | bytes 1048576 | tf_op jit(solution)/shard_map/while/body/eval_jaxpr/all_to_all | solution.py:73
  536.5 8.6 copy.38
  546.4 571.8 %while.34 = (s32[]{:T(128)}, bf16[32,4096]{1,0:T(8,128)(2,1)S(1)}, bf16[5,32,4096]{2,1,0:T(8,128)(2,1)}, pred[]{:T(512)}, s32[11]{0:T(128)S(1)}, /*index=5*/s32[...) while((s32[]{:T(128)}, bf16[32,4096]{1,0:T(8,128)(2,1)S(1)}, ...), condition=%wide.region_15.16_spmd, body=%wide.region_8.15_spmd.sunk | while | flops 1329078400 | bytes 86184744 | solution.py:234
  554.1 8.9 all-to-all-done.2
  567.7 8.9 all-to-all-done.3
  580.9 10.1 collective-permute-done.1
  598.7 8.9 all-to-all-done.2
  612.3 8.9 all-to-all-done.3
  625.5 8.4 collective-permute-done.1
  641.6 8.9 all-to-all-done.2
  655.2 8.9 all-to-all-done.3
  668.4 8.8 collective-permute-done.1
  684.9 8.9 all-to-all-done.2
  698.5 8.9 all-to-all-done.3
  711.7 8.7 collective-permute-done.1
  728.1 8.9 all-to-all-done.2
  741.7 8.9 all-to-all-done.3
  754.8 8.8 collective-permute-done.1
  771.4 8.9 all-to-all-done.2
  785.0 8.9 all-to-all-done.3
  798.1 66.3 %collective-permute-done.1 = bf16[32,4096]{1,0:T(8,128)(2,1)S(1)} collective-permute-done((bf16[32,4096]{1,0:T(8,128)(2,1)S(1)}, bf16[32,4096]{1,0:T(8,128)(2,1)S(1)}, u32[]{:S(2)}, u32[]{:S(2)}) %collective-permute-start.1) | collective-permute-done | bytes 262176 | tf_op jit(solution)/shard_map/while/body/eval_jaxpr/ppermute | solution.py:12
  872.2 8.9 all-to-all-done.2
  881.1 11.9 %conditional.5 = (bf16[16,4,4096]{2,1,0:T(4,128)(2,1)}) conditional(s32[]{:T(128)} %convert_element_type.156, () %tuple.103, (bf16[16,4,4096]{2,1,0:T(4,128)(2,1)S(1)}, bf16[4096,768]{1,0:T(8,128)(2,1)}, f32[5,64,768]{2,1,0:T(8,128)}, s32[]{:T(128)}, f32[5,64,768]{2,1,0:T(8,128)}, /*index=5*/bf16[4096,768]{1,0:T(8,128)(2,1)}, ...), branch_computations={%region_12.12_spmd, %region_13.13_spmd} | conditional | flops 1209270272 | bytes 75629632 | solution.py:194
  896.6 8.9 all-to-all-done.3
  924.4 8.9 all-to-all-done.2
  933.3 11.9 %conditional.5 = (bf16[16,4,4096]{2,1,0:T(4,128)(2,1)}) conditional(s32[]{:T(128)} %convert_element_type.156, () %tuple.103, (bf16[16,4,4096]{2,1,0:T(4,128)(2,1)S(1)}, bf16[4096,768]{1,0:T(8,128)(2,1)}, f32[5,64,768]{2,1,0:T(8,128)}, s32[]{:T(128)}, f32[5,64,768]{2,1,0:T(8,128)}, /*index=5*/bf16[4096,768]{1,0:T(8,128)(2,1)}, ...), branch_computations={%region_12.12_spmd, %region_13.13_spmd} | conditional | flops 1209270272 | bytes 75629632 | solution.py:194
  948.8 8.9 all-to-all-done.3
  977.8 8.9 all-to-all-done.2
  986.8 11.9 %conditional.5 = (bf16[16,4,4096]{2,1,0:T(4,128)(2,1)}) conditional(s32[]{:T(128)} %convert_element_type.156, () %tuple.103, (bf16[16,4,4096]{2,1,0:T(4,128)(2,1)S(1)}, bf16[4096,768]{1,0:T(8,128)(2,1)}, f32[5,64,768]{2,1,0:T(8,128)}, s32[]{:T(128)}, f32[5,64,768]{2,1,0:T(8,128)}, /*index=5*/bf16[4096,768]{1,0:T(8,128)(2,1)}, ...), branch_computations={%region_12.12_spmd, %region_13.13_spmd} | conditional | flops 1209270272 | bytes 75629632 | solution.py:194
  1002.3 8.9 all-to-all-done.3
  1030.2 8.9 all-to-all-done.2
  1039.2 11.9 %conditional.5 = (bf16[16,4,4096]{2,1,0:T(4,128)(2,1)}) conditional(s32[]{:T(128)} %convert_element_type.156, () %tuple.103, (bf16[16,4,4096]{2,1,0:T(4,128)(2,1)S(1)}, bf16[4096,768]{1,0:T(8,128)(2,1)}, f32[5,64,768]{2,1,0:T(8,128)}, s32[]{:T(128)}, f32[5,64,768]{2,1,0:T(8,128)}, /*index=5*/bf16[4096,768]{1,0:T(8,128)(2,1)}, ...), branch_computations={%region_12.12_spmd, %region_13.13_spmd} | conditional | flops 1209270272 | bytes 75629632 | solution.py:194
  1054.7 8.9 all-to-all-done.3
  1081.3 8.9 all-to-all-done.2
  1094.9 8.9 all-to-all-done.3
  1106.2 10.8 collective-permute-start.1
  (440 shorter events, 519.6 us)
Async XLA Ops:
  2.2 5.5 copy-start.6
  15.3 19.0 %all-to-all-start = ((bf16[16,4,4096]{2,1,0:T(4,128)(2,1)}), bf16[16,4,4096]{2,1,0:T(4,128)(2,1)S(1)}, u32[]{:S(2)}, u32[]{:S(2)}) async-start(bf16[16,4,4096]{2,1,0:T(4,128)(2,1)} %copy.60), calls=%async_computation | async-start | bytes 1048576 | tf_op jit(solution)/shard_map/while/body/eval_jaxpr/all_to_all | solution.py:125
  49.0 14.1 %collective-permute-start = (bf16[32,4096]{1,0:T(8,128)(2,1)S(1)}, bf16[32,4096]{1,0:T(8,128)(2,1)S(1)}, u32[]{:S(2)}, u32[]{:S(2)}) collective-permute-start(bf16[32,4096]{1,0:T(8,128)(2,1)S(1)} %get-tuple-element.755), channel_id=1, source_target_pairs={{0,16},{16,32},{32,48},{48,64},{64,80},{80,96},{96,112},{1,17},{17... | collective-permute-start | bytes 786440 | tf_op jit(solution)/shard_map/while/body/eval_jaxpr/ppermute | solution.py:12
  68.7 14.7 %all-to-all-start = ((bf16[16,4,4096]{2,1,0:T(4,128)(2,1)}), bf16[16,4,4096]{2,1,0:T(4,128)(2,1)S(1)}, u32[]{:S(2)}, u32[]{:S(2)}) async-start(bf16[16,4,4096]{2,1,0:T(4,128)(2,1)} %copy.60), calls=%async_computation | async-start | bytes 1048576 | tf_op jit(solution)/shard_map/while/body/eval_jaxpr/all_to_all | solution.py:125
  83.4 4.6 copy-start
  108.4 5.2 collective-permute-start
  119.1 15.0 %all-to-all-start = ((bf16[16,4,4096]{2,1,0:T(4,128)(2,1)}), bf16[16,4,4096]{2,1,0:T(4,128)(2,1)S(1)}, u32[]{:S(2)}, u32[]{:S(2)}) async-start(bf16[16,4,4096]{2,1,0:T(4,128)(2,1)} %copy.60), calls=%async_computation | async-start | bytes 1048576 | tf_op jit(solution)/shard_map/while/body/eval_jaxpr/all_to_all | solution.py:125
  134.1 4.6 copy-start
  158.8 7.7 collective-permute-start
  172.0 12.7 %all-to-all-start = ((bf16[16,4,4096]{2,1,0:T(4,128)(2,1)}), bf16[16,4,4096]{2,1,0:T(4,128)(2,1)S(1)}, u32[]{:S(2)}, u32[]{:S(2)}) async-start(bf16[16,4,4096]{2,1,0:T(4,128)(2,1)} %copy.60), calls=%async_computation | async-start | bytes 1048576 | tf_op jit(solution)/shard_map/while/body/eval_jaxpr/all_to_all | solution.py:125
  184.7 4.6 copy-start
  209.3 8.5 collective-permute-start
  223.3 12.5 %all-to-all-start = ((bf16[16,4,4096]{2,1,0:T(4,128)(2,1)}), bf16[16,4,4096]{2,1,0:T(4,128)(2,1)S(1)}, u32[]{:S(2)}, u32[]{:S(2)}) async-start(bf16[16,4,4096]{2,1,0:T(4,128)(2,1)} %copy.60), calls=%async_computation | async-start | bytes 1048576 | tf_op jit(solution)/shard_map/while/body/eval_jaxpr/all_to_all | solution.py:125
  235.9 4.6 copy-start
  258.9 10.3 collective-permute-start
  274.8 12.5 %all-to-all-start = ((bf16[16,4,4096]{2,1,0:T(4,128)(2,1)}), bf16[16,4,4096]{2,1,0:T(4,128)(2,1)S(1)}, u32[]{:S(2)}, u32[]{:S(2)}) async-start(bf16[16,4,4096]{2,1,0:T(4,128)(2,1)} %copy.60), calls=%async_computation | async-start | bytes 1048576 | tf_op jit(solution)/shard_map/while/body/eval_jaxpr/all_to_all | solution.py:125
  301.4 19.2 %collective-permute-start = (bf16[32,4096]{1,0:T(8,128)(2,1)S(1)}, bf16[32,4096]{1,0:T(8,128)(2,1)S(1)}, u32[]{:S(2)}, u32[]{:S(2)}) collective-permute-start(bf16[32,4096]{1,0:T(8,128)(2,1)S(1)} %get-tuple-element.755), channel_id=1, source_target_pairs={{0,16},{16,32},{32,48},{48,64},{64,80},{80,96},{96,112},{1,17},{17... | collective-permute-start | bytes 786440 | tf_op jit(solution)/shard_map/while/body/eval_jaxpr/ppermute | solution.py:12
  326.1 13.7 %all-to-all-start = ((bf16[16,4,4096]{2,1,0:T(4,128)(2,1)}), bf16[16,4,4096]{2,1,0:T(4,128)(2,1)S(1)}, u32[]{:S(2)}, u32[]{:S(2)}) async-start(bf16[16,4,4096]{2,1,0:T(4,128)(2,1)} %copy.60), calls=%async_computation | async-start | bytes 1048576 | tf_op jit(solution)/shard_map/while/body/eval_jaxpr/all_to_all | solution.py:125
  354.0 10.1 collective-permute-start
  369.5 12.5 %all-to-all-start = ((bf16[16,4,4096]{2,1,0:T(4,128)(2,1)}), bf16[16,4,4096]{2,1,0:T(4,128)(2,1)S(1)}, u32[]{:S(2)}, u32[]{:S(2)}) async-start(bf16[16,4,4096]{2,1,0:T(4,128)(2,1)} %copy.60), calls=%async_computation | async-start | bytes 1048576 | tf_op jit(solution)/shard_map/while/body/eval_jaxpr/all_to_all | solution.py:125
  396.2 11.6 %collective-permute-start = (bf16[32,4096]{1,0:T(8,128)(2,1)S(1)}, bf16[32,4096]{1,0:T(8,128)(2,1)S(1)}, u32[]{:S(2)}, u32[]{:S(2)}) collective-permute-start(bf16[32,4096]{1,0:T(8,128)(2,1)S(1)} %get-tuple-element.755), channel_id=1, source_target_pairs={{0,16},{16,32},{32,48},{48,64},{64,80},{80,96},{96,112},{1,17},{17... | collective-permute-start | bytes 786440 | tf_op jit(solution)/shard_map/while/body/eval_jaxpr/ppermute | solution.py:12
  413.3 12.5 %all-to-all-start = ((bf16[16,4,4096]{2,1,0:T(4,128)(2,1)}), bf16[16,4,4096]{2,1,0:T(4,128)(2,1)S(1)}, u32[]{:S(2)}, u32[]{:S(2)}) async-start(bf16[16,4,4096]{2,1,0:T(4,128)(2,1)} %copy.60), calls=%async_computation | async-start | bytes 1048576 | tf_op jit(solution)/shard_map/while/body/eval_jaxpr/all_to_all | solution.py:125
  439.9 10.4 collective-permute-start
  455.9 12.5 %all-to-all-start = ((bf16[16,4,4096]{2,1,0:T(4,128)(2,1)}), bf16[16,4,4096]{2,1,0:T(4,128)(2,1)S(1)}, u32[]{:S(2)}, u32[]{:S(2)}) async-start(bf16[16,4,4096]{2,1,0:T(4,128)(2,1)} %copy.60), calls=%async_computation | async-start | bytes 1048576 | tf_op jit(solution)/shard_map/while/body/eval_jaxpr/all_to_all | solution.py:125
  482.5 10.3 collective-permute-start
  498.3 12.5 %all-to-all-start = ((bf16[16,4,4096]{2,1,0:T(4,128)(2,1)}), bf16[16,4,4096]{2,1,0:T(4,128)(2,1)S(1)}, u32[]{:S(2)}, u32[]{:S(2)}) async-start(bf16[16,4,4096]{2,1,0:T(4,128)(2,1)} %copy.60), calls=%async_computation | async-start | bytes 1048576 | tf_op jit(solution)/shard_map/while/body/eval_jaxpr/all_to_all | solution.py:125
  525.0 10.7 collective-permute-start
  550.5 12.5 %all-to-all-start.2 = ((bf16[16,4,4096]{2,1,0:T(4,128)(2,1)}), bf16[16,4,4096]{2,1,0:T(4,128)(2,1)S(1)}, u32[]{:S(2)}, u32[]{:S(2)}) async-start(bf16[16,4,4096]{2,1,0:T(4,128)(2,1)} %copy.63), calls=%async_computation.2 | async-start | bytes 1048576 | tf_op jit(solution)/shard_map/while/body/eval_jaxpr/all_to_all | solution.py:199
  564.1 12.5 %all-to-all-start.3 = ((bf16[16,4,4096]{2,1,0:T(4,128)(2,1)}), bf16[16,4,4096]{2,1,0:T(4,128)(2,1)S(1)}, u32[]{:S(2)}, u32[]{:S(2)}) async-start(bf16[16,4,4096]{2,1,0:T(4,128)(2,1)} %get-tuple-element.918), calls=%async_computation.3 | async-start | bytes 1048576 | tf_op jit(solution)/shard_map/while/body/eval_jaxpr/all_to_all | solution.py:73
  578.9 12.1 %collective-permute-start.1 = (bf16[32,4096]{1,0:T(8,128)(2,1)S(1)}, bf16[32,4096]{1,0:T(8,128)(2,1)S(1)}, u32[]{:S(2)}, u32[]{:S(2)}) collective-permute-start(bf16[32,4096]{1,0:T(8,128)(2,1)S(1)} %get-tuple-element.784), channel_id=1, source_target_pairs={{16,0},{32,16},{48,32},{64,48},{80,64},{96,80},{112,96},{17,1},{33... | collective-permute-start | bytes 786440 | tf_op jit(solution)/shard_map/while/body/eval_jaxpr/ppermute | solution.py:12
  595.1 12.5 %all-to-all-start.2 = ((bf16[16,4,4096]{2,1,0:T(4,128)(2,1)}), bf16[16,4,4096]{2,1,0:T(4,128)(2,1)S(1)}, u32[]{:S(2)}, u32[]{:S(2)}) async-start(bf16[16,4,4096]{2,1,0:T(4,128)(2,1)} %copy.63), calls=%async_computation.2 | async-start | bytes 1048576 | tf_op jit(solution)/shard_map/while/body/eval_jaxpr/all_to_all | solution.py:199
  608.7 12.5 %all-to-all-start.3 = ((bf16[16,4,4096]{2,1,0:T(4,128)(2,1)}), bf16[16,4,4096]{2,1,0:T(4,128)(2,1)S(1)}, u32[]{:S(2)}, u32[]{:S(2)}) async-start(bf16[16,4,4096]{2,1,0:T(4,128)(2,1)} %get-tuple-element.918), calls=%async_computation.3 | async-start | bytes 1048576 | tf_op jit(solution)/shard_map/while/body/eval_jaxpr/all_to_all | solution.py:73
  623.6 10.3 collective-permute-start.1
  638.0 12.5 %all-to-all-start.2 = ((bf16[16,4,4096]{2,1,0:T(4,128)(2,1)}), bf16[16,4,4096]{2,1,0:T(4,128)(2,1)S(1)}, u32[]{:S(2)}, u32[]{:S(2)}) async-start(bf16[16,4,4096]{2,1,0:T(4,128)(2,1)} %copy.63), calls=%async_computation.2 | async-start | bytes 1048576 | tf_op jit(solution)/shard_map/while/body/eval_jaxpr/all_to_all | solution.py:199
  651.6 12.5 %all-to-all-start.3 = ((bf16[16,4,4096]{2,1,0:T(4,128)(2,1)}), bf16[16,4,4096]{2,1,0:T(4,128)(2,1)S(1)}, u32[]{:S(2)}, u32[]{:S(2)}) async-start(bf16[16,4,4096]{2,1,0:T(4,128)(2,1)} %get-tuple-element.918), calls=%async_computation.3 | async-start | bytes 1048576 | tf_op jit(solution)/shard_map/while/body/eval_jaxpr/all_to_all | solution.py:73
  666.4 10.7 collective-permute-start.1
  681.3 12.5 %all-to-all-start.2 = ((bf16[16,4,4096]{2,1,0:T(4,128)(2,1)}), bf16[16,4,4096]{2,1,0:T(4,128)(2,1)S(1)}, u32[]{:S(2)}, u32[]{:S(2)}) async-start(bf16[16,4,4096]{2,1,0:T(4,128)(2,1)} %copy.63), calls=%async_computation.2 | async-start | bytes 1048576 | tf_op jit(solution)/shard_map/while/body/eval_jaxpr/all_to_all | solution.py:199
  694.9 12.5 %all-to-all-start.3 = ((bf16[16,4,4096]{2,1,0:T(4,128)(2,1)}), bf16[16,4,4096]{2,1,0:T(4,128)(2,1)S(1)}, u32[]{:S(2)}, u32[]{:S(2)}) async-start(bf16[16,4,4096]{2,1,0:T(4,128)(2,1)} %get-tuple-element.918), calls=%async_computation.3 | async-start | bytes 1048576 | tf_op jit(solution)/shard_map/while/body/eval_jaxpr/all_to_all | solution.py:73
  709.7 10.6 collective-permute-start.1
  724.5 12.5 %all-to-all-start.2 = ((bf16[16,4,4096]{2,1,0:T(4,128)(2,1)}), bf16[16,4,4096]{2,1,0:T(4,128)(2,1)S(1)}, u32[]{:S(2)}, u32[]{:S(2)}) async-start(bf16[16,4,4096]{2,1,0:T(4,128)(2,1)} %copy.63), calls=%async_computation.2 | async-start | bytes 1048576 | tf_op jit(solution)/shard_map/while/body/eval_jaxpr/all_to_all | solution.py:199
  738.1 12.5 %all-to-all-start.3 = ((bf16[16,4,4096]{2,1,0:T(4,128)(2,1)}), bf16[16,4,4096]{2,1,0:T(4,128)(2,1)S(1)}, u32[]{:S(2)}, u32[]{:S(2)}) async-start(bf16[16,4,4096]{2,1,0:T(4,128)(2,1)} %get-tuple-element.918), calls=%async_computation.3 | async-start | bytes 1048576 | tf_op jit(solution)/shard_map/while/body/eval_jaxpr/all_to_all | solution.py:73
  752.9 10.7 collective-permute-start.1
  767.8 12.5 %all-to-all-start.2 = ((bf16[16,4,4096]{2,1,0:T(4,128)(2,1)}), bf16[16,4,4096]{2,1,0:T(4,128)(2,1)S(1)}, u32[]{:S(2)}, u32[]{:S(2)}) async-start(bf16[16,4,4096]{2,1,0:T(4,128)(2,1)} %copy.63), calls=%async_computation.2 | async-start | bytes 1048576 | tf_op jit(solution)/shard_map/while/body/eval_jaxpr/all_to_all | solution.py:199
  781.4 12.5 %all-to-all-start.3 = ((bf16[16,4,4096]{2,1,0:T(4,128)(2,1)}), bf16[16,4,4096]{2,1,0:T(4,128)(2,1)S(1)}, u32[]{:S(2)}, u32[]{:S(2)}) async-start(bf16[16,4,4096]{2,1,0:T(4,128)(2,1)} %get-tuple-element.918), calls=%async_computation.3 | async-start | bytes 1048576 | tf_op jit(solution)/shard_map/while/body/eval_jaxpr/all_to_all | solution.py:73
  796.2 68.2 %collective-permute-start.1 = (bf16[32,4096]{1,0:T(8,128)(2,1)S(1)}, bf16[32,4096]{1,0:T(8,128)(2,1)S(1)}, u32[]{:S(2)}, u32[]{:S(2)}) collective-permute-start(bf16[32,4096]{1,0:T(8,128)(2,1)S(1)} %get-tuple-element.784), channel_id=1, source_target_pairs={{16,0},{32,16},{48,32},{64,48},{80,64},{96,80},{112,96},{17,1},{33... | collective-permute-start | bytes 786440 | tf_op jit(solution)/shard_map/while/body/eval_jaxpr/ppermute | solution.py:12
  868.6 12.5 %all-to-all-start.2 = ((bf16[16,4,4096]{2,1,0:T(4,128)(2,1)}), bf16[16,4,4096]{2,1,0:T(4,128)(2,1)S(1)}, u32[]{:S(2)}, u32[]{:S(2)}) async-start(bf16[16,4,4096]{2,1,0:T(4,128)(2,1)} %copy.63), calls=%async_computation.2 | async-start | bytes 1048576 | tf_op jit(solution)/shard_map/while/body/eval_jaxpr/all_to_all | solution.py:199
  881.2 4.6 copy-start.1
  893.0 12.5 %all-to-all-start.3 = ((bf16[16,4,4096]{2,1,0:T(4,128)(2,1)}), bf16[16,4,4096]{2,1,0:T(4,128)(2,1)S(1)}, u32[]{:S(2)}, u32[]{:S(2)}) async-start(bf16[16,4,4096]{2,1,0:T(4,128)(2,1)} %get-tuple-element.918), calls=%async_computation.3 | async-start | bytes 1048576 | tf_op jit(solution)/shard_map/while/body/eval_jaxpr/all_to_all | solution.py:73
  907.8 8.8 collective-permute-start.1
  920.8 12.5 %all-to-all-start.2 = ((bf16[16,4,4096]{2,1,0:T(4,128)(2,1)}), bf16[16,4,4096]{2,1,0:T(4,128)(2,1)S(1)}, u32[]{:S(2)}, u32[]{:S(2)}) async-start(bf16[16,4,4096]{2,1,0:T(4,128)(2,1)} %copy.63), calls=%async_computation.2 | async-start | bytes 1048576 | tf_op jit(solution)/shard_map/while/body/eval_jaxpr/all_to_all | solution.py:199
  933.5 4.6 copy-start.1
  945.2 12.5 %all-to-all-start.3 = ((bf16[16,4,4096]{2,1,0:T(4,128)(2,1)}), bf16[16,4,4096]{2,1,0:T(4,128)(2,1)S(1)}, u32[]{:S(2)}, u32[]{:S(2)}) async-start(bf16[16,4,4096]{2,1,0:T(4,128)(2,1)} %get-tuple-element.918), calls=%async_computation.3 | async-start | bytes 1048576 | tf_op jit(solution)/shard_map/while/body/eval_jaxpr/all_to_all | solution.py:73
  960.1 10.0 collective-permute-start.1
  974.2 12.5 %all-to-all-start.2 = ((bf16[16,4,4096]{2,1,0:T(4,128)(2,1)}), bf16[16,4,4096]{2,1,0:T(4,128)(2,1)S(1)}, u32[]{:S(2)}, u32[]{:S(2)}) async-start(bf16[16,4,4096]{2,1,0:T(4,128)(2,1)} %copy.63), calls=%async_computation.2 | async-start | bytes 1048576 | tf_op jit(solution)/shard_map/while/body/eval_jaxpr/all_to_all | solution.py:199
  986.9 4.6 copy-start.1
  998.6 12.5 %all-to-all-start.3 = ((bf16[16,4,4096]{2,1,0:T(4,128)(2,1)}), bf16[16,4,4096]{2,1,0:T(4,128)(2,1)S(1)}, u32[]{:S(2)}, u32[]{:S(2)}) async-start(bf16[16,4,4096]{2,1,0:T(4,128)(2,1)} %get-tuple-element.918), calls=%async_computation.3 | async-start | bytes 1048576 | tf_op jit(solution)/shard_map/while/body/eval_jaxpr/all_to_all | solution.py:73
  1013.5 9.0 collective-permute-start.1
  1026.6 12.5 %all-to-all-start.2 = ((bf16[16,4,4096]{2,1,0:T(4,128)(2,1)}), bf16[16,4,4096]{2,1,0:T(4,128)(2,1)S(1)}, u32[]{:S(2)}, u32[]{:S(2)}) async-start(bf16[16,4,4096]{2,1,0:T(4,128)(2,1)} %copy.63), calls=%async_computation.2 | async-start | bytes 1048576 | tf_op jit(solution)/shard_map/while/body/eval_jaxpr/all_to_all | solution.py:199
  1039.3 4.6 copy-start.1
  1051.1 12.5 %all-to-all-start.3 = ((bf16[16,4,4096]{2,1,0:T(4,128)(2,1)}), bf16[16,4,4096]{2,1,0:T(4,128)(2,1)S(1)}, u32[]{:S(2)}, u32[]{:S(2)}) async-start(bf16[16,4,4096]{2,1,0:T(4,128)(2,1)} %get-tuple-element.918), calls=%async_computation.3 | async-start | bytes 1048576 | tf_op jit(solution)/shard_map/while/body/eval_jaxpr/all_to_all | solution.py:73
  1065.9 7.7 collective-permute-start.1
  1077.7 12.5 %all-to-all-start.2 = ((bf16[16,4,4096]{2,1,0:T(4,128)(2,1)}), bf16[16,4,4096]{2,1,0:T(4,128)(2,1)S(1)}, u32[]{:S(2)}, u32[]{:S(2)}) async-start(bf16[16,4,4096]{2,1,0:T(4,128)(2,1)} %copy.63), calls=%async_computation.2 | async-start | bytes 1048576 | tf_op jit(solution)/shard_map/while/body/eval_jaxpr/all_to_all | solution.py:199
  1091.3 12.5 %all-to-all-start.3 = ((bf16[16,4,4096]{2,1,0:T(4,128)(2,1)}), bf16[16,4,4096]{2,1,0:T(4,128)(2,1)S(1)}, u32[]{:S(2)}, u32[]{:S(2)}) async-start(bf16[16,4,4096]{2,1,0:T(4,128)(2,1)} %get-tuple-element.918), calls=%async_computation.3 | async-start | bytes 1048576 | tf_op jit(solution)/shard_map/while/body/eval_jaxpr/all_to_all | solution.py:73
  1106.2 11.9 %collective-permute-start.1 = (bf16[32,4096]{1,0:T(8,128)(2,1)S(1)}, bf16[32,4096]{1,0:T(8,128)(2,1)S(1)}, u32[]{:S(2)}, u32[]{:S(2)}) collective-permute-start(bf16[32,4096]{1,0:T(8,128)(2,1)S(1)} %get-tuple-element.784), channel_id=1, source_target_pairs={{16,0},{32,16},{48,32},{64,48},{80,64},{96,80},{112,96},{17,1},{33... | collective-permute-start | bytes 786440 | tf_op jit(solution)/shard_map/while/body/eval_jaxpr/ppermute | solution.py:12
  (10 other events, 26.5 us)

commit v7 on v5

--- a/solution.py
+++ b/solution.py
@@ -90,6 +90,7 @@
     routes = route[0]
     gates = gate[0]
 
+    weight_both = jnp.concatenate([weight_gate, weight_up], axis=1)
     all_places = jax.vmap(lambda r: slot_places(r, experts, capacity))(routes)
     all_tables = jax.vmap(lambda p: slot_table(p, total_rows))(all_places)
     all_weights = jnp.einsum(
@@ -104,7 +105,11 @@
         ).astype(jnp.bfloat16)
 
         def forward_active(operand):
-            pre_gate, pre_up = pre_products(operand, weight_gate, weight_up)
+            pre_both = jnp.dot(
+                operand.reshape(total_rows, width), weight_both, preferred_element_type=jnp.float32
+            ).reshape(operand.shape[:-1] + (2 * inner,))
+            pre_gate = pre_both[..., :inner]
+            pre_up = pre_both[..., inner:]
             product = (pre_gate * jax.nn.sigmoid(pre_gate) * pre_up).astype(jnp.bfloat16)
             output = jnp.einsum(
                 "ech,hd->ecd", product, weight_down, preferred_element_type=jnp.float32
@@ -182,7 +187,7 @@
                 jnp.bfloat16
             )
             d_up = (d_hidden * gate_pre * sigma).astype(jnp.bfloat16)
-            back = contract_last(d_gate, weight_gate) + contract_last(d_up, weight_up)
+            back = contract_last(jnp.concatenate([d_gate, d_up], axis=-1), weight_both)
             return back.astype(jnp.bfloat16).reshape(rows_grad.shape)
 
         def backward_resting(operands):

time: 1130 us -> 1190 us (1.053)
  matrix products: 110 us -> 135 us
  other arithmetic: 35.9 us -> 54.7 us
  waiting for transfers between devices: 475 us -> 490 us
    ppermute x22, waiting for transfers between devices: 172 us -> 195 us  [passed_along(): lax.ppermute(value, axis, [(source, source + steps) for source in range(l...]
    dot_general x8 -> x4, matrix products: 24.4 us -> 33.8 us  [contract_last(): lax.dot_general(left, right, (((1,), (1,)), ((), ())), preferred_element_...]
    dot_general x8 -> x4, matrix products: 23.6 us -> 28.2 us  [forward_active(): jnp.dot(operand.reshape(total_rows, width), weight_both, preferred_elemen...]
where the time goes in v7:
time: 1190 us; the launch traced here: 1180 us
  waiting for transfers between devices  490 us (41%)
  starting transfers between devices  235 us (20%)
  matrix products  135 us (11%)
  blocking collectives  134 us (11%)
  local copies, waits for them, and re-layouts  112 us (9%)
  other arithmetic  54.7 us (5%)
  loops' own time  16.6 us (1%)
    ppermute x22, waiting for transfers between devices, passed_along(): lax.ppermute(value, axis, [(source, source + steps) for source in range(l...  195 us
    all_to_all x11, blocking collectives, return_rows(): lax.all_to_all(rows, 'expert', split_axis=0, concat_axis=0, tiled=True)  134 us
    ppermute x22, starting transfers between devices, passed_along(): lax.ppermute(value, axis, [(source, source + steps) for source in range(l...  112 us
    all_to_all x11, waiting for transfers between devices, forward_work(): lax.all_to_all(send, 'expert', split_axis=0, concat_axis=0, tiled=True)  107 us
    all_to_all x11, waiting for transfers between devices, backward_work(): lax.all_to_all(grad_send, 'expert', split_axis=0, concat_axis=0, tiled=True)  98.4 us
    all_to_all x11, waiting for transfers between devices, return_rows(): lax.all_to_all(rows, 'expert', split_axis=0, concat_axis=0, tiled=True)  90.3 us
    all_to_all x11, starting transfers between devices, forward_work(): lax.all_to_all(send, 'expert', split_axis=0, concat_axis=0, tiled=True)  44.3 us
    all_to_all x11, starting transfers between devices, return_rows(): lax.all_to_all(rows, 'expert', split_axis=0, concat_axis=0, tiled=True)  39.3 us
  transfers between devices with their start and end apart: 55, of which 55 were waited for; matrix products, arithmetic and copies ran while one was open for 1% of the time, Pallas kernels for 0%

profile of v7, /device:TPU:1, one launch (start us, length us, event | category | flops | bytes accessed | tf_op | source)
XLA Modules:
  0.0 1178.9 jit_solution(7339118995403633799)
XLA Ops:
  5.7 10.3 pad_maximum_fusion
  20.0 543.2 %while.33 = (s32[]{:T(128)}, bf16[32,4096]{1,0:T(8,128)(2,1)S(1)}, bf16[5,32,4096]{2,1,0:T(8,128)(2,1)}, bf16[5,32,4096]{2,1,0:T(8,128)(2,1)S(1)}, f32[5,64,768]...) while((s32[]{:T(128)}, bf16[32,4096]{1,0:T(8,128)(2,1)S(1)}, ...), condition=%wide.region_7.8_spmd, body=%wide.region_2.7_spmd.sunk | while | flops 1327405056 | bytes 34145216 | solution.py:165
  25.6 8.6 all-to-all-start
  34.2 10.4 all-to-all-done
  45.2 12.3 %all_to_all.30 = bf16[16,4,4096]{2,1,0:T(4,128)(2,1)S(1)} all-to-all(bf16[16,4,4096]{2,1,0:T(4,128)(2,1)S(1)} %copy.63), channel_id=1, replica_groups=mesh['section'=8,'expert'=16] {'expert'}, dimensions={0} | all-to-all | bytes 1048576 | tf_op jit(solution)/shard_map/while/body/eval_jaxpr/all_to_all | solution.py:73
  66.7 9.3 collective-permute-done
  85.1 11.1 all-to-all-done
  96.3 11.5 conditional.4
  108.2 13.6 %all_to_all.30 = bf16[16,4,4096]{2,1,0:T(4,128)(2,1)S(1)} all-to-all(bf16[16,4,4096]{2,1,0:T(4,128)(2,1)S(1)} %copy.63), channel_id=1, replica_groups=mesh['section'=8,'expert'=16] {'expert'}, dimensions={0} | all-to-all | bytes 1048576 | tf_op jit(solution)/shard_map/while/body/eval_jaxpr/all_to_all | solution.py:73
  138.1 11.4 all-to-all-done
  149.5 11.5 conditional.4
  161.4 13.3 %all_to_all.30 = bf16[16,4,4096]{2,1,0:T(4,128)(2,1)S(1)} all-to-all(bf16[16,4,4096]{2,1,0:T(4,128)(2,1)S(1)} %copy.63), channel_id=1, replica_groups=mesh['section'=8,'expert'=16] {'expert'}, dimensions={0} | all-to-all | bytes 1048576 | tf_op jit(solution)/shard_map/while/body/eval_jaxpr/all_to_all | solution.py:73
  192.0 10.5 all-to-all-done
  202.5 11.5 conditional.4
  214.4 13.8 %all_to_all.30 = bf16[16,4,4096]{2,1,0:T(4,128)(2,1)S(1)} all-to-all(bf16[16,4,4096]{2,1,0:T(4,128)(2,1)S(1)} %copy.63), channel_id=1, replica_groups=mesh['section'=8,'expert'=16] {'expert'}, dimensions={0} | all-to-all | bytes 1048576 | tf_op jit(solution)/shard_map/while/body/eval_jaxpr/all_to_all | solution.py:73
  245.8 9.5 all-to-all-done
  255.3 11.5 conditional.4
  267.3 11.6 all_to_all.30
  299.7 8.9 all-to-all-done
  309.2 11.6 all_to_all.30
  322.8 18.4 %collective-permute-start = (bf16[32,4096]{1,0:T(8,128)(2,1)S(1)}, bf16[32,4096]{1,0:T(8,128)(2,1)S(1)}, u32[]{:S(2)}, u32[]{:S(2)}) collective-permute-start(bf16[32,4096]{1,0:T(8,128)(2,1)S(1)} %get-tuple-element.726), channel_id=1, source_target_pairs={{0,16},{16,32},{32,48},{48,64},{64,80},{80,96},{96,112},{1,17},{17... | collective-permute-start | bytes 786440 | tf_op jit(solution)/shard_map/while/body/eval_jaxpr/ppermute | solution.py:12
  353.6 8.9 all-to-all-done
  363.1 11.6 all_to_all.30
  396.2 8.9 all-to-all-done
  405.6 11.6 all_to_all.30
  419.2 11.1 collective-permute-start
  442.8 9.1 all-to-all-done
  452.4 11.6 all_to_all.30
  485.3 8.9 all-to-all-done
  494.7 11.6 all_to_all.30
  508.3 9.1 collective-permute-start
  529.9 9.0 all-to-all-done
  539.4 11.6 all_to_all.30
  563.2 8.7 copy.39
  573.1 602.7 %while.34 = (s32[]{:T(128)}, bf16[32,4096]{1,0:T(8,128)(2,1)S(1)}, bf16[5,32,4096]{2,1,0:T(8,128)(2,1)}, pred[]{:T(512)}, s32[11]{0:T(128)S(1)}, /*index=5*/s32[...) while((s32[]{:T(128)}, bf16[32,4096]{1,0:T(8,128)(2,1)S(1)}, ...), condition=%wide.region_14.15_spmd, body=%wide.region_8.14_spmd.sunk | while | flops 1262344320 | bytes 34409968 | solution.py:237
  582.0 8.9 all-to-all-done.2
  607.7 13.0 %collective-permute-done.1 = bf16[32,4096]{1,0:T(8,128)(2,1)S(1)} collective-permute-done((bf16[32,4096]{1,0:T(8,128)(2,1)S(1)}, bf16[32,4096]{1,0:T(8,128)(2,1)S(1)}, u32[]{:S(2)}, u32[]{:S(2)}) %collective-permute-start.1) | collective-permute-done | bytes 262176 | tf_op jit(solution)/shard_map/while/body/eval_jaxpr/ppermute | solution.py:12
  629.6 8.9 all-to-all-done.2
  643.9 8.2 all-to-all-done.3
  672.3 8.9 all-to-all-done.2
  686.6 8.2 all-to-all-done.3
  698.1 10.9 collective-permute-done.1
  717.8 8.9 all-to-all-done.2
  732.1 8.2 all-to-all-done.3
  743.6 8.3 collective-permute-done.1
  760.7 8.9 all-to-all-done.2
  775.0 8.2 all-to-all-done.3
  786.5 10.9 collective-permute-done.1
  806.2 8.9 all-to-all-done.2
  832.0 80.3 %collective-permute-done.1 = bf16[32,4096]{1,0:T(8,128)(2,1)S(1)} collective-permute-done((bf16[32,4096]{1,0:T(8,128)(2,1)S(1)}, bf16[32,4096]{1,0:T(8,128)(2,1)S(1)}, u32[]{:S(2)}, u32[]{:S(2)}) %collective-permute-start.1) | collective-permute-done | bytes 262176 | tf_op jit(solution)/shard_map/while/body/eval_jaxpr/ppermute | solution.py:12
  921.1 8.9 all-to-all-done.2
  930.1 13.7 %conditional.5 = (bf16[16,4,4096]{2,1,0:T(4,128)(2,1)}) conditional(s32[]{:T(128)} %convert_element_type.159, () %tuple.105, (bf16[16,4,4096]{2,1,0:T(4,128)(2,1)S(1)}, bf16[4096,768]{1,0:T(8,128)(2,1)}, f32[5,64,768]{2,1,0:T(8,128)}, s32[]{:T(128)}, f32[5,64,768]{2,1,0:T(8,128)}, /*index=5*/bf16[4096,1536]{1,0:T(8,128)(2,1)}) %tuple.106), branch_computations={%region_11.11_spmd, %region_12.12_spmd} | conditional | flops 1209253888 | bytes 22806540 | solution.py:196
  934.3 8.4 convolution_convert_fusion.1
  975.2 8.9 all-to-all-done.2
  984.2 13.7 %conditional.5 = (bf16[16,4,4096]{2,1,0:T(4,128)(2,1)}) conditional(s32[]{:T(128)} %convert_element_type.159, () %tuple.105, (bf16[16,4,4096]{2,1,0:T(4,128)(2,1)S(1)}, bf16[4096,768]{1,0:T(8,128)(2,1)}, f32[5,64,768]{2,1,0:T(8,128)}, s32[]{:T(128)}, f32[5,64,768]{2,1,0:T(8,128)}, /*index=5*/bf16[4096,1536]{1,0:T(8,128)(2,1)}) %tuple.106), branch_computations={%region_11.11_spmd, %region_12.12_spmd} | conditional | flops 1209253888 | bytes 22806540 | solution.py:196
  988.4 8.4 convolution_convert_fusion.1
  1030.7 8.9 all-to-all-done.2
  1039.6 13.7 %conditional.5 = (bf16[16,4,4096]{2,1,0:T(4,128)(2,1)}) conditional(s32[]{:T(128)} %convert_element_type.159, () %tuple.105, (bf16[16,4,4096]{2,1,0:T(4,128)(2,1)S(1)}, bf16[4096,768]{1,0:T(8,128)(2,1)}, f32[5,64,768]{2,1,0:T(8,128)}, s32[]{:T(128)}, f32[5,64,768]{2,1,0:T(8,128)}, /*index=5*/bf16[4096,1536]{1,0:T(8,128)(2,1)}) %tuple.106), branch_computations={%region_11.11_spmd, %region_12.12_spmd} | conditional | flops 1209253888 | bytes 22806540 | solution.py:196
  1043.9 8.4 convolution_convert_fusion.1
  1085.1 8.9 all-to-all-done.2
  1094.0 13.7 %conditional.5 = (bf16[16,4,4096]{2,1,0:T(4,128)(2,1)}) conditional(s32[]{:T(128)} %convert_element_type.159, () %tuple.105, (bf16[16,4,4096]{2,1,0:T(4,128)(2,1)S(1)}, bf16[4096,768]{1,0:T(8,128)(2,1)}, f32[5,64,768]{2,1,0:T(8,128)}, s32[]{:T(128)}, f32[5,64,768]{2,1,0:T(8,128)}, /*index=5*/bf16[4096,1536]{1,0:T(8,128)(2,1)}) %tuple.106), branch_computations={%region_11.11_spmd, %region_12.12_spmd} | conditional | flops 1209253888 | bytes 22806540 | solution.py:196
  1098.3 8.4 convolution_convert_fusion.1
  1138.2 8.9 all-to-all-done.2
  1162.0 12.7 %collective-permute-start.1 = (bf16[32,4096]{1,0:T(8,128)(2,1)S(1)}, bf16[32,4096]{1,0:T(8,128)(2,1)S(1)}, u32[]{:S(2)}, u32[]{:S(2)}) collective-permute-start(bf16[32,4096]{1,0:T(8,128)(2,1)S(1)} %get-tuple-element.755), channel_id=1, source_target_pairs={{16,0},{32,16},{48,32},{64,48},{80,64},{96,80},{112,96},{17,1},{33... | collective-permute-start | bytes 786440 | tf_op jit(solution)/shard_map/while/body/eval_jaxpr/ppermute | solution.py:12
  (422 shorter events, 551.8 us)
Async XLA Ops:
  5.7 14.3 %copy-start = (f32[1,4096]{1,0:T(1,128)S(1)}, f32[1,4096]{1,0:T(1,128)}, u32[]{:S(2)}) copy-start(f32[1,4096]{1,0:T(1,128)} %param.18) | copy-start | bytes 49156
  25.6 19.0 %all-to-all-start = ((bf16[16,4,4096]{2,1,0:T(4,128)(2,1)}), bf16[16,4,4096]{2,1,0:T(4,128)(2,1)S(1)}, u32[]{:S(2)}, u32[]{:S(2)}) async-start(bf16[16,4,4096]{2,1,0:T(4,128)(2,1)} %copy.62), calls=%async_computation | async-start | bytes 1048576 | tf_op jit(solution)/shard_map/while/body/eval_jaxpr/all_to_all | solution.py:127
  59.4 16.6 %collective-permute-start = (bf16[32,4096]{1,0:T(8,128)(2,1)S(1)}, bf16[32,4096]{1,0:T(8,128)(2,1)S(1)}, u32[]{:S(2)}, u32[]{:S(2)}) collective-permute-start(bf16[32,4096]{1,0:T(8,128)(2,1)S(1)} %get-tuple-element.726), channel_id=1, source_target_pairs={{0,16},{16,32},{32,48},{48,64},{64,80},{80,96},{96,112},{1,17},{17... | collective-permute-start | bytes 786440 | tf_op jit(solution)/shard_map/while/body/eval_jaxpr/ppermute | solution.py:12
  81.5 14.7 %all-to-all-start = ((bf16[16,4,4096]{2,1,0:T(4,128)(2,1)}), bf16[16,4,4096]{2,1,0:T(4,128)(2,1)S(1)}, u32[]{:S(2)}, u32[]{:S(2)}) async-start(bf16[16,4,4096]{2,1,0:T(4,128)(2,1)} %copy.62), calls=%async_computation | async-start | bytes 1048576 | tf_op jit(solution)/shard_map/while/body/eval_jaxpr/all_to_all | solution.py:127
  123.7 5.2 collective-permute-start
  134.5 15.0 %all-to-all-start = ((bf16[16,4,4096]{2,1,0:T(4,128)(2,1)}), bf16[16,4,4096]{2,1,0:T(4,128)(2,1)S(1)}, u32[]{:S(2)}, u32[]{:S(2)}) async-start(bf16[16,4,4096]{2,1,0:T(4,128)(2,1)} %copy.62), calls=%async_computation | async-start | bytes 1048576 | tf_op jit(solution)/shard_map/while/body/eval_jaxpr/all_to_all | solution.py:127
  176.6 6.2 collective-permute-start
  188.4 14.1 %all-to-all-start = ((bf16[16,4,4096]{2,1,0:T(4,128)(2,1)}), bf16[16,4,4096]{2,1,0:T(4,128)(2,1)S(1)}, u32[]{:S(2)}, u32[]{:S(2)}) async-start(bf16[16,4,4096]{2,1,0:T(4,128)(2,1)} %copy.62), calls=%async_computation | async-start | bytes 1048576 | tf_op jit(solution)/shard_map/while/body/eval_jaxpr/all_to_all | solution.py:127
  230.1 6.6 collective-permute-start
  242.3 13.1 %all-to-all-start = ((bf16[16,4,4096]{2,1,0:T(4,128)(2,1)}), bf16[16,4,4096]{2,1,0:T(4,128)(2,1)S(1)}, u32[]{:S(2)}, u32[]{:S(2)}) async-start(bf16[16,4,4096]{2,1,0:T(4,128)(2,1)} %copy.62), calls=%async_computation | async-start | bytes 1048576 | tf_op jit(solution)/shard_map/while/body/eval_jaxpr/all_to_all | solution.py:127
  280.8 9.8 collective-permute-start
  296.1 12.5 %all-to-all-start = ((bf16[16,4,4096]{2,1,0:T(4,128)(2,1)}), bf16[16,4,4096]{2,1,0:T(4,128)(2,1)S(1)}, u32[]{:S(2)}, u32[]{:S(2)}) async-start(bf16[16,4,4096]{2,1,0:T(4,128)(2,1)} %copy.62), calls=%async_computation | async-start | bytes 1048576 | tf_op jit(solution)/shard_map/while/body/eval_jaxpr/all_to_all | solution.py:127
  322.8 21.7 %collective-permute-start = (bf16[32,4096]{1,0:T(8,128)(2,1)S(1)}, bf16[32,4096]{1,0:T(8,128)(2,1)S(1)}, u32[]{:S(2)}, u32[]{:S(2)}) collective-permute-start(bf16[32,4096]{1,0:T(8,128)(2,1)S(1)} %get-tuple-element.726), channel_id=1, source_target_pairs={{0,16},{16,32},{32,48},{48,64},{64,80},{80,96},{96,112},{1,17},{17... | collective-permute-start | bytes 786440 | tf_op jit(solution)/shard_map/while/body/eval_jaxpr/ppermute | solution.py:12
  350.0 12.5 %all-to-all-start = ((bf16[16,4,4096]{2,1,0:T(4,128)(2,1)}), bf16[16,4,4096]{2,1,0:T(4,128)(2,1)S(1)}, u32[]{:S(2)}, u32[]{:S(2)}) async-start(bf16[16,4,4096]{2,1,0:T(4,128)(2,1)} %copy.62), calls=%async_computation | async-start | bytes 1048576 | tf_op jit(solution)/shard_map/while/body/eval_jaxpr/all_to_all | solution.py:127
  376.7 10.4 collective-permute-start
  392.6 12.5 %all-to-all-start = ((bf16[16,4,4096]{2,1,0:T(4,128)(2,1)}), bf16[16,4,4096]{2,1,0:T(4,128)(2,1)S(1)}, u32[]{:S(2)}, u32[]{:S(2)}) async-start(bf16[16,4,4096]{2,1,0:T(4,128)(2,1)} %copy.62), calls=%async_computation | async-start | bytes 1048576 | tf_op jit(solution)/shard_map/while/body/eval_jaxpr/all_to_all | solution.py:127
  419.2 14.4 %collective-permute-start = (bf16[32,4096]{1,0:T(8,128)(2,1)S(1)}, bf16[32,4096]{1,0:T(8,128)(2,1)S(1)}, u32[]{:S(2)}, u32[]{:S(2)}) collective-permute-start(bf16[32,4096]{1,0:T(8,128)(2,1)S(1)} %get-tuple-element.726), channel_id=1, source_target_pairs={{0,16},{16,32},{32,48},{48,64},{64,80},{80,96},{96,112},{1,17},{17... | collective-permute-start | bytes 786440 | tf_op jit(solution)/shard_map/while/body/eval_jaxpr/ppermute | solution.py:12
  439.2 12.6 %all-to-all-start = ((bf16[16,4,4096]{2,1,0:T(4,128)(2,1)}), bf16[16,4,4096]{2,1,0:T(4,128)(2,1)S(1)}, u32[]{:S(2)}, u32[]{:S(2)}) async-start(bf16[16,4,4096]{2,1,0:T(4,128)(2,1)} %copy.62), calls=%async_computation | async-start | bytes 1048576 | tf_op jit(solution)/shard_map/while/body/eval_jaxpr/all_to_all | solution.py:127
  465.9 10.2 collective-permute-start
  481.7 12.5 %all-to-all-start = ((bf16[16,4,4096]{2,1,0:T(4,128)(2,1)}), bf16[16,4,4096]{2,1,0:T(4,128)(2,1)S(1)}, u32[]{:S(2)}, u32[]{:S(2)}) async-start(bf16[16,4,4096]{2,1,0:T(4,128)(2,1)} %copy.62), calls=%async_computation | async-start | bytes 1048576 | tf_op jit(solution)/shard_map/while/body/eval_jaxpr/all_to_all | solution.py:127
  508.3 12.4 %collective-permute-start = (bf16[32,4096]{1,0:T(8,128)(2,1)S(1)}, bf16[32,4096]{1,0:T(8,128)(2,1)S(1)}, u32[]{:S(2)}, u32[]{:S(2)}) collective-permute-start(bf16[32,4096]{1,0:T(8,128)(2,1)S(1)} %get-tuple-element.726), channel_id=1, source_target_pairs={{0,16},{16,32},{32,48},{48,64},{64,80},{80,96},{96,112},{1,17},{17... | collective-permute-start | bytes 786440 | tf_op jit(solution)/shard_map/while/body/eval_jaxpr/ppermute | solution.py:12
  526.3 12.5 %all-to-all-start = ((bf16[16,4,4096]{2,1,0:T(4,128)(2,1)}), bf16[16,4,4096]{2,1,0:T(4,128)(2,1)S(1)}, u32[]{:S(2)}, u32[]{:S(2)}) async-start(bf16[16,4,4096]{2,1,0:T(4,128)(2,1)} %copy.62), calls=%async_computation | async-start | bytes 1048576 | tf_op jit(solution)/shard_map/while/body/eval_jaxpr/all_to_all | solution.py:127
  553.0 10.2 collective-permute-start
  578.4 12.5 %all-to-all-start.2 = ((bf16[16,4,4096]{2,1,0:T(4,128)(2,1)}), bf16[16,4,4096]{2,1,0:T(4,128)(2,1)S(1)}, u32[]{:S(2)}, u32[]{:S(2)}) async-start(bf16[16,4,4096]{2,1,0:T(4,128)(2,1)} %copy.64), calls=%async_computation.2 | async-start | bytes 1048576 | tf_op jit(solution)/shard_map/while/body/eval_jaxpr/all_to_all | solution.py:201
  591.9 12.5 %all-to-all-start.3 = ((bf16[16,4,4096]{2,1,0:T(4,128)(2,1)}), bf16[16,4,4096]{2,1,0:T(4,128)(2,1)S(1)}, u32[]{:S(2)}, u32[]{:S(2)}) async-start(bf16[16,4,4096]{2,1,0:T(4,128)(2,1)} %get-tuple-element.886), calls=%async_computation.3 | async-start | bytes 1048576 | tf_op jit(solution)/shard_map/while/body/eval_jaxpr/all_to_all | solution.py:73
  605.8 15.0 %collective-permute-start.1 = (bf16[32,4096]{1,0:T(8,128)(2,1)S(1)}, bf16[32,4096]{1,0:T(8,128)(2,1)S(1)}, u32[]{:S(2)}, u32[]{:S(2)}) collective-permute-start(bf16[32,4096]{1,0:T(8,128)(2,1)S(1)} %get-tuple-element.755), channel_id=1, source_target_pairs={{16,0},{32,16},{48,32},{64,48},{80,64},{96,80},{112,96},{17,1},{33... | collective-permute-start | bytes 786440 | tf_op jit(solution)/shard_map/while/body/eval_jaxpr/ppermute | solution.py:12
  626.0 12.5 %all-to-all-start.2 = ((bf16[16,4,4096]{2,1,0:T(4,128)(2,1)}), bf16[16,4,4096]{2,1,0:T(4,128)(2,1)S(1)}, u32[]{:S(2)}, u32[]{:S(2)}) async-start(bf16[16,4,4096]{2,1,0:T(4,128)(2,1)} %copy.64), calls=%async_computation.2 | async-start | bytes 1048576 | tf_op jit(solution)/shard_map/while/body/eval_jaxpr/all_to_all | solution.py:201
  639.6 12.5 %all-to-all-start.3 = ((bf16[16,4,4096]{2,1,0:T(4,128)(2,1)}), bf16[16,4,4096]{2,1,0:T(4,128)(2,1)S(1)}, u32[]{:S(2)}, u32[]{:S(2)}) async-start(bf16[16,4,4096]{2,1,0:T(4,128)(2,1)} %get-tuple-element.886), calls=%async_computation.3 | async-start | bytes 1048576 | tf_op jit(solution)/shard_map/while/body/eval_jaxpr/all_to_all | solution.py:73
  653.5 10.0 collective-permute-start.1
  668.7 12.5 %all-to-all-start.2 = ((bf16[16,4,4096]{2,1,0:T(4,128)(2,1)}), bf16[16,4,4096]{2,1,0:T(4,128)(2,1)S(1)}, u32[]{:S(2)}, u32[]{:S(2)}) async-start(bf16[16,4,4096]{2,1,0:T(4,128)(2,1)} %copy.64), calls=%async_computation.2 | async-start | bytes 1048576 | tf_op jit(solution)/shard_map/while/body/eval_jaxpr/all_to_all | solution.py:201
  682.3 12.5 %all-to-all-start.3 = ((bf16[16,4,4096]{2,1,0:T(4,128)(2,1)}), bf16[16,4,4096]{2,1,0:T(4,128)(2,1)S(1)}, u32[]{:S(2)}, u32[]{:S(2)}) async-start(bf16[16,4,4096]{2,1,0:T(4,128)(2,1)} %get-tuple-element.886), calls=%async_computation.3 | async-start | bytes 1048576 | tf_op jit(solution)/shard_map/while/body/eval_jaxpr/all_to_all | solution.py:73
  696.2 12.8 %collective-permute-start.1 = (bf16[32,4096]{1,0:T(8,128)(2,1)S(1)}, bf16[32,4096]{1,0:T(8,128)(2,1)S(1)}, u32[]{:S(2)}, u32[]{:S(2)}) collective-permute-start(bf16[32,4096]{1,0:T(8,128)(2,1)S(1)} %get-tuple-element.755), channel_id=1, source_target_pairs={{16,0},{32,16},{48,32},{64,48},{80,64},{96,80},{112,96},{17,1},{33... | collective-permute-start | bytes 786440 | tf_op jit(solution)/shard_map/while/body/eval_jaxpr/ppermute | solution.py:12
  714.3 12.5 %all-to-all-start.2 = ((bf16[16,4,4096]{2,1,0:T(4,128)(2,1)}), bf16[16,4,4096]{2,1,0:T(4,128)(2,1)S(1)}, u32[]{:S(2)}, u32[]{:S(2)}) async-start(bf16[16,4,4096]{2,1,0:T(4,128)(2,1)} %copy.64), calls=%async_computation.2 | async-start | bytes 1048576 | tf_op jit(solution)/shard_map/while/body/eval_jaxpr/all_to_all | solution.py:201
  727.8 12.5 %all-to-all-start.3 = ((bf16[16,4,4096]{2,1,0:T(4,128)(2,1)}), bf16[16,4,4096]{2,1,0:T(4,128)(2,1)S(1)}, u32[]{:S(2)}, u32[]{:S(2)}) async-start(bf16[16,4,4096]{2,1,0:T(4,128)(2,1)} %get-tuple-element.886), calls=%async_computation.3 | async-start | bytes 1048576 | tf_op jit(solution)/shard_map/while/body/eval_jaxpr/all_to_all | solution.py:73
  741.7 10.2 collective-permute-start.1
  757.1 12.5 %all-to-all-start.2 = ((bf16[16,4,4096]{2,1,0:T(4,128)(2,1)}), bf16[16,4,4096]{2,1,0:T(4,128)(2,1)S(1)}, u32[]{:S(2)}, u32[]{:S(2)}) async-start(bf16[16,4,4096]{2,1,0:T(4,128)(2,1)} %copy.64), calls=%async_computation.2 | async-start | bytes 1048576 | tf_op jit(solution)/shard_map/while/body/eval_jaxpr/all_to_all | solution.py:201
  770.7 12.5 %all-to-all-start.3 = ((bf16[16,4,4096]{2,1,0:T(4,128)(2,1)}), bf16[16,4,4096]{2,1,0:T(4,128)(2,1)S(1)}, u32[]{:S(2)}, u32[]{:S(2)}) async-start(bf16[16,4,4096]{2,1,0:T(4,128)(2,1)} %get-tuple-element.886), calls=%async_computation.3 | async-start | bytes 1048576 | tf_op jit(solution)/shard_map/while/body/eval_jaxpr/all_to_all | solution.py:73
  784.6 12.8 %collective-permute-start.1 = (bf16[32,4096]{1,0:T(8,128)(2,1)S(1)}, bf16[32,4096]{1,0:T(8,128)(2,1)S(1)}, u32[]{:S(2)}, u32[]{:S(2)}) collective-permute-start(bf16[32,4096]{1,0:T(8,128)(2,1)S(1)} %get-tuple-element.755), channel_id=1, source_target_pairs={{16,0},{32,16},{48,32},{64,48},{80,64},{96,80},{112,96},{17,1},{33... | collective-permute-start | bytes 786440 | tf_op jit(solution)/shard_map/while/body/eval_jaxpr/ppermute | solution.py:12
  802.6 12.5 %all-to-all-start.2 = ((bf16[16,4,4096]{2,1,0:T(4,128)(2,1)}), bf16[16,4,4096]{2,1,0:T(4,128)(2,1)S(1)}, u32[]{:S(2)}, u32[]{:S(2)}) async-start(bf16[16,4,4096]{2,1,0:T(4,128)(2,1)} %copy.64), calls=%async_computation.2 | async-start | bytes 1048576 | tf_op jit(solution)/shard_map/while/body/eval_jaxpr/all_to_all | solution.py:201
  816.2 12.5 %all-to-all-start.3 = ((bf16[16,4,4096]{2,1,0:T(4,128)(2,1)}), bf16[16,4,4096]{2,1,0:T(4,128)(2,1)S(1)}, u32[]{:S(2)}, u32[]{:S(2)}) async-start(bf16[16,4,4096]{2,1,0:T(4,128)(2,1)} %get-tuple-element.886), calls=%async_computation.3 | async-start | bytes 1048576 | tf_op jit(solution)/shard_map/while/body/eval_jaxpr/all_to_all | solution.py:73
  830.1 82.2 %collective-permute-start.1 = (bf16[32,4096]{1,0:T(8,128)(2,1)S(1)}, bf16[32,4096]{1,0:T(8,128)(2,1)S(1)}, u32[]{:S(2)}, u32[]{:S(2)}) collective-permute-start(bf16[32,4096]{1,0:T(8,128)(2,1)S(1)} %get-tuple-element.755), channel_id=1, source_target_pairs={{16,0},{32,16},{48,32},{64,48},{80,64},{96,80},{112,96},{17,1},{33... | collective-permute-start | bytes 786440 | tf_op jit(solution)/shard_map/while/body/eval_jaxpr/ppermute | solution.py:12
  917.5 12.5 %all-to-all-start.2 = ((bf16[16,4,4096]{2,1,0:T(4,128)(2,1)}), bf16[16,4,4096]{2,1,0:T(4,128)(2,1)S(1)}, u32[]{:S(2)}, u32[]{:S(2)}) async-start(bf16[16,4,4096]{2,1,0:T(4,128)(2,1)} %copy.64), calls=%async_computation.2 | async-start | bytes 1048576 | tf_op jit(solution)/shard_map/while/body/eval_jaxpr/all_to_all | solution.py:201
  943.8 12.5 %all-to-all-start.3 = ((bf16[16,4,4096]{2,1,0:T(4,128)(2,1)}), bf16[16,4,4096]{2,1,0:T(4,128)(2,1)S(1)}, u32[]{:S(2)}, u32[]{:S(2)}) async-start(bf16[16,4,4096]{2,1,0:T(4,128)(2,1)} %get-tuple-element.886), calls=%async_computation.3 | async-start | bytes 1048576 | tf_op jit(solution)/shard_map/while/body/eval_jaxpr/all_to_all | solution.py:73
  957.7 8.7 collective-permute-start.1
  971.7 12.5 %all-to-all-start.2 = ((bf16[16,4,4096]{2,1,0:T(4,128)(2,1)}), bf16[16,4,4096]{2,1,0:T(4,128)(2,1)S(1)}, u32[]{:S(2)}, u32[]{:S(2)}) async-start(bf16[16,4,4096]{2,1,0:T(4,128)(2,1)} %copy.64), calls=%async_computation.2 | async-start | bytes 1048576 | tf_op jit(solution)/shard_map/while/body/eval_jaxpr/all_to_all | solution.py:201
  997.9 12.5 %all-to-all-start.3 = ((bf16[16,4,4096]{2,1,0:T(4,128)(2,1)}), bf16[16,4,4096]{2,1,0:T(4,128)(2,1)S(1)}, u32[]{:S(2)}, u32[]{:S(2)}) async-start(bf16[16,4,4096]{2,1,0:T(4,128)(2,1)} %get-tuple-element.886), calls=%async_computation.3 | async-start | bytes 1048576 | tf_op jit(solution)/shard_map/while/body/eval_jaxpr/all_to_all | solution.py:73
  1011.8 10.0 collective-permute-start.1
  1027.1 12.5 %all-to-all-start.2 = ((bf16[16,4,4096]{2,1,0:T(4,128)(2,1)}), bf16[16,4,4096]{2,1,0:T(4,128)(2,1)S(1)}, u32[]{:S(2)}, u32[]{:S(2)}) async-start(bf16[16,4,4096]{2,1,0:T(4,128)(2,1)} %copy.64), calls=%async_computation.2 | async-start | bytes 1048576 | tf_op jit(solution)/shard_map/while/body/eval_jaxpr/all_to_all | solution.py:201
  1053.3 12.5 %all-to-all-start.3 = ((bf16[16,4,4096]{2,1,0:T(4,128)(2,1)}), bf16[16,4,4096]{2,1,0:T(4,128)(2,1)S(1)}, u32[]{:S(2)}, u32[]{:S(2)}) async-start(bf16[16,4,4096]{2,1,0:T(4,128)(2,1)} %get-tuple-element.886), calls=%async_computation.3 | async-start | bytes 1048576 | tf_op jit(solution)/shard_map/while/body/eval_jaxpr/all_to_all | solution.py:73
  1067.2 9.0 collective-permute-start.1
  1081.5 12.5 %all-to-all-start.2 = ((bf16[16,4,4096]{2,1,0:T(4,128)(2,1)}), bf16[16,4,4096]{2,1,0:T(4,128)(2,1)S(1)}, u32[]{:S(2)}, u32[]{:S(2)}) async-start(bf16[16,4,4096]{2,1,0:T(4,128)(2,1)} %copy.64), calls=%async_computation.2 | async-start | bytes 1048576 | tf_op jit(solution)/shard_map/while/body/eval_jaxpr/all_to_all | solution.py:201
  1107.7 12.5 %all-to-all-start.3 = ((bf16[16,4,4096]{2,1,0:T(4,128)(2,1)}), bf16[16,4,4096]{2,1,0:T(4,128)(2,1)S(1)}, u32[]{:S(2)}, u32[]{:S(2)}) async-start(bf16[16,4,4096]{2,1,0:T(4,128)(2,1)} %get-tuple-element.886), calls=%async_computation.3 | async-start | bytes 1048576 | tf_op jit(solution)/shard_map/while/body/eval_jaxpr/all_to_all | solution.py:73
  1121.7 7.7 collective-permute-start.1
  1134.6 12.5 %all-to-all-start.2 = ((bf16[16,4,4096]{2,1,0:T(4,128)(2,1)}), bf16[16,4,4096]{2,1,0:T(4,128)(2,1)S(1)}, u32[]{:S(2)}, u32[]{:S(2)}) async-start(bf16[16,4,4096]{2,1,0:T(4,128)(2,1)} %copy.64), calls=%async_computation.2 | async-start | bytes 1048576 | tf_op jit(solution)/shard_map/while/body/eval_jaxpr/all_to_all | solution.py:201
  1148.1 12.5 %all-to-all-start.3 = ((bf16[16,4,4096]{2,1,0:T(4,128)(2,1)}), bf16[16,4,4096]{2,1,0:T(4,128)(2,1)S(1)}, u32[]{:S(2)}, u32[]{:S(2)}) async-start(bf16[16,4,4096]{2,1,0:T(4,128)(2,1)} %get-tuple-element.886), calls=%async_computation.3 | async-start | bytes 1048576 | tf_op jit(solution)/shard_map/while/body/eval_jaxpr/all_to_all | solution.py:73
  1162.0 13.8 %collective-permute-start.1 = (bf16[32,4096]{1,0:T(8,128)(2,1)S(1)}, bf16[32,4096]{1,0:T(8,128)(2,1)S(1)}, u32[]{:S(2)}, u32[]{:S(2)}) collective-permute-start(bf16[32,4096]{1,0:T(8,128)(2,1)S(1)} %get-tuple-element.755), channel_id=1, source_target_pairs={{16,0},{32,16},{48,32},{64,48},{80,64},{96,80},{112,96},{17,1},{33... | collective-permute-start | bytes 786440 | tf_op jit(solution)/shard_map/while/body/eval_jaxpr/ppermute | solution.py:12

commit v8 on v5

--- a/solution.py
+++ b/solution.py
@@ -96,12 +96,24 @@
         "mktj,mtk->mtj", all_tables.astype(jnp.float32), gates, precision=lax.Precision.HIGHEST
     )
     all_tables4 = all_tables.reshape(micro, top, tok, experts, capacity)
-
-    def forward_work(tokens, table4, weights, live):
+    pair_ids = jnp.arange(top * tok, dtype=jnp.float32).reshape(top, tok)
+    token_ids = jnp.broadcast_to(jnp.arange(tok, dtype=jnp.float32)[None, :], (top, tok))
+    filled = jnp.sum(all_tables4.astype(jnp.float32), axis=(1, 2))
+    empty = jnp.float32(top * tok)
+    all_token_src = jnp.where(
+        filled > 0,
+        jnp.einsum("mktec,kt->mec", all_tables4.astype(jnp.float32), token_ids),
+        empty,
+    ).astype(jnp.int32)
+    all_pair_src = jnp.where(
+        filled > 0,
+        jnp.einsum("mktec,kt->mec", all_tables4.astype(jnp.float32), pair_ids),
+        empty,
+    ).astype(jnp.int32)
+
+    def forward_work(tokens, token_src, weights, live):
         values, scale, normed = normalize(tokens, gain_row)
-        send = jnp.einsum(
-            "ktec,td->ecd", table4, normed, preferred_element_type=jnp.float32
-        ).astype(jnp.bfloat16)
+        send = jnp.take(normed, token_src, axis=0, mode="fill", fill_value=0)
 
         def forward_active(operand):
             pre_gate, pre_up = pre_products(operand, weight_gate, weight_up)
@@ -135,9 +147,9 @@
         slot = jnp.where(live, offset, micro)
         fresh = lax.dynamic_index_in_dim(inputs, index, 0, keepdims=False)
         tokens = jnp.where(section == 0, fresh, incoming)
-        table4 = lax.dynamic_index_in_dim(all_tables4, index, 0, keepdims=False)
+        token_src = lax.dynamic_index_in_dim(all_token_src, index, 0, keepdims=False)
         weights = lax.dynamic_index_in_dim(all_weights, index, 0, keepdims=False)
-        mixed, pre_gate, pre_up = forward_work(tokens, table4, weights, live)
+        mixed, pre_gate, pre_up = forward_work(tokens, token_src, weights, live)
         outputs = lax.dynamic_update_index_in_dim(outputs, mixed, slot, 0)
         kept_x = lax.dynamic_update_index_in_dim(kept_x, tokens, slot, 0)
         kept_gate = lax.dynamic_update_index_in_dim(
@@ -161,14 +173,13 @@
     _, outputs, kept_x, kept_gate, kept_up = finished
     down_across = lax.optimization_barrier(jnp.transpose(weight_down))
 
-    def backward_work(tokens, grad_out, table, table4, gate_now, gate_kept, up_kept, live):
+    def backward_work(tokens, grad_out, table, pair_src, gate_now, gate_kept, up_kept, live):
         values, scale, normed = normalize(tokens, gain_row)
         scaled = (gate_now[..., None] * grad_out.astype(jnp.float32)[:, None, :]).astype(
             jnp.bfloat16
         )
-        grad_send = jnp.einsum(
-            "ktec,tkd->ecd", table4, scaled, preferred_element_type=jnp.float32
-        ).astype(jnp.bfloat16)
+        pairs = jnp.swapaxes(scaled, 0, 1).reshape(top * tok, width)
+        grad_send = jnp.take(pairs, pair_src, axis=0, mode="fill", fill_value=0)
 
         def backward_active(operands):
             rows_grad, gate_pre, up_pre = operands
@@ -218,12 +229,12 @@
         grad_out = jnp.where(section == sections - 1, fresh, incoming)
         tokens = lax.dynamic_index_in_dim(kept_x, index, 0, keepdims=False)
         table = lax.dynamic_index_in_dim(all_tables, index, 0, keepdims=False)
-        table4 = lax.dynamic_index_in_dim(all_tables4, index, 0, keepdims=False)
+        pair_src = lax.dynamic_index_in_dim(all_pair_src, index, 0, keepdims=False)
         gate_now = lax.dynamic_index_in_dim(gates, index, 0, keepdims=False)
         gate_kept = lax.dynamic_index_in_dim(kept_gate, index, 0, keepdims=False)
         up_kept = lax.dynamic_index_in_dim(kept_up, index, 0, keepdims=False)
         result = backward_work(
-            tokens, grad_out, table, table4, gate_now, gate_kept, up_kept, live
+            tokens, grad_out, table, pair_src, gate_now, gate_kept, up_kept, live
         )
         results = lax.dynamic_update_index_in_dim(results, result, slot, 0)
         incoming = passed_along(result, "section", -1)

time: 1130 us -> 1150 us (1.018)
  other arithmetic: 35.9 us -> 79.7 us
  matrix products: 110 us -> 94.8 us
    select_n x0 -> x44, other arithmetic: none -> 32.9 us  [the longest x22 19.9 us: forward_work(): send = jnp.take(normed, token_src, axis=0, mode='fill', fill_value=0)]
    convert_element_type x22 -> x0, local copies, waits for them, and re-layouts: 26.9 us -> none  [the longest x11 13.7 us: backward_work(): grad_send = jnp.einsum('ktec,tkd->ecd', table4, scaled, preferred_element...]
    gather x0 -> x44, local copies, waits for them, and re-layouts: none -> 23.4 us  [the longest x22 11.7 us: backward_work(): grad_send = jnp.take(pairs, pair_src, axis=0, mode='fill', fill_value=0)]
    dot_general x22 -> x2, matrix products: 16 us -> 0.67 us  [the longest x1 0.34 us: local(): jnp.einsum('mktec,kt->mec', all_tables4.astype(jnp.float32), pair_ids)]
where the time goes in v8:
time: 1150 us
  waiting for transfers between devices  475 us (41%)
  starting transfers between devices  230 us (20%)
  blocking collectives  134 us (12%)
  local copies, waits for them, and re-layouts  115 us (10%)
  matrix products  94.8 us (8%)
  other arithmetic  79.7 us (7%)
  loops' own time  16.5 us (1%)
    ppermute x22, waiting for transfers between devices, passed_along(): lax.ppermute(value, axis, [(source, source + steps) for source in range(l...  172 us
    all_to_all x11, blocking collectives, return_rows(): lax.all_to_all(rows, 'expert', split_axis=0, concat_axis=0, tiled=True)  134 us
    ppermute x22, starting transfers between devices, passed_along(): lax.ppermute(value, axis, [(source, source + steps) for source in range(l...  107 us
    all_to_all x11, waiting for transfers between devices, forward_work(): lax.all_to_all(send, 'expert', split_axis=0, concat_axis=0, tiled=True)  106 us
    all_to_all x11, waiting for transfers between devices, backward_work(): lax.all_to_all(grad_send, 'expert', split_axis=0, concat_axis=0, tiled=True)  98.4 us
    all_to_all x11, waiting for transfers between devices, return_rows(): lax.all_to_all(rows, 'expert', split_axis=0, concat_axis=0, tiled=True)  98.1 us
    all_to_all x11, starting transfers between devices, forward_work(): lax.all_to_all(send, 'expert', split_axis=0, concat_axis=0, tiled=True)  44.3 us
    all_to_all x11, starting transfers between devices, backward_work(): lax.all_to_all(grad_send, 'expert', split_axis=0, concat_axis=0, tiled=True)  39.3 us
  transfers between devices with their start and end apart: 55, of which 55 were waited for; matrix products, arithmetic and copies ran while one was open for 1% of the time, Pallas kernels for 0%

profile of v8, /device:TPU:1, one launch (start us, length us, event | category | flops | bytes accessed | tf_op | source)
XLA Modules:
  0.0 1145.4 jit_solution(6379811127521921847)
XLA Ops:
  10.5 544.2 %while.33 = (s32[]{:T(128)}, bf16[32,4096]{1,0:T(8,128)(2,1)S(1)}, bf16[5,32,4096]{2,1,0:T(8,128)(2,1)}, bf16[5,32,4096]{2,1,0:T(8,128)(2,1)S(1)}, f32[5,64,768]...) while((s32[]{:T(128)}, bf16[32,4096]{1,0:T(8,128)(2,1)S(1)}, ...), condition=%wide.region_7.8_spmd, body=%wide.region_3.7_spmd.sunk | while | flops 1310885504 | bytes 86023696 | solution.py:172
  17.7 8.6 all-to-all-start
  26.3 10.4 all-to-all-done
  37.3 12.3 %all_to_all.30 = bf16[16,4,4096]{2,1,0:T(4,128)(2,1)S(1)} all-to-all(bf16[16,4,4096]{2,1,0:T(4,128)(2,1)S(1)} %copy.84), channel_id=1, replica_groups=mesh['section'=8,'expert'=16] {'expert'}, dimensions={0} | all-to-all | bytes 1048576 | tf_op jit(solution)/shard_map/while/body/eval_jaxpr/all_to_all | solution.py:73
  76.3 11.1 all-to-all-done
  87.5 9.0 conditional.4
  96.9 13.6 %all_to_all.30 = bf16[16,4,4096]{2,1,0:T(4,128)(2,1)S(1)} all-to-all(bf16[16,4,4096]{2,1,0:T(4,128)(2,1)S(1)} %copy.84), channel_id=1, replica_groups=mesh['section'=8,'expert'=16] {'expert'}, dimensions={0} | all-to-all | bytes 1048576 | tf_op jit(solution)/shard_map/while/body/eval_jaxpr/all_to_all | solution.py:73
  128.4 11.4 all-to-all-done
  139.8 9.0 conditional.4
  149.3 13.3 %all_to_all.30 = bf16[16,4,4096]{2,1,0:T(4,128)(2,1)S(1)} all-to-all(bf16[16,4,4096]{2,1,0:T(4,128)(2,1)S(1)} %copy.84), channel_id=1, replica_groups=mesh['section'=8,'expert'=16] {'expert'}, dimensions={0} | all-to-all | bytes 1048576 | tf_op jit(solution)/shard_map/while/body/eval_jaxpr/all_to_all | solution.py:73
  182.9 9.1 all-to-all-done
  192.0 9.0 conditional.4
  201.5 13.2 %all_to_all.30 = bf16[16,4,4096]{2,1,0:T(4,128)(2,1)S(1)} all-to-all(bf16[16,4,4096]{2,1,0:T(4,128)(2,1)S(1)} %copy.84), channel_id=1, replica_groups=mesh['section'=8,'expert'=16] {'expert'}, dimensions={0} | all-to-all | bytes 1048576 | tf_op jit(solution)/shard_map/while/body/eval_jaxpr/all_to_all | solution.py:73
  236.0 8.9 all-to-all-done
  244.9 9.0 conditional.4
  254.4 11.6 %all_to_all.30 = bf16[16,4,4096]{2,1,0:T(4,128)(2,1)S(1)} all-to-all(bf16[16,4,4096]{2,1,0:T(4,128)(2,1)S(1)} %copy.84), channel_id=1, replica_groups=mesh['section'=8,'expert'=16] {'expert'}, dimensions={0} | all-to-all | bytes 1048576 | tf_op jit(solution)/shard_map/while/body/eval_jaxpr/all_to_all | solution.py:73
  289.1 8.9 all-to-all-done
  298.5 11.6 %all_to_all.30 = bf16[16,4,4096]{2,1,0:T(4,128)(2,1)S(1)} all-to-all(bf16[16,4,4096]{2,1,0:T(4,128)(2,1)S(1)} %copy.84), channel_id=1, replica_groups=mesh['section'=8,'expert'=16] {'expert'}, dimensions={0} | all-to-all | bytes 1048576 | tf_op jit(solution)/shard_map/while/body/eval_jaxpr/all_to_all | solution.py:73
  312.1 15.9 %collective-permute-start = (bf16[32,4096]{1,0:T(8,128)(2,1)S(1)}, bf16[32,4096]{1,0:T(8,128)(2,1)S(1)}, u32[]{:S(2)}, u32[]{:S(2)}) collective-permute-start(bf16[32,4096]{1,0:T(8,128)(2,1)S(1)} %get-tuple-element.781), channel_id=1, source_target_pairs={{0,16},{16,32},{32,48},{48,64},{64,80},{80,96},{96,112},{1,17},{17... | collective-permute-start | bytes 786440 | tf_op jit(solution)/shard_map/while/body/eval_jaxpr/ppermute | solution.py:12
  342.1 10.1 all-to-all-done
  352.8 11.7 %all_to_all.30 = bf16[16,4,4096]{2,1,0:T(4,128)(2,1)S(1)} all-to-all(bf16[16,4,4096]{2,1,0:T(4,128)(2,1)S(1)} %copy.84), channel_id=1, replica_groups=mesh['section'=8,'expert'=16] {'expert'}, dimensions={0} | all-to-all | bytes 1048576 | tf_op jit(solution)/shard_map/while/body/eval_jaxpr/all_to_all | solution.py:73
  387.2 8.9 all-to-all-done
  396.7 11.6 %all_to_all.30 = bf16[16,4,4096]{2,1,0:T(4,128)(2,1)S(1)} all-to-all(bf16[16,4,4096]{2,1,0:T(4,128)(2,1)S(1)} %copy.84), channel_id=1, replica_groups=mesh['section'=8,'expert'=16] {'expert'}, dimensions={0} | all-to-all | bytes 1048576 | tf_op jit(solution)/shard_map/while/body/eval_jaxpr/all_to_all | solution.py:73
  432.6 8.9 all-to-all-done
  442.1 11.6 %all_to_all.30 = bf16[16,4,4096]{2,1,0:T(4,128)(2,1)S(1)} all-to-all(bf16[16,4,4096]{2,1,0:T(4,128)(2,1)S(1)} %copy.84), channel_id=1, replica_groups=mesh['section'=8,'expert'=16] {'expert'}, dimensions={0} | all-to-all | bytes 1048576 | tf_op jit(solution)/shard_map/while/body/eval_jaxpr/all_to_all | solution.py:73
  476.9 8.9 all-to-all-done
  486.3 11.6 %all_to_all.30 = bf16[16,4,4096]{2,1,0:T(4,128)(2,1)S(1)} all-to-all(bf16[16,4,4096]{2,1,0:T(4,128)(2,1)S(1)} %copy.84), channel_id=1, replica_groups=mesh['section'=8,'expert'=16] {'expert'}, dimensions={0} | all-to-all | bytes 1048576 | tf_op jit(solution)/shard_map/while/body/eval_jaxpr/all_to_all | solution.py:73
  521.0 8.9 all-to-all-done
  530.4 11.6 %all_to_all.30 = bf16[16,4,4096]{2,1,0:T(4,128)(2,1)S(1)} all-to-all(bf16[16,4,4096]{2,1,0:T(4,128)(2,1)S(1)} %copy.84), channel_id=1, replica_groups=mesh['section'=8,'expert'=16] {'expert'}, dimensions={0} | all-to-all | bytes 1048576 | tf_op jit(solution)/shard_map/while/body/eval_jaxpr/all_to_all | solution.py:73
  554.7 8.6 copy.60
  564.6 577.7 %while.34 = (s32[]{:T(128)}, bf16[32,4096]{1,0:T(8,128)(2,1)S(1)}, bf16[5,32,4096]{2,1,0:T(8,128)(2,1)}, pred[]{:T(512)}, s32[11]{0:T(128)S(1)}, /*index=5*/s32[...) while((s32[]{:T(128)}, bf16[32,4096]{1,0:T(8,128)(2,1)S(1)}, ...), condition=%wide.region_14.15_spmd, body=%wide.region_8.14_spmd.sunk | while | flops 1228807808 | bytes 89304112 | solution.py:243
  574.0 8.9 all-to-all-done.2
  587.6 8.9 all-to-all-done.3
  599.8 10.1 collective-permute-done.1
  619.1 8.9 all-to-all-done.2
  632.7 8.9 all-to-all-done.3
  644.9 8.4 collective-permute-done.1
  662.5 8.9 all-to-all-done.2
  676.1 8.9 all-to-all-done.3
  688.3 8.8 collective-permute-done.1
  706.3 8.9 all-to-all-done.2
  719.9 8.9 all-to-all-done.3
  732.1 8.7 collective-permute-done.1
  750.0 8.9 all-to-all-done.2
  763.6 8.9 all-to-all-done.3
  775.8 8.8 collective-permute-done.1
  793.8 8.9 all-to-all-done.2
  807.4 8.9 all-to-all-done.3
  819.6 66.3 %collective-permute-done.1 = bf16[32,4096]{1,0:T(8,128)(2,1)S(1)} collective-permute-done((bf16[32,4096]{1,0:T(8,128)(2,1)S(1)}, bf16[32,4096]{1,0:T(8,128)(2,1)S(1)}, u32[]{:S(2)}, u32[]{:S(2)}) %collective-permute-start.1) | collective-permute-done | bytes 262176 | tf_op jit(solution)/shard_map/while/body/eval_jaxpr/ppermute | solution.py:12
  895.2 8.9 all-to-all-done.2
  904.1 11.9 %conditional.5 = (bf16[16,4,4096]{2,1,0:T(4,128)(2,1)}) conditional(s32[]{:T(128)} %convert_element_type.152, () %tuple.104, (bf16[16,4,4096]{2,1,0:T(4,128)(2,1)S(1)}, bf16[4096,768]{1,0:T(8,128)(2,1)}, f32[5,64,768]{2,1,0:T(8,128)}, s32[]{:T(128)}, f32[5,64,768]{2,1,0:T(8,128)}, /*index=5*/bf16[4096,768]{1,0:T(8,128)(2,1)}, ...), branch_computations={%region_11.11_spmd, %region_12.12_spmd} | conditional | flops 1209270272 | bytes 75629632 | solution.py:202
  919.6 8.9 all-to-all-done.3
  947.9 8.9 all-to-all-done.2
  956.8 11.9 %conditional.5 = (bf16[16,4,4096]{2,1,0:T(4,128)(2,1)}) conditional(s32[]{:T(128)} %convert_element_type.152, () %tuple.104, (bf16[16,4,4096]{2,1,0:T(4,128)(2,1)S(1)}, bf16[4096,768]{1,0:T(8,128)(2,1)}, f32[5,64,768]{2,1,0:T(8,128)}, s32[]{:T(128)}, f32[5,64,768]{2,1,0:T(8,128)}, /*index=5*/bf16[4096,768]{1,0:T(8,128)(2,1)}, ...), branch_computations={%region_11.11_spmd, %region_12.12_spmd} | conditional | flops 1209270272 | bytes 75629632 | solution.py:202
  972.3 8.9 all-to-all-done.3
  1001.9 8.9 all-to-all-done.2
  1010.8 11.9 %conditional.5 = (bf16[16,4,4096]{2,1,0:T(4,128)(2,1)}) conditional(s32[]{:T(128)} %convert_element_type.152, () %tuple.104, (bf16[16,4,4096]{2,1,0:T(4,128)(2,1)S(1)}, bf16[4096,768]{1,0:T(8,128)(2,1)}, f32[5,64,768]{2,1,0:T(8,128)}, s32[]{:T(128)}, f32[5,64,768]{2,1,0:T(8,128)}, /*index=5*/bf16[4096,768]{1,0:T(8,128)(2,1)}, ...), branch_computations={%region_11.11_spmd, %region_12.12_spmd} | conditional | flops 1209270272 | bytes 75629632 | solution.py:202
  1026.3 8.9 all-to-all-done.3
  1054.8 8.9 all-to-all-done.2
  1063.8 11.9 %conditional.5 = (bf16[16,4,4096]{2,1,0:T(4,128)(2,1)}) conditional(s32[]{:T(128)} %convert_element_type.152, () %tuple.104, (bf16[16,4,4096]{2,1,0:T(4,128)(2,1)S(1)}, bf16[4096,768]{1,0:T(8,128)(2,1)}, f32[5,64,768]{2,1,0:T(8,128)}, s32[]{:T(128)}, f32[5,64,768]{2,1,0:T(8,128)}, /*index=5*/bf16[4096,768]{1,0:T(8,128)(2,1)}, ...), branch_computations={%region_11.11_spmd, %region_12.12_spmd} | conditional | flops 1209270272 | bytes 75629632 | solution.py:202
  1079.3 8.9 all-to-all-done.3
  1106.5 8.9 all-to-all-done.2
  1120.1 8.9 all-to-all-done.3
  1130.3 10.8 collective-permute-start.1
  (630 shorter events, 544.9 us)
Async XLA Ops:
  17.7 19.0 %all-to-all-start = ((bf16[16,4,4096]{2,1,0:T(4,128)(2,1)}), bf16[16,4,4096]{2,1,0:T(4,128)(2,1)S(1)}, u32[]{:S(2)}, u32[]{:S(2)}) async-start(bf16[16,4,4096]{2,1,0:T(4,128)(2,1)} %broadcast_select_fusion.4), calls=%async_computation | async-start | bytes 1048576 | tf_op jit(solution)/shard_map/while/body/eval_jaxpr/all_to_all | solution.py:134
  51.5 14.1 %collective-permute-start = (bf16[32,4096]{1,0:T(8,128)(2,1)S(1)}, bf16[32,4096]{1,0:T(8,128)(2,1)S(1)}, u32[]{:S(2)}, u32[]{:S(2)}) collective-permute-start(bf16[32,4096]{1,0:T(8,128)(2,1)S(1)} %get-tuple-element.781), channel_id=1, source_target_pairs={{0,16},{16,32},{32,48},{48,64},{64,80},{80,96},{96,112},{1,17},{17... | collective-permute-start | bytes 786440 | tf_op jit(solution)/shard_map/while/body/eval_jaxpr/ppermute | solution.py:12
  72.8 14.7 %all-to-all-start = ((bf16[16,4,4096]{2,1,0:T(4,128)(2,1)}), bf16[16,4,4096]{2,1,0:T(4,128)(2,1)S(1)}, u32[]{:S(2)}, u32[]{:S(2)}) async-start(bf16[16,4,4096]{2,1,0:T(4,128)(2,1)} %broadcast_select_fusion.4), calls=%async_computation | async-start | bytes 1048576 | tf_op jit(solution)/shard_map/while/body/eval_jaxpr/all_to_all | solution.py:134
  87.5 4.6 copy-start
  112.4 5.2 collective-permute-start
  124.8 15.0 %all-to-all-start = ((bf16[16,4,4096]{2,1,0:T(4,128)(2,1)}), bf16[16,4,4096]{2,1,0:T(4,128)(2,1)S(1)}, u32[]{:S(2)}, u32[]{:S(2)}) async-start(bf16[16,4,4096]{2,1,0:T(4,128)(2,1)} %broadcast_select_fusion.4), calls=%async_computation | async-start | bytes 1048576 | tf_op jit(solution)/shard_map/while/body/eval_jaxpr/all_to_all | solution.py:134
  139.8 4.6 copy-start
  164.5 7.7 collective-permute-start
  179.4 12.6 %all-to-all-start = ((bf16[16,4,4096]{2,1,0:T(4,128)(2,1)}), bf16[16,4,4096]{2,1,0:T(4,128)(2,1)S(1)}, u32[]{:S(2)}, u32[]{:S(2)}) async-start(bf16[16,4,4096]{2,1,0:T(4,128)(2,1)} %broadcast_select_fusion.4), calls=%async_computation | async-start | bytes 1048576 | tf_op jit(solution)/shard_map/while/body/eval_jaxpr/all_to_all | solution.py:134
  192.0 4.6 copy-start
  216.6 8.6 collective-permute-start
  232.4 12.5 %all-to-all-start = ((bf16[16,4,4096]{2,1,0:T(4,128)(2,1)}), bf16[16,4,4096]{2,1,0:T(4,128)(2,1)S(1)}, u32[]{:S(2)}, u32[]{:S(2)}) async-start(bf16[16,4,4096]{2,1,0:T(4,128)(2,1)} %broadcast_select_fusion.4), calls=%async_computation | async-start | bytes 1048576 | tf_op jit(solution)/shard_map/while/body/eval_jaxpr/all_to_all | solution.py:134
  244.9 4.6 copy-start
  268.0 10.3 collective-permute-start
  285.5 12.5 %all-to-all-start = ((bf16[16,4,4096]{2,1,0:T(4,128)(2,1)}), bf16[16,4,4096]{2,1,0:T(4,128)(2,1)S(1)}, u32[]{:S(2)}, u32[]{:S(2)}) async-start(bf16[16,4,4096]{2,1,0:T(4,128)(2,1)} %broadcast_select_fusion.4), calls=%async_computation | async-start | bytes 1048576 | tf_op jit(solution)/shard_map/while/body/eval_jaxpr/all_to_all | solution.py:134
  312.1 19.2 %collective-permute-start = (bf16[32,4096]{1,0:T(8,128)(2,1)S(1)}, bf16[32,4096]{1,0:T(8,128)(2,1)S(1)}, u32[]{:S(2)}, u32[]{:S(2)}) collective-permute-start(bf16[32,4096]{1,0:T(8,128)(2,1)S(1)} %get-tuple-element.781), channel_id=1, source_target_pairs={{0,16},{16,32},{32,48},{48,64},{64,80},{80,96},{96,112},{1,17},{17... | collective-permute-start | bytes 786440 | tf_op jit(solution)/shard_map/while/body/eval_jaxpr/ppermute | solution.py:12
  338.5 13.7 %all-to-all-start = ((bf16[16,4,4096]{2,1,0:T(4,128)(2,1)}), bf16[16,4,4096]{2,1,0:T(4,128)(2,1)S(1)}, u32[]{:S(2)}, u32[]{:S(2)}) async-start(bf16[16,4,4096]{2,1,0:T(4,128)(2,1)} %broadcast_select_fusion.4), calls=%async_computation | async-start | bytes 1048576 | tf_op jit(solution)/shard_map/while/body/eval_jaxpr/all_to_all | solution.py:134
  366.3 10.1 collective-permute-start
  383.6 12.5 %all-to-all-start = ((bf16[16,4,4096]{2,1,0:T(4,128)(2,1)}), bf16[16,4,4096]{2,1,0:T(4,128)(2,1)S(1)}, u32[]{:S(2)}, u32[]{:S(2)}) async-start(bf16[16,4,4096]{2,1,0:T(4,128)(2,1)} %broadcast_select_fusion.4), calls=%async_computation | async-start | bytes 1048576 | tf_op jit(solution)/shard_map/while/body/eval_jaxpr/all_to_all | solution.py:134
  410.2 11.6 %collective-permute-start = (bf16[32,4096]{1,0:T(8,128)(2,1)S(1)}, bf16[32,4096]{1,0:T(8,128)(2,1)S(1)}, u32[]{:S(2)}, u32[]{:S(2)}) collective-permute-start(bf16[32,4096]{1,0:T(8,128)(2,1)S(1)} %get-tuple-element.781), channel_id=1, source_target_pairs={{0,16},{16,32},{32,48},{48,64},{64,80},{80,96},{96,112},{1,17},{17... | collective-permute-start | bytes 786440 | tf_op jit(solution)/shard_map/while/body/eval_jaxpr/ppermute | solution.py:12
  429.0 12.5 %all-to-all-start = ((bf16[16,4,4096]{2,1,0:T(4,128)(2,1)}), bf16[16,4,4096]{2,1,0:T(4,128)(2,1)S(1)}, u32[]{:S(2)}, u32[]{:S(2)}) async-start(bf16[16,4,4096]{2,1,0:T(4,128)(2,1)} %broadcast_select_fusion.4), calls=%async_computation | async-start | bytes 1048576 | tf_op jit(solution)/shard_map/while/body/eval_jaxpr/all_to_all | solution.py:134
  455.7 10.4 collective-permute-start
  473.3 12.5 %all-to-all-start = ((bf16[16,4,4096]{2,1,0:T(4,128)(2,1)}), bf16[16,4,4096]{2,1,0:T(4,128)(2,1)S(1)}, u32[]{:S(2)}, u32[]{:S(2)}) async-start(bf16[16,4,4096]{2,1,0:T(4,128)(2,1)} %broadcast_select_fusion.4), calls=%async_computation | async-start | bytes 1048576 | tf_op jit(solution)/shard_map/while/body/eval_jaxpr/all_to_all | solution.py:134
  499.9 10.3 collective-permute-start
  517.4 12.5 %all-to-all-start = ((bf16[16,4,4096]{2,1,0:T(4,128)(2,1)}), bf16[16,4,4096]{2,1,0:T(4,128)(2,1)S(1)}, u32[]{:S(2)}, u32[]{:S(2)}) async-start(bf16[16,4,4096]{2,1,0:T(4,128)(2,1)} %broadcast_select_fusion.4), calls=%async_computation | async-start | bytes 1048576 | tf_op jit(solution)/shard_map/while/body/eval_jaxpr/all_to_all | solution.py:134
  544.0 10.7 collective-permute-start
  570.4 12.5 %all-to-all-start.2 = ((bf16[16,4,4096]{2,1,0:T(4,128)(2,1)}), bf16[16,4,4096]{2,1,0:T(4,128)(2,1)S(1)}, u32[]{:S(2)}, u32[]{:S(2)}) async-start(bf16[16,4,4096]{2,1,0:T(4,128)(2,1)} %broadcast_select_fusion.5), calls=%async_computation.2 | async-start | bytes 1048576 | tf_op jit(solution)/shard_map/while/body/eval_jaxpr/all_to_all | solution.py:207
  584.0 12.5 %all-to-all-start.3 = ((bf16[16,4,4096]{2,1,0:T(4,128)(2,1)}), bf16[16,4,4096]{2,1,0:T(4,128)(2,1)S(1)}, u32[]{:S(2)}, u32[]{:S(2)}) async-start(bf16[16,4,4096]{2,1,0:T(4,128)(2,1)} %get-tuple-element.948), calls=%async_computation.3 | async-start | bytes 1048576 | tf_op jit(solution)/shard_map/while/body/eval_jaxpr/all_to_all | solution.py:73
  597.9 12.0 %collective-permute-start.1 = (bf16[32,4096]{1,0:T(8,128)(2,1)S(1)}, bf16[32,4096]{1,0:T(8,128)(2,1)S(1)}, u32[]{:S(2)}, u32[]{:S(2)}) collective-permute-start(bf16[32,4096]{1,0:T(8,128)(2,1)S(1)} %get-tuple-element.811), channel_id=1, source_target_pairs={{16,0},{32,16},{48,32},{64,48},{80,64},{96,80},{112,96},{17,1},{33... | collective-permute-start | bytes 786440 | tf_op jit(solution)/shard_map/while/body/eval_jaxpr/ppermute | solution.py:12
  615.5 12.5 %all-to-all-start.2 = ((bf16[16,4,4096]{2,1,0:T(4,128)(2,1)}), bf16[16,4,4096]{2,1,0:T(4,128)(2,1)S(1)}, u32[]{:S(2)}, u32[]{:S(2)}) async-start(bf16[16,4,4096]{2,1,0:T(4,128)(2,1)} %broadcast_select_fusion.5), calls=%async_computation.2 | async-start | bytes 1048576 | tf_op jit(solution)/shard_map/while/body/eval_jaxpr/all_to_all | solution.py:207
  629.1 12.5 %all-to-all-start.3 = ((bf16[16,4,4096]{2,1,0:T(4,128)(2,1)}), bf16[16,4,4096]{2,1,0:T(4,128)(2,1)S(1)}, u32[]{:S(2)}, u32[]{:S(2)}) async-start(bf16[16,4,4096]{2,1,0:T(4,128)(2,1)} %get-tuple-element.948), calls=%async_computation.3 | async-start | bytes 1048576 | tf_op jit(solution)/shard_map/while/body/eval_jaxpr/all_to_all | solution.py:73
  643.0 10.3 collective-permute-start.1
  658.9 12.5 %all-to-all-start.2 = ((bf16[16,4,4096]{2,1,0:T(4,128)(2,1)}), bf16[16,4,4096]{2,1,0:T(4,128)(2,1)S(1)}, u32[]{:S(2)}, u32[]{:S(2)}) async-start(bf16[16,4,4096]{2,1,0:T(4,128)(2,1)} %broadcast_select_fusion.5), calls=%async_computation.2 | async-start | bytes 1048576 | tf_op jit(solution)/shard_map/while/body/eval_jaxpr/all_to_all | solution.py:207
  672.5 12.5 %all-to-all-start.3 = ((bf16[16,4,4096]{2,1,0:T(4,128)(2,1)}), bf16[16,4,4096]{2,1,0:T(4,128)(2,1)S(1)}, u32[]{:S(2)}, u32[]{:S(2)}) async-start(bf16[16,4,4096]{2,1,0:T(4,128)(2,1)} %get-tuple-element.948), calls=%async_computation.3 | async-start | bytes 1048576 | tf_op jit(solution)/shard_map/while/body/eval_jaxpr/all_to_all | solution.py:73
  686.4 10.7 collective-permute-start.1
  702.7 12.5 %all-to-all-start.2 = ((bf16[16,4,4096]{2,1,0:T(4,128)(2,1)}), bf16[16,4,4096]{2,1,0:T(4,128)(2,1)S(1)}, u32[]{:S(2)}, u32[]{:S(2)}) async-start(bf16[16,4,4096]{2,1,0:T(4,128)(2,1)} %broadcast_select_fusion.5), calls=%async_computation.2 | async-start | bytes 1048576 | tf_op jit(solution)/shard_map/while/body/eval_jaxpr/all_to_all | solution.py:207
  716.3 12.5 %all-to-all-start.3 = ((bf16[16,4,4096]{2,1,0:T(4,128)(2,1)}), bf16[16,4,4096]{2,1,0:T(4,128)(2,1)S(1)}, u32[]{:S(2)}, u32[]{:S(2)}) async-start(bf16[16,4,4096]{2,1,0:T(4,128)(2,1)} %get-tuple-element.948), calls=%async_computation.3 | async-start | bytes 1048576 | tf_op jit(solution)/shard_map/while/body/eval_jaxpr/all_to_all | solution.py:73
  730.2 10.6 collective-permute-start.1
  746.4 12.5 %all-to-all-start.2 = ((bf16[16,4,4096]{2,1,0:T(4,128)(2,1)}), bf16[16,4,4096]{2,1,0:T(4,128)(2,1)S(1)}, u32[]{:S(2)}, u32[]{:S(2)}) async-start(bf16[16,4,4096]{2,1,0:T(4,128)(2,1)} %broadcast_select_fusion.5), calls=%async_computation.2 | async-start | bytes 1048576 | tf_op jit(solution)/shard_map/while/body/eval_jaxpr/all_to_all | solution.py:207
  760.0 12.5 %all-to-all-start.3 = ((bf16[16,4,4096]{2,1,0:T(4,128)(2,1)}), bf16[16,4,4096]{2,1,0:T(4,128)(2,1)S(1)}, u32[]{:S(2)}, u32[]{:S(2)}) async-start(bf16[16,4,4096]{2,1,0:T(4,128)(2,1)} %get-tuple-element.948), calls=%async_computation.3 | async-start | bytes 1048576 | tf_op jit(solution)/shard_map/while/body/eval_jaxpr/all_to_all | solution.py:73
  773.9 10.7 collective-permute-start.1
  790.2 12.5 %all-to-all-start.2 = ((bf16[16,4,4096]{2,1,0:T(4,128)(2,1)}), bf16[16,4,4096]{2,1,0:T(4,128)(2,1)S(1)}, u32[]{:S(2)}, u32[]{:S(2)}) async-start(bf16[16,4,4096]{2,1,0:T(4,128)(2,1)} %broadcast_select_fusion.5), calls=%async_computation.2 | async-start | bytes 1048576 | tf_op jit(solution)/shard_map/while/body/eval_jaxpr/all_to_all | solution.py:207
  803.8 12.5 %all-to-all-start.3 = ((bf16[16,4,4096]{2,1,0:T(4,128)(2,1)}), bf16[16,4,4096]{2,1,0:T(4,128)(2,1)S(1)}, u32[]{:S(2)}, u32[]{:S(2)}) async-start(bf16[16,4,4096]{2,1,0:T(4,128)(2,1)} %get-tuple-element.948), calls=%async_computation.3 | async-start | bytes 1048576 | tf_op jit(solution)/shard_map/while/body/eval_jaxpr/all_to_all | solution.py:73
  817.7 68.2 %collective-permute-start.1 = (bf16[32,4096]{1,0:T(8,128)(2,1)S(1)}, bf16[32,4096]{1,0:T(8,128)(2,1)S(1)}, u32[]{:S(2)}, u32[]{:S(2)}) collective-permute-start(bf16[32,4096]{1,0:T(8,128)(2,1)S(1)} %get-tuple-element.811), channel_id=1, source_target_pairs={{16,0},{32,16},{48,32},{64,48},{80,64},{96,80},{112,96},{17,1},{33... | collective-permute-start | bytes 786440 | tf_op jit(solution)/shard_map/while/body/eval_jaxpr/ppermute | solution.py:12
  891.6 12.5 %all-to-all-start.2 = ((bf16[16,4,4096]{2,1,0:T(4,128)(2,1)}), bf16[16,4,4096]{2,1,0:T(4,128)(2,1)S(1)}, u32[]{:S(2)}, u32[]{:S(2)}) async-start(bf16[16,4,4096]{2,1,0:T(4,128)(2,1)} %broadcast_select_fusion.5), calls=%async_computation.2 | async-start | bytes 1048576 | tf_op jit(solution)/shard_map/while/body/eval_jaxpr/all_to_all | solution.py:207
  904.2 4.6 copy-start.1
  916.0 12.5 %all-to-all-start.3 = ((bf16[16,4,4096]{2,1,0:T(4,128)(2,1)}), bf16[16,4,4096]{2,1,0:T(4,128)(2,1)S(1)}, u32[]{:S(2)}, u32[]{:S(2)}) async-start(bf16[16,4,4096]{2,1,0:T(4,128)(2,1)} %get-tuple-element.948), calls=%async_computation.3 | async-start | bytes 1048576 | tf_op jit(solution)/shard_map/while/body/eval_jaxpr/all_to_all | solution.py:73
  929.9 8.8 collective-permute-start.1
  944.3 12.5 %all-to-all-start.2 = ((bf16[16,4,4096]{2,1,0:T(4,128)(2,1)}), bf16[16,4,4096]{2,1,0:T(4,128)(2,1)S(1)}, u32[]{:S(2)}, u32[]{:S(2)}) async-start(bf16[16,4,4096]{2,1,0:T(4,128)(2,1)} %broadcast_select_fusion.5), calls=%async_computation.2 | async-start | bytes 1048576 | tf_op jit(solution)/shard_map/while/body/eval_jaxpr/all_to_all | solution.py:207
  957.0 4.6 copy-start.1
  961.6 3.2 copy-start.2
  968.7 12.5 %all-to-all-start.3 = ((bf16[16,4,4096]{2,1,0:T(4,128)(2,1)}), bf16[16,4,4096]{2,1,0:T(4,128)(2,1)S(1)}, u32[]{:S(2)}, u32[]{:S(2)}) async-start(bf16[16,4,4096]{2,1,0:T(4,128)(2,1)} %get-tuple-element.948), calls=%async_computation.3 | async-start | bytes 1048576 | tf_op jit(solution)/shard_map/while/body/eval_jaxpr/all_to_all | solution.py:73
  982.6 10.0 collective-permute-start.1
  998.3 12.5 %all-to-all-start.2 = ((bf16[16,4,4096]{2,1,0:T(4,128)(2,1)}), bf16[16,4,4096]{2,1,0:T(4,128)(2,1)S(1)}, u32[]{:S(2)}, u32[]{:S(2)}) async-start(bf16[16,4,4096]{2,1,0:T(4,128)(2,1)} %broadcast_select_fusion.5), calls=%async_computation.2 | async-start | bytes 1048576 | tf_op jit(solution)/shard_map/while/body/eval_jaxpr/all_to_all | solution.py:207
  1010.9 4.6 copy-start.1
  1022.7 12.5 %all-to-all-start.3 = ((bf16[16,4,4096]{2,1,0:T(4,128)(2,1)}), bf16[16,4,4096]{2,1,0:T(4,128)(2,1)S(1)}, u32[]{:S(2)}, u32[]{:S(2)}) async-start(bf16[16,4,4096]{2,1,0:T(4,128)(2,1)} %get-tuple-element.948), calls=%async_computation.3 | async-start | bytes 1048576 | tf_op jit(solution)/shard_map/while/body/eval_jaxpr/all_to_all | solution.py:73
  1036.6 9.0 collective-permute-start.1
  1051.2 12.5 %all-to-all-start.2 = ((bf16[16,4,4096]{2,1,0:T(4,128)(2,1)}), bf16[16,4,4096]{2,1,0:T(4,128)(2,1)S(1)}, u32[]{:S(2)}, u32[]{:S(2)}) async-start(bf16[16,4,4096]{2,1,0:T(4,128)(2,1)} %broadcast_select_fusion.5), calls=%async_computation.2 | async-start | bytes 1048576 | tf_op jit(solution)/shard_map/while/body/eval_jaxpr/all_to_all | solution.py:207
  1063.9 4.6 copy-start.1
  1075.7 12.5 %all-to-all-start.3 = ((bf16[16,4,4096]{2,1,0:T(4,128)(2,1)}), bf16[16,4,4096]{2,1,0:T(4,128)(2,1)S(1)}, u32[]{:S(2)}, u32[]{:S(2)}) async-start(bf16[16,4,4096]{2,1,0:T(4,128)(2,1)} %get-tuple-element.948), calls=%async_computation.3 | async-start | bytes 1048576 | tf_op jit(solution)/shard_map/while/body/eval_jaxpr/all_to_all | solution.py:73
  1089.6 7.7 collective-permute-start.1
  1102.9 12.5 %all-to-all-start.2 = ((bf16[16,4,4096]{2,1,0:T(4,128)(2,1)}), bf16[16,4,4096]{2,1,0:T(4,128)(2,1)S(1)}, u32[]{:S(2)}, u32[]{:S(2)}) async-start(bf16[16,4,4096]{2,1,0:T(4,128)(2,1)} %broadcast_select_fusion.5), calls=%async_computation.2 | async-start | bytes 1048576 | tf_op jit(solution)/shard_map/while/body/eval_jaxpr/all_to_all | solution.py:207
  1116.4 12.5 %all-to-all-start.3 = ((bf16[16,4,4096]{2,1,0:T(4,128)(2,1)}), bf16[16,4,4096]{2,1,0:T(4,128)(2,1)S(1)}, u32[]{:S(2)}, u32[]{:S(2)}) async-start(bf16[16,4,4096]{2,1,0:T(4,128)(2,1)} %get-tuple-element.948), calls=%async_computation.3 | async-start | bytes 1048576 | tf_op jit(solution)/shard_map/while/body/eval_jaxpr/all_to_all | solution.py:73
  1130.3 12.0 %collective-permute-start.1 = (bf16[32,4096]{1,0:T(8,128)(2,1)S(1)}, bf16[32,4096]{1,0:T(8,128)(2,1)S(1)}, u32[]{:S(2)}, u32[]{:S(2)}) collective-permute-start(bf16[32,4096]{1,0:T(8,128)(2,1)S(1)} %get-tuple-element.811), channel_id=1, source_target_pairs={{16,0},{32,16},{48,32},{64,48},{80,64},{96,80},{112,96},{17,1},{33... | collective-permute-start | bytes 786440 | tf_op jit(solution)/shard_map/while/body/eval_jaxpr/ppermute | solution.py:12
  (9 other events, 24.0 us)

commit v9 on v5

--- a/solution.py
+++ b/solution.py
@@ -97,7 +97,7 @@
     )
     all_tables4 = all_tables.reshape(micro, top, tok, experts, capacity)
 
-    def forward_work(tokens, table4, weights, live):
+    def forward_work(tokens, table4, table, gate_now, live):
         values, scale, normed = normalize(tokens, gain_row)
         send = jnp.einsum(
             "ktec,td->ecd", table4, normed, preferred_element_type=jnp.float32
@@ -122,9 +122,8 @@
             lax.all_to_all(send, "expert", split_axis=0, concat_axis=0, tiled=True),
         )
         back = return_rows(output).reshape(total_rows, width)
-        mixed = values + jnp.dot(
-            weights, back.astype(jnp.float32), precision=lax.Precision.HIGHEST
-        )
+        picked = jnp.einsum("ktj,jd->tkd", table, back, preferred_element_type=jnp.float32)
+        mixed = values + jnp.sum(gate_now[..., None] * picked, axis=1)
         return (mixed.astype(jnp.bfloat16), pre_gate, pre_up)
 
     def forward_tick(carry, tick):
@@ -136,8 +135,9 @@
         fresh = lax.dynamic_index_in_dim(inputs, index, 0, keepdims=False)
         tokens = jnp.where(section == 0, fresh, incoming)
         table4 = lax.dynamic_index_in_dim(all_tables4, index, 0, keepdims=False)
-        weights = lax.dynamic_index_in_dim(all_weights, index, 0, keepdims=False)
-        mixed, pre_gate, pre_up = forward_work(tokens, table4, weights, live)
+        table = lax.dynamic_index_in_dim(all_tables, index, 0, keepdims=False)
+        gate_now = lax.dynamic_index_in_dim(gates, index, 0, keepdims=False)
+        mixed, pre_gate, pre_up = forward_work(tokens, table4, table, gate_now, live)
         outputs = lax.dynamic_update_index_in_dim(outputs, mixed, slot, 0)
         kept_x = lax.dynamic_update_index_in_dim(kept_x, tokens, slot, 0)
         kept_gate = lax.dynamic_update_index_in_dim(

time: 1130 us -> 1130 us (level)
  blocking collectives: 134 us -> 0 us
  waiting for transfers between devices: 475 us -> 574 us
  starting transfers between devices: 230 us -> 265 us
  matrix products: 110 us -> 92.1 us
  local copies, waits for them, and re-layouts: 121 us -> 134 us
    all_to_all x11 -> x0, blocking collectives: 134 us -> none  [return_rows(): lax.all_to_all(rows, 'expert', split_axis=0, concat_axis=0, tiled=True)]
    all_to_all x11 -> x22, waiting for transfers between devices: 98.1 us -> 194 us  [return_rows(): lax.all_to_all(rows, 'expert', split_axis=0, concat_axis=0, tiled=True)]
    all_to_all x11 -> x22, starting transfers between devices: 39.3 us -> 78.6 us  [return_rows(): lax.all_to_all(rows, 'expert', split_axis=0, concat_axis=0, tiled=True)]
    dot_general x12 -> x11, matrix products: 21.2 us -> 3.22 us  [forward_work(): jnp.einsum('ktj,jd->tkd', table, back, preferred_element_type=jnp.float32)]
  transfers between devices with their start and end apart: 55 -> 66, of which waited for: 55 -> 66; matrix products, arithmetic and copies ran while one was open for 1% -> 1% of each run, Pallas kernels for 0% -> 0%
where the time goes in v9:
time: 1130 us
  waiting for transfers between devices  574 us (51%)
  starting transfers between devices  265 us (23%)
  local copies, waits for them, and re-layouts  134 us (12%)
  matrix products  92.1 us (8%)
  other arithmetic  44.6 us (4%)
  loops' own time  15.6 us (1%)
    all_to_all x22, waiting for transfers between devices, return_rows(): lax.all_to_all(rows, 'expert', split_axis=0, concat_axis=0, tiled=True)  194 us
    ppermute x22, waiting for transfers between devices, passed_along(): lax.ppermute(value, axis, [(source, source + steps) for source in range(l...  173 us
    all_to_all x11, waiting for transfers between devices, forward_work(): lax.all_to_all(send, 'expert', split_axis=0, concat_axis=0, tiled=True)  108 us
    ppermute x22, starting transfers between devices, passed_along(): lax.ppermute(value, axis, [(source, source + steps) for source in range(l...  103 us
    all_to_all x11, waiting for transfers between devices, backward_work(): lax.all_to_all(grad_send, 'expert', split_axis=0, concat_axis=0, tiled=True)  98.4 us
    all_to_all x22, starting transfers between devices, return_rows(): lax.all_to_all(rows, 'expert', split_axis=0, concat_axis=0, tiled=True)  78.6 us
    all_to_all x11, starting transfers between devices, forward_work(): lax.all_to_all(send, 'expert', split_axis=0, concat_axis=0, tiled=True)  44.3 us
    all_to_all x11, starting transfers between devices, backward_work(): lax.all_to_all(grad_send, 'expert', split_axis=0, concat_axis=0, tiled=True)  39.3 us
  transfers between devices with their start and end apart: 66, of which 66 were waited for; matrix products, arithmetic and copies ran while one was open for 1% of the time, Pallas kernels for 0%

profile of v9, /device:TPU:1, one launch (start us, length us, event | category | flops | bytes accessed | tf_op | source)
XLA Modules:
  0.0 1125.5 jit_solution(10640480765348225651)
XLA Ops:
  7.1 531.1 %while.33 = (s32[]{:T(128)}, bf16[32,4096]{1,0:T(8,128)(2,1)S(1)}, bf16[5,32,4096]{2,1,0:T(8,128)(2,1)}, bf16[5,32,4096]{2,1,0:T(8,128)(2,1)S(1)}, f32[5,64,768]...) while((s32[]{:T(128)}, bf16[32,4096]{1,0:T(8,128)(2,1)S(1)}, ...), condition=%wide.region_8.9_spmd, body=%wide.region_2.8_spmd.sunk | while | flops 1260689408 | bytes 85789224 | solution.py:160
  12.4 8.6 all-to-all-start
  21.0 10.4 all-to-all-done
  37.0 8.3 all-to-all-done.1
  69.8 11.1 all-to-all-done
  80.9 9.0 conditional.4
  95.4 9.7 all-to-all-done.1
  120.4 11.8 %all-to-all-done = bf16[16,4,4096]{2,1,0:T(4,128)(2,1)S(1)} async-done(((bf16[16,4,4096]{2,1,0:T(4,128)(2,1)}), bf16[16,4,4096]{2,1,0:T(4,128)(2,1)S(1)}, u32[]{:S(2)}, u32[]{:S(2)}) %all-to-all-start) | async-done | bytes 524320 | tf_op jit(solution)/shard_map/while/body/eval_jaxpr/all_to_all | solution.py:122
  132.2 9.0 conditional.4
  146.7 10.2 all-to-all-done.1
  174.7 8.9 all-to-all-done
  183.6 9.0 conditional.4
  198.1 9.2 all-to-all-done.1
  226.5 8.9 all-to-all-done
  235.4 9.0 conditional.4
  249.9 8.3 all-to-all-done.1
  278.3 8.9 all-to-all-done
  292.8 8.3 all-to-all-done.1
  302.3 15.6 %collective-permute-start = (bf16[32,4096]{1,0:T(8,128)(2,1)S(1)}, bf16[32,4096]{1,0:T(8,128)(2,1)S(1)}, u32[]{:S(2)}, u32[]{:S(2)}) collective-permute-start(bf16[32,4096]{1,0:T(8,128)(2,1)S(1)} %get-tuple-element.791), channel_id=1, source_target_pairs={{0,16},{16,32},{32,48},{48,64},{64,80},{80,96},{96,112},{1,17},{17... | collective-permute-start | bytes 786440 | tf_op jit(solution)/shard_map/while/body/eval_jaxpr/ppermute | solution.py:12
  330.1 12.3 %all-to-all-done = bf16[16,4,4096]{2,1,0:T(4,128)(2,1)S(1)} async-done(((bf16[16,4,4096]{2,1,0:T(4,128)(2,1)}), bf16[16,4,4096]{2,1,0:T(4,128)(2,1)S(1)}, u32[]{:S(2)}, u32[]{:S(2)}) %all-to-all-start) | async-done | bytes 524320 | tf_op jit(solution)/shard_map/while/body/eval_jaxpr/all_to_all | solution.py:122
  347.9 8.3 all-to-all-done.1
  373.5 8.9 all-to-all-done
  388.0 9.2 all-to-all-done.1
  418.3 8.9 all-to-all-done
  432.8 8.3 all-to-all-done.1
  461.2 8.9 all-to-all-done
  475.7 8.3 all-to-all-done.1
  504.1 8.9 all-to-all-done
  518.6 8.3 all-to-all-done.1
  538.2 8.6 copy.39
  548.1 574.3 %while.34 = (s32[]{:T(128)}, bf16[32,4096]{1,0:T(8,128)(2,1)S(1)}, bf16[5,32,4096]{2,1,0:T(8,128)(2,1)}, pred[]{:T(512)}, s32[11]{0:T(128)S(1)}, /*index=5*/s32[...) while((s32[]{:T(128)}, bf16[32,4096]{1,0:T(8,128)(2,1)S(1)}, ...), condition=%wide.region_15.16_spmd, body=%wide.region_9.15_spmd.sunk | while | flops 1262360704 | bytes 87233072 | solution.py:232
  557.0 8.9 all-to-all-done.2
  570.6 8.9 all-to-all-done.3
  582.8 10.8 collective-permute-done.1
  602.5 8.9 all-to-all-done.2
  616.1 8.9 all-to-all-done.3
  645.1 8.9 all-to-all-done.2
  658.7 8.9 all-to-all-done.3
  670.9 8.9 collective-permute-done.1
  688.6 8.9 all-to-all-done.2
  702.2 8.9 all-to-all-done.3
  714.4 8.1 collective-permute-done.1
  731.4 8.9 all-to-all-done.2
  745.0 8.9 all-to-all-done.3
  757.2 8.8 collective-permute-done.1
  774.9 8.9 all-to-all-done.2
  788.4 8.9 all-to-all-done.3
  800.6 67.0 %collective-permute-done.1 = bf16[32,4096]{1,0:T(8,128)(2,1)S(1)} collective-permute-done((bf16[32,4096]{1,0:T(8,128)(2,1)S(1)}, bf16[32,4096]{1,0:T(8,128)(2,1)S(1)}, u32[]{:S(2)}, u32[]{:S(2)}) %collective-permute-start.1) | collective-permute-done | bytes 262176 | tf_op jit(solution)/shard_map/while/body/eval_jaxpr/ppermute | solution.py:12
  876.5 8.9 all-to-all-done.2
  885.5 11.9 %conditional.5 = (bf16[16,4,4096]{2,1,0:T(4,128)(2,1)}) conditional(s32[]{:T(128)} %convert_element_type.163, () %tuple.102, (bf16[16,4,4096]{2,1,0:T(4,128)(2,1)S(1)}, bf16[4096,768]{1,0:T(8,128)(2,1)}, f32[5,64,768]{2,1,0:T(8,128)}, s32[]{:T(128)}, f32[5,64,768]{2,1,0:T(8,128)}, /*index=5*/bf16[4096,768]{1,0:T(8,128)(2,1)}, ...), branch_computations={%region_12.12_spmd, %region_13.13_spmd} | conditional | flops 1209270272 | bytes 75629632 | solution.py:191
  901.0 8.9 all-to-all-done.3
  929.1 8.9 all-to-all-done.2
  938.0 11.9 %conditional.5 = (bf16[16,4,4096]{2,1,0:T(4,128)(2,1)}) conditional(s32[]{:T(128)} %convert_element_type.163, () %tuple.102, (bf16[16,4,4096]{2,1,0:T(4,128)(2,1)S(1)}, bf16[4096,768]{1,0:T(8,128)(2,1)}, f32[5,64,768]{2,1,0:T(8,128)}, s32[]{:T(128)}, f32[5,64,768]{2,1,0:T(8,128)}, /*index=5*/bf16[4096,768]{1,0:T(8,128)(2,1)}, ...), branch_computations={%region_12.12_spmd, %region_13.13_spmd} | conditional | flops 1209270272 | bytes 75629632 | solution.py:191
  953.5 8.9 all-to-all-done.3
  965.7 8.0 collective-permute-done.1
  982.7 8.9 all-to-all-done.2
  991.6 11.9 %conditional.5 = (bf16[16,4,4096]{2,1,0:T(4,128)(2,1)}) conditional(s32[]{:T(128)} %convert_element_type.163, () %tuple.102, (bf16[16,4,4096]{2,1,0:T(4,128)(2,1)S(1)}, bf16[4096,768]{1,0:T(8,128)(2,1)}, f32[5,64,768]{2,1,0:T(8,128)}, s32[]{:T(128)}, f32[5,64,768]{2,1,0:T(8,128)}, /*index=5*/bf16[4096,768]{1,0:T(8,128)(2,1)}, ...), branch_computations={%region_12.12_spmd, %region_13.13_spmd} | conditional | flops 1209270272 | bytes 75629632 | solution.py:191
  1007.1 8.9 all-to-all-done.3
  1035.3 8.9 all-to-all-done.2
  1044.2 11.9 %conditional.5 = (bf16[16,4,4096]{2,1,0:T(4,128)(2,1)}) conditional(s32[]{:T(128)} %convert_element_type.163, () %tuple.102, (bf16[16,4,4096]{2,1,0:T(4,128)(2,1)S(1)}, bf16[4096,768]{1,0:T(8,128)(2,1)}, f32[5,64,768]{2,1,0:T(8,128)}, s32[]{:T(128)}, f32[5,64,768]{2,1,0:T(8,128)}, /*index=5*/bf16[4096,768]{1,0:T(8,128)(2,1)}, ...), branch_computations={%region_12.12_spmd, %region_13.13_spmd} | conditional | flops 1209270272 | bytes 75629632 | solution.py:191
  1059.7 8.9 all-to-all-done.3
  1086.5 8.9 all-to-all-done.2
  1100.1 8.9 all-to-all-done.3
  1110.4 10.8 collective-permute-start.1
  (488 shorter events, 560.9 us)
Async XLA Ops:
  12.4 19.0 %all-to-all-start = ((bf16[16,4,4096]{2,1,0:T(4,128)(2,1)}), bf16[16,4,4096]{2,1,0:T(4,128)(2,1)S(1)}, u32[]{:S(2)}, u32[]{:S(2)}) async-start(bf16[16,4,4096]{2,1,0:T(4,128)(2,1)} %copy.60), calls=%async_computation | async-start | bytes 1048576 | tf_op jit(solution)/shard_map/while/body/eval_jaxpr/all_to_all | solution.py:122
  32.7 12.5 %all-to-all-start.1 = ((bf16[16,4,4096]{2,1,0:T(4,128)(2,1)}), bf16[16,4,4096]{2,1,0:T(4,128)(2,1)S(1)}, u32[]{:S(2)}, u32[]{:S(2)}) async-start(bf16[16,4,4096]{2,1,0:T(4,128)(2,1)} %copy.61), calls=%async_computation.1 | async-start | bytes 1048576 | tf_op jit(solution)/shard_map/while/body/eval_jaxpr/all_to_all | solution.py:73
  46.5 14.4 %collective-permute-start = (bf16[32,4096]{1,0:T(8,128)(2,1)S(1)}, bf16[32,4096]{1,0:T(8,128)(2,1)S(1)}, u32[]{:S(2)}, u32[]{:S(2)}) collective-permute-start(bf16[32,4096]{1,0:T(8,128)(2,1)S(1)} %get-tuple-element.791), channel_id=1, source_target_pairs={{0,16},{16,32},{32,48},{48,64},{64,80},{80,96},{96,112},{1,17},{17... | collective-permute-start | bytes 786440 | tf_op jit(solution)/shard_map/while/body/eval_jaxpr/ppermute | solution.py:12
  66.2 14.7 %all-to-all-start = ((bf16[16,4,4096]{2,1,0:T(4,128)(2,1)}), bf16[16,4,4096]{2,1,0:T(4,128)(2,1)S(1)}, u32[]{:S(2)}, u32[]{:S(2)}) async-start(bf16[16,4,4096]{2,1,0:T(4,128)(2,1)} %copy.60), calls=%async_computation | async-start | bytes 1048576 | tf_op jit(solution)/shard_map/while/body/eval_jaxpr/all_to_all | solution.py:122
  91.2 13.9 %all-to-all-start.1 = ((bf16[16,4,4096]{2,1,0:T(4,128)(2,1)}), bf16[16,4,4096]{2,1,0:T(4,128)(2,1)S(1)}, u32[]{:S(2)}, u32[]{:S(2)}) async-start(bf16[16,4,4096]{2,1,0:T(4,128)(2,1)} %copy.61), calls=%async_computation.1 | async-start | bytes 1048576 | tf_op jit(solution)/shard_map/while/body/eval_jaxpr/all_to_all | solution.py:73
  116.8 15.4 %all-to-all-start = ((bf16[16,4,4096]{2,1,0:T(4,128)(2,1)}), bf16[16,4,4096]{2,1,0:T(4,128)(2,1)S(1)}, u32[]{:S(2)}, u32[]{:S(2)}) async-start(bf16[16,4,4096]{2,1,0:T(4,128)(2,1)} %copy.60), calls=%async_computation | async-start | bytes 1048576 | tf_op jit(solution)/shard_map/while/body/eval_jaxpr/all_to_all | solution.py:122
  142.5 14.5 %all-to-all-start.1 = ((bf16[16,4,4096]{2,1,0:T(4,128)(2,1)}), bf16[16,4,4096]{2,1,0:T(4,128)(2,1)S(1)}, u32[]{:S(2)}, u32[]{:S(2)}) async-start(bf16[16,4,4096]{2,1,0:T(4,128)(2,1)} %copy.61), calls=%async_computation.1 | async-start | bytes 1048576 | tf_op jit(solution)/shard_map/while/body/eval_jaxpr/all_to_all | solution.py:73
  158.1 7.7 collective-permute-start
  171.1 12.5 %all-to-all-start = ((bf16[16,4,4096]{2,1,0:T(4,128)(2,1)}), bf16[16,4,4096]{2,1,0:T(4,128)(2,1)S(1)}, u32[]{:S(2)}, u32[]{:S(2)}) async-start(bf16[16,4,4096]{2,1,0:T(4,128)(2,1)} %copy.60), calls=%async_computation | async-start | bytes 1048576 | tf_op jit(solution)/shard_map/while/body/eval_jaxpr/all_to_all | solution.py:122
  193.9 13.4 %all-to-all-start.1 = ((bf16[16,4,4096]{2,1,0:T(4,128)(2,1)}), bf16[16,4,4096]{2,1,0:T(4,128)(2,1)S(1)}, u32[]{:S(2)}, u32[]{:S(2)}) async-start(bf16[16,4,4096]{2,1,0:T(4,128)(2,1)} %copy.61), calls=%async_computation.1 | async-start | bytes 1048576 | tf_op jit(solution)/shard_map/while/body/eval_jaxpr/all_to_all | solution.py:73
  208.5 9.0 collective-permute-start
  222.9 12.5 %all-to-all-start = ((bf16[16,4,4096]{2,1,0:T(4,128)(2,1)}), bf16[16,4,4096]{2,1,0:T(4,128)(2,1)S(1)}, u32[]{:S(2)}, u32[]{:S(2)}) async-start(bf16[16,4,4096]{2,1,0:T(4,128)(2,1)} %copy.60), calls=%async_computation | async-start | bytes 1048576 | tf_op jit(solution)/shard_map/while/body/eval_jaxpr/all_to_all | solution.py:122
  245.6 12.5 %all-to-all-start.1 = ((bf16[16,4,4096]{2,1,0:T(4,128)(2,1)}), bf16[16,4,4096]{2,1,0:T(4,128)(2,1)S(1)}, u32[]{:S(2)}, u32[]{:S(2)}) async-start(bf16[16,4,4096]{2,1,0:T(4,128)(2,1)} %copy.61), calls=%async_computation.1 | async-start | bytes 1048576 | tf_op jit(solution)/shard_map/while/body/eval_jaxpr/all_to_all | solution.py:73
  259.4 10.0 collective-permute-start
  274.7 12.5 %all-to-all-start = ((bf16[16,4,4096]{2,1,0:T(4,128)(2,1)}), bf16[16,4,4096]{2,1,0:T(4,128)(2,1)S(1)}, u32[]{:S(2)}, u32[]{:S(2)}) async-start(bf16[16,4,4096]{2,1,0:T(4,128)(2,1)} %copy.60), calls=%async_computation | async-start | bytes 1048576 | tf_op jit(solution)/shard_map/while/body/eval_jaxpr/all_to_all | solution.py:122
  288.5 12.5 %all-to-all-start.1 = ((bf16[16,4,4096]{2,1,0:T(4,128)(2,1)}), bf16[16,4,4096]{2,1,0:T(4,128)(2,1)S(1)}, u32[]{:S(2)}, u32[]{:S(2)}) async-start(bf16[16,4,4096]{2,1,0:T(4,128)(2,1)} %copy.61), calls=%async_computation.1 | async-start | bytes 1048576 | tf_op jit(solution)/shard_map/while/body/eval_jaxpr/all_to_all | solution.py:73
  302.3 18.9 %collective-permute-start = (bf16[32,4096]{1,0:T(8,128)(2,1)S(1)}, bf16[32,4096]{1,0:T(8,128)(2,1)S(1)}, u32[]{:S(2)}, u32[]{:S(2)}) collective-permute-start(bf16[32,4096]{1,0:T(8,128)(2,1)S(1)} %get-tuple-element.791), channel_id=1, source_target_pairs={{0,16},{16,32},{32,48},{48,64},{64,80},{80,96},{96,112},{1,17},{17... | collective-permute-start | bytes 786440 | tf_op jit(solution)/shard_map/while/body/eval_jaxpr/ppermute | solution.py:12
  326.5 15.9 %all-to-all-start = ((bf16[16,4,4096]{2,1,0:T(4,128)(2,1)}), bf16[16,4,4096]{2,1,0:T(4,128)(2,1)S(1)}, u32[]{:S(2)}, u32[]{:S(2)}) async-start(bf16[16,4,4096]{2,1,0:T(4,128)(2,1)} %copy.60), calls=%async_computation | async-start | bytes 1048576 | tf_op jit(solution)/shard_map/while/body/eval_jaxpr/all_to_all | solution.py:122
  343.7 12.5 %all-to-all-start.1 = ((bf16[16,4,4096]{2,1,0:T(4,128)(2,1)}), bf16[16,4,4096]{2,1,0:T(4,128)(2,1)S(1)}, u32[]{:S(2)}, u32[]{:S(2)}) async-start(bf16[16,4,4096]{2,1,0:T(4,128)(2,1)} %copy.61), calls=%async_computation.1 | async-start | bytes 1048576 | tf_op jit(solution)/shard_map/while/body/eval_jaxpr/all_to_all | solution.py:73
  369.9 12.5 %all-to-all-start = ((bf16[16,4,4096]{2,1,0:T(4,128)(2,1)}), bf16[16,4,4096]{2,1,0:T(4,128)(2,1)S(1)}, u32[]{:S(2)}, u32[]{:S(2)}) async-start(bf16[16,4,4096]{2,1,0:T(4,128)(2,1)} %copy.60), calls=%async_computation | async-start | bytes 1048576 | tf_op jit(solution)/shard_map/while/body/eval_jaxpr/all_to_all | solution.py:122
  383.7 13.5 %all-to-all-start.1 = ((bf16[16,4,4096]{2,1,0:T(4,128)(2,1)}), bf16[16,4,4096]{2,1,0:T(4,128)(2,1)S(1)}, u32[]{:S(2)}, u32[]{:S(2)}) async-start(bf16[16,4,4096]{2,1,0:T(4,128)(2,1)} %copy.61), calls=%async_computation.1 | async-start | bytes 1048576 | tf_op jit(solution)/shard_map/while/body/eval_jaxpr/all_to_all | solution.py:73
  398.4 11.0 collective-permute-start
  414.7 12.5 %all-to-all-start = ((bf16[16,4,4096]{2,1,0:T(4,128)(2,1)}), bf16[16,4,4096]{2,1,0:T(4,128)(2,1)S(1)}, u32[]{:S(2)}, u32[]{:S(2)}) async-start(bf16[16,4,4096]{2,1,0:T(4,128)(2,1)} %copy.60), calls=%async_computation | async-start | bytes 1048576 | tf_op jit(solution)/shard_map/while/body/eval_jaxpr/all_to_all | solution.py:122
  428.5 12.5 %all-to-all-start.1 = ((bf16[16,4,4096]{2,1,0:T(4,128)(2,1)}), bf16[16,4,4096]{2,1,0:T(4,128)(2,1)S(1)}, u32[]{:S(2)}, u32[]{:S(2)}) async-start(bf16[16,4,4096]{2,1,0:T(4,128)(2,1)} %copy.61), calls=%async_computation.1 | async-start | bytes 1048576 | tf_op jit(solution)/shard_map/while/body/eval_jaxpr/all_to_all | solution.py:73
  442.3 10.0 collective-permute-start
  457.6 12.5 %all-to-all-start = ((bf16[16,4,4096]{2,1,0:T(4,128)(2,1)}), bf16[16,4,4096]{2,1,0:T(4,128)(2,1)S(1)}, u32[]{:S(2)}, u32[]{:S(2)}) async-start(bf16[16,4,4096]{2,1,0:T(4,128)(2,1)} %copy.60), calls=%async_computation | async-start | bytes 1048576 | tf_op jit(solution)/shard_map/while/body/eval_jaxpr/all_to_all | solution.py:122
  471.4 12.5 %all-to-all-start.1 = ((bf16[16,4,4096]{2,1,0:T(4,128)(2,1)}), bf16[16,4,4096]{2,1,0:T(4,128)(2,1)S(1)}, u32[]{:S(2)}, u32[]{:S(2)}) async-start(bf16[16,4,4096]{2,1,0:T(4,128)(2,1)} %copy.61), calls=%async_computation.1 | async-start | bytes 1048576 | tf_op jit(solution)/shard_map/while/body/eval_jaxpr/all_to_all | solution.py:73
  485.2 10.0 collective-permute-start
  500.5 12.5 %all-to-all-start = ((bf16[16,4,4096]{2,1,0:T(4,128)(2,1)}), bf16[16,4,4096]{2,1,0:T(4,128)(2,1)S(1)}, u32[]{:S(2)}, u32[]{:S(2)}) async-start(bf16[16,4,4096]{2,1,0:T(4,128)(2,1)} %copy.60), calls=%async_computation | async-start | bytes 1048576 | tf_op jit(solution)/shard_map/while/body/eval_jaxpr/all_to_all | solution.py:122
  514.3 12.5 %all-to-all-start.1 = ((bf16[16,4,4096]{2,1,0:T(4,128)(2,1)}), bf16[16,4,4096]{2,1,0:T(4,128)(2,1)S(1)}, u32[]{:S(2)}, u32[]{:S(2)}) async-start(bf16[16,4,4096]{2,1,0:T(4,128)(2,1)} %copy.61), calls=%async_computation.1 | async-start | bytes 1048576 | tf_op jit(solution)/shard_map/while/body/eval_jaxpr/all_to_all | solution.py:73
  528.1 10.2 collective-permute-start
  553.4 12.5 %all-to-all-start.2 = ((bf16[16,4,4096]{2,1,0:T(4,128)(2,1)}), bf16[16,4,4096]{2,1,0:T(4,128)(2,1)S(1)}, u32[]{:S(2)}, u32[]{:S(2)}) async-start(bf16[16,4,4096]{2,1,0:T(4,128)(2,1)} %copy.62), calls=%async_computation.2 | async-start | bytes 1048576 | tf_op jit(solution)/shard_map/while/body/eval_jaxpr/all_to_all | solution.py:196
  567.0 12.5 %all-to-all-start.3 = ((bf16[16,4,4096]{2,1,0:T(4,128)(2,1)}), bf16[16,4,4096]{2,1,0:T(4,128)(2,1)S(1)}, u32[]{:S(2)}, u32[]{:S(2)}) async-start(bf16[16,4,4096]{2,1,0:T(4,128)(2,1)} %get-tuple-element.961), calls=%async_computation.3 | async-start | bytes 1048576 | tf_op jit(solution)/shard_map/while/body/eval_jaxpr/all_to_all | solution.py:73
  580.9 12.8 %collective-permute-start.1 = (bf16[32,4096]{1,0:T(8,128)(2,1)S(1)}, bf16[32,4096]{1,0:T(8,128)(2,1)S(1)}, u32[]{:S(2)}, u32[]{:S(2)}) collective-permute-start(bf16[32,4096]{1,0:T(8,128)(2,1)S(1)} %get-tuple-element.821), channel_id=1, source_target_pairs={{16,0},{32,16},{48,32},{64,48},{80,64},{96,80},{112,96},{17,1},{33... | collective-permute-start | bytes 786440 | tf_op jit(solution)/shard_map/while/body/eval_jaxpr/ppermute | solution.py:12
  598.9 12.5 %all-to-all-start.2 = ((bf16[16,4,4096]{2,1,0:T(4,128)(2,1)}), bf16[16,4,4096]{2,1,0:T(4,128)(2,1)S(1)}, u32[]{:S(2)}, u32[]{:S(2)}) async-start(bf16[16,4,4096]{2,1,0:T(4,128)(2,1)} %copy.62), calls=%async_computation.2 | async-start | bytes 1048576 | tf_op jit(solution)/shard_map/while/body/eval_jaxpr/all_to_all | solution.py:196
  612.5 12.5 %all-to-all-start.3 = ((bf16[16,4,4096]{2,1,0:T(4,128)(2,1)}), bf16[16,4,4096]{2,1,0:T(4,128)(2,1)S(1)}, u32[]{:S(2)}, u32[]{:S(2)}) async-start(bf16[16,4,4096]{2,1,0:T(4,128)(2,1)} %get-tuple-element.961), calls=%async_computation.3 | async-start | bytes 1048576 | tf_op jit(solution)/shard_map/while/body/eval_jaxpr/all_to_all | solution.py:73
  626.4 9.8 collective-permute-start.1
  641.5 12.5 %all-to-all-start.2 = ((bf16[16,4,4096]{2,1,0:T(4,128)(2,1)}), bf16[16,4,4096]{2,1,0:T(4,128)(2,1)S(1)}, u32[]{:S(2)}, u32[]{:S(2)}) async-start(bf16[16,4,4096]{2,1,0:T(4,128)(2,1)} %copy.62), calls=%async_computation.2 | async-start | bytes 1048576 | tf_op jit(solution)/shard_map/while/body/eval_jaxpr/all_to_all | solution.py:196
  655.1 12.5 %all-to-all-start.3 = ((bf16[16,4,4096]{2,1,0:T(4,128)(2,1)}), bf16[16,4,4096]{2,1,0:T(4,128)(2,1)S(1)}, u32[]{:S(2)}, u32[]{:S(2)}) async-start(bf16[16,4,4096]{2,1,0:T(4,128)(2,1)} %get-tuple-element.961), calls=%async_computation.3 | async-start | bytes 1048576 | tf_op jit(solution)/shard_map/while/body/eval_jaxpr/all_to_all | solution.py:73
  669.0 10.8 collective-permute-start.1
  685.0 12.5 %all-to-all-start.2 = ((bf16[16,4,4096]{2,1,0:T(4,128)(2,1)}), bf16[16,4,4096]{2,1,0:T(4,128)(2,1)S(1)}, u32[]{:S(2)}, u32[]{:S(2)}) async-start(bf16[16,4,4096]{2,1,0:T(4,128)(2,1)} %copy.62), calls=%async_computation.2 | async-start | bytes 1048576 | tf_op jit(solution)/shard_map/while/body/eval_jaxpr/all_to_all | solution.py:196
  698.6 12.5 %all-to-all-start.3 = ((bf16[16,4,4096]{2,1,0:T(4,128)(2,1)}), bf16[16,4,4096]{2,1,0:T(4,128)(2,1)S(1)}, u32[]{:S(2)}, u32[]{:S(2)}) async-start(bf16[16,4,4096]{2,1,0:T(4,128)(2,1)} %get-tuple-element.961), calls=%async_computation.3 | async-start | bytes 1048576 | tf_op jit(solution)/shard_map/while/body/eval_jaxpr/all_to_all | solution.py:73
  712.5 10.0 collective-permute-start.1
  727.8 12.5 %all-to-all-start.2 = ((bf16[16,4,4096]{2,1,0:T(4,128)(2,1)}), bf16[16,4,4096]{2,1,0:T(4,128)(2,1)S(1)}, u32[]{:S(2)}, u32[]{:S(2)}) async-start(bf16[16,4,4096]{2,1,0:T(4,128)(2,1)} %copy.62), calls=%async_computation.2 | async-start | bytes 1048576 | tf_op jit(solution)/shard_map/while/body/eval_jaxpr/all_to_all | solution.py:196
  741.4 12.5 %all-to-all-start.3 = ((bf16[16,4,4096]{2,1,0:T(4,128)(2,1)}), bf16[16,4,4096]{2,1,0:T(4,128)(2,1)S(1)}, u32[]{:S(2)}, u32[]{:S(2)}) async-start(bf16[16,4,4096]{2,1,0:T(4,128)(2,1)} %get-tuple-element.961), calls=%async_computation.3 | async-start | bytes 1048576 | tf_op jit(solution)/shard_map/while/body/eval_jaxpr/all_to_all | solution.py:73
  755.3 10.7 collective-permute-start.1
  771.3 12.5 %all-to-all-start.2 = ((bf16[16,4,4096]{2,1,0:T(4,128)(2,1)}), bf16[16,4,4096]{2,1,0:T(4,128)(2,1)S(1)}, u32[]{:S(2)}, u32[]{:S(2)}) async-start(bf16[16,4,4096]{2,1,0:T(4,128)(2,1)} %copy.62), calls=%async_computation.2 | async-start | bytes 1048576 | tf_op jit(solution)/shard_map/while/body/eval_jaxpr/all_to_all | solution.py:196
  784.8 12.5 %all-to-all-start.3 = ((bf16[16,4,4096]{2,1,0:T(4,128)(2,1)}), bf16[16,4,4096]{2,1,0:T(4,128)(2,1)S(1)}, u32[]{:S(2)}, u32[]{:S(2)}) async-start(bf16[16,4,4096]{2,1,0:T(4,128)(2,1)} %get-tuple-element.961), calls=%async_computation.3 | async-start | bytes 1048576 | tf_op jit(solution)/shard_map/while/body/eval_jaxpr/all_to_all | solution.py:73
  798.7 68.9 %collective-permute-start.1 = (bf16[32,4096]{1,0:T(8,128)(2,1)S(1)}, bf16[32,4096]{1,0:T(8,128)(2,1)S(1)}, u32[]{:S(2)}, u32[]{:S(2)}) collective-permute-start(bf16[32,4096]{1,0:T(8,128)(2,1)S(1)} %get-tuple-element.821), channel_id=1, source_target_pairs={{16,0},{32,16},{48,32},{64,48},{80,64},{96,80},{112,96},{17,1},{33... | collective-permute-start | bytes 786440 | tf_op jit(solution)/shard_map/while/body/eval_jaxpr/ppermute | solution.py:12
  873.0 12.5 %all-to-all-start.2 = ((bf16[16,4,4096]{2,1,0:T(4,128)(2,1)}), bf16[16,4,4096]{2,1,0:T(4,128)(2,1)S(1)}, u32[]{:S(2)}, u32[]{:S(2)}) async-start(bf16[16,4,4096]{2,1,0:T(4,128)(2,1)} %copy.62), calls=%async_computation.2 | async-start | bytes 1048576 | tf_op jit(solution)/shard_map/while/body/eval_jaxpr/all_to_all | solution.py:196
  897.4 12.5 %all-to-all-start.3 = ((bf16[16,4,4096]{2,1,0:T(4,128)(2,1)}), bf16[16,4,4096]{2,1,0:T(4,128)(2,1)S(1)}, u32[]{:S(2)}, u32[]{:S(2)}) async-start(bf16[16,4,4096]{2,1,0:T(4,128)(2,1)} %get-tuple-element.961), calls=%async_computation.3 | async-start | bytes 1048576 | tf_op jit(solution)/shard_map/while/body/eval_jaxpr/all_to_all | solution.py:73
  911.3 8.9 collective-permute-start.1
  925.5 12.5 %all-to-all-start.2 = ((bf16[16,4,4096]{2,1,0:T(4,128)(2,1)}), bf16[16,4,4096]{2,1,0:T(4,128)(2,1)S(1)}, u32[]{:S(2)}, u32[]{:S(2)}) async-start(bf16[16,4,4096]{2,1,0:T(4,128)(2,1)} %copy.62), calls=%async_computation.2 | async-start | bytes 1048576 | tf_op jit(solution)/shard_map/while/body/eval_jaxpr/all_to_all | solution.py:196
  949.9 12.5 %all-to-all-start.3 = ((bf16[16,4,4096]{2,1,0:T(4,128)(2,1)}), bf16[16,4,4096]{2,1,0:T(4,128)(2,1)S(1)}, u32[]{:S(2)}, u32[]{:S(2)}) async-start(bf16[16,4,4096]{2,1,0:T(4,128)(2,1)} %get-tuple-element.961), calls=%async_computation.3 | async-start | bytes 1048576 | tf_op jit(solution)/shard_map/while/body/eval_jaxpr/all_to_all | solution.py:73
  963.8 10.0 collective-permute-start.1
  979.1 12.5 %all-to-all-start.2 = ((bf16[16,4,4096]{2,1,0:T(4,128)(2,1)}), bf16[16,4,4096]{2,1,0:T(4,128)(2,1)S(1)}, u32[]{:S(2)}, u32[]{:S(2)}) async-start(bf16[16,4,4096]{2,1,0:T(4,128)(2,1)} %copy.62), calls=%async_computation.2 | async-start | bytes 1048576 | tf_op jit(solution)/shard_map/while/body/eval_jaxpr/all_to_all | solution.py:196
  1003.5 12.5 %all-to-all-start.3 = ((bf16[16,4,4096]{2,1,0:T(4,128)(2,1)}), bf16[16,4,4096]{2,1,0:T(4,128)(2,1)S(1)}, u32[]{:S(2)}, u32[]{:S(2)}) async-start(bf16[16,4,4096]{2,1,0:T(4,128)(2,1)} %get-tuple-element.961), calls=%async_computation.3 | async-start | bytes 1048576 | tf_op jit(solution)/shard_map/while/body/eval_jaxpr/all_to_all | solution.py:73
  1017.4 9.0 collective-permute-start.1
  1031.7 12.5 %all-to-all-start.2 = ((bf16[16,4,4096]{2,1,0:T(4,128)(2,1)}), bf16[16,4,4096]{2,1,0:T(4,128)(2,1)S(1)}, u32[]{:S(2)}, u32[]{:S(2)}) async-start(bf16[16,4,4096]{2,1,0:T(4,128)(2,1)} %copy.62), calls=%async_computation.2 | async-start | bytes 1048576 | tf_op jit(solution)/shard_map/while/body/eval_jaxpr/all_to_all | solution.py:196
  1056.1 12.5 %all-to-all-start.3 = ((bf16[16,4,4096]{2,1,0:T(4,128)(2,1)}), bf16[16,4,4096]{2,1,0:T(4,128)(2,1)S(1)}, u32[]{:S(2)}, u32[]{:S(2)}) async-start(bf16[16,4,4096]{2,1,0:T(4,128)(2,1)} %get-tuple-element.961), calls=%async_computation.3 | async-start | bytes 1048576 | tf_op jit(solution)/shard_map/while/body/eval_jaxpr/all_to_all | solution.py:73
  1070.0 7.7 collective-permute-start.1
  1083.0 12.5 %all-to-all-start.2 = ((bf16[16,4,4096]{2,1,0:T(4,128)(2,1)}), bf16[16,4,4096]{2,1,0:T(4,128)(2,1)S(1)}, u32[]{:S(2)}, u32[]{:S(2)}) async-start(bf16[16,4,4096]{2,1,0:T(4,128)(2,1)} %copy.62), calls=%async_computation.2 | async-start | bytes 1048576 | tf_op jit(solution)/shard_map/while/body/eval_jaxpr/all_to_all | solution.py:196
  1096.5 12.5 %all-to-all-start.3 = ((bf16[16,4,4096]{2,1,0:T(4,128)(2,1)}), bf16[16,4,4096]{2,1,0:T(4,128)(2,1)S(1)}, u32[]{:S(2)}, u32[]{:S(2)}) async-start(bf16[16,4,4096]{2,1,0:T(4,128)(2,1)} %get-tuple-element.961), calls=%async_computation.3 | async-start | bytes 1048576 | tf_op jit(solution)/shard_map/while/body/eval_jaxpr/all_to_all | solution.py:73
  1110.4 12.0 %collective-permute-start.1 = (bf16[32,4096]{1,0:T(8,128)(2,1)S(1)}, bf16[32,4096]{1,0:T(8,128)(2,1)S(1)}, u32[]{:S(2)}, u32[]{:S(2)}) collective-permute-start(bf16[32,4096]{1,0:T(8,128)(2,1)S(1)} %get-tuple-element.821), channel_id=1, source_target_pairs={{16,0},{32,16},{48,32},{64,48},{80,64},{96,80},{112,96},{17,1},{33... | collective-permute-start | bytes 786440 | tf_op jit(solution)/shard_map/while/body/eval_jaxpr/ppermute | solution.py:12
  (19 other events, 75.1 us)

commit v10 on v6

--- a/solution.py
+++ b/solution.py
@@ -100,7 +100,7 @@
         :, :, :, None, None
     ]
 
-    def forward_work(tokens, table4, weights, live):
+    def forward_work(tokens, table4, table, gate_now, live):
         values, scale, normed = normalize(tokens, gain_row)
         send = jnp.einsum(
             "ktec,td->ecd", table4, normed, preferred_element_type=jnp.float32
@@ -125,9 +125,8 @@
             lax.all_to_all(send, "expert", split_axis=0, concat_axis=0, tiled=True),
         )
         back = return_rows(output).reshape(total_rows, width)
-        mixed = values + jnp.dot(
-            weights, back.astype(jnp.float32), precision=lax.Precision.HIGHEST
-        )
+        picked = jnp.einsum("ktj,jd->tkd", table, back, preferred_element_type=jnp.float32)
+        mixed = values + jnp.sum(gate_now[..., None] * picked, axis=1)
         return (mixed.astype(jnp.bfloat16), pre_gate, pre_up)
 
     def forward_tick(carry, tick):
@@ -139,8 +138,9 @@
         fresh = lax.dynamic_index_in_dim(inputs, index, 0, keepdims=False)
         tokens = jnp.where(section == 0, fresh, incoming)
         table4 = lax.dynamic_index_in_dim(all_tables4, index, 0, keepdims=False)
-        weights = lax.dynamic_index_in_dim(all_weights, index, 0, keepdims=False)
-        mixed, pre_gate, pre_up = forward_work(tokens, table4, weights, live)
+        table = lax.dynamic_index_in_dim(all_tables, index, 0, keepdims=False)
+        gate_now = lax.dynamic_index_in_dim(gates, index, 0, keepdims=False)
+        mixed, pre_gate, pre_up = forward_work(tokens, table4, table, gate_now, live)
         outputs = lax.dynamic_update_index_in_dim(outputs, mixed, slot, 0)
         kept_x = lax.dynamic_update_index_in_dim(kept_x, tokens, slot, 0)
         kept_gate = lax.dynamic_update_index_in_dim(

time: 1130 us -> 1130 us (level)
  blocking collectives: 134 us -> 0 us
  waiting for transfers between devices: 475 us -> 574 us
  starting transfers between devices: 230 us -> 265 us
  matrix products: 114 us -> 96.5 us
  local copies, waits for them, and re-layouts: 105 us -> 118 us
    all_to_all x11 -> x0, blocking collectives: 134 us -> none  [return_rows(): lax.all_to_all(rows, 'expert', split_axis=0, concat_axis=0, tiled=True)]
    all_to_all x11 -> x22, waiting for transfers between devices: 98.1 us -> 194 us  [return_rows(): lax.all_to_all(rows, 'expert', split_axis=0, concat_axis=0, tiled=True)]
    all_to_all x11 -> x22, starting transfers between devices: 39.3 us -> 78.6 us  [return_rows(): lax.all_to_all(rows, 'expert', split_axis=0, concat_axis=0, tiled=True)]
    dot_general x12 -> x11, matrix products: 21.1 us -> 3.22 us  [forward_work(): jnp.einsum('ktj,jd->tkd', table, back, preferred_element_type=jnp.float32)]
  transfers between devices with their start and end apart: 55 -> 66, of which waited for: 55 -> 66; matrix products, arithmetic and copies ran while one was open for 1% -> 1% of each run, Pallas kernels for 0% -> 0%
where the time goes in v10:
time: 1130 us; the launch traced here: 1120 us
  waiting for transfers between devices  574 us (51%)
  starting transfers between devices  265 us (23%)
  local copies, waits for them, and re-layouts  118 us (10%)
  matrix products  96.5 us (9%)
  other arithmetic  53.7 us (5%)
  loops' own time  14.7 us (1%)
    all_to_all x22, waiting for transfers between devices, return_rows(): lax.all_to_all(rows, 'expert', split_axis=0, concat_axis=0, tiled=True)  194 us
    ppermute x22, waiting for transfers between devices, passed_along(): lax.ppermute(value, axis, [(source, source + steps) for source in range(l...  173 us
    all_to_all x11, waiting for transfers between devices, forward_work(): lax.all_to_all(send, 'expert', split_axis=0, concat_axis=0, tiled=True)  108 us
    ppermute x22, starting transfers between devices, passed_along(): lax.ppermute(value, axis, [(source, source + steps) for source in range(l...  103 us
    all_to_all x11, waiting for transfers between devices, backward_work(): lax.all_to_all(grad_send, 'expert', split_axis=0, concat_axis=0, tiled=True)  98.4 us
    all_to_all x22, starting transfers between devices, return_rows(): lax.all_to_all(rows, 'expert', split_axis=0, concat_axis=0, tiled=True)  78.6 us
    all_to_all x11, starting transfers between devices, forward_work(): lax.all_to_all(send, 'expert', split_axis=0, concat_axis=0, tiled=True)  44.3 us
    all_to_all x11, starting transfers between devices, backward_work(): lax.all_to_all(grad_send, 'expert', split_axis=0, concat_axis=0, tiled=True)  39.3 us
  transfers between devices with their start and end apart: 66, of which 66 were waited for; matrix products, arithmetic and copies ran while one was open for 1% of the time, Pallas kernels for 0%

profile of v10, /device:TPU:1, one launch (start us, length us, event | category | flops | bytes accessed | tf_op | source)
XLA Modules:
  0.0 1122.9 jit_solution(141984624115199071)
XLA Ops:
  7.7 531.1 %while.33 = (s32[]{:T(128)}, bf16[32,4096]{1,0:T(8,128)(2,1)S(1)}, bf16[5,32,4096]{2,1,0:T(8,128)(2,1)}, bf16[5,32,4096]{2,1,0:T(8,128)(2,1)S(1)}, f32[5,64,768]...) while((s32[]{:T(128)}, bf16[32,4096]{1,0:T(8,128)(2,1)S(1)}, ...), condition=%wide.region_8.9_spmd, body=%wide.region_2.8_spmd.sunk | while | flops 1260689408 | bytes 85772840 | solution.py:163
  13.0 8.6 all-to-all-start
  21.6 10.4 all-to-all-done
  37.6 8.3 all-to-all-done.1
  70.4 11.2 all-to-all-done
  81.5 9.0 conditional.4
  96.0 9.7 all-to-all-done.1
  121.0 11.8 %all-to-all-done = bf16[16,4,4096]{2,1,0:T(4,128)(2,1)S(1)} async-done(((bf16[16,4,4096]{2,1,0:T(4,128)(2,1)}), bf16[16,4,4096]{2,1,0:T(4,128)(2,1)S(1)}, u32[]{:S(2)}, u32[]{:S(2)}) %all-to-all-start) | async-done | bytes 524320 | tf_op jit(solution)/shard_map/while/body/eval_jaxpr/all_to_all | solution.py:125
  132.7 9.0 conditional.4
  147.2 10.2 all-to-all-done.1
  175.3 8.9 all-to-all-done
  184.3 9.0 conditional.4
  198.8 8.9 all-to-all-done.1
  227.1 8.9 all-to-all-done
  236.1 9.0 conditional.4
  250.6 8.3 all-to-all-done.1
  278.9 8.9 all-to-all-done
  293.4 8.3 all-to-all-done.1
  302.9 15.6 %collective-permute-start = (bf16[32,4096]{1,0:T(8,128)(2,1)S(1)}, bf16[32,4096]{1,0:T(8,128)(2,1)S(1)}, u32[]{:S(2)}, u32[]{:S(2)}) collective-permute-start(bf16[32,4096]{1,0:T(8,128)(2,1)S(1)} %get-tuple-element.773), channel_id=1, source_target_pairs={{0,16},{16,32},{32,48},{48,64},{64,80},{80,96},{96,112},{1,17},{17... | collective-permute-start | bytes 786440 | tf_op jit(solution)/shard_map/while/body/eval_jaxpr/ppermute | solution.py:12
  330.7 12.4 %all-to-all-done = bf16[16,4,4096]{2,1,0:T(4,128)(2,1)S(1)} async-done(((bf16[16,4,4096]{2,1,0:T(4,128)(2,1)}), bf16[16,4,4096]{2,1,0:T(4,128)(2,1)S(1)}, u32[]{:S(2)}, u32[]{:S(2)}) %all-to-all-start) | async-done | bytes 524320 | tf_op jit(solution)/shard_map/while/body/eval_jaxpr/all_to_all | solution.py:125
  348.6 8.3 all-to-all-done.1
  374.1 8.9 all-to-all-done
  388.6 9.4 all-to-all-done.1
  418.9 8.9 all-to-all-done
  433.4 8.3 all-to-all-done.1
  461.8 8.9 all-to-all-done
  476.3 8.3 all-to-all-done.1
  504.6 8.9 all-to-all-done
  519.2 8.3 all-to-all-done.1
  539.6 8.6 copy.38
  549.5 570.4 %while.34 = (s32[]{:T(128)}, bf16[32,4096]{1,0:T(8,128)(2,1)S(1)}, bf16[5,32,4096]{2,1,0:T(8,128)(2,1)}, pred[]{:T(512)}, s32[11]{0:T(128)S(1)}, /*index=5*/s32[...) while((s32[]{:T(128)}, bf16[32,4096]{1,0:T(8,128)(2,1)S(1)}, ...), condition=%wide.region_16.17_spmd, body=%wide.region_9.16_spmd.sunk | while | flops 1329078400 | bytes 86184744 | solution.py:234
  557.0 8.9 all-to-all-done.2
  570.6 8.9 all-to-all-done.3
  583.8 10.8 collective-permute-done.1
  602.2 8.9 all-to-all-done.2
  615.8 8.9 all-to-all-done.3
  644.5 8.9 all-to-all-done.2
  658.1 8.9 all-to-all-done.3
  671.2 8.9 collective-permute-done.1
  687.7 8.9 all-to-all-done.2
  701.3 8.9 all-to-all-done.3
  714.4 8.1 collective-permute-done.1
  730.0 8.9 all-to-all-done.2
  743.6 8.9 all-to-all-done.3
  756.8 8.8 collective-permute-done.1
  773.1 8.9 all-to-all-done.2
  786.7 8.9 all-to-all-done.3
  799.9 67.0 %collective-permute-done.1 = bf16[32,4096]{1,0:T(8,128)(2,1)S(1)} collective-permute-done((bf16[32,4096]{1,0:T(8,128)(2,1)S(1)}, bf16[32,4096]{1,0:T(8,128)(2,1)S(1)}, u32[]{:S(2)}, u32[]{:S(2)}) %collective-permute-start.1) | collective-permute-done | bytes 262176 | tf_op jit(solution)/shard_map/while/body/eval_jaxpr/ppermute | solution.py:12
  874.4 8.9 all-to-all-done.2
  883.4 11.9 %conditional.5 = (bf16[16,4,4096]{2,1,0:T(4,128)(2,1)}) conditional(s32[]{:T(128)} %convert_element_type.158, () %tuple.102, (bf16[16,4,4096]{2,1,0:T(4,128)(2,1)S(1)}, bf16[4096,768]{1,0:T(8,128)(2,1)}, f32[5,64,768]{2,1,0:T(8,128)}, s32[]{:T(128)}, f32[5,64,768]{2,1,0:T(8,128)}, /*index=5*/bf16[4096,768]{1,0:T(8,128)(2,1)}, ...), branch_computations={%region_13.13_spmd, %region_14.14_spmd} | conditional | flops 1209270272 | bytes 75629632 | solution.py:194
  898.9 8.9 all-to-all-done.3
  926.6 8.9 all-to-all-done.2
  935.5 11.9 %conditional.5 = (bf16[16,4,4096]{2,1,0:T(4,128)(2,1)}) conditional(s32[]{:T(128)} %convert_element_type.158, () %tuple.102, (bf16[16,4,4096]{2,1,0:T(4,128)(2,1)S(1)}, bf16[4096,768]{1,0:T(8,128)(2,1)}, f32[5,64,768]{2,1,0:T(8,128)}, s32[]{:T(128)}, f32[5,64,768]{2,1,0:T(8,128)}, /*index=5*/bf16[4096,768]{1,0:T(8,128)(2,1)}, ...), branch_computations={%region_13.13_spmd, %region_14.14_spmd} | conditional | flops 1209270272 | bytes 75629632 | solution.py:194
  951.0 8.9 all-to-all-done.3
  964.2 8.1 collective-permute-done.1
  979.8 8.9 all-to-all-done.2
  988.8 11.9 %conditional.5 = (bf16[16,4,4096]{2,1,0:T(4,128)(2,1)}) conditional(s32[]{:T(128)} %convert_element_type.158, () %tuple.102, (bf16[16,4,4096]{2,1,0:T(4,128)(2,1)S(1)}, bf16[4096,768]{1,0:T(8,128)(2,1)}, f32[5,64,768]{2,1,0:T(8,128)}, s32[]{:T(128)}, f32[5,64,768]{2,1,0:T(8,128)}, /*index=5*/bf16[4096,768]{1,0:T(8,128)(2,1)}, ...), branch_computations={%region_13.13_spmd, %region_14.14_spmd} | conditional | flops 1209270272 | bytes 75629632 | solution.py:194
  1004.3 8.9 all-to-all-done.3
  1032.1 8.9 all-to-all-done.2
  1041.0 11.9 %conditional.5 = (bf16[16,4,4096]{2,1,0:T(4,128)(2,1)}) conditional(s32[]{:T(128)} %convert_element_type.158, () %tuple.102, (bf16[16,4,4096]{2,1,0:T(4,128)(2,1)S(1)}, bf16[4096,768]{1,0:T(8,128)(2,1)}, f32[5,64,768]{2,1,0:T(8,128)}, s32[]{:T(128)}, f32[5,64,768]{2,1,0:T(8,128)}, /*index=5*/bf16[4096,768]{1,0:T(8,128)(2,1)}, ...), branch_computations={%region_13.13_spmd, %region_14.14_spmd} | conditional | flops 1209270272 | bytes 75629632 | solution.py:194
  1056.5 8.9 all-to-all-done.3
  1083.0 8.9 all-to-all-done.2
  1096.6 8.9 all-to-all-done.3
  1107.9 10.8 collective-permute-start.1
  (471 shorter events, 559.3 us)
Async XLA Ops:
  13.0 19.0 %all-to-all-start = ((bf16[16,4,4096]{2,1,0:T(4,128)(2,1)}), bf16[16,4,4096]{2,1,0:T(4,128)(2,1)S(1)}, u32[]{:S(2)}, u32[]{:S(2)}) async-start(bf16[16,4,4096]{2,1,0:T(4,128)(2,1)} %copy.56), calls=%async_computation | async-start | bytes 1048576 | tf_op jit(solution)/shard_map/while/body/eval_jaxpr/all_to_all | solution.py:125
  33.3 12.5 %all-to-all-start.1 = ((bf16[16,4,4096]{2,1,0:T(4,128)(2,1)}), bf16[16,4,4096]{2,1,0:T(4,128)(2,1)S(1)}, u32[]{:S(2)}, u32[]{:S(2)}) async-start(bf16[16,4,4096]{2,1,0:T(4,128)(2,1)} %copy.57), calls=%async_computation.1 | async-start | bytes 1048576 | tf_op jit(solution)/shard_map/while/body/eval_jaxpr/all_to_all | solution.py:73
  47.1 14.4 %collective-permute-start = (bf16[32,4096]{1,0:T(8,128)(2,1)S(1)}, bf16[32,4096]{1,0:T(8,128)(2,1)S(1)}, u32[]{:S(2)}, u32[]{:S(2)}) collective-permute-start(bf16[32,4096]{1,0:T(8,128)(2,1)S(1)} %get-tuple-element.773), channel_id=1, source_target_pairs={{0,16},{16,32},{32,48},{48,64},{64,80},{80,96},{96,112},{1,17},{17... | collective-permute-start | bytes 786440 | tf_op jit(solution)/shard_map/while/body/eval_jaxpr/ppermute | solution.py:12
  66.8 14.7 %all-to-all-start = ((bf16[16,4,4096]{2,1,0:T(4,128)(2,1)}), bf16[16,4,4096]{2,1,0:T(4,128)(2,1)S(1)}, u32[]{:S(2)}, u32[]{:S(2)}) async-start(bf16[16,4,4096]{2,1,0:T(4,128)(2,1)} %copy.56), calls=%async_computation | async-start | bytes 1048576 | tf_op jit(solution)/shard_map/while/body/eval_jaxpr/all_to_all | solution.py:125
  91.7 13.9 %all-to-all-start.1 = ((bf16[16,4,4096]{2,1,0:T(4,128)(2,1)}), bf16[16,4,4096]{2,1,0:T(4,128)(2,1)S(1)}, u32[]{:S(2)}, u32[]{:S(2)}) async-start(bf16[16,4,4096]{2,1,0:T(4,128)(2,1)} %copy.57), calls=%async_computation.1 | async-start | bytes 1048576 | tf_op jit(solution)/shard_map/while/body/eval_jaxpr/all_to_all | solution.py:73
  117.4 15.4 %all-to-all-start = ((bf16[16,4,4096]{2,1,0:T(4,128)(2,1)}), bf16[16,4,4096]{2,1,0:T(4,128)(2,1)S(1)}, u32[]{:S(2)}, u32[]{:S(2)}) async-start(bf16[16,4,4096]{2,1,0:T(4,128)(2,1)} %copy.56), calls=%async_computation | async-start | bytes 1048576 | tf_op jit(solution)/shard_map/while/body/eval_jaxpr/all_to_all | solution.py:125
  143.0 14.5 %all-to-all-start.1 = ((bf16[16,4,4096]{2,1,0:T(4,128)(2,1)}), bf16[16,4,4096]{2,1,0:T(4,128)(2,1)S(1)}, u32[]{:S(2)}, u32[]{:S(2)}) async-start(bf16[16,4,4096]{2,1,0:T(4,128)(2,1)} %copy.57), calls=%async_computation.1 | async-start | bytes 1048576 | tf_op jit(solution)/shard_map/while/body/eval_jaxpr/all_to_all | solution.py:73
  158.6 7.8 collective-permute-start
  171.8 12.5 %all-to-all-start = ((bf16[16,4,4096]{2,1,0:T(4,128)(2,1)}), bf16[16,4,4096]{2,1,0:T(4,128)(2,1)S(1)}, u32[]{:S(2)}, u32[]{:S(2)}) async-start(bf16[16,4,4096]{2,1,0:T(4,128)(2,1)} %copy.56), calls=%async_computation | async-start | bytes 1048576 | tf_op jit(solution)/shard_map/while/body/eval_jaxpr/all_to_all | solution.py:125
  194.5 13.2 %all-to-all-start.1 = ((bf16[16,4,4096]{2,1,0:T(4,128)(2,1)}), bf16[16,4,4096]{2,1,0:T(4,128)(2,1)S(1)}, u32[]{:S(2)}, u32[]{:S(2)}) async-start(bf16[16,4,4096]{2,1,0:T(4,128)(2,1)} %copy.57), calls=%async_computation.1 | async-start | bytes 1048576 | tf_op jit(solution)/shard_map/while/body/eval_jaxpr/all_to_all | solution.py:73
  208.9 9.3 collective-permute-start
  223.5 12.5 %all-to-all-start = ((bf16[16,4,4096]{2,1,0:T(4,128)(2,1)}), bf16[16,4,4096]{2,1,0:T(4,128)(2,1)S(1)}, u32[]{:S(2)}, u32[]{:S(2)}) async-start(bf16[16,4,4096]{2,1,0:T(4,128)(2,1)} %copy.56), calls=%async_computation | async-start | bytes 1048576 | tf_op jit(solution)/shard_map/while/body/eval_jaxpr/all_to_all | solution.py:125
  246.3 12.5 %all-to-all-start.1 = ((bf16[16,4,4096]{2,1,0:T(4,128)(2,1)}), bf16[16,4,4096]{2,1,0:T(4,128)(2,1)S(1)}, u32[]{:S(2)}, u32[]{:S(2)}) async-start(bf16[16,4,4096]{2,1,0:T(4,128)(2,1)} %copy.57), calls=%async_computation.1 | async-start | bytes 1048576 | tf_op jit(solution)/shard_map/while/body/eval_jaxpr/all_to_all | solution.py:73
  260.1 10.0 collective-permute-start
  275.3 12.5 %all-to-all-start = ((bf16[16,4,4096]{2,1,0:T(4,128)(2,1)}), bf16[16,4,4096]{2,1,0:T(4,128)(2,1)S(1)}, u32[]{:S(2)}, u32[]{:S(2)}) async-start(bf16[16,4,4096]{2,1,0:T(4,128)(2,1)} %copy.56), calls=%async_computation | async-start | bytes 1048576 | tf_op jit(solution)/shard_map/while/body/eval_jaxpr/all_to_all | solution.py:125
  289.2 12.5 %all-to-all-start.1 = ((bf16[16,4,4096]{2,1,0:T(4,128)(2,1)}), bf16[16,4,4096]{2,1,0:T(4,128)(2,1)S(1)}, u32[]{:S(2)}, u32[]{:S(2)}) async-start(bf16[16,4,4096]{2,1,0:T(4,128)(2,1)} %copy.57), calls=%async_computation.1 | async-start | bytes 1048576 | tf_op jit(solution)/shard_map/while/body/eval_jaxpr/all_to_all | solution.py:73
  302.9 18.9 %collective-permute-start = (bf16[32,4096]{1,0:T(8,128)(2,1)S(1)}, bf16[32,4096]{1,0:T(8,128)(2,1)S(1)}, u32[]{:S(2)}, u32[]{:S(2)}) collective-permute-start(bf16[32,4096]{1,0:T(8,128)(2,1)S(1)} %get-tuple-element.773), channel_id=1, source_target_pairs={{0,16},{16,32},{32,48},{48,64},{64,80},{80,96},{96,112},{1,17},{17... | collective-permute-start | bytes 786440 | tf_op jit(solution)/shard_map/while/body/eval_jaxpr/ppermute | solution.py:12
  327.1 15.9 %all-to-all-start = ((bf16[16,4,4096]{2,1,0:T(4,128)(2,1)}), bf16[16,4,4096]{2,1,0:T(4,128)(2,1)S(1)}, u32[]{:S(2)}, u32[]{:S(2)}) async-start(bf16[16,4,4096]{2,1,0:T(4,128)(2,1)} %copy.56), calls=%async_computation | async-start | bytes 1048576 | tf_op jit(solution)/shard_map/while/body/eval_jaxpr/all_to_all | solution.py:125
  344.4 12.5 %all-to-all-start.1 = ((bf16[16,4,4096]{2,1,0:T(4,128)(2,1)}), bf16[16,4,4096]{2,1,0:T(4,128)(2,1)S(1)}, u32[]{:S(2)}, u32[]{:S(2)}) async-start(bf16[16,4,4096]{2,1,0:T(4,128)(2,1)} %copy.57), calls=%async_computation.1 | async-start | bytes 1048576 | tf_op jit(solution)/shard_map/while/body/eval_jaxpr/all_to_all | solution.py:73
  370.5 12.5 %all-to-all-start = ((bf16[16,4,4096]{2,1,0:T(4,128)(2,1)}), bf16[16,4,4096]{2,1,0:T(4,128)(2,1)S(1)}, u32[]{:S(2)}, u32[]{:S(2)}) async-start(bf16[16,4,4096]{2,1,0:T(4,128)(2,1)} %copy.56), calls=%async_computation | async-start | bytes 1048576 | tf_op jit(solution)/shard_map/while/body/eval_jaxpr/all_to_all | solution.py:125
  384.3 13.6 %all-to-all-start.1 = ((bf16[16,4,4096]{2,1,0:T(4,128)(2,1)}), bf16[16,4,4096]{2,1,0:T(4,128)(2,1)S(1)}, u32[]{:S(2)}, u32[]{:S(2)}) async-start(bf16[16,4,4096]{2,1,0:T(4,128)(2,1)} %copy.57), calls=%async_computation.1 | async-start | bytes 1048576 | tf_op jit(solution)/shard_map/while/body/eval_jaxpr/all_to_all | solution.py:73
  399.1 10.9 collective-permute-start
  415.3 12.5 %all-to-all-start = ((bf16[16,4,4096]{2,1,0:T(4,128)(2,1)}), bf16[16,4,4096]{2,1,0:T(4,128)(2,1)S(1)}, u32[]{:S(2)}, u32[]{:S(2)}) async-start(bf16[16,4,4096]{2,1,0:T(4,128)(2,1)} %copy.56), calls=%async_computation | async-start | bytes 1048576 | tf_op jit(solution)/shard_map/while/body/eval_jaxpr/all_to_all | solution.py:125
  429.1 12.5 %all-to-all-start.1 = ((bf16[16,4,4096]{2,1,0:T(4,128)(2,1)}), bf16[16,4,4096]{2,1,0:T(4,128)(2,1)S(1)}, u32[]{:S(2)}, u32[]{:S(2)}) async-start(bf16[16,4,4096]{2,1,0:T(4,128)(2,1)} %copy.57), calls=%async_computation.1 | async-start | bytes 1048576 | tf_op jit(solution)/shard_map/while/body/eval_jaxpr/all_to_all | solution.py:73
  442.9 10.1 collective-permute-start
  458.2 12.5 %all-to-all-start = ((bf16[16,4,4096]{2,1,0:T(4,128)(2,1)}), bf16[16,4,4096]{2,1,0:T(4,128)(2,1)S(1)}, u32[]{:S(2)}, u32[]{:S(2)}) async-start(bf16[16,4,4096]{2,1,0:T(4,128)(2,1)} %copy.56), calls=%async_computation | async-start | bytes 1048576 | tf_op jit(solution)/shard_map/while/body/eval_jaxpr/all_to_all | solution.py:125
  472.0 12.5 %all-to-all-start.1 = ((bf16[16,4,4096]{2,1,0:T(4,128)(2,1)}), bf16[16,4,4096]{2,1,0:T(4,128)(2,1)S(1)}, u32[]{:S(2)}, u32[]{:S(2)}) async-start(bf16[16,4,4096]{2,1,0:T(4,128)(2,1)} %copy.57), calls=%async_computation.1 | async-start | bytes 1048576 | tf_op jit(solution)/shard_map/while/body/eval_jaxpr/all_to_all | solution.py:73
  485.8 10.0 collective-permute-start
  501.1 12.5 %all-to-all-start = ((bf16[16,4,4096]{2,1,0:T(4,128)(2,1)}), bf16[16,4,4096]{2,1,0:T(4,128)(2,1)S(1)}, u32[]{:S(2)}, u32[]{:S(2)}) async-start(bf16[16,4,4096]{2,1,0:T(4,128)(2,1)} %copy.56), calls=%async_computation | async-start | bytes 1048576 | tf_op jit(solution)/shard_map/while/body/eval_jaxpr/all_to_all | solution.py:125
  514.9 12.5 %all-to-all-start.1 = ((bf16[16,4,4096]{2,1,0:T(4,128)(2,1)}), bf16[16,4,4096]{2,1,0:T(4,128)(2,1)S(1)}, u32[]{:S(2)}, u32[]{:S(2)}) async-start(bf16[16,4,4096]{2,1,0:T(4,128)(2,1)} %copy.57), calls=%async_computation.1 | async-start | bytes 1048576 | tf_op jit(solution)/shard_map/while/body/eval_jaxpr/all_to_all | solution.py:73
  528.6 10.1 collective-permute-start
  553.4 12.5 %all-to-all-start.2 = ((bf16[16,4,4096]{2,1,0:T(4,128)(2,1)}), bf16[16,4,4096]{2,1,0:T(4,128)(2,1)S(1)}, u32[]{:S(2)}, u32[]{:S(2)}) async-start(bf16[16,4,4096]{2,1,0:T(4,128)(2,1)} %copy.59), calls=%async_computation.2 | async-start | bytes 1048576 | tf_op jit(solution)/shard_map/while/body/eval_jaxpr/all_to_all | solution.py:199
  567.0 12.5 %all-to-all-start.3 = ((bf16[16,4,4096]{2,1,0:T(4,128)(2,1)}), bf16[16,4,4096]{2,1,0:T(4,128)(2,1)S(1)}, u32[]{:S(2)}, u32[]{:S(2)}) async-start(bf16[16,4,4096]{2,1,0:T(4,128)(2,1)} %get-tuple-element.939), calls=%async_computation.3 | async-start | bytes 1048576 | tf_op jit(solution)/shard_map/while/body/eval_jaxpr/all_to_all | solution.py:73
  581.9 12.7 %collective-permute-start.1 = (bf16[32,4096]{1,0:T(8,128)(2,1)S(1)}, bf16[32,4096]{1,0:T(8,128)(2,1)S(1)}, u32[]{:S(2)}, u32[]{:S(2)}) collective-permute-start(bf16[32,4096]{1,0:T(8,128)(2,1)S(1)} %get-tuple-element.802), channel_id=1, source_target_pairs={{16,0},{32,16},{48,32},{64,48},{80,64},{96,80},{112,96},{17,1},{33... | collective-permute-start | bytes 786440 | tf_op jit(solution)/shard_map/while/body/eval_jaxpr/ppermute | solution.py:12
  598.6 12.5 %all-to-all-start.2 = ((bf16[16,4,4096]{2,1,0:T(4,128)(2,1)}), bf16[16,4,4096]{2,1,0:T(4,128)(2,1)S(1)}, u32[]{:S(2)}, u32[]{:S(2)}) async-start(bf16[16,4,4096]{2,1,0:T(4,128)(2,1)} %copy.59), calls=%async_computation.2 | async-start | bytes 1048576 | tf_op jit(solution)/shard_map/while/body/eval_jaxpr/all_to_all | solution.py:199
  612.2 12.5 %all-to-all-start.3 = ((bf16[16,4,4096]{2,1,0:T(4,128)(2,1)}), bf16[16,4,4096]{2,1,0:T(4,128)(2,1)S(1)}, u32[]{:S(2)}, u32[]{:S(2)}) async-start(bf16[16,4,4096]{2,1,0:T(4,128)(2,1)} %get-tuple-element.939), calls=%async_computation.3 | async-start | bytes 1048576 | tf_op jit(solution)/shard_map/while/body/eval_jaxpr/all_to_all | solution.py:73
  627.0 9.9 collective-permute-start.1
  640.9 12.5 %all-to-all-start.2 = ((bf16[16,4,4096]{2,1,0:T(4,128)(2,1)}), bf16[16,4,4096]{2,1,0:T(4,128)(2,1)S(1)}, u32[]{:S(2)}, u32[]{:S(2)}) async-start(bf16[16,4,4096]{2,1,0:T(4,128)(2,1)} %copy.59), calls=%async_computation.2 | async-start | bytes 1048576 | tf_op jit(solution)/shard_map/while/body/eval_jaxpr/all_to_all | solution.py:199
  654.5 12.5 %all-to-all-start.3 = ((bf16[16,4,4096]{2,1,0:T(4,128)(2,1)}), bf16[16,4,4096]{2,1,0:T(4,128)(2,1)S(1)}, u32[]{:S(2)}, u32[]{:S(2)}) async-start(bf16[16,4,4096]{2,1,0:T(4,128)(2,1)} %get-tuple-element.939), calls=%async_computation.3 | async-start | bytes 1048576 | tf_op jit(solution)/shard_map/while/body/eval_jaxpr/all_to_all | solution.py:73
  669.3 10.8 collective-permute-start.1
  684.1 12.5 %all-to-all-start.2 = ((bf16[16,4,4096]{2,1,0:T(4,128)(2,1)}), bf16[16,4,4096]{2,1,0:T(4,128)(2,1)S(1)}, u32[]{:S(2)}, u32[]{:S(2)}) async-start(bf16[16,4,4096]{2,1,0:T(4,128)(2,1)} %copy.59), calls=%async_computation.2 | async-start | bytes 1048576 | tf_op jit(solution)/shard_map/while/body/eval_jaxpr/all_to_all | solution.py:199
  697.7 12.5 %all-to-all-start.3 = ((bf16[16,4,4096]{2,1,0:T(4,128)(2,1)}), bf16[16,4,4096]{2,1,0:T(4,128)(2,1)S(1)}, u32[]{:S(2)}, u32[]{:S(2)}) async-start(bf16[16,4,4096]{2,1,0:T(4,128)(2,1)} %get-tuple-element.939), calls=%async_computation.3 | async-start | bytes 1048576 | tf_op jit(solution)/shard_map/while/body/eval_jaxpr/all_to_all | solution.py:73
  712.5 10.0 collective-permute-start.1
  726.4 12.5 %all-to-all-start.2 = ((bf16[16,4,4096]{2,1,0:T(4,128)(2,1)}), bf16[16,4,4096]{2,1,0:T(4,128)(2,1)S(1)}, u32[]{:S(2)}, u32[]{:S(2)}) async-start(bf16[16,4,4096]{2,1,0:T(4,128)(2,1)} %copy.59), calls=%async_computation.2 | async-start | bytes 1048576 | tf_op jit(solution)/shard_map/while/body/eval_jaxpr/all_to_all | solution.py:199
  740.0 12.5 %all-to-all-start.3 = ((bf16[16,4,4096]{2,1,0:T(4,128)(2,1)}), bf16[16,4,4096]{2,1,0:T(4,128)(2,1)S(1)}, u32[]{:S(2)}, u32[]{:S(2)}) async-start(bf16[16,4,4096]{2,1,0:T(4,128)(2,1)} %get-tuple-element.939), calls=%async_computation.3 | async-start | bytes 1048576 | tf_op jit(solution)/shard_map/while/body/eval_jaxpr/all_to_all | solution.py:73
  754.9 10.7 collective-permute-start.1
  769.5 12.5 %all-to-all-start.2 = ((bf16[16,4,4096]{2,1,0:T(4,128)(2,1)}), bf16[16,4,4096]{2,1,0:T(4,128)(2,1)S(1)}, u32[]{:S(2)}, u32[]{:S(2)}) async-start(bf16[16,4,4096]{2,1,0:T(4,128)(2,1)} %copy.59), calls=%async_computation.2 | async-start | bytes 1048576 | tf_op jit(solution)/shard_map/while/body/eval_jaxpr/all_to_all | solution.py:199
  783.1 12.5 %all-to-all-start.3 = ((bf16[16,4,4096]{2,1,0:T(4,128)(2,1)}), bf16[16,4,4096]{2,1,0:T(4,128)(2,1)S(1)}, u32[]{:S(2)}, u32[]{:S(2)}) async-start(bf16[16,4,4096]{2,1,0:T(4,128)(2,1)} %get-tuple-element.939), calls=%async_computation.3 | async-start | bytes 1048576 | tf_op jit(solution)/shard_map/while/body/eval_jaxpr/all_to_all | solution.py:73
  797.9 69.0 %collective-permute-start.1 = (bf16[32,4096]{1,0:T(8,128)(2,1)S(1)}, bf16[32,4096]{1,0:T(8,128)(2,1)S(1)}, u32[]{:S(2)}, u32[]{:S(2)}) collective-permute-start(bf16[32,4096]{1,0:T(8,128)(2,1)S(1)} %get-tuple-element.802), channel_id=1, source_target_pairs={{16,0},{32,16},{48,32},{64,48},{80,64},{96,80},{112,96},{17,1},{33... | collective-permute-start | bytes 786440 | tf_op jit(solution)/shard_map/while/body/eval_jaxpr/ppermute | solution.py:12
  870.9 12.5 %all-to-all-start.2 = ((bf16[16,4,4096]{2,1,0:T(4,128)(2,1)}), bf16[16,4,4096]{2,1,0:T(4,128)(2,1)S(1)}, u32[]{:S(2)}, u32[]{:S(2)}) async-start(bf16[16,4,4096]{2,1,0:T(4,128)(2,1)} %copy.59), calls=%async_computation.2 | async-start | bytes 1048576 | tf_op jit(solution)/shard_map/while/body/eval_jaxpr/all_to_all | solution.py:199
  895.3 12.5 %all-to-all-start.3 = ((bf16[16,4,4096]{2,1,0:T(4,128)(2,1)}), bf16[16,4,4096]{2,1,0:T(4,128)(2,1)S(1)}, u32[]{:S(2)}, u32[]{:S(2)}) async-start(bf16[16,4,4096]{2,1,0:T(4,128)(2,1)} %get-tuple-element.939), calls=%async_computation.3 | async-start | bytes 1048576 | tf_op jit(solution)/shard_map/while/body/eval_jaxpr/all_to_all | solution.py:73
  910.1 8.9 collective-permute-start.1
  923.0 12.5 %all-to-all-start.2 = ((bf16[16,4,4096]{2,1,0:T(4,128)(2,1)}), bf16[16,4,4096]{2,1,0:T(4,128)(2,1)S(1)}, u32[]{:S(2)}, u32[]{:S(2)}) async-start(bf16[16,4,4096]{2,1,0:T(4,128)(2,1)} %copy.59), calls=%async_computation.2 | async-start | bytes 1048576 | tf_op jit(solution)/shard_map/while/body/eval_jaxpr/all_to_all | solution.py:199
  947.4 12.5 %all-to-all-start.3 = ((bf16[16,4,4096]{2,1,0:T(4,128)(2,1)}), bf16[16,4,4096]{2,1,0:T(4,128)(2,1)S(1)}, u32[]{:S(2)}, u32[]{:S(2)}) async-start(bf16[16,4,4096]{2,1,0:T(4,128)(2,1)} %get-tuple-element.939), calls=%async_computation.3 | async-start | bytes 1048576 | tf_op jit(solution)/shard_map/while/body/eval_jaxpr/all_to_all | solution.py:73
  962.3 10.0 collective-permute-start.1
  976.2 12.5 %all-to-all-start.2 = ((bf16[16,4,4096]{2,1,0:T(4,128)(2,1)}), bf16[16,4,4096]{2,1,0:T(4,128)(2,1)S(1)}, u32[]{:S(2)}, u32[]{:S(2)}) async-start(bf16[16,4,4096]{2,1,0:T(4,128)(2,1)} %copy.59), calls=%async_computation.2 | async-start | bytes 1048576 | tf_op jit(solution)/shard_map/while/body/eval_jaxpr/all_to_all | solution.py:199
  1000.7 12.5 %all-to-all-start.3 = ((bf16[16,4,4096]{2,1,0:T(4,128)(2,1)}), bf16[16,4,4096]{2,1,0:T(4,128)(2,1)S(1)}, u32[]{:S(2)}, u32[]{:S(2)}) async-start(bf16[16,4,4096]{2,1,0:T(4,128)(2,1)} %get-tuple-element.939), calls=%async_computation.3 | async-start | bytes 1048576 | tf_op jit(solution)/shard_map/while/body/eval_jaxpr/all_to_all | solution.py:73
  1015.5 9.0 collective-permute-start.1
  1028.5 12.5 %all-to-all-start.2 = ((bf16[16,4,4096]{2,1,0:T(4,128)(2,1)}), bf16[16,4,4096]{2,1,0:T(4,128)(2,1)S(1)}, u32[]{:S(2)}, u32[]{:S(2)}) async-start(bf16[16,4,4096]{2,1,0:T(4,128)(2,1)} %copy.59), calls=%async_computation.2 | async-start | bytes 1048576 | tf_op jit(solution)/shard_map/while/body/eval_jaxpr/all_to_all | solution.py:199
  1052.9 12.5 %all-to-all-start.3 = ((bf16[16,4,4096]{2,1,0:T(4,128)(2,1)}), bf16[16,4,4096]{2,1,0:T(4,128)(2,1)S(1)}, u32[]{:S(2)}, u32[]{:S(2)}) async-start(bf16[16,4,4096]{2,1,0:T(4,128)(2,1)} %get-tuple-element.939), calls=%async_computation.3 | async-start | bytes 1048576 | tf_op jit(solution)/shard_map/while/body/eval_jaxpr/all_to_all | solution.py:73
  1067.8 7.7 collective-permute-start.1
  1079.4 12.5 %all-to-all-start.2 = ((bf16[16,4,4096]{2,1,0:T(4,128)(2,1)}), bf16[16,4,4096]{2,1,0:T(4,128)(2,1)S(1)}, u32[]{:S(2)}, u32[]{:S(2)}) async-start(bf16[16,4,4096]{2,1,0:T(4,128)(2,1)} %copy.59), calls=%async_computation.2 | async-start | bytes 1048576 | tf_op jit(solution)/shard_map/while/body/eval_jaxpr/all_to_all | solution.py:199
  1093.0 12.5 %all-to-all-start.3 = ((bf16[16,4,4096]{2,1,0:T(4,128)(2,1)}), bf16[16,4,4096]{2,1,0:T(4,128)(2,1)S(1)}, u32[]{:S(2)}, u32[]{:S(2)}) async-start(bf16[16,4,4096]{2,1,0:T(4,128)(2,1)} %get-tuple-element.939), calls=%async_computation.3 | async-start | bytes 1048576 | tf_op jit(solution)/shard_map/while/body/eval_jaxpr/all_to_all | solution.py:73
  1107.9 12.0 %collective-permute-start.1 = (bf16[32,4096]{1,0:T(8,128)(2,1)S(1)}, bf16[32,4096]{1,0:T(8,128)(2,1)S(1)}, u32[]{:S(2)}, u32[]{:S(2)}) collective-permute-start(bf16[32,4096]{1,0:T(8,128)(2,1)S(1)} %get-tuple-element.802), channel_id=1, source_target_pairs={{16,0},{32,16},{48,32},{64,48},{80,64},{96,80},{112,96},{17,1},{33... | collective-permute-start | bytes 786440 | tf_op jit(solution)/shard_map/while/body/eval_jaxpr/ppermute | solution.py:12
  (21 other events, 79.0 us)

commit v11 on v5

--- a/solution.py
+++ b/solution.py
@@ -133,8 +133,11 @@
         live = (offset >= 0) & (offset < micro)
         index = jnp.clip(offset, 0, micro - 1)
         slot = jnp.where(live, offset, micro)
-        fresh = lax.dynamic_index_in_dim(inputs, index, 0, keepdims=False)
-        tokens = jnp.where(section == 0, fresh, incoming)
+        tokens = lax.cond(
+            section == 0,
+            lambda: lax.dynamic_index_in_dim(inputs, index, 0, keepdims=False),
+            lambda: incoming,
+        )
         table4 = lax.dynamic_index_in_dim(all_tables4, index, 0, keepdims=False)
         weights = lax.dynamic_index_in_dim(all_weights, index, 0, keepdims=False)
         mixed, pre_gate, pre_up = forward_work(tokens, table4, weights, live)
@@ -214,8 +217,11 @@
         live = (offset >= 0) & (offset < micro)
         index = jnp.clip(offset, 0, micro - 1)
         slot = jnp.where(live, offset, micro)
-        fresh = lax.dynamic_index_in_dim(cotangent, index, 0, keepdims=False)
-        grad_out = jnp.where(section == sections - 1, fresh, incoming)
+        grad_out = lax.cond(
+            section == sections - 1,
+            lambda: lax.dynamic_index_in_dim(cotangent, index, 0, keepdims=False),
+            lambda: incoming,
+        )
         tokens = lax.dynamic_index_in_dim(kept_x, index, 0, keepdims=False)
         table = lax.dynamic_index_in_dim(all_tables, index, 0, keepdims=False)
         table4 = lax.dynamic_index_in_dim(all_tables4, index, 0, keepdims=False)

time: 1130 us -> 1120 us (level)
  blocking collectives: 134 us -> 0 us
  waiting for transfers between devices: 475 us -> 578 us
  starting transfers between devices: 230 us -> 264 us
  other arithmetic: 35.9 us -> 14.3 us
    all_to_all x11 -> x0, blocking collectives: 134 us -> none  [return_rows(): lax.all_to_all(rows, 'expert', split_axis=0, concat_axis=0, tiled=True)]
    all_to_all x11 -> x22, waiting for transfers between devices: 98.1 us -> 200 us  [return_rows(): lax.all_to_all(rows, 'expert', split_axis=0, concat_axis=0, tiled=True)]
    all_to_all x11 -> x22, starting transfers between devices: 39.3 us -> 78.6 us  [return_rows(): lax.all_to_all(rows, 'expert', split_axis=0, concat_axis=0, tiled=True)]
  transfers between devices with their start and end apart: 55 -> 66, of which waited for: 55 -> 66; matrix products, arithmetic and copies ran while one was open for 1% -> 1% of each run, Pallas kernels for 0% -> 0%
where the time goes in v11:
time: 1120 us; the launch traced here: 1110 us
  waiting for transfers between devices  578 us (52%)
  starting transfers between devices  264 us (24%)
  local copies, waits for them, and re-layouts  129 us (12%)
  matrix products  110 us (10%)
  loops' own time  17.3 us (2%)
  other arithmetic  14.3 us (1%)
    all_to_all x22, waiting for transfers between devices, return_rows(): lax.all_to_all(rows, 'expert', split_axis=0, concat_axis=0, tiled=True)  200 us
    ppermute x22, waiting for transfers between devices, passed_along(): lax.ppermute(value, axis, [(source, source + steps) for source in range(l...  176 us
    all_to_all x11, waiting for transfers between devices, forward_work(): lax.all_to_all(send, 'expert', split_axis=0, concat_axis=0, tiled=True)  104 us
    ppermute x22, starting transfers between devices, passed_along(): lax.ppermute(value, axis, [(source, source + steps) for source in range(l...  102 us
    all_to_all x11, waiting for transfers between devices, backward_work(): lax.all_to_all(grad_send, 'expert', split_axis=0, concat_axis=0, tiled=True)  98.4 us
    all_to_all x22, starting transfers between devices, return_rows(): lax.all_to_all(rows, 'expert', split_axis=0, concat_axis=0, tiled=True)  78.6 us
    all_to_all x11, starting transfers between devices, forward_work(): lax.all_to_all(send, 'expert', split_axis=0, concat_axis=0, tiled=True)  44.3 us
    all_to_all x11, starting transfers between devices, backward_work(): lax.all_to_all(grad_send, 'expert', split_axis=0, concat_axis=0, tiled=True)  39.3 us
  transfers between devices with their start and end apart: 66, of which 66 were waited for; matrix products, arithmetic and copies ran while one was open for 1% of the time, Pallas kernels for 0%

profile of v11, /device:TPU:1, one launch (start us, length us, event | category | flops | bytes accessed | tf_op | source)
XLA Modules:
  0.0 1114.3 jit_solution(12681941098418391351)
XLA Ops:
  9.1 526.8 %while.40 = (s32[]{:T(128)}, bf16[32,4096]{1,0:T(8,128)(2,1)S(1)}, bf16[5,32,4096]{2,1,0:T(8,128)(2,1)}, bf16[5,32,4096]{2,1,0:T(8,128)(2,1)S(1)}, f32[5,64,768]...) while((s32[]{:T(128)}, bf16[32,4096]{1,0:T(8,128)(2,1)S(1)}, ...), condition=%wide.region_9.10_spmd, body=%wide.region_2.9_spmd.sunk | while | flops 1327273984 | bytes 85263984 | solution.py:163
  13.7 8.6 all-to-all-start
  22.3 9.0 all-to-all-done
  36.2 8.9 all-to-all-done.1
  71.7 9.6 all-to-all-done
  81.2 9.0 conditional.14
  95.1 8.9 all-to-all-done.1
  120.4 9.6 all-to-all-done
  130.0 9.0 conditional.14
  143.9 8.9 all-to-all-done.1
  171.5 11.9 %all-to-all-done = bf16[16,4,4096]{2,1,0:T(4,128)(2,1)S(1)} async-done(((bf16[16,4,4096]{2,1,0:T(4,128)(2,1)}), bf16[16,4,4096]{2,1,0:T(4,128)(2,1)S(1)}, u32[]{:S(2)}, u32[]{:S(2)}) %all-to-all-start) | async-done | bytes 524320 | tf_op jit(solution)/shard_map/while/body/eval_jaxpr/all_to_all | solution.py:122
  183.4 9.0 conditional.14
  197.2 10.7 all-to-all-done.1
  223.3 10.5 all-to-all-done
  233.8 9.0 conditional.14
  247.6 8.9 all-to-all-done.1
  275.3 9.2 all-to-all-done
  289.3 10.5 all-to-all-done.1
  301.8 13.8 %collective-permute-start = (bf16[32,4096]{1,0:T(8,128)(2,1)S(1)}, bf16[32,4096]{1,0:T(8,128)(2,1)S(1)}, u32[]{:S(2)}, u32[]{:S(2)}) collective-permute-start(bf16[32,4096]{1,0:T(8,128)(2,1)S(1)} %get-tuple-element.819), channel_id=1, source_target_pairs={{0,16},{16,32},{32,48},{48,64},{64,80},{80,96},{96,112},{1,17},{17... | collective-permute-start | bytes 786440 | tf_op jit(solution)/shard_map/while/body/eval_jaxpr/ppermute | solution.py:12
  327.1 8.9 all-to-all-done
  340.9 8.9 all-to-all-done.1
  370.4 8.9 all-to-all-done
  384.3 8.9 all-to-all-done.1
  395.1 8.7 collective-permute-start
  415.3 8.9 all-to-all-done
  429.1 8.9 all-to-all-done.1
  458.3 8.9 all-to-all-done
  472.1 9.0 all-to-all-done.1
  501.3 8.9 all-to-all-done
  515.1 9.0 all-to-all-done.1
  536.0 8.6 copy.39
  545.8 565.3 %while.41 = (s32[]{:T(128)}, bf16[32,4096]{1,0:T(8,128)(2,1)S(1)}, bf16[5,32,4096]{2,1,0:T(8,128)(2,1)}, pred[]{:T(512)}, s32[11]{0:T(128)S(1)}, /*index=5*/s32[...) while((s32[]{:T(128)}, bf16[32,4096]{1,0:T(8,128)(2,1)S(1)}, ...), condition=%wide.region_18.19_spmd, body=%wide.region_10.18_spmd.sunk | while | flops 1262360704 | bytes 87233136 | solution.py:238
  553.8 8.9 all-to-all-done.2
  567.4 8.9 all-to-all-done.3
  579.6 10.8 collective-permute-done.1
  598.3 8.9 all-to-all-done.2
  611.9 8.9 all-to-all-done.3
  624.1 8.1 collective-permute-done.1
  640.1 8.9 all-to-all-done.2
  653.6 8.9 all-to-all-done.3
  665.8 9.0 collective-permute-done.1
  682.8 8.9 all-to-all-done.2
  696.4 8.9 all-to-all-done.3
  724.3 8.9 all-to-all-done.2
  737.9 8.9 all-to-all-done.3
  750.1 9.5 collective-permute-done.1
  767.5 8.9 all-to-all-done.2
  781.1 8.9 all-to-all-done.3
  793.3 69.8 %collective-permute-done.1 = bf16[32,4096]{1,0:T(8,128)(2,1)S(1)} collective-permute-done((bf16[32,4096]{1,0:T(8,128)(2,1)S(1)}, bf16[32,4096]{1,0:T(8,128)(2,1)S(1)}, u32[]{:S(2)}, u32[]{:S(2)}) %collective-permute-start.1) | collective-permute-done | bytes 262176 | tf_op jit(solution)/shard_map/while/body/eval_jaxpr/ppermute | solution.py:12
  871.1 8.9 all-to-all-done.2
  880.0 11.9 %conditional.16 = (bf16[16,4,4096]{2,1,0:T(4,128)(2,1)}) conditional(s32[]{:T(128)} %convert_element_type.184, () %tuple.142, (bf16[16,4,4096]{2,1,0:T(4,128)(2,1)S(1)}, bf16[4096,768]{1,0:T(8,128)(2,1)}, f32[5,64,768]{2,1,0:T(8,128)}, s32[]{:T(128)}, f32[5,64,768]{2,1,0:T(8,128)}, /*index=5*/bf16[4096,768]{1,0:T(8,128)(2,1)}, ...), branch_computations={%region_15.15_spmd, %region_16.16_spmd} | conditional | flops 1209270272 | bytes 75629632 | solution.py:194
  895.5 8.9 all-to-all-done.3
  922.4 8.9 all-to-all-done.2
  931.3 11.9 %conditional.16 = (bf16[16,4,4096]{2,1,0:T(4,128)(2,1)}) conditional(s32[]{:T(128)} %convert_element_type.184, () %tuple.142, (bf16[16,4,4096]{2,1,0:T(4,128)(2,1)S(1)}, bf16[4096,768]{1,0:T(8,128)(2,1)}, f32[5,64,768]{2,1,0:T(8,128)}, s32[]{:T(128)}, f32[5,64,768]{2,1,0:T(8,128)}, /*index=5*/bf16[4096,768]{1,0:T(8,128)(2,1)}, ...), branch_computations={%region_15.15_spmd, %region_16.16_spmd} | conditional | flops 1209270272 | bytes 75629632 | solution.py:194
  946.8 8.9 all-to-all-done.3
  973.7 8.9 all-to-all-done.2
  982.7 11.9 %conditional.16 = (bf16[16,4,4096]{2,1,0:T(4,128)(2,1)}) conditional(s32[]{:T(128)} %convert_element_type.184, () %tuple.142, (bf16[16,4,4096]{2,1,0:T(4,128)(2,1)S(1)}, bf16[4096,768]{1,0:T(8,128)(2,1)}, f32[5,64,768]{2,1,0:T(8,128)}, s32[]{:T(128)}, f32[5,64,768]{2,1,0:T(8,128)}, /*index=5*/bf16[4096,768]{1,0:T(8,128)(2,1)}, ...), branch_computations={%region_15.15_spmd, %region_16.16_spmd} | conditional | flops 1209270272 | bytes 75629632 | solution.py:194
  998.1 8.9 all-to-all-done.3
  1025.0 8.9 all-to-all-done.2
  1033.9 11.9 %conditional.16 = (bf16[16,4,4096]{2,1,0:T(4,128)(2,1)}) conditional(s32[]{:T(128)} %convert_element_type.184, () %tuple.142, (bf16[16,4,4096]{2,1,0:T(4,128)(2,1)S(1)}, bf16[4096,768]{1,0:T(8,128)(2,1)}, f32[5,64,768]{2,1,0:T(8,128)}, s32[]{:T(128)}, f32[5,64,768]{2,1,0:T(8,128)}, /*index=5*/bf16[4096,768]{1,0:T(8,128)(2,1)}, ...), branch_computations={%region_15.15_spmd, %region_16.16_spmd} | conditional | flops 1209270272 | bytes 75629632 | solution.py:194
  1049.4 8.9 all-to-all-done.3
  1075.3 8.9 all-to-all-done.2
  1088.9 8.9 all-to-all-done.3
  1099.2 10.8 collective-permute-start.1
  (501 shorter events, 544.4 us)
Async XLA Ops:
  13.7 17.6 %all-to-all-start = ((bf16[16,4,4096]{2,1,0:T(4,128)(2,1)}), bf16[16,4,4096]{2,1,0:T(4,128)(2,1)S(1)}, u32[]{:S(2)}, u32[]{:S(2)}) async-start(bf16[16,4,4096]{2,1,0:T(4,128)(2,1)} %copy.64), calls=%async_computation | async-start | bytes 1048576 | tf_op jit(solution)/shard_map/while/body/eval_jaxpr/all_to_all | solution.py:122
  32.6 12.5 %all-to-all-start.1 = ((bf16[16,4,4096]{2,1,0:T(4,128)(2,1)}), bf16[16,4,4096]{2,1,0:T(4,128)(2,1)S(1)}, u32[]{:S(2)}, u32[]{:S(2)}) async-start(bf16[16,4,4096]{2,1,0:T(4,128)(2,1)} %copy.65), calls=%async_computation.1 | async-start | bytes 1048576 | tf_op jit(solution)/shard_map/while/body/eval_jaxpr/all_to_all | solution.py:73
  47.1 16.4 %collective-permute-start = (bf16[32,4096]{1,0:T(8,128)(2,1)S(1)}, bf16[32,4096]{1,0:T(8,128)(2,1)S(1)}, u32[]{:S(2)}, u32[]{:S(2)}) collective-permute-start(bf16[32,4096]{1,0:T(8,128)(2,1)S(1)} %get-tuple-element.819), channel_id=1, source_target_pairs={{0,16},{16,32},{32,48},{48,64},{64,80},{80,96},{96,112},{1,17},{17... | collective-permute-start | bytes 786440 | tf_op jit(solution)/shard_map/while/body/eval_jaxpr/ppermute | solution.py:12
  68.1 13.2 %all-to-all-start = ((bf16[16,4,4096]{2,1,0:T(4,128)(2,1)}), bf16[16,4,4096]{2,1,0:T(4,128)(2,1)S(1)}, u32[]{:S(2)}, u32[]{:S(2)}) async-start(bf16[16,4,4096]{2,1,0:T(4,128)(2,1)} %copy.64), calls=%async_computation | async-start | bytes 1048576 | tf_op jit(solution)/shard_map/while/body/eval_jaxpr/all_to_all | solution.py:122
  91.5 12.5 %all-to-all-start.1 = ((bf16[16,4,4096]{2,1,0:T(4,128)(2,1)}), bf16[16,4,4096]{2,1,0:T(4,128)(2,1)S(1)}, u32[]{:S(2)}, u32[]{:S(2)}) async-start(bf16[16,4,4096]{2,1,0:T(4,128)(2,1)} %copy.65), calls=%async_computation.1 | async-start | bytes 1048576 | tf_op jit(solution)/shard_map/while/body/eval_jaxpr/all_to_all | solution.py:73
  116.9 13.2 %all-to-all-start = ((bf16[16,4,4096]{2,1,0:T(4,128)(2,1)}), bf16[16,4,4096]{2,1,0:T(4,128)(2,1)S(1)}, u32[]{:S(2)}, u32[]{:S(2)}) async-start(bf16[16,4,4096]{2,1,0:T(4,128)(2,1)} %copy.64), calls=%async_computation | async-start | bytes 1048576 | tf_op jit(solution)/shard_map/while/body/eval_jaxpr/all_to_all | solution.py:122
  140.3 12.5 %all-to-all-start.1 = ((bf16[16,4,4096]{2,1,0:T(4,128)(2,1)}), bf16[16,4,4096]{2,1,0:T(4,128)(2,1)S(1)}, u32[]{:S(2)}, u32[]{:S(2)}) async-start(bf16[16,4,4096]{2,1,0:T(4,128)(2,1)} %copy.65), calls=%async_computation.1 | async-start | bytes 1048576 | tf_op jit(solution)/shard_map/while/body/eval_jaxpr/all_to_all | solution.py:73
  154.7 8.7 collective-permute-start
  168.0 15.5 %all-to-all-start = ((bf16[16,4,4096]{2,1,0:T(4,128)(2,1)}), bf16[16,4,4096]{2,1,0:T(4,128)(2,1)S(1)}, u32[]{:S(2)}, u32[]{:S(2)}) async-start(bf16[16,4,4096]{2,1,0:T(4,128)(2,1)} %copy.64), calls=%async_computation | async-start | bytes 1048576 | tf_op jit(solution)/shard_map/while/body/eval_jaxpr/all_to_all | solution.py:122
  193.6 14.3 %all-to-all-start.1 = ((bf16[16,4,4096]{2,1,0:T(4,128)(2,1)}), bf16[16,4,4096]{2,1,0:T(4,128)(2,1)S(1)}, u32[]{:S(2)}, u32[]{:S(2)}) async-start(bf16[16,4,4096]{2,1,0:T(4,128)(2,1)} %copy.65), calls=%async_computation.1 | async-start | bytes 1048576 | tf_op jit(solution)/shard_map/while/body/eval_jaxpr/all_to_all | solution.py:73
  219.7 14.1 %all-to-all-start = ((bf16[16,4,4096]{2,1,0:T(4,128)(2,1)}), bf16[16,4,4096]{2,1,0:T(4,128)(2,1)S(1)}, u32[]{:S(2)}, u32[]{:S(2)}) async-start(bf16[16,4,4096]{2,1,0:T(4,128)(2,1)} %copy.64), calls=%async_computation | async-start | bytes 1048576 | tf_op jit(solution)/shard_map/while/body/eval_jaxpr/all_to_all | solution.py:122
  244.0 12.5 %all-to-all-start.1 = ((bf16[16,4,4096]{2,1,0:T(4,128)(2,1)}), bf16[16,4,4096]{2,1,0:T(4,128)(2,1)S(1)}, u32[]{:S(2)}, u32[]{:S(2)}) async-start(bf16[16,4,4096]{2,1,0:T(4,128)(2,1)} %copy.65), calls=%async_computation.1 | async-start | bytes 1048576 | tf_op jit(solution)/shard_map/while/body/eval_jaxpr/all_to_all | solution.py:73
  258.5 8.6 collective-permute-start
  271.7 12.8 %all-to-all-start = ((bf16[16,4,4096]{2,1,0:T(4,128)(2,1)}), bf16[16,4,4096]{2,1,0:T(4,128)(2,1)S(1)}, u32[]{:S(2)}, u32[]{:S(2)}) async-start(bf16[16,4,4096]{2,1,0:T(4,128)(2,1)} %copy.64), calls=%async_computation | async-start | bytes 1048576 | tf_op jit(solution)/shard_map/while/body/eval_jaxpr/all_to_all | solution.py:122
  285.7 14.1 %all-to-all-start.1 = ((bf16[16,4,4096]{2,1,0:T(4,128)(2,1)}), bf16[16,4,4096]{2,1,0:T(4,128)(2,1)S(1)}, u32[]{:S(2)}, u32[]{:S(2)}) async-start(bf16[16,4,4096]{2,1,0:T(4,128)(2,1)} %copy.65), calls=%async_computation.1 | async-start | bytes 1048576 | tf_op jit(solution)/shard_map/while/body/eval_jaxpr/all_to_all | solution.py:73
  301.8 17.1 %collective-permute-start = (bf16[32,4096]{1,0:T(8,128)(2,1)S(1)}, bf16[32,4096]{1,0:T(8,128)(2,1)S(1)}, u32[]{:S(2)}, u32[]{:S(2)}) collective-permute-start(bf16[32,4096]{1,0:T(8,128)(2,1)S(1)} %get-tuple-element.819), channel_id=1, source_target_pairs={{0,16},{16,32},{32,48},{48,64},{64,80},{80,96},{96,112},{1,17},{17... | collective-permute-start | bytes 786440 | tf_op jit(solution)/shard_map/while/body/eval_jaxpr/ppermute | solution.py:12
  323.5 12.5 %all-to-all-start = ((bf16[16,4,4096]{2,1,0:T(4,128)(2,1)}), bf16[16,4,4096]{2,1,0:T(4,128)(2,1)S(1)}, u32[]{:S(2)}, u32[]{:S(2)}) async-start(bf16[16,4,4096]{2,1,0:T(4,128)(2,1)} %copy.64), calls=%async_computation | async-start | bytes 1048576 | tf_op jit(solution)/shard_map/while/body/eval_jaxpr/all_to_all | solution.py:122
  337.3 12.5 %all-to-all-start.1 = ((bf16[16,4,4096]{2,1,0:T(4,128)(2,1)}), bf16[16,4,4096]{2,1,0:T(4,128)(2,1)S(1)}, u32[]{:S(2)}, u32[]{:S(2)}) async-start(bf16[16,4,4096]{2,1,0:T(4,128)(2,1)} %copy.65), calls=%async_computation.1 | async-start | bytes 1048576 | tf_op jit(solution)/shard_map/while/body/eval_jaxpr/all_to_all | solution.py:73
  351.8 10.5 collective-permute-start
  366.8 12.5 %all-to-all-start = ((bf16[16,4,4096]{2,1,0:T(4,128)(2,1)}), bf16[16,4,4096]{2,1,0:T(4,128)(2,1)S(1)}, u32[]{:S(2)}, u32[]{:S(2)}) async-start(bf16[16,4,4096]{2,1,0:T(4,128)(2,1)} %copy.64), calls=%async_computation | async-start | bytes 1048576 | tf_op jit(solution)/shard_map/while/body/eval_jaxpr/all_to_all | solution.py:122
  380.7 12.5 %all-to-all-start.1 = ((bf16[16,4,4096]{2,1,0:T(4,128)(2,1)}), bf16[16,4,4096]{2,1,0:T(4,128)(2,1)S(1)}, u32[]{:S(2)}, u32[]{:S(2)}) async-start(bf16[16,4,4096]{2,1,0:T(4,128)(2,1)} %copy.65), calls=%async_computation.1 | async-start | bytes 1048576 | tf_op jit(solution)/shard_map/while/body/eval_jaxpr/all_to_all | solution.py:73
  395.1 12.0 %collective-permute-start = (bf16[32,4096]{1,0:T(8,128)(2,1)S(1)}, bf16[32,4096]{1,0:T(8,128)(2,1)S(1)}, u32[]{:S(2)}, u32[]{:S(2)}) collective-permute-start(bf16[32,4096]{1,0:T(8,128)(2,1)S(1)} %get-tuple-element.819), channel_id=1, source_target_pairs={{0,16},{16,32},{32,48},{48,64},{64,80},{80,96},{96,112},{1,17},{17... | collective-permute-start | bytes 786440 | tf_op jit(solution)/shard_map/while/body/eval_jaxpr/ppermute | solution.py:12
  411.7 12.5 %all-to-all-start = ((bf16[16,4,4096]{2,1,0:T(4,128)(2,1)}), bf16[16,4,4096]{2,1,0:T(4,128)(2,1)S(1)}, u32[]{:S(2)}, u32[]{:S(2)}) async-start(bf16[16,4,4096]{2,1,0:T(4,128)(2,1)} %copy.64), calls=%async_computation | async-start | bytes 1048576 | tf_op jit(solution)/shard_map/while/body/eval_jaxpr/all_to_all | solution.py:122
  425.5 12.5 %all-to-all-start.1 = ((bf16[16,4,4096]{2,1,0:T(4,128)(2,1)}), bf16[16,4,4096]{2,1,0:T(4,128)(2,1)S(1)}, u32[]{:S(2)}, u32[]{:S(2)}) async-start(bf16[16,4,4096]{2,1,0:T(4,128)(2,1)} %copy.65), calls=%async_computation.1 | async-start | bytes 1048576 | tf_op jit(solution)/shard_map/while/body/eval_jaxpr/all_to_all | solution.py:73
  440.0 10.1 collective-permute-start
  454.7 12.5 %all-to-all-start = ((bf16[16,4,4096]{2,1,0:T(4,128)(2,1)}), bf16[16,4,4096]{2,1,0:T(4,128)(2,1)S(1)}, u32[]{:S(2)}, u32[]{:S(2)}) async-start(bf16[16,4,4096]{2,1,0:T(4,128)(2,1)} %copy.64), calls=%async_computation | async-start | bytes 1048576 | tf_op jit(solution)/shard_map/while/body/eval_jaxpr/all_to_all | solution.py:122
  468.5 12.5 %all-to-all-start.1 = ((bf16[16,4,4096]{2,1,0:T(4,128)(2,1)}), bf16[16,4,4096]{2,1,0:T(4,128)(2,1)S(1)}, u32[]{:S(2)}, u32[]{:S(2)}) async-start(bf16[16,4,4096]{2,1,0:T(4,128)(2,1)} %copy.65), calls=%async_computation.1 | async-start | bytes 1048576 | tf_op jit(solution)/shard_map/while/body/eval_jaxpr/all_to_all | solution.py:73
  483.0 10.1 collective-permute-start
  497.7 12.5 %all-to-all-start = ((bf16[16,4,4096]{2,1,0:T(4,128)(2,1)}), bf16[16,4,4096]{2,1,0:T(4,128)(2,1)S(1)}, u32[]{:S(2)}, u32[]{:S(2)}) async-start(bf16[16,4,4096]{2,1,0:T(4,128)(2,1)} %copy.64), calls=%async_computation | async-start | bytes 1048576 | tf_op jit(solution)/shard_map/while/body/eval_jaxpr/all_to_all | solution.py:122
  511.5 12.5 %all-to-all-start.1 = ((bf16[16,4,4096]{2,1,0:T(4,128)(2,1)}), bf16[16,4,4096]{2,1,0:T(4,128)(2,1)S(1)}, u32[]{:S(2)}, u32[]{:S(2)}) async-start(bf16[16,4,4096]{2,1,0:T(4,128)(2,1)} %copy.65), calls=%async_computation.1 | async-start | bytes 1048576 | tf_op jit(solution)/shard_map/while/body/eval_jaxpr/all_to_all | solution.py:73
  526.0 10.0 collective-permute-start
  550.2 12.5 %all-to-all-start.2 = ((bf16[16,4,4096]{2,1,0:T(4,128)(2,1)}), bf16[16,4,4096]{2,1,0:T(4,128)(2,1)S(1)}, u32[]{:S(2)}, u32[]{:S(2)}) async-start(bf16[16,4,4096]{2,1,0:T(4,128)(2,1)} %copy.66), calls=%async_computation.2 | async-start | bytes 1048576 | tf_op jit(solution)/shard_map/while/body/eval_jaxpr/all_to_all | solution.py:199
  563.8 12.5 %all-to-all-start.3 = ((bf16[16,4,4096]{2,1,0:T(4,128)(2,1)}), bf16[16,4,4096]{2,1,0:T(4,128)(2,1)S(1)}, u32[]{:S(2)}, u32[]{:S(2)}) async-start(bf16[16,4,4096]{2,1,0:T(4,128)(2,1)} %get-tuple-element.991), calls=%async_computation.3 | async-start | bytes 1048576 | tf_op jit(solution)/shard_map/while/body/eval_jaxpr/all_to_all | solution.py:73
  577.7 12.7 %collective-permute-start.1 = (bf16[32,4096]{1,0:T(8,128)(2,1)S(1)}, bf16[32,4096]{1,0:T(8,128)(2,1)S(1)}, u32[]{:S(2)}, u32[]{:S(2)}) collective-permute-start(bf16[32,4096]{1,0:T(8,128)(2,1)S(1)} %get-tuple-element.849), channel_id=1, source_target_pairs={{16,0},{32,16},{48,32},{64,48},{80,64},{96,80},{112,96},{17,1},{33... | collective-permute-start | bytes 786440 | tf_op jit(solution)/shard_map/while/body/eval_jaxpr/ppermute | solution.py:12
  594.7 12.5 %all-to-all-start.2 = ((bf16[16,4,4096]{2,1,0:T(4,128)(2,1)}), bf16[16,4,4096]{2,1,0:T(4,128)(2,1)S(1)}, u32[]{:S(2)}, u32[]{:S(2)}) async-start(bf16[16,4,4096]{2,1,0:T(4,128)(2,1)} %copy.66), calls=%async_computation.2 | async-start | bytes 1048576 | tf_op jit(solution)/shard_map/while/body/eval_jaxpr/all_to_all | solution.py:199
  608.3 12.5 %all-to-all-start.3 = ((bf16[16,4,4096]{2,1,0:T(4,128)(2,1)}), bf16[16,4,4096]{2,1,0:T(4,128)(2,1)S(1)}, u32[]{:S(2)}, u32[]{:S(2)}) async-start(bf16[16,4,4096]{2,1,0:T(4,128)(2,1)} %get-tuple-element.991), calls=%async_computation.3 | async-start | bytes 1048576 | tf_op jit(solution)/shard_map/while/body/eval_jaxpr/all_to_all | solution.py:73
  622.2 10.0 collective-permute-start.1
  636.5 12.5 %all-to-all-start.2 = ((bf16[16,4,4096]{2,1,0:T(4,128)(2,1)}), bf16[16,4,4096]{2,1,0:T(4,128)(2,1)S(1)}, u32[]{:S(2)}, u32[]{:S(2)}) async-start(bf16[16,4,4096]{2,1,0:T(4,128)(2,1)} %copy.66), calls=%async_computation.2 | async-start | bytes 1048576 | tf_op jit(solution)/shard_map/while/body/eval_jaxpr/all_to_all | solution.py:199
  650.0 12.5 %all-to-all-start.3 = ((bf16[16,4,4096]{2,1,0:T(4,128)(2,1)}), bf16[16,4,4096]{2,1,0:T(4,128)(2,1)S(1)}, u32[]{:S(2)}, u32[]{:S(2)}) async-start(bf16[16,4,4096]{2,1,0:T(4,128)(2,1)} %get-tuple-element.991), calls=%async_computation.3 | async-start | bytes 1048576 | tf_op jit(solution)/shard_map/while/body/eval_jaxpr/all_to_all | solution.py:73
  663.9 10.9 collective-permute-start.1
  679.2 12.5 %all-to-all-start.2 = ((bf16[16,4,4096]{2,1,0:T(4,128)(2,1)}), bf16[16,4,4096]{2,1,0:T(4,128)(2,1)S(1)}, u32[]{:S(2)}, u32[]{:S(2)}) async-start(bf16[16,4,4096]{2,1,0:T(4,128)(2,1)} %copy.66), calls=%async_computation.2 | async-start | bytes 1048576 | tf_op jit(solution)/shard_map/while/body/eval_jaxpr/all_to_all | solution.py:199
  692.8 12.5 %all-to-all-start.3 = ((bf16[16,4,4096]{2,1,0:T(4,128)(2,1)}), bf16[16,4,4096]{2,1,0:T(4,128)(2,1)S(1)}, u32[]{:S(2)}, u32[]{:S(2)}) async-start(bf16[16,4,4096]{2,1,0:T(4,128)(2,1)} %get-tuple-element.991), calls=%async_computation.3 | async-start | bytes 1048576 | tf_op jit(solution)/shard_map/while/body/eval_jaxpr/all_to_all | solution.py:73
  706.7 9.7 collective-permute-start.1
  720.7 12.5 %all-to-all-start.2 = ((bf16[16,4,4096]{2,1,0:T(4,128)(2,1)}), bf16[16,4,4096]{2,1,0:T(4,128)(2,1)S(1)}, u32[]{:S(2)}, u32[]{:S(2)}) async-start(bf16[16,4,4096]{2,1,0:T(4,128)(2,1)} %copy.66), calls=%async_computation.2 | async-start | bytes 1048576 | tf_op jit(solution)/shard_map/while/body/eval_jaxpr/all_to_all | solution.py:199
  734.3 12.5 %all-to-all-start.3 = ((bf16[16,4,4096]{2,1,0:T(4,128)(2,1)}), bf16[16,4,4096]{2,1,0:T(4,128)(2,1)S(1)}, u32[]{:S(2)}, u32[]{:S(2)}) async-start(bf16[16,4,4096]{2,1,0:T(4,128)(2,1)} %get-tuple-element.991), calls=%async_computation.3 | async-start | bytes 1048576 | tf_op jit(solution)/shard_map/while/body/eval_jaxpr/all_to_all | solution.py:73
  748.2 11.5 %collective-permute-start.1 = (bf16[32,4096]{1,0:T(8,128)(2,1)S(1)}, bf16[32,4096]{1,0:T(8,128)(2,1)S(1)}, u32[]{:S(2)}, u32[]{:S(2)}) collective-permute-start(bf16[32,4096]{1,0:T(8,128)(2,1)S(1)} %get-tuple-element.849), channel_id=1, source_target_pairs={{16,0},{32,16},{48,32},{64,48},{80,64},{96,80},{112,96},{17,1},{33... | collective-permute-start | bytes 786440 | tf_op jit(solution)/shard_map/while/body/eval_jaxpr/ppermute | solution.py:12
  764.0 12.5 %all-to-all-start.2 = ((bf16[16,4,4096]{2,1,0:T(4,128)(2,1)}), bf16[16,4,4096]{2,1,0:T(4,128)(2,1)S(1)}, u32[]{:S(2)}, u32[]{:S(2)}) async-start(bf16[16,4,4096]{2,1,0:T(4,128)(2,1)} %copy.66), calls=%async_computation.2 | async-start | bytes 1048576 | tf_op jit(solution)/shard_map/while/body/eval_jaxpr/all_to_all | solution.py:199
  777.5 12.5 %all-to-all-start.3 = ((bf16[16,4,4096]{2,1,0:T(4,128)(2,1)}), bf16[16,4,4096]{2,1,0:T(4,128)(2,1)S(1)}, u32[]{:S(2)}, u32[]{:S(2)}) async-start(bf16[16,4,4096]{2,1,0:T(4,128)(2,1)} %get-tuple-element.991), calls=%async_computation.3 | async-start | bytes 1048576 | tf_op jit(solution)/shard_map/while/body/eval_jaxpr/all_to_all | solution.py:73
  791.4 71.7 %collective-permute-start.1 = (bf16[32,4096]{1,0:T(8,128)(2,1)S(1)}, bf16[32,4096]{1,0:T(8,128)(2,1)S(1)}, u32[]{:S(2)}, u32[]{:S(2)}) collective-permute-start(bf16[32,4096]{1,0:T(8,128)(2,1)S(1)} %get-tuple-element.849), channel_id=1, source_target_pairs={{16,0},{32,16},{48,32},{64,48},{80,64},{96,80},{112,96},{17,1},{33... | collective-permute-start | bytes 786440 | tf_op jit(solution)/shard_map/while/body/eval_jaxpr/ppermute | solution.py:12
  867.5 12.5 %all-to-all-start.2 = ((bf16[16,4,4096]{2,1,0:T(4,128)(2,1)}), bf16[16,4,4096]{2,1,0:T(4,128)(2,1)S(1)}, u32[]{:S(2)}, u32[]{:S(2)}) async-start(bf16[16,4,4096]{2,1,0:T(4,128)(2,1)} %copy.66), calls=%async_computation.2 | async-start | bytes 1048576 | tf_op jit(solution)/shard_map/while/body/eval_jaxpr/all_to_all | solution.py:199
  891.9 12.5 %all-to-all-start.3 = ((bf16[16,4,4096]{2,1,0:T(4,128)(2,1)}), bf16[16,4,4096]{2,1,0:T(4,128)(2,1)S(1)}, u32[]{:S(2)}, u32[]{:S(2)}) async-start(bf16[16,4,4096]{2,1,0:T(4,128)(2,1)} %get-tuple-element.991), calls=%async_computation.3 | async-start | bytes 1048576 | tf_op jit(solution)/shard_map/while/body/eval_jaxpr/all_to_all | solution.py:73
  905.8 8.7 collective-permute-start.1
  918.8 12.5 %all-to-all-start.2 = ((bf16[16,4,4096]{2,1,0:T(4,128)(2,1)}), bf16[16,4,4096]{2,1,0:T(4,128)(2,1)S(1)}, u32[]{:S(2)}, u32[]{:S(2)}) async-start(bf16[16,4,4096]{2,1,0:T(4,128)(2,1)} %copy.66), calls=%async_computation.2 | async-start | bytes 1048576 | tf_op jit(solution)/shard_map/while/body/eval_jaxpr/all_to_all | solution.py:199
  943.2 12.5 %all-to-all-start.3 = ((bf16[16,4,4096]{2,1,0:T(4,128)(2,1)}), bf16[16,4,4096]{2,1,0:T(4,128)(2,1)S(1)}, u32[]{:S(2)}, u32[]{:S(2)}) async-start(bf16[16,4,4096]{2,1,0:T(4,128)(2,1)} %get-tuple-element.991), calls=%async_computation.3 | async-start | bytes 1048576 | tf_op jit(solution)/shard_map/while/body/eval_jaxpr/all_to_all | solution.py:73
  957.1 8.7 collective-permute-start.1
  970.1 12.5 %all-to-all-start.2 = ((bf16[16,4,4096]{2,1,0:T(4,128)(2,1)}), bf16[16,4,4096]{2,1,0:T(4,128)(2,1)S(1)}, u32[]{:S(2)}, u32[]{:S(2)}) async-start(bf16[16,4,4096]{2,1,0:T(4,128)(2,1)} %copy.66), calls=%async_computation.2 | async-start | bytes 1048576 | tf_op jit(solution)/shard_map/while/body/eval_jaxpr/all_to_all | solution.py:199
  994.5 12.5 %all-to-all-start.3 = ((bf16[16,4,4096]{2,1,0:T(4,128)(2,1)}), bf16[16,4,4096]{2,1,0:T(4,128)(2,1)S(1)}, u32[]{:S(2)}, u32[]{:S(2)}) async-start(bf16[16,4,4096]{2,1,0:T(4,128)(2,1)} %get-tuple-element.991), calls=%async_computation.3 | async-start | bytes 1048576 | tf_op jit(solution)/shard_map/while/body/eval_jaxpr/all_to_all | solution.py:73
  1008.4 8.6 collective-permute-start.1
  1021.4 12.5 %all-to-all-start.2 = ((bf16[16,4,4096]{2,1,0:T(4,128)(2,1)}), bf16[16,4,4096]{2,1,0:T(4,128)(2,1)S(1)}, u32[]{:S(2)}, u32[]{:S(2)}) async-start(bf16[16,4,4096]{2,1,0:T(4,128)(2,1)} %copy.66), calls=%async_computation.2 | async-start | bytes 1048576 | tf_op jit(solution)/shard_map/while/body/eval_jaxpr/all_to_all | solution.py:199
  1045.8 12.5 %all-to-all-start.3 = ((bf16[16,4,4096]{2,1,0:T(4,128)(2,1)}), bf16[16,4,4096]{2,1,0:T(4,128)(2,1)S(1)}, u32[]{:S(2)}, u32[]{:S(2)}) async-start(bf16[16,4,4096]{2,1,0:T(4,128)(2,1)} %get-tuple-element.991), calls=%async_computation.3 | async-start | bytes 1048576 | tf_op jit(solution)/shard_map/while/body/eval_jaxpr/all_to_all | solution.py:73
  1059.7 7.7 collective-permute-start.1
  1071.7 12.5 %all-to-all-start.2 = ((bf16[16,4,4096]{2,1,0:T(4,128)(2,1)}), bf16[16,4,4096]{2,1,0:T(4,128)(2,1)S(1)}, u32[]{:S(2)}, u32[]{:S(2)}) async-start(bf16[16,4,4096]{2,1,0:T(4,128)(2,1)} %copy.66), calls=%async_computation.2 | async-start | bytes 1048576 | tf_op jit(solution)/shard_map/while/body/eval_jaxpr/all_to_all | solution.py:199
  1085.3 12.5 %all-to-all-start.3 = ((bf16[16,4,4096]{2,1,0:T(4,128)(2,1)}), bf16[16,4,4096]{2,1,0:T(4,128)(2,1)S(1)}, u32[]{:S(2)}, u32[]{:S(2)}) async-start(bf16[16,4,4096]{2,1,0:T(4,128)(2,1)} %get-tuple-element.991), calls=%async_computation.3 | async-start | bytes 1048576 | tf_op jit(solution)/shard_map/while/body/eval_jaxpr/all_to_all | solution.py:73
  1099.2 12.0 %collective-permute-start.1 = (bf16[32,4096]{1,0:T(8,128)(2,1)S(1)}, bf16[32,4096]{1,0:T(8,128)(2,1)S(1)}, u32[]{:S(2)}, u32[]{:S(2)}) collective-permute-start(bf16[32,4096]{1,0:T(8,128)(2,1)S(1)} %get-tuple-element.849), channel_id=1, source_target_pairs={{16,0},{32,16},{48,32},{64,48},{80,64},{96,80},{112,96},{17,1},{33... | collective-permute-start | bytes 786440 | tf_op jit(solution)/shard_map/while/body/eval_jaxpr/ppermute | solution.py:12
  (19 other events, 74.3 us)
